TPU v7x, 32 devices: a whole 2x2x4 slice. The times are simulated.
32 devices in a mesh: req: 8 (over y, x, core), tp: 4 (over z).
Axes of the slice: x: 2, y: 2, z: 4, core: 2. Of those that a mesh axis runs over, the one named last changes fastest.
Arguments:
- residual: bfloat16 [2048, 2048], P('req', 'tp'), may hold values from -0.29882812 to 0.29882812
- queries: bfloat16 [2048, 1280], P('req', 'tp'), may hold values from -6 to 6
- suffix_kv: bfloat16 [2048, 4, 256], P('req', 'tp'), may hold values from -4 to 4
- prefix_cache: bfloat16 [8192, 4, 256], P('req', 'tp'), may hold values from -6 to 6
- out_weight: bfloat16 [1280, 2048], P('tp'), may hold values from -0.15625 to 0.15625
- norm_gain: bfloat16 [2048], replicated, may hold values from 0.5 to 1.5
- next_query_weight: bfloat16 [2048, 1280], P(None, 'tp'), may hold values from -0.125 to 0.125
- lengths: int32 [8, 4], P('req'), may hold values from 1 to 128, 256 in all within a row
- tenant: int32 [8, 4], P('req'), may hold values from 0 to 3
- owners: int32 [4], replicated, may hold values from 0 to 7, as said below
Outputs:
- new_residual: bfloat16 [2048, 2048], P('req', 'tp')
- next_queries: bfloat16 [2048, 1280], P('req', 'tp')
Inputs may be any that keep to these rules, and one draw needn't show every extreme that they name: `lengths`: each device's 4 requests fill its 256 rows in order. `owners`: distinct.
All inputs are finite; a program needn't handle non-finite values.
Results may differ from a plain program's by a relative error of at most 0.0065.
Values may be sent and summed in bfloat16 or wider, within the bound.
No kernel may reach another device: no remote copies, remote signals or barrier semaphores. Data moves between devices by JAX's collectives and lax.ppermute only.
A program may use at most 64 MiB of HBM per device.

v0:
```python
import jax
import jax.numpy as jnp
from jax import lax
from jax.sharding import PartitionSpec as P

QH = 20
KVH = 5
HD = 64
TENANTS = 4


def from_root(block, axis, source):
    block = jnp.where(lax.axis_index(axis) == source, block, jnp.zeros_like(block))
    return lax.psum(block, axis)


def pick_heads(pair_rows, select):
    split_pair = pair_rows.reshape(pair_rows.shape[0], 2, 2, HD)
    key_heads = jnp.einsum(
        "njd,hj->nhd", split_pair[:, :, 0], select, preferred_element_type=jnp.float32
    ).astype(jnp.bfloat16)
    value_heads = jnp.einsum(
        "njd,hj->nhd", split_pair[:, :, 1], select, preferred_element_type=jnp.float32
    ).astype(jnp.bfloat16)
    return (key_heads, value_heads)


def local(
    residual,
    queries,
    suffix_kv,
    prefix_cache,
    out_weight,
    norm_gain,
    next_query_weight,
    lengths,
    tenant,
    owners,
):
    row_count = queries.shape[0]
    head_count = queries.shape[1] // HD
    tp_index = lax.axis_index("tp")
    head_ids = tp_index * head_count + jnp.arange(head_count, dtype=jnp.int32)
    pair_ids = head_ids // (QH // KVH) - tp_index
    select = (pair_ids[:, None] == jnp.arange(2, dtype=jnp.int32)[None, :]).astype(jnp.bfloat16)
    req_lengths = lengths[0]
    req_tenant = tenant[0]
    req_ends = jnp.cumsum(req_lengths)
    req_starts = req_ends - req_lengths
    position = jnp.arange(row_count, dtype=jnp.int32)
    request_ids = jnp.sum((position[:, None] >= req_ends[None, :]).astype(jnp.int32), axis=1)
    member = request_ids[:, None] == jnp.arange(req_lengths.shape[0], dtype=jnp.int32)[None, :]
    row_start = jnp.sum(jnp.where(member, req_starts[None, :], 0), axis=1)
    row_tenant = jnp.sum(jnp.where(member, req_tenant[None, :], 0), axis=1)
    score_scale = HD ** (-0.5)
    query_heads = queries.reshape(row_count, head_count, HD)
    suffix_keys, suffix_values = pick_heads(suffix_kv.reshape(row_count, -1), select)
    suffix_scores = (
        jnp.einsum("rhd,khd->hrk", query_heads, suffix_keys, preferred_element_type=jnp.float32)
        * score_scale
    )
    suffix_mask = (
        (position[None, :] >= row_start[:, None]) & (position[None, :] <= position[:, None])
    )[None]
    own_slot = prefix_cache.reshape(prefix_cache.shape[0], -1)
    prefix_blocks = [from_root(own_slot, "req", owners[tenant_id]) for tenant_id in range(TENANTS)]
    picked = [pick_heads(block_rows, select) for block_rows in prefix_blocks]
    row_top = jnp.max(jnp.where(suffix_mask, suffix_scores, -jnp.inf), axis=2)
    for tenant_id in range(TENANTS):
        tenant_mask = (row_tenant == tenant_id)[None, :, None]
        prefix_scores = (
            jnp.einsum(
                "rhd,phd->hrp",
                query_heads,
                picked[tenant_id][0],
                preferred_element_type=jnp.float32,
            )
            * score_scale
        )
        row_top = jnp.maximum(
            row_top, jnp.max(jnp.where(tenant_mask, prefix_scores, -jnp.inf), axis=2)
        )
    suffix_weights = jnp.where(suffix_mask, jnp.exp(suffix_scores - row_top[:, :, None]), 0.0)
    denominator = jnp.sum(suffix_weights, axis=2)
    accumulated = jnp.einsum(
        "hrk,khd->rhd",
        suffix_weights.astype(jnp.bfloat16),
        suffix_values,
        preferred_element_type=jnp.float32,
    )
    for tenant_id in range(TENANTS):
        tenant_mask = (row_tenant == tenant_id)[None, :, None]
        prefix_scores = (
            jnp.einsum(
                "rhd,phd->hrp",
                query_heads,
                picked[tenant_id][0],
                preferred_element_type=jnp.float32,
            )
            * score_scale
        )
        prefix_weights = jnp.where(tenant_mask, jnp.exp(prefix_scores - row_top[:, :, None]), 0.0)
        denominator = denominator + jnp.sum(prefix_weights, axis=2)
        accumulated = accumulated + jnp.einsum(
            "hrp,phd->rhd",
            prefix_weights.astype(jnp.bfloat16),
            picked[tenant_id][1],
            preferred_element_type=jnp.float32,
        )
    attended = (
        (accumulated / jnp.transpose(denominator)[:, :, None])
        .astype(jnp.bfloat16)
        .reshape(row_count, -1)
    )
    partial_sums = jnp.dot(attended, out_weight, preferred_element_type=jnp.float32)
    width = residual.shape[1]
    full_sums = lax.psum(partial_sums, "tp")
    full_residual = lax.all_gather(residual, "tp", axis=1, tiled=True)
    full_new = (full_residual.astype(jnp.float32) + full_sums).astype(jnp.bfloat16)
    widened = full_new.astype(jnp.float32)
    mean_square = jnp.mean(widened * widened, axis=1, keepdims=True)
    normed = (widened * lax.rsqrt(mean_square + 1e-05) * norm_gain.astype(jnp.float32)).astype(
        jnp.bfloat16
    )
    next_sums = jnp.dot(normed, next_query_weight, preferred_element_type=jnp.float32)
    new_residual = lax.dynamic_slice_in_dim(full_new, tp_index * width, width, 1)
    return (new_residual, next_sums.astype(jnp.bfloat16))


def solution(mesh):
    return jax.shard_map(
        local,
        mesh=mesh,
        in_specs=(
            P("req", "tp"),
            P("req", "tp"),
            P("req", "tp", None),
            P("req", "tp", None),
            P("tp", None),
            P(),
            P(None, "tp"),
            P("req", None),
            P("req", None),
            P(),
        ),
        out_specs=(P("req", "tp"), P("req", "tp")),
        check_vma=False,
    )
```

profile of v0, /device:TPU:8, one launch (start us, length us, event | category | flops | bytes accessed | tf_op | source)
XLA Modules:
  0.0 198.8 jit_solution(11461890090996612394)
XLA Ops:
  8.0 0.0 copy-start
  8.1 0.0 all-reduce.6.cloned.1.call-start
  8.1 1.5 fusion.93
  12.2 1.2 copy.31
  13.4 1.4 broadcast_select_fusion.3
  14.8 0.0 all-reduce.6.cloned.1.call-update
  14.8 0.0 all-gather.2.cloned.1.call-start
  14.8 0.5 all-gather.2.cloned.1.call-update
  15.4 0.0 all-reduce.4.cloned.1.call-start
  15.4 0.0 copy-done.6
  15.5 0.2 reduce-window.4
  15.6 0.1 convert_reduce_fusion
  15.7 0.1 select_reduce_fusion.6
  15.8 0.1 copy.27
  16.0 0.3 fusion.26
  16.3 0.3 fusion.25
  16.6 0.0 copy-done.1
  16.6 0.4 select_reduce_fusion.4
  17.0 61.0 %all-reduce.6.cloned.1.call-done = (bf16[1024,2,2,64]{0,3,2,1:T(8,128)(2,1)}, bf16[1024,2,2,64]{0,3,2,1:T(8,128)(2,1)}, bf16[1024,2,2,64]{0,3,2,1:T(8,128)(2,1)}, bf16[1024,2,2,64]{0,3,2,1:T(8,128)(2,1)}) async-done(((bf16[1024,2,2,64]{0,3,2,1:T(8,128)(2,1)}, bf16[1024,2,2,64]{0,3,2,1:T(8,128)(2,1)}, bf16[1024,2,2,64]{0,3,2,1:T(8,128)(2,1)}, bf16[1024,2,2,64]{0,3,2,1:T(8,128)(2,1)}), ...) | async-done | bytes 2097168 | tf_op jit(solution)/shard_map/psum | solution.py:14
  78.0 1.3 slice_bitcast_fusion.2
  79.3 0.5 fusion.13
  79.8 0.5 fusion.12
  80.3 1.3 slice_bitcast_fusion
  81.6 0.5 fusion.14
  82.1 0.5 fusion.15
  82.6 0.5 fusion.16
  83.2 0.5 fusion.17
  83.7 0.5 fusion.18
  84.2 0.5 fusion.19
  84.7 1.3 select_reduce_fusion.2
  86.1 1.3 select_reduce_fusion.3
  87.4 1.3 select_reduce_fusion.1
  88.8 1.3 select_reduce_fusion
  90.2 0.2 fusion.28
  90.4 1.6 fusion
  92.0 1.4 fusion.1
  93.5 4.1 %bitcast_reduce_fusion.3 = (f32[5,256]{1,0:T(8,128)S(1)}, f32[5,256]{1,0:T(8,128)S(1)}, f32[5,256]{1,0:T(8,128)S(1)}, f32[5,256]{1,0:T(8,128)S(1)}) fusion(f32[5,1024,256]{2,1,0:T(8,128)S(1)} %get-tuple-element.45, f32[5,256]{1,0:T(8,128)S(1)} %maximum_maximum_fusion, pred[256]{0:T(512)(128)(4,1)S(1)} %get-tuple-element.28, ...), kind=kLoop, calls=%fused_computation.6 | loop fusion | flops 20966400 | bytes 20998144 | tf_op jit(solution)/shard_map/reduce_sum | solution.py:103
  97.6 1.4 fusion.2
  99.0 1.4 fusion.3
  100.5 0.3 fusion.27
  100.8 0.0 copy-start.5
  100.8 2.0 %fusion.94 = f32[256,2048]{1,0:T(8,128)} fusion(bf16[256,320]{0,1:T(8,128)(2,1)S(1)} %bitcast.125, bf16[320,2048]{1,0:T(8,128)(2,1)S(1)} %copy-done), kind=kOutput, calls=%fused_computation.161 | convolution fusion | flops 335544320 | bytes 3571712 | tf_op jit(solution)/shard_map/dot_general | solution.py:115
  102.9 0.0 all-reduce.4.cloned.1.call-update
  102.9 0.0 all-gather.2.cloned.1.call-done
  103.0 84.2 %all-reduce.4.cloned.1.call-done = f32[256,2048]{1,0:T(8,128)} async-done(((f32[256,2048]{1,0:T(8,128)}), f32[256,2048]{1,0:T(8,128)}) %all-reduce.4.cloned.1.call-update) | async-done | bytes 2097168 | tf_op jit(solution)/shard_map/psum | solution.py:117
  187.1 2.2 %fusion.8 = (f32[256]{0:T(256)S(1)}, bf16[256,2048]{1,0:T(8,128)(2,1)S(1)}) fusion(f32[256,2048]{1,0:T(8,128)} %all-reduce.4.cloned.1.call-done, bf16[256,2048]{1,0:T(8,128)(2,1)} %all-gather.2.cloned.1.call-done), kind=kLoop, calls=%fused_computation.26 | loop fusion | flops 3145472 | bytes 4195328 | tf_op jit(solution)/shard_map/reduce_sum | solution.py:121
  189.4 0.7 constant_dynamic-slice_fusion
  190.1 1.3 convolution_convert_fusion.10
  (19 shorter events, 0.1 us)
Async XLA Ops:
  8.0 92.8 %copy-start = (bf16[320,2048]{1,0:T(8,128)(2,1)S(1)}, bf16[320,2048]{1,0:T(8,128)(2,1)}, u32[]{:S(2)}) copy-start(bf16[320,2048]{1,0:T(8,128)(2,1)} %param.14) | copy-start | bytes 3932164
  8.0 7.4 %copy-start.6 = (s32[1,4]{1,0:T(1,128)S(1)}, s32[1,4]{1,0:T(1,128)}, u32[]{:S(2)}) copy-start(s32[1,4]{1,0:T(1,128)} %param.17) | copy-start | bytes 52
  8.0 7.7 %copy-start.4 = (s32[1,4]{1,0:T(1,128)S(1)}, s32[1,4]{1,0:T(1,128)}, u32[]{:S(2)}) copy-start(s32[1,4]{1,0:T(1,128)} %param.18) | copy-start | bytes 52
  8.0 7.8 %copy-start.2 = (bf16[256,1,256]{2,0,1:T(8,128)(2,1)S(1)}, bf16[256,1,256]{2,0,1:T(8,128)(2,1)}, u32[]{:S(2)}) copy-start(bf16[256,1,256]{2,0,1:T(8,128)(2,1)} %param.12) | copy-start | bytes 393220
  8.0 8.5 %copy-start.1 = (bf16[256,320]{0,1:T(8,128)(2,1)S(1)}, bf16[256,320]{0,1:T(8,128)(2,1)}, u32[]{:S(2)}) copy-start(bf16[256,320]{0,1:T(8,128)(2,1)} %param.11) | copy-start | bytes 491524
  8.1 69.9 %all-reduce.6.cloned.1.call-start = ((), (), s32[]{:S(2)}) async-start(), calls=%async_computation.2 | async-start | bytes 4194304 | tf_op jit(solution)/shard_map/psum | solution.py:14
  14.8 88.2 %all-gather.2.cloned.1.call-start = ((), (), s32[]{:S(2)}) async-start(), calls=%async_computation | async-start | bytes 1310720 | tf_op jit(solution)/shard_map/all_gather | solution.py:118
  15.4 171.8 %all-reduce.4.cloned.1.call-start = ((), (), s32[]{:S(2)}) async-start(), calls=%async_computation.1 | async-start | bytes 4194304 | tf_op jit(solution)/shard_map/psum | solution.py:117
  100.5 2.4 %copy-start.3 = (bf16[2048]{0:T(1024)(128)(2,1)S(1)}, bf16[2048]{0:T(1024)(128)(2,1)}, u32[]{:S(2)}) copy-start(bf16[2048]{0:T(1024)(128)(2,1)} %param.15) | copy-start | bytes 12292
  100.8 89.3 %copy-start.5 = (bf16[2048,320]{0,1:T(8,128)(2,1)S(1)}, bf16[2048,320]{0,1:T(8,128)(2,1)}, u32[]{:S(2)}) copy-start(bf16[2048,320]{0,1:T(8,128)(2,1)} %param.16) | copy-start | bytes 3932164
Sparse Core Ops, SparseCore 0:
  14.9 63.0 all-reduce.5
Sparse Core Ops, SparseCore 1:
  16.8 29.0 all-gather.1
  103.0 84.1 all-reduce.3
where the time goes:
time: 202 us; the launch traced here: 199 us
  waiting for transfers between devices  146 us (72%)
  matrix products  20.1 us (10%)
  between operations  18.3 us (9%)
  other arithmetic  8.42 us (4%)
  local copies, waits for them, and re-layouts  6.14 us (3%)
    psum x1, waiting for transfers between devices, local(): full_sums = lax.psum(partial_sums, 'tp')  84.2 us
    psum x1, waiting for transfers between devices, from_root(): return lax.psum(block, axis)  61 us
    dot_general x4, matrix products, local(): jnp.einsum('hrp,phd->rhd', prefix_weights.astype(jnp.bfloat16), picked[te...  5.93 us
    dot_general x4, matrix products, local(): jnp.einsum('rhd,phd->hrp', query_heads, picked[tenant_id][0], preferred_e...  5.38 us
    reduce_sum x1, other arithmetic, local(): denominator = denominator + jnp.sum(prefix_weights, axis=2)  4.12 us
  transfers between devices with their start and end apart: 3, of which 2 were waited for; matrix products, arithmetic and copies ran while one was open for 13% of the time, Pallas kernels for 0%

commit v1 on v0

--- a/solution.py
+++ b/solution.py
@@ -7,6 +7,7 @@
 KVH = 5
 HD = 64
 TENANTS = 4
+GATHER_SLOTS_MAX = 16
 
 
 def from_root(block, axis, source):
@@ -25,6 +26,22 @@
     return (key_heads, value_heads)
 
 
+def tenant_prefixes(own_slot, owners, n_req):
+    slot_rows = own_slot.shape[0]
+    if n_req <= GATHER_SLOTS_MAX:
+        every_slot = lax.all_gather(own_slot, "req", axis=0, tiled=True)
+        return [
+            lax.dynamic_slice_in_dim(every_slot, owners[tenant_id] * slot_rows, slot_rows, 0)
+            for tenant_id in range(TENANTS)
+        ]
+    return [from_root(own_slot, "req", owners[tenant_id]) for tenant_id in range(TENANTS)]
+
+
+def shifted(block, shift, n_tp):
+    pairs = [(source, (source + shift) % n_tp) for source in range(n_tp)]
+    return lax.ppermute(block, "tp", pairs)
+
+
 def local(
     residual,
     queries,
@@ -36,10 +53,20 @@
     lengths,
     tenant,
     owners,
+    n_req,
+    n_tp,
 ):
     row_count = queries.shape[0]
     head_count = queries.shape[1] // HD
+    width = residual.shape[1]
     tp_index = lax.axis_index("tp")
+
+    weight_pieces = []
+    for shift in range(n_tp):
+        target = (tp_index + shift) % n_tp
+        piece = lax.dynamic_slice_in_dim(out_weight, target * width, width, 1)
+        weight_pieces.append(piece if shift == 0 else shifted(piece, shift, n_tp))
+
     head_ids = tp_index * head_count + jnp.arange(head_count, dtype=jnp.int32)
     pair_ids = head_ids // (QH // KVH) - tp_index
     select = (pair_ids[:, None] == jnp.arange(2, dtype=jnp.int32)[None, :]).astype(jnp.bfloat16)
@@ -63,7 +90,7 @@
         (position[None, :] >= row_start[:, None]) & (position[None, :] <= position[:, None])
     )[None]
     own_slot = prefix_cache.reshape(prefix_cache.shape[0], -1)
-    prefix_blocks = [from_root(own_slot, "req", owners[tenant_id]) for tenant_id in range(TENANTS)]
+    prefix_blocks = tenant_prefixes(own_slot, owners, n_req)
     picked = [pick_heads(block_rows, select) for block_rows in prefix_blocks]
     row_top = jnp.max(jnp.where(suffix_mask, suffix_scores, -jnp.inf), axis=2)
     for tenant_id in range(TENANTS):
@@ -112,24 +139,34 @@
         .astype(jnp.bfloat16)
         .reshape(row_count, -1)
     )
-    partial_sums = jnp.dot(attended, out_weight, preferred_element_type=jnp.float32)
-    width = residual.shape[1]
-    full_sums = lax.psum(partial_sums, "tp")
-    full_residual = lax.all_gather(residual, "tp", axis=1, tiled=True)
-    full_new = (full_residual.astype(jnp.float32) + full_sums).astype(jnp.bfloat16)
+
+    projected = jnp.dot(attended, weight_pieces[0], preferred_element_type=jnp.float32)
+    for shift in range(1, n_tp):
+        head_block = shifted(attended, shift, n_tp)
+        projected = projected + jnp.dot(
+            head_block, weight_pieces[shift], preferred_element_type=jnp.float32
+        )
+    new_residual = (residual.astype(jnp.float32) + projected).astype(jnp.bfloat16)
+
+    full_new = lax.all_gather(new_residual, "tp", axis=1, tiled=True)
     widened = full_new.astype(jnp.float32)
     mean_square = jnp.mean(widened * widened, axis=1, keepdims=True)
     normed = (widened * lax.rsqrt(mean_square + 1e-05) * norm_gain.astype(jnp.float32)).astype(
         jnp.bfloat16
     )
     next_sums = jnp.dot(normed, next_query_weight, preferred_element_type=jnp.float32)
-    new_residual = lax.dynamic_slice_in_dim(full_new, tp_index * width, width, 1)
     return (new_residual, next_sums.astype(jnp.bfloat16))
 
 
 def solution(mesh):
+    n_req = mesh.shape["req"]
+    n_tp = mesh.shape["tp"]
+
+    def body(*args):
+        return local(*args, n_req=n_req, n_tp=n_tp)
+
     return jax.shard_map(
-        local,
+        body,
         mesh=mesh,
         in_specs=(
             P("req", "tp"),

time: 202 us -> 129 us (0.64)
  waiting for transfers between devices: 146 us -> 59 us
  starting transfers between devices: 0.12 us -> 9.25 us
  matrix products: 20.1 us -> 24.9 us
  local copies, waits for them, and re-layouts: 6.14 us -> 8.66 us
    psum x2 -> x0, waiting for transfers between devices: 145 us -> none  [the longest x1 84.2 us: local(): full_sums = lax.psum(partial_sums, 'tp')]
    all_gather x1 -> x2, waiting for transfers between devices: 0.03 us -> 50.6 us  [the longest x1 29 us: local(): full_new = lax.all_gather(new_residual, 'tp', axis=1, tiled=True)]
    ppermute x0 -> x6, starting transfers between devices: none -> 9.18 us  [shifted(): return lax.ppermute(block, 'tp', pairs)]
    ppermute x0 -> x6, waiting for transfers between devices: none -> 8.46 us  [shifted(): return lax.ppermute(block, 'tp', pairs)]
    dynamic_slice x1 -> x2, local copies, waits for them, and re-layouts: 0.73 us -> 3.93 us  [the longest x1 2.2 us: local(): piece = lax.dynamic_slice_in_dim(out_weight, target * width, width, 1)]
    squeeze x3 -> x5, local copies, waits for them, and re-layouts: 2.54 us -> 0.16 us  [pick_heads(): split_pair[:, :, 1]]
  transfers between devices with their start and end apart: 3 -> 8, of which waited for: 2 -> 5; matrix products, arithmetic and copies ran while one was open for 13% -> 27% of each run, Pallas kernels for 0% -> 0%
where the time goes in v1:
time: 129 us; the launch traced here: 127 us
  waiting for transfers between devices  59 us (46%)
  matrix products  24.9 us (19%)
  between operations  17 us (13%)
  starting transfers between devices  9.25 us (7%)
  local copies, waits for them, and re-layouts  8.66 us (7%)
  other arithmetic  8.29 us (6%)
    all_gather x1, waiting for transfers between devices, local(): full_new = lax.all_gather(new_residual, 'tp', axis=1, tiled=True)  29 us
    all_gather x1, waiting for transfers between devices, tenant_prefixes(): every_slot = lax.all_gather(own_slot, 'req', axis=0, tiled=True)  21.5 us
    ppermute x6, starting transfers between devices, shifted(): return lax.ppermute(block, 'tp', pairs)  9.18 us
    ppermute x6, waiting for transfers between devices, shifted(): return lax.ppermute(block, 'tp', pairs)  8.46 us
    dot_general x4, matrix products, local(): jnp.einsum('hrp,phd->rhd', prefix_weights.astype(jnp.bfloat16), picked[te...  5.93 us
    dot_general x4, matrix products, local(): jnp.einsum('rhd,phd->hrp', query_heads, picked[tenant_id][0], preferred_e...  5.4 us
    reduce_sum x1, other arithmetic, local(): denominator = denominator + jnp.sum(prefix_weights, axis=2)  4.12 us
    unnamed x12, local copies, waits for them, and re-layouts  3.16 us
  transfers between devices with their start and end apart: 8, of which 5 were waited for; matrix products, arithmetic and copies ran while one was open for 27% of the time, Pallas kernels for 0%

profile of v1, /device:TPU:8, one launch (start us, length us, event | category | flops | bytes accessed | tf_op | source)
XLA Modules:
  0.0 127.1 jit_solution(14149164900442091874)
XLA Ops:
  7.2 2.1 %copy.28 = bf16[1024,1,256]{0,2,1:T(8,128)(2,1)} copy(bf16[1024,1,256]{2,0,1:T(8,128)(2,1)} %param.13) | data formatting | bytes 1048576 | tf_op args[3]
  9.5 2.2 %constant_dynamic-slice_fusion = (bf16[320,512]{1,0:T(8,128)(2,1)}, bf16[320,512]{1,0:T(8,128)(2,1)}, bf16[320,512]{1,0:T(8,128)(2,1)}) fusion(bf16[320,2048]{1,0:T(8,128)(2,1)} %param.14, s32[]{:T(128)S(6)} %select_n.133, s32[]{:T(128)S(6)} %select_n.131, s32[]{:T(128)S(6)} %select_n.135), kind=kLoop, calls=%fused_computation.119 | loop fusion | bytes 1966092 | tf_op jit(solution)/shard_map/dynamic_slice | solution.py:67
  11.7 1.6 %collective-permute-start.1 = (bf16[320,512]{1,0:T(8,128)(2,1)}, bf16[320,512]{1,0:T(8,128)(2,1)}, u32[]{:S(2)}, u32[]{:S(2)}) collective-permute-start(bf16[320,512]{1,0:T(8,128)(2,1)} %get-tuple-element.13), channel_id=1, source_target_pairs={{0,1},{1,2},{2,3},{3,0},{4,5},{5,6},{6,7},{7,4},{8,9},{9,10},{10,1... | collective-permute-start | bytes 983048 | tf_op jit(solution)/shard_map/ppermute | solution.py:42
  13.3 0.4 collective-permute-start.5
  13.7 2.6 %collective-permute-start.3 = (bf16[320,512]{1,0:T(8,128)(2,1)}, bf16[320,512]{1,0:T(8,128)(2,1)S(1)}, u32[]{:S(2)}, u32[]{:S(2)}) collective-permute-start(bf16[320,512]{1,0:T(8,128)(2,1)} %get-tuple-element.12), channel_id=1, source_target_pairs={{0,2},{1,3},{2,0},{3,1},{4,6},{5,7},{6,4},{7,5},{8,10},{9,11},{10,... | collective-permute-start | bytes 983048 | tf_op jit(solution)/shard_map/ppermute | solution.py:42
  16.3 1.4 %fusion.99 = (s32[1]{0:T(128)}, s32[1]{0:T(128)}, s32[1]{0:T(128)}, s32[1]{0:T(128)}) fusion(s32[4]{0:T(128)} %param.19), kind=kLoop, calls=%fused_computation.169 | loop fusion | bytes 32 | tf_op jit(solution)/shard_map/slice | solution.py:34
  20.2 0.8 reduce-window.4
  21.0 1.0 copy.24
  22.1 0.1 convert_reduce_fusion
  22.2 0.7 fusion.78
  22.8 0.7 select_reduce_fusion.6
  23.7 0.3 fusion.29
  23.9 1.0 fusion.28
  24.9 1.3 %select_reduce_fusion.4 = (f32[5,256]{1,0:T(8,128)S(1)}, f32[5,256,256]{1,2,0:T(8,128)S(1)}) fusion(pred[256,256]{0,1:T(8,128)(4,1)S(1)} %fusion.62, bf16[256,5,64]{0,2,1:T(8,128)(2,1)} %bitcast.120, bf16[256,5,64]{0,1,2:T(8,128)(2,1)S(1)} %fusion.29), kind=kOutput, calls=%fused_computation.48 | convolution fusion | flops 42924800 | bytes 1709056 | tf_op jit(solution)/shard_map/rhd,khd->hrk/dot_general | solution.py:86
  26.3 21.5 %all-gather.6.cloned.1.call-done = bf16[8192,1,256]{0,2,1:T(8,128)(2,1)} async-done(((bf16[1024,1,256]{0,2,1:T(8,128)(2,1)}), bf16[8192,1,256]{0,2,1:T(8,128)(2,1)}) %all-gather.6.cloned.1.call-update) | async-done | bytes 4194320 | tf_op jit(solution)/shard_map/all_gather | solution.py:32
  47.8 1.7 %constant_dynamic-slice_fusion.5 = (bf16[1024,1,256]{0,2,1:T(8,128)(2,1)S(1)}, bf16[1024,1,256]{0,2,1:T(8,128)(2,1)S(1)}, bf16[1024,1,256]{0,2,1:T(8,128)(2,1)S(1)}, bf16[1024,1,256]{0,2,1:T(8,128)(2,1)S(1)}) fusion(bf16[8192,1,256]{0,2,1:T(8,128)(2,1)} %all-gather.6.cloned.1.call-done, s32[]{:T(128)S(6)} %select_n.111, s32[]{:T(128)S(6)} %select_n.115, ...), kind=kLoop, calls=%fused_computation.125 | loop fusion | bytes 4194320 | tf_op jit(solution)/shard_map/dynamic_slice | solution.py:34
  49.6 0.5 fusion.14
  50.2 0.5 fusion.13
  50.8 0.5 fusion.12
  51.3 0.5 fusion.15
  51.9 0.5 fusion.16
  52.4 0.5 fusion.17
  52.9 0.5 fusion.18
  53.5 1.4 %select_reduce_fusion.1 = (f32[5,256]{1,0:T(8,128)S(1)}, f32[5,1024,256]{2,1,0:T(8,128)S(1)}) fusion(pred[256]{0:T(512)(128)(4,1)S(1)} %get-tuple-element.27, bf16[256,5,64]{0,2,1:T(8,128)(2,1)S(1)} %bitcast.121, bf16[1024,5,64]{0,1,2:T(8,128)(2,1)S(1)} %fusion.14), kind=kOutput, calls=%fused_computation.13 | convolution fusion | flops 171703040 | bytes 6067456 | tf_op jit(solution)/shard_map/rhd,phd->hrp/dot_general | solution.py:99
  54.8 1.3 %select_reduce_fusion.2 = (f32[5,256]{1,0:T(8,128)S(1)}, f32[5,1024,256]{2,1,0:T(8,128)S(1)}) fusion(pred[256]{0:T(512)(128)(4,1)S(1)} %get-tuple-element.28, bf16[256,5,64]{0,2,1:T(8,128)(2,1)S(1)} %bitcast.122, bf16[1024,5,64]{0,1,2:T(8,128)(2,1)S(1)} %fusion.13), kind=kOutput, calls=%fused_computation.14 | convolution fusion | flops 171703040 | bytes 6067456 | tf_op jit(solution)/shard_map/rhd,phd->hrp/dot_general | solution.py:99
  56.2 1.3 %select_reduce_fusion.3 = (f32[5,256]{1,0:T(8,128)S(1)}, f32[5,1024,256]{2,1,0:T(8,128)S(1)}) fusion(pred[256]{0:T(512)(128)(4,1)S(1)} %get-tuple-element.25, bf16[256,5,64]{0,2,1:T(8,128)(2,1)S(1)} %bitcast.123, bf16[1024,5,64]{0,1,2:T(8,128)(2,1)S(1)} %fusion.12), kind=kOutput, calls=%fused_computation.15 | convolution fusion | flops 171703040 | bytes 6067456 | tf_op jit(solution)/shard_map/rhd,phd->hrp/dot_general | solution.py:99
  57.5 1.3 %select_reduce_fusion = (f32[5,256]{1,0:T(8,128)S(1)}, f32[5,1024,256]{2,1,0:T(8,128)S(1)}) fusion(pred[256]{0:T(512)(128)(4,1)S(1)} %get-tuple-element.26, bf16[256,5,64]{0,2,1:T(8,128)(2,1)S(1)} %bitcast.124, bf16[1024,5,64]{0,1,2:T(8,128)(2,1)S(1)} %fusion.15), kind=kOutput, calls=%fused_computation.12 | convolution fusion | flops 171703040 | bytes 6067456 | tf_op jit(solution)/shard_map/rhd,phd->hrp/dot_general | solution.py:99
  58.9 0.2 fusion.31
  59.2 1.4 %fusion = f32[5,64,256]{2,1,0:T(8,128)S(1)} fusion(f32[5,1024,256]{2,1,0:T(8,128)S(1)} %get-tuple-element.42, f32[5,256]{1,0:T(8,128)S(1)} %maximum_maximum_fusion, pred[256]{0:T(512)(128)(4,1)S(1)} %get-tuple-element.25, bf16[1024,5,64]{0,1,2:T(8,128)(2,1)S(1)} %fusion.16), kind=kOutput, calls=%fused_computation.18 | convolution fusion | flops 173015040 | bytes 6231296 | tf_op jit(solution)/shard_map/hrp,phd->rhd/dot_general | solution.py:131
  60.6 1.6 %fusion.1 = f32[5,64,256]{2,1,0:T(8,128)S(1)} fusion(f32[5,1024,256]{2,1,0:T(8,128)S(1)} %get-tuple-element.38, f32[5,256]{1,0:T(8,128)S(1)} %maximum_maximum_fusion, pred[256]{0:T(512)(128)(4,1)S(1)} %get-tuple-element.28, bf16[1024,5,64]{0,1,2:T(8,128)(2,1)S(1)} %fusion.17), kind=kOutput, calls=%fused_computation.19 | convolution fusion | flops 173015040 | bytes 6231296 | tf_op jit(solution)/shard_map/hrp,phd->rhd/dot_general | solution.py:131
  62.2 4.1 %bitcast_reduce_fusion.3 = (f32[5,256]{1,0:T(8,128)S(1)}, f32[5,256]{1,0:T(8,128)S(1)}, f32[5,256]{1,0:T(8,128)S(1)}, f32[5,256]{1,0:T(8,128)S(1)}) fusion(f32[5,1024,256]{2,1,0:T(8,128)S(1)} %get-tuple-element.42, f32[5,256]{1,0:T(8,128)S(1)} %maximum_maximum_fusion, pred[256]{0:T(512)(128)(4,1)S(1)} %get-tuple-element.25, ...), kind=kLoop, calls=%fused_computation.6 | loop fusion | flops 20966400 | bytes 20998144 | tf_op jit(solution)/shard_map/reduce_sum | solution.py:130
  66.3 1.4 %fusion.2 = f32[5,64,256]{2,1,0:T(8,128)S(1)} fusion(f32[5,1024,256]{2,1,0:T(8,128)S(1)} %get-tuple-element.36, f32[5,256]{1,0:T(8,128)S(1)} %maximum_maximum_fusion, pred[256]{0:T(512)(128)(4,1)S(1)} %get-tuple-element.27, bf16[1024,5,64]{0,1,2:T(8,128)(2,1)S(1)} %fusion.18), kind=kOutput, calls=%fused_computation.20 | convolution fusion | flops 173015040 | bytes 6231296 | tf_op jit(solution)/shard_map/hrp,phd->rhd/dot_general | solution.py:131
  67.8 0.5 fusion.19
  68.3 1.4 %fusion.3 = f32[5,64,256]{2,1,0:T(8,128)S(1)} fusion(f32[5,1024,256]{2,1,0:T(8,128)S(1)} %get-tuple-element.34, f32[5,256]{1,0:T(8,128)S(1)} %maximum_maximum_fusion, pred[256]{0:T(512)(128)(4,1)S(1)} %get-tuple-element.26, bf16[1024,5,64]{0,1,2:T(8,128)(2,1)S(1)} %fusion.19), kind=kOutput, calls=%fused_computation.21 | convolution fusion | flops 173015040 | bytes 6231296 | tf_op jit(solution)/shard_map/hrp,phd->rhd/dot_general | solution.py:131
  69.8 0.3 fusion.30
  70.1 1.5 %collective-permute-start = (bf16[256,320]{0,1:T(8,128)(2,1)S(1)}, bf16[256,320]{0,1:T(8,128)(2,1)S(1)}, u32[]{:S(2)}, u32[]{:S(2)}) collective-permute-start(bf16[256,320]{0,1:T(8,128)(2,1)S(1)} %bitcast.130), channel_id=1, source_target_pairs={{0,1},{1,2},{2,3},{3,0},{4,5},{5,6},{6,7},{7,4},{8,9},{9,10},{10,1... | collective-permute-start | bytes 491528 | tf_op jit(solution)/shard_map/ppermute | solution.py:42
  71.7 0.5 collective-permute-start.4
  72.2 1.3 %fusion.52 = f32[256,512]{1,0:T(8,128)S(1)} fusion(bf16[256,320]{0,1:T(8,128)(2,1)S(1)} %bitcast.132, bf16[320,2048]{1,0:T(8,128)(2,1)} %param.14, s32[]{:T(128)S(6)} %select_n.129), kind=kOutput, calls=%fused_computation.85 | convolution fusion | flops 83886080 | bytes 1015812 | tf_op jit(solution)/shard_map/dot_general | solution.py:143
  73.5 2.5 %collective-permute-start.2 = (bf16[256,320]{0,1:T(8,128)(2,1)S(1)}, bf16[256,320]{0,1:T(8,128)(2,1)S(1)}, u32[]{:S(2)}, u32[]{:S(2)}) collective-permute-start(bf16[256,320]{0,1:T(8,128)(2,1)S(1)} %bitcast.133), channel_id=1, source_target_pairs={{0,2},{1,3},{2,0},{3,1},{4,6},{5,7},{6,4},{7,5},{8,10},{9,11},{10,... | collective-permute-start | bytes 491528 | tf_op jit(solution)/shard_map/ppermute | solution.py:42
  76.0 1.2 collective-permute-done
  77.2 1.3 %convolution_add_fusion.1 = f32[256,512]{1,0:T(8,128)S(1)} fusion(f32[256,512]{1,0:T(8,128)S(1)} %fusion.52, bf16[256,320]{0,1:T(8,128)(2,1)S(1)} %collective-permute-done, bf16[320,512]{1,0:T(8,128)(2,1)} %collective-permute-done.1), kind=kOutput, calls=%fused_computation.52 | convolution fusion | flops 84017152 | bytes 1540096 | tf_op jit(solution)/shard_map/dot_general | solution.py:146
  78.5 3.2 %collective-permute-done.4 = bf16[256,320]{0,1:T(8,128)(2,1)S(1)} collective-permute-done((bf16[256,320]{0,1:T(8,128)(2,1)S(1)}, bf16[256,320]{0,1:T(8,128)(2,1)S(1)}, u32[]{:S(2)}, u32[]{:S(2)}) %collective-permute-start.4) | collective-permute-done | bytes 163872 | tf_op jit(solution)/shard_map/ppermute | solution.py:42
  81.7 0.3 fusion.100
  82.0 4.1 %collective-permute-done.2 = bf16[256,320]{0,1:T(8,128)(2,1)S(1)} collective-permute-done((bf16[256,320]{0,1:T(8,128)(2,1)S(1)}, bf16[256,320]{0,1:T(8,128)(2,1)S(1)}, u32[]{:S(2)}, u32[]{:S(2)}) %collective-permute-start.2) | collective-permute-done | bytes 163872 | tf_op jit(solution)/shard_map/ppermute | solution.py:42
  86.1 1.0 fusion.22
  87.2 29.0 %all-gather.4.cloned.1.call-done = bf16[256,2048]{1,0:T(8,128)(2,1)} async-done(((bf16[256,512]{1,0:T(8,128)(2,1)}), bf16[256,2048]{1,0:T(8,128)(2,1)}) %all-gather.4.cloned.1.call-update) | async-done | bytes 1048592 | tf_op jit(solution)/shard_map/all_gather | solution.py:151
  116.2 1.5 %fusion.8 = f32[256]{0:T(256)S(1)} fusion(bf16[256,2048]{1,0:T(8,128)(2,1)} %all-gather.4.cloned.1.call-done), kind=kLoop, calls=%fused_computation.26 | loop fusion | flops 1572608 | bytes 1049600 | tf_op jit(solution)/shard_map/reduce_sum | solution.py:153
  117.7 2.5 %convolution_convert_fusion.10 = bf16[256,320]{0,1:T(8,128)(2,1)} fusion(bf16[2048,320]{0,1:T(8,128)(2,1)S(1)} %copy-done, bf16[256,2048]{1,0:T(8,128)(2,1)} %all-gather.4.cloned.1.call-done, f32[2048]{0:T(1024)S(1)} %convert_element_type.130, f32[256]{0:T(256)S(1)} %add_rsqrt_fusion), kind=kOutput, calls=%fused_computation.65 | convolution fusion | flops 337723392 | bytes 2532352 | tf_op jit(solution)/shard_map/dot_general | solution.py:157
  (29 shorter events, 0.4 us)
Async XLA Ops:
  7.2 110.5 %copy-start = (bf16[2048,320]{0,1:T(8,128)(2,1)S(1)}, bf16[2048,320]{0,1:T(8,128)(2,1)}, u32[]{:S(2)}) copy-start(bf16[2048,320]{0,1:T(8,128)(2,1)} %param.16) | copy-start | bytes 3932164
  7.2 40.7 %all-gather.6.cloned.1.call-start = ((), (), s32[]{:S(2)}) async-start(), calls=%async_computation.1 | async-start | bytes 4718592 | tf_op jit(solution)/shard_map/all_gather | solution.py:32
  9.4 106.8 %all-gather.4.cloned.1.call-start = ((), (), s32[]{:S(2)}) async-start(), calls=%async_computation | async-start | bytes 1310720 | tf_op jit(solution)/shard_map/all_gather | solution.py:151
  11.7 61.8 %collective-permute-start.1 = (bf16[320,512]{1,0:T(8,128)(2,1)}, bf16[320,512]{1,0:T(8,128)(2,1)}, u32[]{:S(2)}, u32[]{:S(2)}) collective-permute-start(bf16[320,512]{1,0:T(8,128)(2,1)} %get-tuple-element.13), channel_id=1, source_target_pairs={{0,1},{1,2},{2,3},{3,0},{4,5},{5,6},{6,7},{7,4},{8,9},{9,10},{10,1... | collective-permute-start | bytes 983048 | tf_op jit(solution)/shard_map/ppermute | solution.py:42
  13.3 65.3 %collective-permute-start.5 = (bf16[320,512]{1,0:T(8,128)(2,1)}, bf16[320,512]{1,0:T(8,128)(2,1)S(1)}, u32[]{:S(2)}, u32[]{:S(2)}) collective-permute-start(bf16[320,512]{1,0:T(8,128)(2,1)} %get-tuple-element.14), channel_id=1, source_target_pairs={{0,3},{1,0},{2,1},{3,2},{4,7},{5,4},{6,5},{7,6},{8,11},{9,8},{10,9... | collective-permute-start | bytes 983048 | tf_op jit(solution)/shard_map/ppermute | solution.py:42
  13.7 68.3 %collective-permute-start.3 = (bf16[320,512]{1,0:T(8,128)(2,1)}, bf16[320,512]{1,0:T(8,128)(2,1)S(1)}, u32[]{:S(2)}, u32[]{:S(2)}) collective-permute-start(bf16[320,512]{1,0:T(8,128)(2,1)} %get-tuple-element.12), channel_id=1, source_target_pairs={{0,2},{1,3},{2,0},{3,1},{4,6},{5,7},{6,4},{7,5},{8,10},{9,11},{10,... | collective-permute-start | bytes 983048 | tf_op jit(solution)/shard_map/ppermute | solution.py:42
  50.2 3.3 %copy-start.1 = (bf16[256,320]{0,1:T(8,128)(2,1)S(1)}, bf16[256,320]{0,1:T(8,128)(2,1)}, u32[]{:S(2)}) copy-start(bf16[256,320]{0,1:T(8,128)(2,1)} %param.11) | copy-start | bytes 491524
  67.8 2.0 %copy-start.2 = (bf16[256,5,64]{0,1,2:T(8,128)(2,1)S(1)}, bf16[256,5,64]{0,1,2:T(8,128)(2,1)}, u32[]{:S(2)}) copy-start(bf16[256,5,64]{0,1,2:T(8,128)(2,1)} %fusion.28) | copy-start | bytes 491524
  69.7 16.4 %copy-start.3 = (bf16[256,512]{1,0:T(8,128)(2,1)S(1)}, bf16[256,512]{1,0:T(8,128)(2,1)}, u32[]{:S(2)}) copy-start(bf16[256,512]{1,0:T(8,128)(2,1)} %param.10) | copy-start | bytes 786436
  69.7 17.4 %copy-start.4 = (bf16[2048]{0:T(1024)(128)(2,1)S(1)}, bf16[2048]{0:T(1024)(128)(2,1)}, u32[]{:S(2)}) copy-start(bf16[2048]{0:T(1024)(128)(2,1)} %param.15) | copy-start | bytes 12292
  70.1 7.1 %collective-permute-start = (bf16[256,320]{0,1:T(8,128)(2,1)S(1)}, bf16[256,320]{0,1:T(8,128)(2,1)S(1)}, u32[]{:S(2)}, u32[]{:S(2)}) collective-permute-start(bf16[256,320]{0,1:T(8,128)(2,1)S(1)} %bitcast.130), channel_id=1, source_target_pairs={{0,1},{1,2},{2,3},{3,0},{4,5},{5,6},{6,7},{7,4},{8,9},{9,10},{10,1... | collective-permute-start | bytes 491528 | tf_op jit(solution)/shard_map/ppermute | solution.py:42
  71.7 10.0 %collective-permute-start.4 = (bf16[256,320]{0,1:T(8,128)(2,1)S(1)}, bf16[256,320]{0,1:T(8,128)(2,1)S(1)}, u32[]{:S(2)}, u32[]{:S(2)}) collective-permute-start(bf16[256,320]{0,1:T(8,128)(2,1)S(1)} %bitcast.131), channel_id=1, source_target_pairs={{0,3},{1,0},{2,1},{3,2},{4,7},{5,4},{6,5},{7,6},{8,11},{9,8},{10,9... | collective-permute-start | bytes 491528 | tf_op jit(solution)/shard_map/ppermute | solution.py:42
  73.5 12.6 %collective-permute-start.2 = (bf16[256,320]{0,1:T(8,128)(2,1)S(1)}, bf16[256,320]{0,1:T(8,128)(2,1)S(1)}, u32[]{:S(2)}, u32[]{:S(2)}) collective-permute-start(bf16[256,320]{0,1:T(8,128)(2,1)S(1)} %bitcast.133), channel_id=1, source_target_pairs={{0,2},{1,3},{2,0},{3,1},{4,6},{5,7},{6,4},{7,5},{8,10},{9,11},{10,... | collective-permute-start | bytes 491528 | tf_op jit(solution)/shard_map/ppermute | solution.py:42
Sparse Core Ops, SparseCore 0:
  9.9 37.8 all-gather.5
  87.3 28.8 all-gather.3

commit v2 on v1

--- a/solution.py
+++ b/solution.py
@@ -26,14 +26,29 @@
     return (key_heads, value_heads)
 
 
+def xor_permute(block, mask, n_req):
+    pairs = [(source, source ^ mask) for source in range(n_req)]
+    return lax.ppermute(block, "req", pairs)
+
+
 def tenant_prefixes(own_slot, owners, n_req):
     slot_rows = own_slot.shape[0]
-    if n_req <= GATHER_SLOTS_MAX:
-        every_slot = lax.all_gather(own_slot, "req", axis=0, tiled=True)
-        return [
-            lax.dynamic_slice_in_dim(every_slot, owners[tenant_id] * slot_rows, slot_rows, 0)
-            for tenant_id in range(TENANTS)
+    if n_req <= GATHER_SLOTS_MAX and n_req % 2 == 0 and (n_req & (n_req - 1)) == 0:
+        n_chips = n_req // 2
+        req_index = lax.axis_index("req")
+        same_core = [own_slot] + [
+            xor_permute(own_slot, 2 * chip_mask, n_req) for chip_mask in range(1, n_chips)
         ]
+        own_stack = jnp.stack(same_core)
+        other_stack = xor_permute(own_stack, 1, n_req)
+        blocks = []
+        for tenant_id in range(TENANTS):
+            owner = owners[tenant_id]
+            position = (owner // 2) ^ (req_index // 2)
+            mine = lax.dynamic_index_in_dim(own_stack, position, 0, keepdims=False)
+            theirs = lax.dynamic_index_in_dim(other_stack, position, 0, keepdims=False)
+            blocks.append(jnp.where(owner % 2 == req_index % 2, mine, theirs))
+        return blocks
     return [from_root(own_slot, "req", owners[tenant_id]) for tenant_id in range(TENANTS)]
 
 

time: 129 us -> 140 us (1.085)
  between operations: 17 us -> 24.8 us
  local copies, waits for them, and re-layouts: 8.66 us -> 6.34 us
  starting transfers between devices: 9.25 us -> 11.2 us
  other arithmetic: 8.29 us -> 9.84 us
    ppermute x0 -> x4, waiting for transfers between devices: none -> 22.6 us  [xor_permute(): return lax.ppermute(block, 'req', pairs)]
    all_gather x1 -> x0, waiting for transfers between devices: 21.5 us -> none  [tenant_prefixes(): every_slot = lax.all_gather(own_slot, 'req', axis=0, tiled=True)]
    ppermute x0 -> x4, starting transfers between devices: none -> 3.63 us  [xor_permute(): return lax.ppermute(block, 'req', pairs)]
    dot_general x3, matrix products: 2.65 us -> 4.59 us  [local(): jnp.dot(head_block, weight_pieces[shift], preferred_element_type=jnp.floa...]
    select_n x0 -> x1, other arithmetic: none -> 1.74 us  [tenant_prefixes(): blocks.append(jnp.where(owner % 2 == req_index % 2, mine, theirs))]
    dynamic_slice x1 -> x0, local copies, waits for them, and re-layouts: 1.74 us -> none  [tenant_prefixes(): lax.dynamic_slice_in_dim(every_slot, owners[tenant_id] * slot_rows, slot_...]
    ppermute x6, starting transfers between devices: 9.18 us -> 7.55 us  [shifted(): return lax.ppermute(block, 'tp', pairs)]
    unnamed x12 -> x24, local copies, waits for them, and re-layouts: 3.16 us -> 3.35 us
  transfers between devices with their start and end apart: 8 -> 11, of which waited for: 5 -> 5; matrix products, arithmetic and copies ran while one was open for 27% -> 23% of each run, Pallas kernels for 0% -> 0%
where the time goes in v2:
time: 140 us; the launch traced here: 138 us
  waiting for transfers between devices  59.9 us (43%)
  matrix products  26.1 us (19%)
  between operations  24.8 us (18%)
  starting transfers between devices  11.2 us (8%)
  other arithmetic  9.84 us (7%)
  local copies, waits for them, and re-layouts  6.34 us (5%)
    all_gather x1, waiting for transfers between devices, local(): full_new = lax.all_gather(new_residual, 'tp', axis=1, tiled=True)  29.1 us
    ppermute x4, waiting for transfers between devices, xor_permute(): return lax.ppermute(block, 'req', pairs)  22.6 us
    ppermute x6, waiting for transfers between devices, shifted(): return lax.ppermute(block, 'tp', pairs)  8.19 us
    ppermute x6, starting transfers between devices, shifted(): return lax.ppermute(block, 'tp', pairs)  7.55 us
    dot_general x4, matrix products, local(): jnp.einsum('hrp,phd->rhd', prefix_weights.astype(jnp.bfloat16), picked[te...  5.93 us
    dot_general x4, matrix products, local(): jnp.einsum('rhd,phd->hrp', query_heads, picked[tenant_id][0], preferred_e...  5.4 us
    dot_general x3, matrix products, local(): jnp.dot(head_block, weight_pieces[shift], preferred_element_type=jnp.floa...  4.59 us
    reduce_sum x1, other arithmetic, local(): denominator = denominator + jnp.sum(prefix_weights, axis=2)  4.12 us
  transfers between devices with their start and end apart: 11, of which 5 were waited for; matrix products, arithmetic and copies ran while one was open for 23% of the time, Pallas kernels for 0%

profile of v2, /device:TPU:8, one launch (start us, length us, event | category | flops | bytes accessed | tf_op | source)
XLA Modules:
  0.0 138.2 jit_solution(11576430386398614496)
XLA Ops:
  7.3 1.3 copy.29
  8.6 1.6 %collective-permute-start = (bf16[1024,256]{0,1:T(8,128)(2,1)S(1)}, bf16[1024,256]{0,1:T(8,128)(2,1)S(1)}, u32[]{:S(2)}, u32[]{:S(2)}) collective-permute-start(bf16[1024,256]{0,1:T(8,128)(2,1)S(1)} %bitcast.130), channel_id=1, source_target_pairs={{0,8},{4,12},{8,0},{12,4},{16,24},{20,28},{24,16},{28,20},{1,9},{5... | collective-permute-start | bytes 1572872 | tf_op jit(solution)/shard_map/ppermute | solution.py:31
  10.2 1.5 %collective-permute-start.1 = (bf16[1024,256]{0,1:T(8,128)(2,1)S(1)}, bf16[1024,256]{0,1:T(8,128)(2,1)S(1)}, u32[]{:S(2)}, u32[]{:S(2)}) collective-permute-start(bf16[1024,256]{0,1:T(8,128)(2,1)S(1)} %bitcast.131), channel_id=1, source_target_pairs={{0,16},{4,20},{8,24},{12,28},{16,0},{20,4},{24,8},{28,12},{1,17},{... | collective-permute-start | bytes 1572872 | tf_op jit(solution)/shard_map/ppermute | solution.py:31
  11.7 0.5 collective-permute-start.2
  12.2 11.3 %collective-permute-done = bf16[1024,256]{0,1:T(8,128)(2,1)S(1)} collective-permute-done((bf16[1024,256]{0,1:T(8,128)(2,1)S(1)}, bf16[1024,256]{0,1:T(8,128)(2,1)S(1)}, u32[]{:S(2)}, u32[]{:S(2)}) %collective-permute-start) | collective-permute-done | bytes 524320 | tf_op jit(solution)/shard_map/ppermute | solution.py:31
  23.5 11.3 %collective-permute-done.1 = bf16[1024,256]{0,1:T(8,128)(2,1)S(1)} collective-permute-done((bf16[1024,256]{0,1:T(8,128)(2,1)S(1)}, bf16[1024,256]{0,1:T(8,128)(2,1)S(1)}, u32[]{:S(2)}, u32[]{:S(2)}) %collective-permute-start.1) | collective-permute-done | bytes 524320 | tf_op jit(solution)/shard_map/ppermute | solution.py:31
  34.8 0.8 copy-done.4
  35.8 1.8 %pad_maximum_fusion = bf16[4,1024,256]{1,2,0:T(8,128)(2,1)S(1)} fusion(bf16[1,1024,256]{1,2,0:T(8,128)(2,1)} %bitcast.141, bf16[1,1024,256]{1,2,0:T(8,128)(2,1)} %bitcast.140, bf16[1,1024,256]{1,2,0:T(8,128)(2,1)} %bitcast.139, bf16[1,1024,256]{1,2,0:T(8,128)(2,1)} %bitcast.133), kind=kLoop, calls=%fused_computation.29 | loop fusion | flops 3145728 | bytes 4194304 | tf_op jit(solution)/shard_map/stack | solution.py:42
  37.6 2.2 %constant_dynamic-slice_fusion = (bf16[320,512]{1,0:T(8,128)(2,1)}, bf16[320,512]{1,0:T(8,128)(2,1)}, bf16[320,512]{1,0:T(8,128)(2,1)}) fusion(bf16[320,2048]{1,0:T(8,128)(2,1)} %param.14, s32[]{:T(128)S(6)} %select_n.247, s32[]{:T(128)S(6)} %select_n.245, s32[]{:T(128)S(6)} %select_n.249), kind=kLoop, calls=%fused_computation.124 | loop fusion | bytes 1966092 | tf_op jit(solution)/shard_map/dynamic_slice | solution.py:82
  39.8 1.6 %collective-permute-start.5 = (bf16[320,512]{1,0:T(8,128)(2,1)}, bf16[320,512]{1,0:T(8,128)(2,1)}, u32[]{:S(2)}, u32[]{:S(2)}) collective-permute-start(bf16[320,512]{1,0:T(8,128)(2,1)} %get-tuple-element.13), channel_id=1, source_target_pairs={{0,1},{1,2},{2,3},{3,0},{4,5},{5,6},{6,7},{7,4},{8,9},{9,10},{10,1... | collective-permute-start | bytes 983048 | tf_op jit(solution)/shard_map/ppermute | solution.py:57
  41.4 0.4 collective-permute-start.9
  41.8 2.6 %collective-permute-start.7 = (bf16[320,512]{1,0:T(8,128)(2,1)}, bf16[320,512]{1,0:T(8,128)(2,1)}, u32[]{:S(2)}, u32[]{:S(2)}) collective-permute-start(bf16[320,512]{1,0:T(8,128)(2,1)} %get-tuple-element.12), channel_id=1, source_target_pairs={{0,2},{1,3},{2,0},{3,1},{4,6},{5,7},{6,4},{7,5},{8,10},{9,11},{10,... | collective-permute-start | bytes 983048 | tf_op jit(solution)/shard_map/ppermute | solution.py:57
  44.4 0.7 fusion.99
  55.6 1.0 copy.25
  57.0 0.3 fusion.29
  57.2 0.3 fusion.28
  57.5 1.3 select_reduce_fusion.4
  58.9 1.7 %dynamic-slice_select_fusion.3 = (bf16[1,1024,256]{1,2,0:T(8,128)(2,1)S(1)}, bf16[1,1024,256]{1,2,0:T(8,128)(2,1)S(1)}, bf16[1,1024,256]{1,2,0:T(8,128)(2,1)S(1)}, bf16[1,1024,256]{1,2,0:T(8,128)(2,1)S(1)}) fusion(bf16[4,1024,256]{1,2,0:T(8,128)(2,1)} %collective-permute-done.3, s32[]{:T(128)S(6)} %select_n.208, ...), kind=kLoop, calls=%fused_computation.89 | loop fusion | flops 1048576 | bytes 6291476 | tf_op jit(solution)/shard_map/jit(_where)/select_n | solution.py:50
  60.7 0.5 fusion.14
  61.3 0.5 fusion.13
  61.8 0.5 fusion.12
  62.4 0.5 fusion.15
  62.9 0.5 fusion.16
  63.4 0.5 fusion.17
  64.0 0.5 fusion.18
  64.5 1.4 select_reduce_fusion.1
  65.9 1.3 select_reduce_fusion.2
  67.2 1.3 select_reduce_fusion.3
  68.6 1.3 select_reduce_fusion
  70.0 0.2 fusion.31
  70.2 1.6 %fusion = f32[5,64,256]{2,1,0:T(8,128)S(1)} fusion(f32[5,1024,256]{2,1,0:T(8,128)S(1)} %get-tuple-element.42, f32[5,256]{1,0:T(8,128)S(1)} %maximum_maximum_fusion, pred[256]{0:T(512)(128)(4,1)S(1)} %get-tuple-element.25, bf16[1024,5,64]{0,1,2:T(8,128)(2,1)S(1)} %fusion.16), kind=kOutput, calls=%fused_computation.18 | convolution fusion | flops 173015040 | bytes 6231296 | tf_op jit(solution)/shard_map/hrp,phd->rhd/dot_general | solution.py:146
  71.8 1.4 %fusion.1 = f32[5,64,256]{2,1,0:T(8,128)S(1)} fusion(f32[5,1024,256]{2,1,0:T(8,128)S(1)} %get-tuple-element.38, f32[5,256]{1,0:T(8,128)S(1)} %maximum_maximum_fusion, pred[256]{0:T(512)(128)(4,1)S(1)} %get-tuple-element.28, bf16[1024,5,64]{0,1,2:T(8,128)(2,1)S(1)} %fusion.17), kind=kOutput, calls=%fused_computation.19 | convolution fusion | flops 173015040 | bytes 6231296 | tf_op jit(solution)/shard_map/hrp,phd->rhd/dot_general | solution.py:146
  73.3 4.1 %bitcast_reduce_fusion.3 = (f32[5,256]{1,0:T(8,128)S(1)}, f32[5,256]{1,0:T(8,128)S(1)}, f32[5,256]{1,0:T(8,128)S(1)}, f32[5,256]{1,0:T(8,128)S(1)}) fusion(f32[5,1024,256]{2,1,0:T(8,128)S(1)} %get-tuple-element.42, f32[5,256]{1,0:T(8,128)S(1)} %maximum_maximum_fusion, pred[256]{0:T(512)(128)(4,1)S(1)} %get-tuple-element.25, ...), kind=kLoop, calls=%fused_computation.6 | loop fusion | flops 20966400 | bytes 20998144 | tf_op jit(solution)/shard_map/reduce_sum | solution.py:145
  77.4 1.4 %fusion.2 = f32[5,64,256]{2,1,0:T(8,128)S(1)} fusion(f32[5,1024,256]{2,1,0:T(8,128)S(1)} %get-tuple-element.36, f32[5,256]{1,0:T(8,128)S(1)} %maximum_maximum_fusion, pred[256]{0:T(512)(128)(4,1)S(1)} %get-tuple-element.27, bf16[1024,5,64]{0,1,2:T(8,128)(2,1)S(1)} %fusion.18), kind=kOutput, calls=%fused_computation.20 | convolution fusion | flops 173015040 | bytes 6231296 | tf_op jit(solution)/shard_map/hrp,phd->rhd/dot_general | solution.py:146
  78.8 0.5 fusion.19
  79.4 1.4 %fusion.3 = f32[5,64,256]{2,1,0:T(8,128)S(1)} fusion(f32[5,1024,256]{2,1,0:T(8,128)S(1)} %get-tuple-element.34, f32[5,256]{1,0:T(8,128)S(1)} %maximum_maximum_fusion, pred[256]{0:T(512)(128)(4,1)S(1)} %get-tuple-element.26, bf16[1024,5,64]{0,1,2:T(8,128)(2,1)S(1)} %fusion.19), kind=kOutput, calls=%fused_computation.21 | convolution fusion | flops 173015040 | bytes 6231296 | tf_op jit(solution)/shard_map/hrp,phd->rhd/dot_general | solution.py:146
  80.8 0.3 fusion.30
  81.2 1.2 collective-permute-start.4
  82.3 0.9 collective-permute-start.8
  83.2 1.3 fusion.52
  84.5 0.9 collective-permute-start.6
  85.4 8.0 %collective-permute-done.4 = bf16[256,320]{0,1:T(8,128)(2,1)S(1)} collective-permute-done((bf16[256,320]{0,1:T(8,128)(2,1)S(1)}, bf16[256,320]{0,1:T(8,128)(2,1)S(1)}, u32[]{:S(2)}, u32[]{:S(2)}) %collective-permute-start.4) | collective-permute-done | bytes 163872 | tf_op jit(solution)/shard_map/ppermute | solution.py:57
  93.4 1.3 convolution_add_fusion.1
  94.7 1.3 fusion.100
  96.2 2.0 %fusion.22 = bf16[256,512]{1,0:T(8,128)(2,1)} fusion(f32[256,512]{1,0:T(8,128)S(1)} %fusion.100, f32[256,512]{1,0:T(8,128)S(1)} %convolution_add_fusion.1, bf16[256,320]{0,1:T(8,128)(2,1)S(1)} %collective-permute-done.6, bf16[320,512]{1,0:T(8,128)(2,1)} %collective-permute-done.7, bf16[256,512]{1,0:T(8,128)(2,1)S(1)} %copy-done.6), kind=kOutput, calls=%fused_computation.54 | convolution fusion | flops 84541440 | bytes 2064384 | tf_op jit(solution)/shard_map/dot_general | solution.py:161
  98.3 29.1 %all-gather.2.cloned.1.call-done = bf16[256,2048]{1,0:T(8,128)(2,1)} async-done(((bf16[256,512]{1,0:T(8,128)(2,1)}), bf16[256,2048]{1,0:T(8,128)(2,1)}) %all-gather.2.cloned.1.call-update) | async-done | bytes 1048592 | tf_op jit(solution)/shard_map/all_gather | solution.py:166
  127.3 1.5 %fusion.8 = f32[256]{0:T(256)S(1)} fusion(bf16[256,2048]{1,0:T(8,128)(2,1)} %all-gather.2.cloned.1.call-done), kind=kLoop, calls=%fused_computation.26 | loop fusion | flops 1572608 | bytes 1049600 | tf_op jit(solution)/shard_map/reduce_sum | solution.py:168
  128.9 2.5 %convolution_convert_fusion.10 = bf16[256,320]{0,1:T(8,128)(2,1)} fusion(bf16[2048,320]{0,1:T(8,128)(2,1)S(1)} %copy-done, bf16[256,2048]{1,0:T(8,128)(2,1)} %all-gather.2.cloned.1.call-done, f32[2048]{0:T(1024)S(1)} %convert_element_type.130, f32[256]{0:T(256)S(1)} %add_rsqrt_fusion), kind=kOutput, calls=%fused_computation.66 | convolution fusion | flops 337723392 | bytes 2532352 | tf_op jit(solution)/shard_map/dot_general | solution.py:172
  (47 shorter events, 1.1 us)
Async XLA Ops:
  7.2 121.7 %copy-start = (bf16[2048,320]{0,1:T(8,128)(2,1)S(1)}, bf16[2048,320]{0,1:T(8,128)(2,1)}, u32[]{:S(2)}) copy-start(bf16[2048,320]{0,1:T(8,128)(2,1)} %param.16) | copy-start | bytes 3932164
  7.2 37.2 %copy-start.7 = (s32[4]{0:T(128)S(1)}, s32[4]{0:T(128)}, u32[]{:S(2)}) copy-start(s32[4]{0:T(128)} %param.19) | copy-start | bytes 52
  7.2 48.3 %copy-start.10 = (s32[1,4]{1,0:T(1,128)S(1)}, s32[1,4]{1,0:T(1,128)}, u32[]{:S(2)}) copy-start(s32[1,4]{1,0:T(1,128)} %param.17) | copy-start | bytes 52
  7.2 49.6 %copy-start.9 = (s32[1,4]{1,0:T(1,128)S(1)}, s32[1,4]{1,0:T(1,128)}, u32[]{:S(2)}) copy-start(s32[1,4]{1,0:T(1,128)} %param.18) | copy-start | bytes 52
  7.2 120.1 %all-gather.2.cloned.1.call-start = ((), (), s32[]{:S(2)}) async-start(), calls=%async_computation | async-start | bytes 1310720 | tf_op jit(solution)/shard_map/all_gather | solution.py:166
  8.6 26.2 %copy-start.2 = (bf16[1024,1,256]{0,2,1:T(8,128)(2,1)}, bf16[1024,1,256]{0,2,1:T(8,128)(2,1)S(1)}, u32[]{:S(2)}) copy-start(bf16[1024,1,256]{0,2,1:T(8,128)(2,1)S(1)} %copy.29) | copy-start | bytes 1572868
  8.6 14.9 %collective-permute-start = (bf16[1024,256]{0,1:T(8,128)(2,1)S(1)}, bf16[1024,256]{0,1:T(8,128)(2,1)S(1)}, u32[]{:S(2)}, u32[]{:S(2)}) collective-permute-start(bf16[1024,256]{0,1:T(8,128)(2,1)S(1)} %bitcast.130), channel_id=1, source_target_pairs={{0,8},{4,12},{8,0},{12,4},{16,24},{20,28},{24,16},{28,20},{1,9},{5... | collective-permute-start | bytes 1572872 | tf_op jit(solution)/shard_map/ppermute | solution.py:31
  10.2 24.6 %collective-permute-start.1 = (bf16[1024,256]{0,1:T(8,128)(2,1)S(1)}, bf16[1024,256]{0,1:T(8,128)(2,1)S(1)}, u32[]{:S(2)}, u32[]{:S(2)}) collective-permute-start(bf16[1024,256]{0,1:T(8,128)(2,1)S(1)} %bitcast.131), channel_id=1, source_target_pairs={{0,16},{4,20},{8,24},{12,28},{16,0},{20,4},{24,8},{28,12},{1,17},{... | collective-permute-start | bytes 1572872 | tf_op jit(solution)/shard_map/ppermute | solution.py:31
  11.7 23.1 %collective-permute-start.2 = (bf16[1024,256]{0,1:T(8,128)(2,1)S(1)}, bf16[1024,256]{0,1:T(8,128)(2,1)S(1)}, u32[]{:S(2)}, u32[]{:S(2)}) collective-permute-start(bf16[1024,256]{0,1:T(8,128)(2,1)S(1)} %bitcast.132), channel_id=1, source_target_pairs={{0,24},{4,28},{8,16},{12,20},{16,8},{20,12},{24,0},{28,4},{1,25},{... | collective-permute-start | bytes 1572872 | tf_op jit(solution)/shard_map/ppermute | solution.py:31
  23.5 11.3 %copy-start.3 = (bf16[1024,256]{0,1:T(8,128)(2,1)}, bf16[1024,256]{0,1:T(8,128)(2,1)S(1)}, u32[]{:S(2)}) copy-start(bf16[1024,256]{0,1:T(8,128)(2,1)S(1)} %collective-permute-done) | copy-start | bytes 1572868
  34.8 0.8 copy-start.4
  34.8 1.0 copy-start.5
  37.6 21.3 %collective-permute-start.3 = (bf16[4,1024,256]{1,2,0:T(8,128)(2,1)S(1)}, bf16[4,1024,256]{1,2,0:T(8,128)(2,1)}, u32[]{:S(2)}, u32[]{:S(2)}) collective-permute-start(bf16[4,1024,256]{1,2,0:T(8,128)(2,1)S(1)} %pad_maximum_fusion), channel_id=1, source_target_pairs={{0,4},{4,0},{8,12},{12,8},{16,20},{20,16},{24,28},{28,24},{1,5},{5... | collective-permute-start | bytes 6291464 | tf_op jit(solution)/shard_map/ppermute | solution.py:31
  39.8 44.7 %collective-permute-start.5 = (bf16[320,512]{1,0:T(8,128)(2,1)}, bf16[320,512]{1,0:T(8,128)(2,1)}, u32[]{:S(2)}, u32[]{:S(2)}) collective-permute-start(bf16[320,512]{1,0:T(8,128)(2,1)} %get-tuple-element.13), channel_id=1, source_target_pairs={{0,1},{1,2},{2,3},{3,0},{4,5},{5,6},{6,7},{7,4},{8,9},{9,10},{10,1... | collective-permute-start | bytes 983048 | tf_op jit(solution)/shard_map/ppermute | solution.py:57
  41.4 53.3 %collective-permute-start.9 = (bf16[320,512]{1,0:T(8,128)(2,1)}, bf16[320,512]{1,0:T(8,128)(2,1)}, u32[]{:S(2)}, u32[]{:S(2)}) collective-permute-start(bf16[320,512]{1,0:T(8,128)(2,1)} %get-tuple-element.14), channel_id=1, source_target_pairs={{0,3},{1,0},{2,1},{3,2},{4,7},{5,4},{6,5},{7,6},{8,11},{9,8},{10,9... | collective-permute-start | bytes 983048 | tf_op jit(solution)/shard_map/ppermute | solution.py:57
  41.8 54.2 %collective-permute-start.7 = (bf16[320,512]{1,0:T(8,128)(2,1)}, bf16[320,512]{1,0:T(8,128)(2,1)}, u32[]{:S(2)}, u32[]{:S(2)}) collective-permute-start(bf16[320,512]{1,0:T(8,128)(2,1)} %get-tuple-element.12), channel_id=1, source_target_pairs={{0,2},{1,3},{2,0},{3,1},{4,6},{5,7},{6,4},{7,5},{8,10},{9,11},{10,... | collective-permute-start | bytes 983048 | tf_op jit(solution)/shard_map/ppermute | solution.py:57
  61.2 3.3 %copy-start.1 = (bf16[256,320]{0,1:T(8,128)(2,1)S(1)}, bf16[256,320]{0,1:T(8,128)(2,1)}, u32[]{:S(2)}) copy-start(bf16[256,320]{0,1:T(8,128)(2,1)} %param.11) | copy-start | bytes 491524
  80.8 15.4 %copy-start.6 = (bf16[256,512]{1,0:T(8,128)(2,1)S(1)}, bf16[256,512]{1,0:T(8,128)(2,1)}, u32[]{:S(2)}) copy-start(bf16[256,512]{1,0:T(8,128)(2,1)} %param.10) | copy-start | bytes 786436
  80.8 17.5 %copy-start.8 = (bf16[2048]{0:T(1024)(128)(2,1)S(1)}, bf16[2048]{0:T(1024)(128)(2,1)}, u32[]{:S(2)}) copy-start(bf16[2048]{0:T(1024)(128)(2,1)} %param.15) | copy-start | bytes 12292
  81.2 12.3 %collective-permute-start.4 = (bf16[256,320]{0,1:T(8,128)(2,1)S(1)}, bf16[256,320]{0,1:T(8,128)(2,1)S(1)}, u32[]{:S(2)}, u32[]{:S(2)}) collective-permute-start(bf16[256,320]{0,1:T(8,128)(2,1)S(1)} %bitcast.142), channel_id=1, source_target_pairs={{0,1},{1,2},{2,3},{3,0},{4,5},{5,6},{6,7},{7,4},{8,9},{9,10},{10,1... | collective-permute-start | bytes 491528 | tf_op jit(solution)/shard_map/ppermute | solution.py:57
  82.3 12.4 %collective-permute-start.8 = (bf16[256,320]{0,1:T(8,128)(2,1)S(1)}, bf16[256,320]{0,1:T(8,128)(2,1)S(1)}, u32[]{:S(2)}, u32[]{:S(2)}) collective-permute-start(bf16[256,320]{0,1:T(8,128)(2,1)S(1)} %bitcast.143), channel_id=1, source_target_pairs={{0,3},{1,0},{2,1},{3,2},{4,7},{5,4},{6,5},{7,6},{8,11},{9,8},{10,9... | collective-permute-start | bytes 491528 | tf_op jit(solution)/shard_map/ppermute | solution.py:57
  84.5 11.7 %collective-permute-start.6 = (bf16[256,320]{0,1:T(8,128)(2,1)S(1)}, bf16[256,320]{0,1:T(8,128)(2,1)S(1)}, u32[]{:S(2)}, u32[]{:S(2)}) collective-permute-start(bf16[256,320]{0,1:T(8,128)(2,1)S(1)} %bitcast.145), channel_id=1, source_target_pairs={{0,2},{1,3},{2,0},{3,1},{4,6},{5,7},{6,4},{7,5},{8,10},{9,11},{10,... | collective-permute-start | bytes 491528 | tf_op jit(solution)/shard_map/ppermute | solution.py:57
Sparse Core Ops, SparseCore 0:
  98.4 28.9 all-gather.1

commit v3 on v1

--- a/solution.py
+++ b/solution.py
@@ -26,15 +26,24 @@
     return (key_heads, value_heads)
 
 
-def tenant_prefixes(own_slot, owners, n_req):
-    slot_rows = own_slot.shape[0]
+def every_slot_of(part, n_req):
+    return lax.all_gather(part, "req", axis=0, tiled=True)
+
+
+def slots_of_tenants(part, every_slot, owners, n_req):
+    slot_rows = part.shape[0]
     if n_req <= GATHER_SLOTS_MAX:
-        every_slot = lax.all_gather(own_slot, "req", axis=0, tiled=True)
         return [
             lax.dynamic_slice_in_dim(every_slot, owners[tenant_id] * slot_rows, slot_rows, 0)
             for tenant_id in range(TENANTS)
         ]
-    return [from_root(own_slot, "req", owners[tenant_id]) for tenant_id in range(TENANTS)]
+    return [from_root(part, "req", owners[tenant_id]) for tenant_id in range(TENANTS)]
+
+
+def pick_part(part_rows, select):
+    return jnp.einsum(
+        "njd,hj->nhd", part_rows, select, preferred_element_type=jnp.float32
+    ).astype(jnp.bfloat16)
 
 
 def shifted(block, shift, n_tp):
@@ -89,9 +98,21 @@
     suffix_mask = (
         (position[None, :] >= row_start[:, None]) & (position[None, :] <= position[:, None])
     )[None]
-    own_slot = prefix_cache.reshape(prefix_cache.shape[0], -1)
-    prefix_blocks = tenant_prefixes(own_slot, owners, n_req)
-    picked = [pick_heads(block_rows, select) for block_rows in prefix_blocks]
+    own_slot = prefix_cache.reshape(prefix_cache.shape[0], 2, 2, HD)
+    own_keys = own_slot[:, :, 0]
+    own_values = own_slot[:, :, 1]
+    if n_req <= GATHER_SLOTS_MAX:
+        every_key = every_slot_of(own_keys, n_req)
+        own_values, every_key = lax.optimization_barrier((own_values, every_key))
+        every_value = every_slot_of(own_values, n_req)
+    else:
+        every_key = every_value = None
+    key_blocks = slots_of_tenants(own_keys, every_key, owners, n_req)
+    value_blocks = slots_of_tenants(own_values, every_value, owners, n_req)
+    picked = [
+        (pick_part(key_rows, select), pick_part(value_rows, select))
+        for key_rows, value_rows in zip(key_blocks, value_blocks)
+    ]
     row_top = jnp.max(jnp.where(suffix_mask, suffix_scores, -jnp.inf), axis=2)
     for tenant_id in range(TENANTS):
         tenant_mask = (row_tenant == tenant_id)[None, :, None]

time: 129 us -> 151 us (1.17)
  matrix products: 24.9 us -> 37.2 us
  waiting for transfers between devices: 59 us -> 65.6 us
  local copies, waits for them, and re-layouts: 8.66 us -> 11.6 us
    dot_general x0 -> x8, matrix products: none -> 12.6 us  [pick_part(): jnp.einsum('njd,hj->nhd', part_rows, select, preferred_element_type=jnp.f...]
    all_gather x1 -> x2, waiting for transfers between devices: 21.5 us -> 29.1 us  [every_slot_of(): return lax.all_gather(part, 'req', axis=0, tiled=True)]
    optimization_barrier x0 -> x2, local copies, waits for them, and re-layouts: none -> 4.73 us  [local(): own_values, every_key = lax.optimization_barrier((own_values, every_key))]
    dot_general x4, matrix products: 5.93 us -> 8.43 us  [local(): jnp.einsum('hrp,phd->rhd', prefix_weights.astype(jnp.bfloat16), picked[te...]
    dot_general x5 -> x1, matrix products: 3.07 us -> 0.99 us  [pick_heads(): jnp.einsum('njd,hj->nhd', split_pair[:, :, 1], select, preferred_element_...]
    dot_general x5 -> x1, matrix products: 2.35 us -> 0.28 us  [pick_heads(): jnp.einsum('njd,hj->nhd', split_pair[:, :, 0], select, preferred_element_...]
    dynamic_slice x1 -> x0, local copies, waits for them, and re-layouts: 1.74 us -> none  [tenant_prefixes(): lax.dynamic_slice_in_dim(every_slot, owners[tenant_id] * slot_rows, slot_...]
    unnamed x12 -> x38, local copies, waits for them, and re-layouts: 3.16 us -> 2.45 us
  transfers between devices with their start and end apart: 8 -> 9, of which waited for: 5 -> 6; matrix products, arithmetic and copies ran while one was open for 27% -> 34% of each run, Pallas kernels for 0% -> 0%
where the time goes in v3:
time: 151 us; the launch traced here: 149 us
  waiting for transfers between devices  65.6 us (43%)
  matrix products  37.2 us (25%)
  between operations  16.9 us (11%)
  local copies, waits for them, and re-layouts  11.6 us (8%)
  starting transfers between devices  9.47 us (6%)
  other arithmetic  8.57 us (6%)
    all_gather x2, waiting for transfers between devices, every_slot_of(): return lax.all_gather(part, 'req', axis=0, tiled=True)  29.1 us
    all_gather x1, waiting for transfers between devices, local(): full_new = lax.all_gather(new_residual, 'tp', axis=1, tiled=True)  29 us
    dot_general x8, matrix products, pick_part(): jnp.einsum('njd,hj->nhd', part_rows, select, preferred_element_type=jnp.f...  12.6 us
    ppermute x6, starting transfers between devices, shifted(): return lax.ppermute(block, 'tp', pairs)  9.17 us
    dot_general x4, matrix products, local(): jnp.einsum('hrp,phd->rhd', prefix_weights.astype(jnp.bfloat16), picked[te...  8.43 us
    ppermute x6, waiting for transfers between devices, shifted(): return lax.ppermute(block, 'tp', pairs)  7.5 us
    dot_general x4, matrix products, local(): jnp.einsum('rhd,phd->hrp', query_heads, picked[tenant_id][0], preferred_e...  6.74 us
    optimization_barrier x2, local copies, waits for them, and re-layouts, local(): own_values, every_key = lax.optimization_barrier((own_values, every_key))  4.73 us
  transfers between devices with their start and end apart: 9, of which 6 were waited for; matrix products, arithmetic and copies ran while one was open for 34% of the time, Pallas kernels for 0%

profile of v3, /device:TPU:8, one launch (start us, length us, event | category | flops | bytes accessed | tf_op | source)
XLA Modules:
  0.0 149.4 jit_solution(15637092772348222072)
XLA Ops:
  7.2 1.4 copy.28
  8.6 0.7 fusion.107
  9.5 2.2 %constant_dynamic-slice_fusion.1 = (bf16[320,512]{1,0:T(8,128)(2,1)}, bf16[320,512]{1,0:T(8,128)(2,1)}, bf16[320,512]{1,0:T(8,128)(2,1)}) fusion(bf16[320,2048]{1,0:T(8,128)(2,1)} %param.14, s32[]{:T(128)S(6)} %select_n.137, s32[]{:T(128)S(6)} %select_n.135, s32[]{:T(128)S(6)} %select_n.139), kind=kLoop, calls=%fused_computation.113 | loop fusion | bytes 1966092 | tf_op jit(solution)/shard_map/dynamic_slice | solution.py:76
  11.7 1.6 %collective-permute-start.1 = (bf16[320,512]{1,0:T(8,128)(2,1)}, bf16[320,512]{1,0:T(8,128)(2,1)}, u32[]{:S(2)}, u32[]{:S(2)}) collective-permute-start(bf16[320,512]{1,0:T(8,128)(2,1)} %get-tuple-element.13), channel_id=1, source_target_pairs={{0,1},{1,2},{2,3},{3,0},{4,5},{5,6},{6,7},{7,4},{8,9},{9,10},{10,1... | collective-permute-start | bytes 983048 | tf_op jit(solution)/shard_map/ppermute | solution.py:51
  13.2 0.5 collective-permute-start.5
  13.7 2.6 %collective-permute-start.3 = (bf16[320,512]{1,0:T(8,128)(2,1)}, bf16[320,512]{1,0:T(8,128)(2,1)S(1)}, u32[]{:S(2)}, u32[]{:S(2)}) collective-permute-start(bf16[320,512]{1,0:T(8,128)(2,1)} %get-tuple-element.12), channel_id=1, source_target_pairs={{0,2},{1,3},{2,0},{3,1},{4,6},{5,7},{6,4},{7,5},{8,10},{9,11},{10,... | collective-permute-start | bytes 983048 | tf_op jit(solution)/shard_map/ppermute | solution.py:51
  16.3 1.5 fusion.108
  20.4 0.8 reduce-window.4
  21.2 1.0 copy.24
  22.3 0.7 fusion.86
  23.0 0.7 select_reduce_fusion.6
  24.1 1.0 fusion.28
  25.1 0.4 select_reduce_fusion.4
  25.5 14.1 %all-gather.9.cloned.1.call-done = bf16[8192,2,1,64]{0,3,2,1:T(8,128)(2,1)} async-done(((bf16[1024,2,1,64]{0,3,2,1:T(8,128)(2,1)}), bf16[8192,2,1,64]{0,3,2,1:T(8,128)(2,1)}) %all-gather.9.cloned.1.call-update) | async-done | bytes 2097168 | tf_op jit(solution)/shard_map/all_gather | solution.py:30
  39.6 3.8 %copy.29 = bf16[8192,2,64]{0,1,2:T(2,128)(2,1)S(1)} copy(bf16[8192,2,64]{0,2,1:T(8,128)(2,1)} %bitcast.115) | data formatting | bytes 4194304 | tf_op jit(solution)/shard_map/optimization_barrier | solution.py:106
  43.4 1.6 %fusion.14 = bf16[1024,5,64]{0,1,2:T(8,128)(2,1)} fusion(bf16[8192,2,64]{0,1,2:T(2,128)(2,1)S(1)} %copy.29, s32[]{:T(128)S(6)} %select_n.119, s32[5]{0:T(128)S(1)} %fusion.97), kind=kOutput, calls=%fused_computation.41 | convolution fusion | flops 1638410 | bytes 918020 | tf_op jit(solution)/shard_map/njd,hj->nhd/dot_general | solution.py:44
  45.0 1.5 %fusion.13 = bf16[1024,5,64]{0,1,2:T(8,128)(2,1)} fusion(bf16[8192,2,64]{0,1,2:T(2,128)(2,1)S(1)} %copy.29, s32[]{:T(128)S(6)} %select_n.117, s32[5]{0:T(128)S(1)} %fusion.97), kind=kOutput, calls=%fused_computation.40 | convolution fusion | flops 1638410 | bytes 918020 | tf_op jit(solution)/shard_map/njd,hj->nhd/dot_general | solution.py:44
  46.5 1.5 %fusion.12 = bf16[1024,5,64]{0,1,2:T(8,128)(2,1)} fusion(bf16[8192,2,64]{0,1,2:T(2,128)(2,1)S(1)} %copy.29, s32[]{:T(128)S(6)} %select_n.115, s32[5]{0:T(128)S(1)} %fusion.97), kind=kOutput, calls=%fused_computation.39 | convolution fusion | flops 1638410 | bytes 918020 | tf_op jit(solution)/shard_map/njd,hj->nhd/dot_general | solution.py:44
  48.1 1.0 copy.39
  49.3 1.6 %fusion.15 = bf16[1024,5,64]{0,1,2:T(8,128)(2,1)S(1)} fusion(bf16[8192,2,64]{0,1,2:T(2,128)(2,1)} %copy-done.5, s32[]{:T(128)S(6)} %select_n.121, s32[5]{0:T(128)S(1)} %fusion.97), kind=kOutput, calls=%fused_computation.42 | convolution fusion | flops 1638410 | bytes 917528 | tf_op jit(solution)/shard_map/njd,hj->nhd/dot_general | solution.py:44
  50.9 2.7 %select_reduce_fusion.1 = (f32[5,256]{1,0:T(8,128)S(1)}, f32[5,1024,256]{2,1,0:T(8,128)S(1)}) fusion(pred[256]{0:T(512)(128)(4,1)S(1)} %get-tuple-element.21, bf16[256,5,64]{0,2,1:T(8,128)(2,1)S(1)} %bitcast.111, bf16[1024,5,64]{0,1,2:T(8,128)(2,1)} %fusion.14), kind=kOutput, calls=%fused_computation.13 | convolution fusion | flops 171703040 | bytes 6067456 | tf_op jit(solution)/shard_map/rhd,phd->hrp/dot_general | solution.py:120
  53.6 1.3 select_reduce_fusion.2
  55.0 1.3 select_reduce_fusion.3
  56.3 1.3 select_reduce_fusion
  58.0 4.4 %bitcast_reduce_fusion.3 = (f32[5,256]{1,0:T(8,128)S(1)}, f32[5,256]{1,0:T(8,128)S(1)}, f32[5,256]{1,0:T(8,128)S(1)}, f32[5,256]{1,0:T(8,128)S(1)}) fusion(f32[5,1024,256]{2,1,0:T(8,128)S(1)} %get-tuple-element.36, f32[5,256]{1,0:T(8,128)S(1)} %maximum_maximum_fusion, pred[256]{0:T(512)(128)(4,1)S(1)} %get-tuple-element.19, ...), kind=kLoop, calls=%fused_computation.6 | loop fusion | flops 20966400 | bytes 20998144 | tf_op jit(solution)/shard_map/reduce_sum | solution.py:151
  62.4 15.0 %all-gather.5.cloned.1.call-done = bf16[8192,2,64]{0,1,2:T(2,128)(2,1)} async-done(((bf16[1024,2,64]{0,1,2:T(2,128)(2,1)}), bf16[8192,2,64]{0,1,2:T(2,128)(2,1)}) %all-gather.5.cloned.1.call-update) | async-done | bytes 2097168 | tf_op jit(solution)/shard_map/all_gather | solution.py:30
  77.4 1.6 %fusion.16 = bf16[1024,5,64]{0,1,2:T(8,128)(2,1)S(1)} fusion(bf16[8192,2,64]{0,1,2:T(2,128)(2,1)} %all-gather.5.cloned.1.call-done, s32[]{:T(128)S(6)} %select_n.115, s32[5]{0:T(128)S(1)} %fusion.97), kind=kOutput, calls=%fused_computation.43 | convolution fusion | flops 1638410 | bytes 917528 | tf_op jit(solution)/shard_map/njd,hj->nhd/dot_general | solution.py:44
  79.0 4.1 %fusion = f32[5,64,256]{2,1,0:T(8,128)S(1)} fusion(f32[5,1024,256]{2,1,0:T(8,128)} %copy-done.4, f32[5,256]{1,0:T(8,128)S(1)} %maximum_maximum_fusion, pred[256]{0:T(512)(128)(4,1)S(1)} %get-tuple-element.19, bf16[1024,5,64]{0,1,2:T(8,128)(2,1)S(1)} %fusion.16), kind=kOutput, calls=%fused_computation.18 | convolution fusion | flops 173015040 | bytes 6231296 | tf_op jit(solution)/shard_map/hrp,phd->rhd/dot_general | solution.py:152
  83.1 1.6 %fusion.17 = bf16[1024,5,64]{0,1,2:T(8,128)(2,1)S(1)} fusion(bf16[8192,2,64]{0,1,2:T(2,128)(2,1)} %all-gather.5.cloned.1.call-done, s32[]{:T(128)S(6)} %select_n.117, s32[5]{0:T(128)S(1)} %fusion.97), kind=kOutput, calls=%fused_computation.44 | convolution fusion | flops 1638410 | bytes 917528 | tf_op jit(solution)/shard_map/njd,hj->nhd/dot_general | solution.py:44
  84.8 1.4 fusion.1
  86.2 1.6 %fusion.18 = bf16[1024,5,64]{0,1,2:T(8,128)(2,1)S(1)} fusion(bf16[8192,2,64]{0,1,2:T(2,128)(2,1)} %all-gather.5.cloned.1.call-done, s32[]{:T(128)S(6)} %select_n.119, s32[5]{0:T(128)S(1)} %fusion.97), kind=kOutput, calls=%fused_computation.45 | convolution fusion | flops 1638410 | bytes 917528 | tf_op jit(solution)/shard_map/njd,hj->nhd/dot_general | solution.py:44
  87.9 1.4 fusion.2
  89.4 1.5 %fusion.19 = bf16[1024,5,64]{0,1,2:T(8,128)(2,1)S(1)} fusion(bf16[8192,2,64]{0,1,2:T(2,128)(2,1)} %all-gather.5.cloned.1.call-done, s32[]{:T(128)S(6)} %select_n.121, s32[5]{0:T(128)S(1)} %fusion.97), kind=kOutput, calls=%fused_computation.46 | convolution fusion | flops 1638410 | bytes 917528 | tf_op jit(solution)/shard_map/njd,hj->nhd/dot_general | solution.py:44
  90.9 1.4 fusion.3
  92.4 0.3 fusion.30
  92.7 1.5 %collective-permute-start = (bf16[256,320]{0,1:T(8,128)(2,1)S(1)}, bf16[256,320]{0,1:T(8,128)(2,1)S(1)}, u32[]{:S(2)}, u32[]{:S(2)}) collective-permute-start(bf16[256,320]{0,1:T(8,128)(2,1)S(1)} %bitcast.118), channel_id=1, source_target_pairs={{0,1},{1,2},{2,3},{3,0},{4,5},{5,6},{6,7},{7,4},{8,9},{9,10},{10,1... | collective-permute-start | bytes 491528 | tf_op jit(solution)/shard_map/ppermute | solution.py:51
  94.3 0.5 collective-permute-start.4
  94.8 1.3 fusion.52
  96.1 2.5 %collective-permute-start.2 = (bf16[256,320]{0,1:T(8,128)(2,1)S(1)}, bf16[256,320]{0,1:T(8,128)(2,1)S(1)}, u32[]{:S(2)}, u32[]{:S(2)}) collective-permute-start(bf16[256,320]{0,1:T(8,128)(2,1)S(1)} %bitcast.121), channel_id=1, source_target_pairs={{0,2},{1,3},{2,0},{3,1},{4,6},{5,7},{6,4},{7,5},{8,10},{9,11},{10,... | collective-permute-start | bytes 491528 | tf_op jit(solution)/shard_map/ppermute | solution.py:51
  98.6 1.2 collective-permute-done
  99.8 1.3 convolution_add_fusion.1
  101.1 3.2 %collective-permute-done.4 = bf16[256,320]{0,1:T(8,128)(2,1)S(1)} collective-permute-done((bf16[256,320]{0,1:T(8,128)(2,1)S(1)}, bf16[256,320]{0,1:T(8,128)(2,1)S(1)}, u32[]{:S(2)}, u32[]{:S(2)}) %collective-permute-start.4) | collective-permute-done | bytes 163872 | tf_op jit(solution)/shard_map/ppermute | solution.py:51
  104.3 1.3 fusion.109
  105.6 3.1 %collective-permute-done.2 = bf16[256,320]{0,1:T(8,128)(2,1)S(1)} collective-permute-done((bf16[256,320]{0,1:T(8,128)(2,1)S(1)}, bf16[256,320]{0,1:T(8,128)(2,1)S(1)}, u32[]{:S(2)}, u32[]{:S(2)}) %collective-permute-start.2) | collective-permute-done | bytes 163872 | tf_op jit(solution)/shard_map/ppermute | solution.py:51
  108.7 1.0 fusion.22
  109.8 29.0 %all-gather.7.cloned.1.call-done = bf16[256,2048]{1,0:T(8,128)(2,1)} async-done(((bf16[256,512]{1,0:T(8,128)(2,1)}), bf16[256,2048]{1,0:T(8,128)(2,1)}) %all-gather.7.cloned.1.call-update) | async-done | bytes 1048592 | tf_op jit(solution)/shard_map/all_gather | solution.py:172
  138.8 1.5 %fusion.8 = f32[256]{0:T(256)S(1)} fusion(bf16[256,2048]{1,0:T(8,128)(2,1)} %all-gather.7.cloned.1.call-done), kind=kLoop, calls=%fused_computation.26 | loop fusion | flops 1572608 | bytes 1049600 | tf_op jit(solution)/shard_map/reduce_sum | solution.py:174
  140.3 2.5 %convolution_convert_fusion.10 = bf16[256,320]{0,1:T(8,128)(2,1)} fusion(bf16[2048,320]{0,1:T(8,128)(2,1)S(1)} %copy-done, bf16[256,2048]{1,0:T(8,128)(2,1)} %all-gather.7.cloned.1.call-done, f32[2048]{0:T(1024)S(1)} %convert_element_type.130, f32[256]{0:T(256)S(1)} %add_rsqrt_fusion), kind=kOutput, calls=%fused_computation.65 | convolution fusion | flops 337723392 | bytes 2532352 | tf_op jit(solution)/shard_map/dot_general | solution.py:178
  (59 shorter events, 1.2 us)
Async XLA Ops:
  7.2 133.1 %copy-start = (bf16[2048,320]{0,1:T(8,128)(2,1)S(1)}, bf16[2048,320]{0,1:T(8,128)(2,1)}, u32[]{:S(2)}) copy-start(bf16[2048,320]{0,1:T(8,128)(2,1)} %param.16) | copy-start | bytes 3932164
  7.2 17.9 %copy-start.6 = (bf16[256,320]{0,1:T(8,128)(2,1)S(1)}, bf16[256,320]{0,1:T(8,128)(2,1)}, u32[]{:S(2)}) copy-start(bf16[256,320]{0,1:T(8,128)(2,1)} %param.11) | copy-start | bytes 491524
  7.2 32.4 %all-gather.9.cloned.1.call-start = ((), (), s32[]{:S(2)}) async-start(), calls=%async_computation.2 | async-start | bytes 2359296 | tf_op jit(solution)/shard_map/all_gather | solution.py:30
  9.4 68.0 %all-gather.5.cloned.1.call-start = ((), (), s32[]{:S(2)}) async-start(), calls=%async_computation | async-start | bytes 2359296 | tf_op jit(solution)/shard_map/all_gather | solution.py:30
  11.7 84.4 %collective-permute-start.1 = (bf16[320,512]{1,0:T(8,128)(2,1)}, bf16[320,512]{1,0:T(8,128)(2,1)}, u32[]{:S(2)}, u32[]{:S(2)}) collective-permute-start(bf16[320,512]{1,0:T(8,128)(2,1)} %get-tuple-element.13), channel_id=1, source_target_pairs={{0,1},{1,2},{2,3},{3,0},{4,5},{5,6},{6,7},{7,4},{8,9},{9,10},{10,1... | collective-permute-start | bytes 983048 | tf_op jit(solution)/shard_map/ppermute | solution.py:51
  13.2 87.9 %collective-permute-start.5 = (bf16[320,512]{1,0:T(8,128)(2,1)}, bf16[320,512]{1,0:T(8,128)(2,1)}, u32[]{:S(2)}, u32[]{:S(2)}) collective-permute-start(bf16[320,512]{1,0:T(8,128)(2,1)} %get-tuple-element.14), channel_id=1, source_target_pairs={{0,3},{1,0},{2,1},{3,2},{4,7},{5,4},{6,5},{7,6},{8,11},{9,8},{10,9... | collective-permute-start | bytes 983048 | tf_op jit(solution)/shard_map/ppermute | solution.py:51
  13.7 91.9 %collective-permute-start.3 = (bf16[320,512]{1,0:T(8,128)(2,1)}, bf16[320,512]{1,0:T(8,128)(2,1)S(1)}, u32[]{:S(2)}, u32[]{:S(2)}) collective-permute-start(bf16[320,512]{1,0:T(8,128)(2,1)} %get-tuple-element.12), channel_id=1, source_target_pairs={{0,2},{1,3},{2,0},{3,1},{4,6},{5,7},{6,4},{7,5},{8,10},{9,11},{10,... | collective-permute-start | bytes 983048 | tf_op jit(solution)/shard_map/ppermute | solution.py:51
  43.4 3.2 %copy-start.5 = (bf16[8192,2,64]{0,1,2:T(2,128)(2,1)}, bf16[8192,2,64]{0,1,2:T(2,128)(2,1)S(1)}, u32[]{:S(2)}) copy-start(bf16[8192,2,64]{0,1,2:T(2,128)(2,1)S(1)} %copy.29) | copy-start | bytes 6291460
  49.1 89.7 %all-gather.7.cloned.1.call-start = ((), (), s32[]{:S(2)}) async-start(), calls=%async_computation.1 | async-start | bytes 1310720 | tf_op jit(solution)/shard_map/all_gather | solution.py:172
  49.3 4.3 %copy-start.8 = (bf16[1024,5,64]{0,1,2:T(8,128)(2,1)S(1)}, bf16[1024,5,64]{0,1,2:T(8,128)(2,1)}, u32[]{:S(2)}) copy-start(bf16[1024,5,64]{0,1,2:T(8,128)(2,1)} %fusion.13) | copy-start | bytes 1966084
  50.9 4.1 %copy-start.7 = (bf16[1024,5,64]{0,1,2:T(8,128)(2,1)S(1)}, bf16[1024,5,64]{0,1,2:T(8,128)(2,1)}, u32[]{:S(2)}) copy-start(bf16[1024,5,64]{0,1,2:T(8,128)(2,1)} %fusion.12) | copy-start | bytes 1966084
  53.6 4.4 %copy-start.1 = (f32[5,1024,256]{2,1,0:T(8,128)}, f32[5,1024,256]{2,1,0:T(8,128)S(1)}, u32[]{:S(2)}) copy-start(f32[5,1024,256]{2,1,0:T(8,128)S(1)} %get-tuple-element.30) | copy-start | bytes 15728644
  55.0 3.0 %copy-start.3 = (f32[5,1024,256]{2,1,0:T(8,128)}, f32[5,1024,256]{2,1,0:T(8,128)S(1)}, u32[]{:S(2)}) copy-start(f32[5,1024,256]{2,1,0:T(8,128)S(1)} %get-tuple-element.32) | copy-start | bytes 15728644
  56.3 6.1 %copy-start.4 = (f32[5,1024,256]{2,1,0:T(8,128)}, f32[5,1024,256]{2,1,0:T(8,128)S(1)}, u32[]{:S(2)}) copy-start(f32[5,1024,256]{2,1,0:T(8,128)S(1)} %get-tuple-element.36) | copy-start | bytes 15728644
  57.7 4.7 %copy-start.2 = (f32[5,1024,256]{2,1,0:T(8,128)}, f32[5,1024,256]{2,1,0:T(8,128)S(1)}, u32[]{:S(2)}) copy-start(f32[5,1024,256]{2,1,0:T(8,128)S(1)} %get-tuple-element.28) | copy-start | bytes 15728644
  77.4 7.4 %slice-start.4 = ((s8[5242880]{0:T(1024)(128)(4,1)}), s8[4194304]{0:T(1024)(128)(4,1)S(1)}, s32[]{:S(2)}) async-start(s8[5242880]{0:T(1024)(128)(4,1)} %bitcast.108), calls=%async_computation.7 | async-start | bytes 8388608
  79.0 5.7 %slice-start.5 = ((s8[5242880]{0:T(1024)(128)(4,1)}), s8[1048576]{0:T(1024)(128)(4,1)S(1)}, s32[]{:S(2)}) async-start(s8[5242880]{0:T(1024)(128)(4,1)} %bitcast.108), calls=%async_computation.8 | async-start | bytes 2097152
  83.1 4.7 %slice-start = ((s8[5242880]{0:T(1024)(128)(4,1)}), s8[4194304]{0:T(1024)(128)(4,1)S(1)}, s32[]{:S(2)}) async-start(s8[5242880]{0:T(1024)(128)(4,1)} %bitcast.104), calls=%async_computation.3 | async-start | bytes 8388608
  84.8 3.1 %slice-start.1 = ((s8[5242880]{0:T(1024)(128)(4,1)}), s8[1048576]{0:T(1024)(128)(4,1)S(1)}, s32[]{:S(2)}) async-start(s8[5242880]{0:T(1024)(128)(4,1)} %bitcast.104), calls=%async_computation.4 | async-start | bytes 2097152
  86.2 4.6 %slice-start.2 = ((s8[5242880]{0:T(1024)(128)(4,1)}), s8[4194304]{0:T(1024)(128)(4,1)S(1)}, s32[]{:S(2)}) async-start(s8[5242880]{0:T(1024)(128)(4,1)} %bitcast.106), calls=%async_computation.5 | async-start | bytes 8388608
  87.9 3.0 %slice-start.3 = ((s8[5242880]{0:T(1024)(128)(4,1)}), s8[1048576]{0:T(1024)(128)(4,1)S(1)}, s32[]{:S(2)}) async-start(s8[5242880]{0:T(1024)(128)(4,1)} %bitcast.106), calls=%async_computation.6 | async-start | bytes 2097152
  89.4 3.0 %copy-start.9 = (bf16[256,5,64]{0,1,2:T(8,128)(2,1)S(1)}, bf16[256,5,64]{0,1,2:T(8,128)(2,1)}, u32[]{:S(2)}) copy-start(bf16[256,5,64]{0,1,2:T(8,128)(2,1)} %fusion.28) | copy-start | bytes 491524
  92.4 16.3 %copy-start.10 = (bf16[256,512]{1,0:T(8,128)(2,1)S(1)}, bf16[256,512]{1,0:T(8,128)(2,1)}, u32[]{:S(2)}) copy-start(bf16[256,512]{1,0:T(8,128)(2,1)} %param.10) | copy-start | bytes 786436
  92.4 17.4 %copy-start.11 = (bf16[2048]{0:T(1024)(128)(2,1)S(1)}, bf16[2048]{0:T(1024)(128)(2,1)}, u32[]{:S(2)}) copy-start(bf16[2048]{0:T(1024)(128)(2,1)} %param.15) | copy-start | bytes 12292
  92.7 7.1 %collective-permute-start = (bf16[256,320]{0,1:T(8,128)(2,1)S(1)}, bf16[256,320]{0,1:T(8,128)(2,1)S(1)}, u32[]{:S(2)}, u32[]{:S(2)}) collective-permute-start(bf16[256,320]{0,1:T(8,128)(2,1)S(1)} %bitcast.118), channel_id=1, source_target_pairs={{0,1},{1,2},{2,3},{3,0},{4,5},{5,6},{6,7},{7,4},{8,9},{9,10},{10,1... | collective-permute-start | bytes 491528 | tf_op jit(solution)/shard_map/ppermute | solution.py:51
  94.3 10.0 %collective-permute-start.4 = (bf16[256,320]{0,1:T(8,128)(2,1)S(1)}, bf16[256,320]{0,1:T(8,128)(2,1)S(1)}, u32[]{:S(2)}, u32[]{:S(2)}) collective-permute-start(bf16[256,320]{0,1:T(8,128)(2,1)S(1)} %bitcast.119), channel_id=1, source_target_pairs={{0,3},{1,0},{2,1},{3,2},{4,7},{5,4},{6,5},{7,6},{8,11},{9,8},{10,9... | collective-permute-start | bytes 491528 | tf_op jit(solution)/shard_map/ppermute | solution.py:51
  96.1 12.6 %collective-permute-start.2 = (bf16[256,320]{0,1:T(8,128)(2,1)S(1)}, bf16[256,320]{0,1:T(8,128)(2,1)S(1)}, u32[]{:S(2)}, u32[]{:S(2)}) collective-permute-start(bf16[256,320]{0,1:T(8,128)(2,1)S(1)} %bitcast.121), channel_id=1, source_target_pairs={{0,2},{1,3},{2,0},{3,1},{4,6},{5,7},{6,4},{7,5},{8,10},{9,11},{10,... | collective-permute-start | bytes 491528 | tf_op jit(solution)/shard_map/ppermute | solution.py:51
Sparse Core Ops, SparseCore 0:
  10.5 29.0 all-gather.8
  49.2 28.1 all-gather.4
  109.9 28.8 all-gather.6

commit v4 on v1

--- a/solution.py
+++ b/solution.py
@@ -148,13 +148,20 @@
         )
     new_residual = (residual.astype(jnp.float32) + projected).astype(jnp.bfloat16)
 
-    full_new = lax.all_gather(new_residual, "tp", axis=1, tiled=True)
-    widened = full_new.astype(jnp.float32)
-    mean_square = jnp.mean(widened * widened, axis=1, keepdims=True)
-    normed = (widened * lax.rsqrt(mean_square + 1e-05) * norm_gain.astype(jnp.float32)).astype(
-        jnp.bfloat16
-    )
-    next_sums = jnp.dot(normed, next_query_weight, preferred_element_type=jnp.float32)
+    blocks = [new_residual] + [shifted(new_residual, shift, n_tp) for shift in range(1, n_tp)]
+    widened = [block.astype(jnp.float32) for block in blocks]
+    square_sums = sum(jnp.sum(block * block, axis=1, keepdims=True) for block in widened)
+    mean_square = square_sums / (width * n_tp)
+    scale = lax.rsqrt(mean_square + 1e-05)
+    gain = norm_gain.astype(jnp.float32)
+    next_sums = None
+    for shift in range(n_tp):
+        source = (tp_index - shift) % n_tp
+        block_gain = lax.dynamic_slice_in_dim(gain, source * width, width, 0)
+        block_weight = lax.dynamic_slice_in_dim(next_query_weight, source * width, width, 0)
+        normed = (widened[shift] * scale * block_gain).astype(jnp.bfloat16)
+        part = jnp.dot(normed, block_weight, preferred_element_type=jnp.float32)
+        next_sums = part if next_sums is None else next_sums + part
     return (new_residual, next_sums.astype(jnp.bfloat16))
 
 

time: 129 us -> 124 us (0.961); the launches traced: 127 us -> 124 us
  waiting for transfers between devices: 59 us -> 52 us
  starting transfers between devices: 9.25 us -> 15 us
    all_gather x1 -> x0, waiting for transfers between devices: 29 us -> none  [local(): full_new = lax.all_gather(new_residual, 'tp', axis=1, tiled=True)]
    ppermute x6 -> x9, waiting for transfers between devices: 8.46 us -> 30.4 us  [shifted(): return lax.ppermute(block, 'tp', pairs)]
    ppermute x6 -> x9, starting transfers between devices: 9.18 us -> 14.9 us  [shifted(): return lax.ppermute(block, 'tp', pairs)]
    unnamed x12 -> x14, local copies, waits for them, and re-layouts: 3.16 us -> 3.17 us
  transfers between devices with their start and end apart: 8 -> 10, of which waited for: 5 -> 7; matrix products, arithmetic and copies ran while one was open for 27% -> 28% of each run, Pallas kernels for 0% -> 0%
where the time goes in v4:
time: 124 us
  waiting for transfers between devices  52 us (42%)
  matrix products  23.9 us (19%)
  between operations  17 us (14%)
  starting transfers between devices  15 us (12%)
  local copies, waits for them, and re-layouts  8.75 us (7%)
  other arithmetic  7.16 us (6%)
    ppermute x9, waiting for transfers between devices, shifted(): return lax.ppermute(block, 'tp', pairs)  30.4 us
    all_gather x1, waiting for transfers between devices, tenant_prefixes(): every_slot = lax.all_gather(own_slot, 'req', axis=0, tiled=True)  21.6 us
    ppermute x9, starting transfers between devices, shifted(): return lax.ppermute(block, 'tp', pairs)  14.9 us
    dot_general x4, matrix products, local(): jnp.einsum('hrp,phd->rhd', prefix_weights.astype(jnp.bfloat16), picked[te...  5.93 us
    dot_general x4, matrix products, local(): jnp.einsum('rhd,phd->hrp', query_heads, picked[tenant_id][0], preferred_e...  5.4 us
    reduce_sum x1, other arithmetic, local(): denominator = denominator + jnp.sum(prefix_weights, axis=2)  4.12 us
    unnamed x14, local copies, waits for them, and re-layouts  3.17 us
    dot_general x5, matrix products, pick_heads(): jnp.einsum('njd,hj->nhd', split_pair[:, :, 1], select, preferred_element_...  3.07 us
  transfers between devices with their start and end apart: 10, of which 7 were waited for; matrix products, arithmetic and copies ran while one was open for 28% of the time, Pallas kernels for 0%

profile of v4, /device:TPU:8, one launch (start us, length us, event | category | flops | bytes accessed | tf_op | source)
XLA Modules:
  0.0 123.7 jit_solution(8804984965935445479)
XLA Ops:
  7.2 2.1 %copy.28 = bf16[1024,1,256]{0,2,1:T(8,128)(2,1)} copy(bf16[1024,1,256]{2,0,1:T(8,128)(2,1)} %param.13) | data formatting | bytes 1048576 | tf_op args[3]
  9.4 2.2 %constant_dynamic-slice_fusion.1 = (bf16[320,512]{1,0:T(8,128)(2,1)}, bf16[320,512]{1,0:T(8,128)(2,1)}, bf16[320,512]{1,0:T(8,128)(2,1)}) fusion(bf16[320,2048]{1,0:T(8,128)(2,1)} %param.14, s32[]{:T(128)S(6)} %select_n.161, s32[]{:T(128)S(6)} %select_n.159, s32[]{:T(128)S(6)} %select_n.163), kind=kLoop, calls=%fused_computation.153 | loop fusion | bytes 1966092 | tf_op jit(solution)/shard_map/dynamic_slice | solution.py:67
  11.6 1.6 %collective-permute-start.1 = (bf16[320,512]{1,0:T(8,128)(2,1)}, bf16[320,512]{1,0:T(8,128)(2,1)}, u32[]{:S(2)}, u32[]{:S(2)}) collective-permute-start(bf16[320,512]{1,0:T(8,128)(2,1)} %get-tuple-element.13), channel_id=1, source_target_pairs={{0,1},{1,2},{2,3},{3,0},{4,5},{5,6},{6,7},{7,4},{8,9},{9,10},{10,1... | collective-permute-start | bytes 983048 | tf_op jit(solution)/shard_map/ppermute | solution.py:42
  13.2 0.4 collective-permute-start.5
  13.7 2.6 %collective-permute-start.3 = (bf16[320,512]{1,0:T(8,128)(2,1)}, bf16[320,512]{1,0:T(8,128)(2,1)S(1)}, u32[]{:S(2)}, u32[]{:S(2)}) collective-permute-start(bf16[320,512]{1,0:T(8,128)(2,1)} %get-tuple-element.12), channel_id=1, source_target_pairs={{0,2},{1,3},{2,0},{3,1},{4,6},{5,7},{6,4},{7,5},{8,10},{9,11},{10,... | collective-permute-start | bytes 983048 | tf_op jit(solution)/shard_map/ppermute | solution.py:42
  16.2 1.4 %fusion.128 = (s32[1]{0:T(128)}, s32[1]{0:T(128)}, s32[1]{0:T(128)}, s32[1]{0:T(128)}) fusion(s32[4]{0:T(128)} %param.19), kind=kLoop, calls=%fused_computation.203 | loop fusion | bytes 32 | tf_op jit(solution)/shard_map/slice | solution.py:34
  20.2 0.8 reduce-window.4
  21.0 1.0 copy.24
  22.1 0.7 fusion.106
  22.8 0.7 select_reduce_fusion.6
  23.9 1.0 fusion.25
  24.9 1.3 %select_reduce_fusion.4 = (f32[5,256]{1,0:T(8,128)S(1)}, f32[5,256,256]{1,2,0:T(8,128)S(1)}) fusion(pred[256,256]{0,1:T(8,128)(4,1)S(1)} %fusion.86, bf16[256,5,64]{0,2,1:T(8,128)(2,1)} %bitcast.119, bf16[256,5,64]{0,1,2:T(8,128)(2,1)S(1)} %fusion.26), kind=kOutput, calls=%fused_computation.43 | convolution fusion | flops 42924800 | bytes 1709056 | tf_op jit(solution)/shard_map/rhd,khd->hrk/dot_general | solution.py:86
  26.2 21.6 %all-gather.3.cloned.1.call-done = bf16[8192,1,256]{0,2,1:T(8,128)(2,1)} async-done(((bf16[1024,1,256]{0,2,1:T(8,128)(2,1)}), bf16[8192,1,256]{0,2,1:T(8,128)(2,1)}) %all-gather.3.cloned.1.call-update) | async-done | bytes 4194320 | tf_op jit(solution)/shard_map/all_gather | solution.py:32
  47.8 1.7 %constant_dynamic-slice_fusion.6 = (bf16[1024,1,256]{0,2,1:T(8,128)(2,1)S(1)}, bf16[1024,1,256]{0,2,1:T(8,128)(2,1)S(1)}, bf16[1024,1,256]{0,2,1:T(8,128)(2,1)S(1)}, bf16[1024,1,256]{0,2,1:T(8,128)(2,1)S(1)}) fusion(bf16[8192,1,256]{0,2,1:T(8,128)(2,1)} %all-gather.3.cloned.1.call-done, s32[]{:T(128)S(6)} %select_n.139, s32[]{:T(128)S(6)} %select_n.143, ...), kind=kLoop, calls=%fused_computation.159 | loop fusion | bytes 4194320 | tf_op jit(solution)/shard_map/dynamic_slice | solution.py:34
  49.6 0.5 fusion.11
  50.2 0.5 fusion.10
  50.8 0.5 fusion.9
  51.3 0.5 fusion.12
  51.9 0.5 fusion.13
  52.4 0.5 fusion.14
  52.9 0.5 fusion.15
  53.5 1.4 %select_reduce_fusion.1 = (f32[5,256]{1,0:T(8,128)S(1)}, f32[5,1024,256]{2,1,0:T(8,128)S(1)}) fusion(pred[256]{0:T(512)(128)(4,1)S(1)} %get-tuple-element.31, bf16[256,5,64]{0,2,1:T(8,128)(2,1)S(1)} %bitcast.120, bf16[1024,5,64]{0,1,2:T(8,128)(2,1)S(1)} %fusion.11), kind=kOutput, calls=%fused_computation.13 | convolution fusion | flops 171703040 | bytes 6067456 | tf_op jit(solution)/shard_map/rhd,phd->hrp/dot_general | solution.py:99
  54.8 1.3 %select_reduce_fusion.2 = (f32[5,256]{1,0:T(8,128)S(1)}, f32[5,1024,256]{2,1,0:T(8,128)S(1)}) fusion(pred[256]{0:T(512)(128)(4,1)S(1)} %get-tuple-element.32, bf16[256,5,64]{0,2,1:T(8,128)(2,1)S(1)} %bitcast.121, bf16[1024,5,64]{0,1,2:T(8,128)(2,1)S(1)} %fusion.10), kind=kOutput, calls=%fused_computation.14 | convolution fusion | flops 171703040 | bytes 6067456 | tf_op jit(solution)/shard_map/rhd,phd->hrp/dot_general | solution.py:99
  56.2 1.3 %select_reduce_fusion.3 = (f32[5,256]{1,0:T(8,128)S(1)}, f32[5,1024,256]{2,1,0:T(8,128)S(1)}) fusion(pred[256]{0:T(512)(128)(4,1)S(1)} %get-tuple-element.29, bf16[256,5,64]{0,2,1:T(8,128)(2,1)S(1)} %bitcast.122, bf16[1024,5,64]{0,1,2:T(8,128)(2,1)S(1)} %fusion.9), kind=kOutput, calls=%fused_computation.15 | convolution fusion | flops 171703040 | bytes 6067456 | tf_op jit(solution)/shard_map/rhd,phd->hrp/dot_general | solution.py:99
  57.5 1.3 %select_reduce_fusion = (f32[5,256]{1,0:T(8,128)S(1)}, f32[5,1024,256]{2,1,0:T(8,128)S(1)}) fusion(pred[256]{0:T(512)(128)(4,1)S(1)} %get-tuple-element.30, bf16[256,5,64]{0,2,1:T(8,128)(2,1)S(1)} %bitcast.123, bf16[1024,5,64]{0,1,2:T(8,128)(2,1)S(1)} %fusion.12), kind=kOutput, calls=%fused_computation.12 | convolution fusion | flops 171703040 | bytes 6067456 | tf_op jit(solution)/shard_map/rhd,phd->hrp/dot_general | solution.py:99
  59.2 1.4 %fusion = f32[5,64,256]{2,1,0:T(8,128)S(1)} fusion(f32[5,1024,256]{2,1,0:T(8,128)S(1)} %get-tuple-element.46, f32[5,256]{1,0:T(8,128)S(1)} %maximum_maximum_fusion, pred[256]{0:T(512)(128)(4,1)S(1)} %get-tuple-element.29, bf16[1024,5,64]{0,1,2:T(8,128)(2,1)S(1)} %fusion.13), kind=kOutput, calls=%fused_computation.16 | convolution fusion | flops 173015040 | bytes 6231296 | tf_op jit(solution)/shard_map/hrp,phd->rhd/dot_general | solution.py:131
  60.6 1.6 %fusion.1 = f32[5,64,256]{2,1,0:T(8,128)S(1)} fusion(f32[5,1024,256]{2,1,0:T(8,128)S(1)} %get-tuple-element.42, f32[5,256]{1,0:T(8,128)S(1)} %maximum_maximum_fusion, pred[256]{0:T(512)(128)(4,1)S(1)} %get-tuple-element.32, bf16[1024,5,64]{0,1,2:T(8,128)(2,1)S(1)} %fusion.14), kind=kOutput, calls=%fused_computation.17 | convolution fusion | flops 173015040 | bytes 6231296 | tf_op jit(solution)/shard_map/hrp,phd->rhd/dot_general | solution.py:131
  62.2 4.1 %bitcast_reduce_fusion.3 = (f32[5,256]{1,0:T(8,128)S(1)}, f32[5,256]{1,0:T(8,128)S(1)}, f32[5,256]{1,0:T(8,128)S(1)}, f32[5,256]{1,0:T(8,128)S(1)}) fusion(f32[5,1024,256]{2,1,0:T(8,128)S(1)} %get-tuple-element.46, f32[5,256]{1,0:T(8,128)S(1)} %maximum_maximum_fusion, pred[256]{0:T(512)(128)(4,1)S(1)} %get-tuple-element.29, ...), kind=kLoop, calls=%fused_computation.6 | loop fusion | flops 20966400 | bytes 20998144 | tf_op jit(solution)/shard_map/reduce_sum | solution.py:130
  66.3 1.4 %fusion.2 = f32[5,64,256]{2,1,0:T(8,128)S(1)} fusion(f32[5,1024,256]{2,1,0:T(8,128)S(1)} %get-tuple-element.40, f32[5,256]{1,0:T(8,128)S(1)} %maximum_maximum_fusion, pred[256]{0:T(512)(128)(4,1)S(1)} %get-tuple-element.31, bf16[1024,5,64]{0,1,2:T(8,128)(2,1)S(1)} %fusion.15), kind=kOutput, calls=%fused_computation.18 | convolution fusion | flops 173015040 | bytes 6231296 | tf_op jit(solution)/shard_map/hrp,phd->rhd/dot_general | solution.py:131
  67.8 0.5 fusion.16
  68.3 1.4 %fusion.3 = f32[5,64,256]{2,1,0:T(8,128)S(1)} fusion(f32[5,1024,256]{2,1,0:T(8,128)S(1)} %get-tuple-element.38, f32[5,256]{1,0:T(8,128)S(1)} %maximum_maximum_fusion, pred[256]{0:T(512)(128)(4,1)S(1)} %get-tuple-element.30, bf16[1024,5,64]{0,1,2:T(8,128)(2,1)S(1)} %fusion.16), kind=kOutput, calls=%fused_computation.19 | convolution fusion | flops 173015040 | bytes 6231296 | tf_op jit(solution)/shard_map/hrp,phd->rhd/dot_general | solution.py:131
  70.1 1.5 %collective-permute-start = (bf16[256,320]{0,1:T(8,128)(2,1)S(1)}, bf16[256,320]{0,1:T(8,128)(2,1)S(1)}, u32[]{:S(2)}, u32[]{:S(2)}) collective-permute-start(bf16[256,320]{0,1:T(8,128)(2,1)S(1)} %bitcast.129), channel_id=1, source_target_pairs={{0,1},{1,2},{2,3},{3,0},{4,5},{5,6},{6,7},{7,4},{8,9},{9,10},{10,1... | collective-permute-start | bytes 491528 | tf_op jit(solution)/shard_map/ppermute | solution.py:42
  71.7 0.5 collective-permute-start.4
  72.2 1.3 %fusion.64 = f32[256,512]{1,0:T(8,128)S(1)} fusion(bf16[256,320]{0,1:T(8,128)(2,1)S(1)} %bitcast.131, bf16[320,2048]{1,0:T(8,128)(2,1)} %param.14, s32[]{:T(128)S(6)} %select_n.157), kind=kOutput, calls=%fused_computation.106 | convolution fusion | flops 83886080 | bytes 1015812 | tf_op jit(solution)/shard_map/dot_general | solution.py:143
  73.5 2.5 %collective-permute-start.2 = (bf16[256,320]{0,1:T(8,128)(2,1)S(1)}, bf16[256,320]{0,1:T(8,128)(2,1)S(1)}, u32[]{:S(2)}, u32[]{:S(2)}) collective-permute-start(bf16[256,320]{0,1:T(8,128)(2,1)S(1)} %bitcast.132), channel_id=1, source_target_pairs={{0,2},{1,3},{2,0},{3,1},{4,6},{5,7},{6,4},{7,5},{8,10},{9,11},{10,... | collective-permute-start | bytes 491528 | tf_op jit(solution)/shard_map/ppermute | solution.py:42
  76.0 1.2 collective-permute-done
  77.2 1.3 %convolution_add_fusion.1 = f32[256,512]{1,0:T(8,128)S(1)} fusion(f32[256,512]{1,0:T(8,128)S(1)} %fusion.64, bf16[256,320]{0,1:T(8,128)(2,1)S(1)} %collective-permute-done, bf16[320,512]{1,0:T(8,128)(2,1)} %collective-permute-done.1), kind=kOutput, calls=%fused_computation.47 | convolution fusion | flops 84017152 | bytes 1540096 | tf_op jit(solution)/shard_map/dot_general | solution.py:146
  78.5 3.2 %collective-permute-done.4 = bf16[256,320]{0,1:T(8,128)(2,1)S(1)} collective-permute-done((bf16[256,320]{0,1:T(8,128)(2,1)S(1)}, bf16[256,320]{0,1:T(8,128)(2,1)S(1)}, u32[]{:S(2)}, u32[]{:S(2)}) %collective-permute-start.4) | collective-permute-done | bytes 163872 | tf_op jit(solution)/shard_map/ppermute | solution.py:42
  82.0 4.1 %collective-permute-done.2 = bf16[256,320]{0,1:T(8,128)(2,1)S(1)} collective-permute-done((bf16[256,320]{0,1:T(8,128)(2,1)S(1)}, bf16[256,320]{0,1:T(8,128)(2,1)S(1)}, u32[]{:S(2)}, u32[]{:S(2)}) %collective-permute-start.2) | collective-permute-done | bytes 163872 | tf_op jit(solution)/shard_map/ppermute | solution.py:42
  86.1 0.5 fusion.47
  86.6 1.5 %collective-permute-start.6 = (bf16[256,512]{1,0:T(8,128)(2,1)S(1)}, bf16[256,512]{1,0:T(8,128)(2,1)S(1)}, u32[]{:S(2)}, u32[]{:S(2)}) collective-permute-start(bf16[256,512]{1,0:T(8,128)(2,1)S(1)} %get-tuple-element.48), channel_id=1, source_target_pairs={{0,1},{1,2},{2,3},{3,0},{4,5},{5,6},{6,7},{7,4},{8,9},{9,10},{10,1... | collective-permute-start | bytes 786440 | tf_op jit(solution)/shard_map/ppermute | solution.py:42
  88.0 4.3 %collective-permute-start.7 = (bf16[256,512]{1,0:T(8,128)(2,1)S(1)}, bf16[256,512]{1,0:T(8,128)(2,1)S(1)}, u32[]{:S(2)}, u32[]{:S(2)}) collective-permute-start(bf16[256,512]{1,0:T(8,128)(2,1)S(1)} %get-tuple-element.48), channel_id=1, source_target_pairs={{0,2},{1,3},{2,0},{3,1},{4,6},{5,7},{6,4},{7,5},{8,10},{9,11},{10,... | collective-permute-start | bytes 786440 | tf_op jit(solution)/shard_map/ppermute | solution.py:42
  92.4 4.7 %collective-permute-done.6 = bf16[256,512]{1,0:T(8,128)(2,1)S(1)} collective-permute-done((bf16[256,512]{1,0:T(8,128)(2,1)S(1)}, bf16[256,512]{1,0:T(8,128)(2,1)S(1)}, u32[]{:S(2)}, u32[]{:S(2)}) %collective-permute-start.6) | collective-permute-done | bytes 262176 | tf_op jit(solution)/shard_map/ppermute | solution.py:42
  97.2 13.5 %collective-permute-done.7 = bf16[256,512]{1,0:T(8,128)(2,1)S(1)} collective-permute-done((bf16[256,512]{1,0:T(8,128)(2,1)S(1)}, bf16[256,512]{1,0:T(8,128)(2,1)S(1)}, u32[]{:S(2)}, u32[]{:S(2)}) %collective-permute-start.7) | collective-permute-done | bytes 262176 | tf_op jit(solution)/shard_map/ppermute | solution.py:42
  110.8 3.8 %collective-permute-done.8 = bf16[256,512]{1,0:T(8,128)(2,1)S(1)} collective-permute-done((bf16[256,512]{1,0:T(8,128)(2,1)S(1)}, bf16[256,512]{1,0:T(8,128)(2,1)S(1)}, u32[]{:S(2)}, u32[]{:S(2)}) %collective-permute-start.8) | collective-permute-done | bytes 262176 | tf_op jit(solution)/shard_map/ppermute | solution.py:42
  115.1 0.4 convolution_add_fusion.4
  115.5 0.4 convolution_add_fusion.3
  115.8 1.0 fusion.28
  (39 shorter events, 2.4 us)
Async XLA Ops:
  7.2 107.6 %copy-start = (bf16[2048,320]{0,1:T(8,128)(2,1)S(1)}, bf16[2048,320]{0,1:T(8,128)(2,1)}, u32[]{:S(2)}) copy-start(bf16[2048,320]{0,1:T(8,128)(2,1)} %param.16) | copy-start | bytes 3932164
  7.2 40.7 %all-gather.3.cloned.1.call-start = ((), (), s32[]{:S(2)}) async-start(), calls=%async_computation | async-start | bytes 4718592 | tf_op jit(solution)/shard_map/all_gather | solution.py:32
  11.6 61.9 %collective-permute-start.1 = (bf16[320,512]{1,0:T(8,128)(2,1)}, bf16[320,512]{1,0:T(8,128)(2,1)}, u32[]{:S(2)}, u32[]{:S(2)}) collective-permute-start(bf16[320,512]{1,0:T(8,128)(2,1)} %get-tuple-element.13), channel_id=1, source_target_pairs={{0,1},{1,2},{2,3},{3,0},{4,5},{5,6},{6,7},{7,4},{8,9},{9,10},{10,1... | collective-permute-start | bytes 983048 | tf_op jit(solution)/shard_map/ppermute | solution.py:42
  13.2 65.3 %collective-permute-start.5 = (bf16[320,512]{1,0:T(8,128)(2,1)}, bf16[320,512]{1,0:T(8,128)(2,1)S(1)}, u32[]{:S(2)}, u32[]{:S(2)}) collective-permute-start(bf16[320,512]{1,0:T(8,128)(2,1)} %get-tuple-element.14), channel_id=1, source_target_pairs={{0,3},{1,0},{2,1},{3,2},{4,7},{5,4},{6,5},{7,6},{8,11},{9,8},{10,9... | collective-permute-start | bytes 983048 | tf_op jit(solution)/shard_map/ppermute | solution.py:42
  13.7 68.4 %collective-permute-start.3 = (bf16[320,512]{1,0:T(8,128)(2,1)}, bf16[320,512]{1,0:T(8,128)(2,1)S(1)}, u32[]{:S(2)}, u32[]{:S(2)}) collective-permute-start(bf16[320,512]{1,0:T(8,128)(2,1)} %get-tuple-element.12), channel_id=1, source_target_pairs={{0,2},{1,3},{2,0},{3,1},{4,6},{5,7},{6,4},{7,5},{8,10},{9,11},{10,... | collective-permute-start | bytes 983048 | tf_op jit(solution)/shard_map/ppermute | solution.py:42
  50.2 3.3 %copy-start.1 = (bf16[256,320]{0,1:T(8,128)(2,1)S(1)}, bf16[256,320]{0,1:T(8,128)(2,1)}, u32[]{:S(2)}) copy-start(bf16[256,320]{0,1:T(8,128)(2,1)} %param.11) | copy-start | bytes 491524
  67.8 2.0 %copy-start.4 = (bf16[256,5,64]{0,1,2:T(8,128)(2,1)S(1)}, bf16[256,5,64]{0,1,2:T(8,128)(2,1)}, u32[]{:S(2)}) copy-start(bf16[256,5,64]{0,1,2:T(8,128)(2,1)} %fusion.25) | copy-start | bytes 491524
  69.7 16.4 %copy-start.3 = (bf16[256,512]{1,0:T(8,128)(2,1)S(1)}, bf16[256,512]{1,0:T(8,128)(2,1)}, u32[]{:S(2)}) copy-start(bf16[256,512]{1,0:T(8,128)(2,1)} %param.10) | copy-start | bytes 786436
  69.7 22.6 %copy-start.5 = (bf16[2048]{0:T(1024)(128)(2,1)S(1)}, bf16[2048]{0:T(1024)(128)(2,1)}, u32[]{:S(2)}) copy-start(bf16[2048]{0:T(1024)(128)(2,1)} %param.15) | copy-start | bytes 12292
  70.1 7.1 %collective-permute-start = (bf16[256,320]{0,1:T(8,128)(2,1)S(1)}, bf16[256,320]{0,1:T(8,128)(2,1)S(1)}, u32[]{:S(2)}, u32[]{:S(2)}) collective-permute-start(bf16[256,320]{0,1:T(8,128)(2,1)S(1)} %bitcast.129), channel_id=1, source_target_pairs={{0,1},{1,2},{2,3},{3,0},{4,5},{5,6},{6,7},{7,4},{8,9},{9,10},{10,1... | collective-permute-start | bytes 491528 | tf_op jit(solution)/shard_map/ppermute | solution.py:42
  71.7 10.0 %collective-permute-start.4 = (bf16[256,320]{0,1:T(8,128)(2,1)S(1)}, bf16[256,320]{0,1:T(8,128)(2,1)S(1)}, u32[]{:S(2)}, u32[]{:S(2)}) collective-permute-start(bf16[256,320]{0,1:T(8,128)(2,1)S(1)} %bitcast.130), channel_id=1, source_target_pairs={{0,3},{1,0},{2,1},{3,2},{4,7},{5,4},{6,5},{7,6},{8,11},{9,8},{10,9... | collective-permute-start | bytes 491528 | tf_op jit(solution)/shard_map/ppermute | solution.py:42
  73.5 12.6 %collective-permute-start.2 = (bf16[256,320]{0,1:T(8,128)(2,1)S(1)}, bf16[256,320]{0,1:T(8,128)(2,1)S(1)}, u32[]{:S(2)}, u32[]{:S(2)}) collective-permute-start(bf16[256,320]{0,1:T(8,128)(2,1)S(1)} %bitcast.132), channel_id=1, source_target_pairs={{0,2},{1,3},{2,0},{3,1},{4,6},{5,7},{6,4},{7,5},{8,10},{9,11},{10,... | collective-permute-start | bytes 491528 | tf_op jit(solution)/shard_map/ppermute | solution.py:42
  86.5 30.3 %copy-start.2 = (bf16[256,512]{1,0:T(8,128)(2,1)}, bf16[256,512]{1,0:T(8,128)(2,1)S(1)}, u32[]{:S(2)}) copy-start(bf16[256,512]{1,0:T(8,128)(2,1)S(1)} %get-tuple-element.48) | copy-start | bytes 786436
  86.6 10.5 %collective-permute-start.6 = (bf16[256,512]{1,0:T(8,128)(2,1)S(1)}, bf16[256,512]{1,0:T(8,128)(2,1)S(1)}, u32[]{:S(2)}, u32[]{:S(2)}) collective-permute-start(bf16[256,512]{1,0:T(8,128)(2,1)S(1)} %get-tuple-element.48), channel_id=1, source_target_pairs={{0,1},{1,2},{2,3},{3,0},{4,5},{5,6},{6,7},{7,4},{8,9},{9,10},{10,1... | collective-permute-start | bytes 786440 | tf_op jit(solution)/shard_map/ppermute | solution.py:42
  88.0 22.6 %collective-permute-start.7 = (bf16[256,512]{1,0:T(8,128)(2,1)S(1)}, bf16[256,512]{1,0:T(8,128)(2,1)S(1)}, u32[]{:S(2)}, u32[]{:S(2)}) collective-permute-start(bf16[256,512]{1,0:T(8,128)(2,1)S(1)} %get-tuple-element.48), channel_id=1, source_target_pairs={{0,2},{1,3},{2,0},{3,1},{4,6},{5,7},{6,4},{7,5},{8,10},{9,11},{10,... | collective-permute-start | bytes 786440 | tf_op jit(solution)/shard_map/ppermute | solution.py:42
  92.3 22.3 %collective-permute-start.8 = (bf16[256,512]{1,0:T(8,128)(2,1)S(1)}, bf16[256,512]{1,0:T(8,128)(2,1)S(1)}, u32[]{:S(2)}, u32[]{:S(2)}) collective-permute-start(bf16[256,512]{1,0:T(8,128)(2,1)S(1)} %get-tuple-element.48), channel_id=1, source_target_pairs={{0,3},{1,0},{2,1},{3,2},{4,7},{5,4},{6,5},{7,6},{8,11},{9,8},{10,9... | collective-permute-start | bytes 786440 | tf_op jit(solution)/shard_map/ppermute | solution.py:42
Sparse Core Ops, SparseCore 0:
  9.9 37.8 all-gather.2

commit v5 on v1

--- a/solution.py
+++ b/solution.py
@@ -8,6 +8,7 @@
 HD = 64
 TENANTS = 4
 GATHER_SLOTS_MAX = 16
+N_CHUNKS = 2
 
 
 def from_root(block, axis, source):
@@ -82,80 +83,108 @@
     score_scale = HD ** (-0.5)
     query_heads = queries.reshape(row_count, head_count, HD)
     suffix_keys, suffix_values = pick_heads(suffix_kv.reshape(row_count, -1), select)
-    suffix_scores = (
-        jnp.einsum("rhd,khd->hrk", query_heads, suffix_keys, preferred_element_type=jnp.float32)
-        * score_scale
-    )
-    suffix_mask = (
-        (position[None, :] >= row_start[:, None]) & (position[None, :] <= position[:, None])
-    )[None]
     own_slot = prefix_cache.reshape(prefix_cache.shape[0], -1)
     prefix_blocks = tenant_prefixes(own_slot, owners, n_req)
     picked = [pick_heads(block_rows, select) for block_rows in prefix_blocks]
-    row_top = jnp.max(jnp.where(suffix_mask, suffix_scores, -jnp.inf), axis=2)
-    for tenant_id in range(TENANTS):
-        tenant_mask = (row_tenant == tenant_id)[None, :, None]
-        prefix_scores = (
+    gain = norm_gain.astype(jnp.float32)
+
+    def attend(first, count):
+        rows = slice(first, first + count)
+        chunk_queries = query_heads[rows]
+        chunk_tenant = row_tenant[rows]
+        chunk_position = position[rows]
+        suffix_scores = (
             jnp.einsum(
-                "rhd,phd->hrp",
-                query_heads,
-                picked[tenant_id][0],
+                "rhd,khd->hrk", chunk_queries, suffix_keys, preferred_element_type=jnp.float32
+            )
+            * score_scale
+        )
+        suffix_mask = (
+            (position[None, :] >= row_start[rows][:, None])
+            & (position[None, :] <= chunk_position[:, None])
+        )[None]
+        row_top = jnp.max(jnp.where(suffix_mask, suffix_scores, -jnp.inf), axis=2)
+        prefix_scores = []
+        for tenant_id in range(TENANTS):
+            tenant_mask = (chunk_tenant == tenant_id)[None, :, None]
+            scores = (
+                jnp.einsum(
+                    "rhd,phd->hrp",
+                    chunk_queries,
+                    picked[tenant_id][0],
+                    preferred_element_type=jnp.float32,
+                )
+                * score_scale
+            )
+            prefix_scores.append(scores)
+            row_top = jnp.maximum(
+                row_top, jnp.max(jnp.where(tenant_mask, scores, -jnp.inf), axis=2)
+            )
+        suffix_weights = jnp.where(
+            suffix_mask, jnp.exp(suffix_scores - row_top[:, :, None]), 0.0
+        )
+        denominator = jnp.sum(suffix_weights, axis=2)
+        accumulated = jnp.einsum(
+            "hrk,khd->rhd",
+            suffix_weights.astype(jnp.bfloat16),
+            suffix_values,
+            preferred_element_type=jnp.float32,
+        )
+        for tenant_id in range(TENANTS):
+            tenant_mask = (chunk_tenant == tenant_id)[None, :, None]
+            prefix_weights = jnp.where(
+                tenant_mask, jnp.exp(prefix_scores[tenant_id] - row_top[:, :, None]), 0.0
+            )
+            denominator = denominator + jnp.sum(prefix_weights, axis=2)
+            accumulated = accumulated + jnp.einsum(
+                "hrp,phd->rhd",
+                prefix_weights.astype(jnp.bfloat16),
+                picked[tenant_id][1],
                 preferred_element_type=jnp.float32,
             )
-            * score_scale
-        )
-        row_top = jnp.maximum(
-            row_top, jnp.max(jnp.where(tenant_mask, prefix_scores, -jnp.inf), axis=2)
-        )
-    suffix_weights = jnp.where(suffix_mask, jnp.exp(suffix_scores - row_top[:, :, None]), 0.0)
-    denominator = jnp.sum(suffix_weights, axis=2)
-    accumulated = jnp.einsum(
-        "hrk,khd->rhd",
-        suffix_weights.astype(jnp.bfloat16),
-        suffix_values,
-        preferred_element_type=jnp.float32,
+        return (
+            (accumulated / jnp.transpose(denominator)[:, :, None])
+            .astype(jnp.bfloat16)
+            .reshape(count, -1)
+        )
+
+    def finish(first, count, attended):
+        projected = jnp.dot(attended, weight_pieces[0], preferred_element_type=jnp.float32)
+        for shift in range(1, n_tp):
+            head_block = shifted(attended, shift, n_tp)
+            projected = projected + jnp.dot(
+                head_block, weight_pieces[shift], preferred_element_type=jnp.float32
+            )
+        chunk_residual = residual[first:first + count]
+        new_residual = (chunk_residual.astype(jnp.float32) + projected).astype(jnp.bfloat16)
+
+        blocks = [new_residual] + [
+            shifted(new_residual, shift, n_tp) for shift in range(1, n_tp)
+        ]
+        widened = [block.astype(jnp.float32) for block in blocks]
+        square_sums = sum(jnp.sum(block * block, axis=1, keepdims=True) for block in widened)
+        mean_square = square_sums / (width * n_tp)
+        scale = lax.rsqrt(mean_square + 1e-05)
+        next_sums = None
+        for shift in range(n_tp):
+            source = (tp_index - shift) % n_tp
+            block_gain = lax.dynamic_slice_in_dim(gain, source * width, width, 0)
+            block_weight = lax.dynamic_slice_in_dim(next_query_weight, source * width, width, 0)
+            normed = (widened[shift] * scale * block_gain).astype(jnp.bfloat16)
+            part = jnp.dot(normed, block_weight, preferred_element_type=jnp.float32)
+            next_sums = part if next_sums is None else next_sums + part
+        return new_residual, next_sums.astype(jnp.bfloat16)
+
+    chunk = row_count // N_CHUNKS if row_count % (8 * N_CHUNKS) == 0 else row_count
+    results = []
+    for first in range(0, row_count, chunk):
+        results.append(finish(first, chunk, attend(first, chunk)))
+    if len(results) == 1:
+        return results[0]
+    return (
+        jnp.concatenate([result[0] for result in results], axis=0),
+        jnp.concatenate([result[1] for result in results], axis=0),
     )
-    for tenant_id in range(TENANTS):
-        tenant_mask = (row_tenant == tenant_id)[None, :, None]
-        prefix_scores = (
-            jnp.einsum(
-                "rhd,phd->hrp",
-                query_heads,
-                picked[tenant_id][0],
-                preferred_element_type=jnp.float32,
-            )
-            * score_scale
-        )
-        prefix_weights = jnp.where(tenant_mask, jnp.exp(prefix_scores - row_top[:, :, None]), 0.0)
-        denominator = denominator + jnp.sum(prefix_weights, axis=2)
-        accumulated = accumulated + jnp.einsum(
-            "hrp,phd->rhd",
-            prefix_weights.astype(jnp.bfloat16),
-            picked[tenant_id][1],
-            preferred_element_type=jnp.float32,
-        )
-    attended = (
-        (accumulated / jnp.transpose(denominator)[:, :, None])
-        .astype(jnp.bfloat16)
-        .reshape(row_count, -1)
-    )
-
-    projected = jnp.dot(attended, weight_pieces[0], preferred_element_type=jnp.float32)
-    for shift in range(1, n_tp):
-        head_block = shifted(attended, shift, n_tp)
-        projected = projected + jnp.dot(
-            head_block, weight_pieces[shift], preferred_element_type=jnp.float32
-        )
-    new_residual = (residual.astype(jnp.float32) + projected).astype(jnp.bfloat16)
-
-    full_new = lax.all_gather(new_residual, "tp", axis=1, tiled=True)
-    widened = full_new.astype(jnp.float32)
-    mean_square = jnp.mean(widened * widened, axis=1, keepdims=True)
-    normed = (widened * lax.rsqrt(mean_square + 1e-05) * norm_gain.astype(jnp.float32)).astype(
-        jnp.bfloat16
-    )
-    next_sums = jnp.dot(normed, next_query_weight, preferred_element_type=jnp.float32)
-    return (new_residual, next_sums.astype(jnp.bfloat16))
 
 
 def solution(mesh):

time: 129 us -> 126 us (0.977); the launches traced: 127 us -> 126 us
  waiting for transfers between devices: 59 us -> 33.1 us
  starting transfers between devices: 9.25 us -> 29.5 us
  matrix products: 24.9 us -> 29.9 us
    all_gather x1 -> x0, waiting for transfers between devices: 29 us -> none  [local(): full_new = lax.all_gather(new_residual, 'tp', axis=1, tiled=True)]
    ppermute x6 -> x15, starting transfers between devices: 9.18 us -> 29.5 us  [shifted(): return lax.ppermute(block, 'tp', pairs)]
    dot_general x15 -> x36, matrix products: 19.4 us -> 25.2 us  [the longest x8 8.68 us: attend(): jnp.einsum('hrp,phd->rhd', prefix_weights.astype(jnp.bfloat16), picked[te...]
    ppermute x6 -> x15, waiting for transfers between devices: 8.46 us -> 10.1 us  [shifted(): return lax.ppermute(block, 'tp', pairs)]
    concatenate x0 -> x2, other arithmetic: none -> 1.41 us  [the longest x1 0.72 us: local(): jnp.concatenate([result[0] for result in results], axis=0)]
    all_gather x1, waiting for transfers between devices: 21.5 us -> 22.9 us  [tenant_prefixes(): every_slot = lax.all_gather(own_slot, 'req', axis=0, tiled=True)]
    unnamed x12 -> x60, local copies, waits for them, and re-layouts: 3.16 us -> 2.44 us
    reduce_sum x3 -> x9, other arithmetic: 5.88 us -> 5.3 us  [the longest x1 4.39 us: attend(): denominator = denominator + jnp.sum(prefix_weights, axis=2)]
  transfers between devices with their start and end apart: 8 -> 16, of which waited for: 5 -> 8; matrix products, arithmetic and copies ran while one was open for 27% -> 32% of each run, Pallas kernels for 0% -> 0%
where the time goes in v5:
time: 126 us
  waiting for transfers between devices  33.1 us (26%)
  matrix products  29.9 us (24%)
  starting transfers between devices  29.5 us (23%)
  between operations  17.7 us (14%)
  other arithmetic  7.82 us (6%)
  local copies, waits for them, and re-layouts  7.78 us (6%)
    ppermute x15, starting transfers between devices, shifted(): return lax.ppermute(block, 'tp', pairs)  29.5 us
    all_gather x1, waiting for transfers between devices, tenant_prefixes(): every_slot = lax.all_gather(own_slot, 'req', axis=0, tiled=True)  22.9 us
    ppermute x15, waiting for transfers between devices, shifted(): return lax.ppermute(block, 'tp', pairs)  10.1 us
    dot_general x8, matrix products, attend(): jnp.einsum('hrp,phd->rhd', prefix_weights.astype(jnp.bfloat16), picked[te...  8.68 us
    dot_general x8, matrix products, attend(): jnp.einsum('rhd,phd->hrp', chunk_queries, picked[tenant_id][0], preferred...  8.59 us
    reduce_sum x1, other arithmetic, attend(): denominator = denominator + jnp.sum(prefix_weights, axis=2)  4.39 us
    dot_general x2, matrix products, attend(): jnp.einsum('rhd,khd->hrk', chunk_queries, suffix_keys, preferred_element_...  2.66 us
    dot_general x8, matrix products, finish(): part = jnp.dot(normed, block_weight, preferred_element_type=jnp.float32)  2.57 us
  transfers between devices with their start and end apart: 16, of which 8 were waited for; matrix products, arithmetic and copies ran while one was open for 32% of the time, Pallas kernels for 0%

profile of v5, /device:TPU:8, one launch (start us, length us, event | category | flops | bytes accessed | tf_op | source)
XLA Modules:
  0.0 125.8 jit_solution(18142783611301239412)
XLA Ops:
  7.3 2.2 %copy.88 = bf16[1024,1,256]{0,2,1:T(8,128)(2,1)} copy(bf16[1024,1,256]{2,0,1:T(8,128)(2,1)} %param.13) | data formatting | bytes 1048576 | tf_op args[3]
  9.6 2.1 %constant_dynamic-slice_fusion.1 = (bf16[320,512]{1,0:T(8,128)(2,1)S(1)}, bf16[320,512]{1,0:T(8,128)(2,1)}, bf16[320,512]{1,0:T(8,128)(2,1)}) fusion(bf16[320,2048]{1,0:T(8,128)(2,1)} %param.14, s32[]{:T(128)S(6)} %select_n.223, s32[]{:T(128)S(6)} %select_n.221, s32[]{:T(128)S(6)} %select_n.225), kind=kLoop, calls=%fused_computation.253 | loop fusion | bytes 1966092 | tf_op jit(solution)/shard_map/dynamic_slice | solution.py:68
  11.7 1.6 %collective-permute-start.1 = (bf16[320,512]{1,0:T(8,128)(2,1)}, bf16[320,512]{1,0:T(8,128)(2,1)S(1)}, u32[]{:S(2)}, u32[]{:S(2)}) collective-permute-start(bf16[320,512]{1,0:T(8,128)(2,1)} %get-tuple-element.17), channel_id=1, source_target_pairs={{0,1},{1,2},{2,3},{3,0},{4,5},{5,6},{6,7},{7,4},{8,9},{9,10},{10,1... | collective-permute-start | bytes 983048 | tf_op jit(solution)/shard_map/ppermute | solution.py:43
  13.7 2.6 %collective-permute-start.3 = (bf16[320,512]{1,0:T(8,128)(2,1)S(1)}, bf16[320,512]{1,0:T(8,128)(2,1)S(1)}, u32[]{:S(2)}, u32[]{:S(2)}) collective-permute-start(bf16[320,512]{1,0:T(8,128)(2,1)S(1)} %get-tuple-element.16), channel_id=1, source_target_pairs={{0,2},{1,3},{2,0},{3,1},{4,6},{5,7},{6,4},{7,5},{8,10},{9,11},{10,... | collective-permute-start | bytes 983048 | tf_op jit(solution)/shard_map/ppermute | solution.py:43
  16.3 0.7 fusion.210
  20.1 0.7 fusion.208
  20.9 0.6 broadcast_compare_fusion.7
  22.3 1.8 %select_reduce_fusion.9 = (f32[5,128]{1,0:T(8,128)}, f32[5,128,256]{1,2,0:T(8,128)}) fusion(pred[128,256]{0,1:T(8,128)(4,1)S(1)} %fusion.146, bf16[128,5,64]{0,2,1:T(8,128)(2,1)S(1)} %bitcast.187, bf16[256,5,64]{0,1,2:T(8,128)(2,1)S(1)} %fusion.27), kind=kOutput, calls=%fused_computation.107 | convolution fusion | flops 21462400 | bytes 936448 | tf_op jit(solution)/shard_map/rhd,khd->hrk/dot_general | solution.py:97
  24.1 0.9 select_reduce_fusion.8
  25.0 22.9 %all-gather.3.cloned.1.call-done = bf16[8192,1,256]{0,2,1:T(8,128)(2,1)} async-done(((bf16[1024,1,256]{0,2,1:T(8,128)(2,1)}), bf16[8192,1,256]{0,2,1:T(8,128)(2,1)}) %all-gather.3.cloned.1.call-update) | async-done | bytes 4194320 | tf_op jit(solution)/shard_map/all_gather | solution.py:33
  47.9 1.7 %constant_dynamic-slice_fusion.6 = (bf16[1024,1,256]{0,2,1:T(8,128)(2,1)S(1)}, bf16[1024,1,256]{0,2,1:T(8,128)(2,1)S(1)}, bf16[1024,1,256]{0,2,1:T(8,128)(2,1)S(1)}, bf16[1024,1,256]{0,2,1:T(8,128)(2,1)S(1)}) fusion(bf16[8192,1,256]{0,2,1:T(8,128)(2,1)} %all-gather.3.cloned.1.call-done, s32[]{:T(128)S(6)} %select_n.201, s32[]{:T(128)S(6)} %select_n.205, ...), kind=kLoop, calls=%fused_computation.259 | loop fusion | bytes 4194320 | tf_op jit(solution)/shard_map/dynamic_slice | solution.py:35
  51.4 0.5 fusion
  51.9 1.1 select_reduce_fusion.5
  53.0 1.1 select_reduce_fusion.1
  54.1 1.1 select_reduce_fusion.6
  55.2 1.1 select_reduce_fusion.2
  56.3 1.1 select_reduce_fusion.7
  57.3 1.1 select_reduce_fusion.3
  58.4 1.1 select_reduce_fusion.4
  59.5 1.2 select_reduce_fusion
  63.0 1.1 fusion.8
  64.1 1.1 fusion.9
  65.2 1.1 fusion.10
  66.3 1.1 fusion.11
  67.4 4.4 %bitcast_reduce_fusion.3 = (f32[5,128]{1,0:T(8,128)S(1)}, f32[5,128]{1,0:T(8,128)S(1)}, f32[5,128]{1,0:T(8,128)S(1)}, f32[5,128]{1,0:T(8,128)S(1)}, f32[5,128]{1...) fusion(f32[5,1024,128]{2,1,0:T(8,128)S(1)} %get-tuple-element.58, ...), kind=kLoop, calls=%fused_computation.6 | loop fusion | flops 20966400 | bytes 20998144 | tf_op jit(solution)/shard_map/reduce_sum | solution.py:138
  72.4 1.5 %collective-permute-start = (bf16[128,320]{0,1:T(8,128)(2,1)S(1)}, bf16[128,320]{0,1:T(8,128)(2,1)S(1)}, u32[]{:S(2)}, u32[]{:S(2)}) collective-permute-start(bf16[128,320]{0,1:T(8,128)(2,1)S(1)} %bitcast.175), channel_id=1, source_target_pairs={{0,1},{1,2},{2,3},{3,0},{4,5},{5,6},{6,7},{7,4},{8,9},{9,10},{10,1... | collective-permute-start | bytes 245768 | tf_op jit(solution)/shard_map/ppermute | solution.py:43
  73.9 0.6 collective-permute-start.4
  74.5 1.1 fusion.12
  75.5 1.1 fusion.13
  76.6 1.1 fusion.14
  77.7 1.1 fusion.15
  79.5 2.5 %collective-permute-start.2 = (bf16[128,320]{0,1:T(8,128)(2,1)S(1)}, bf16[128,320]{0,1:T(8,128)(2,1)S(1)}, u32[]{:S(2)}, u32[]{:S(2)}) collective-permute-start(bf16[128,320]{0,1:T(8,128)(2,1)S(1)} %bitcast.177), channel_id=1, source_target_pairs={{0,2},{1,3},{2,0},{3,1},{4,6},{5,7},{6,4},{7,5},{8,10},{9,11},{10,... | collective-permute-start | bytes 245768 | tf_op jit(solution)/shard_map/ppermute | solution.py:43
  82.0 1.4 %collective-permute-start.6 = (bf16[128,320]{0,1:T(8,128)(2,1)S(1)}, bf16[128,320]{0,1:T(8,128)(2,1)S(1)}, u32[]{:S(2)}, u32[]{:S(2)}) collective-permute-start(bf16[128,320]{0,1:T(8,128)(2,1)S(1)} %bitcast.179), channel_id=1, source_target_pairs={{0,1},{1,2},{2,3},{3,0},{4,5},{5,6},{6,7},{7,4},{8,9},{9,10},{10,1... | collective-permute-start | bytes 245768 | tf_op jit(solution)/shard_map/ppermute | solution.py:43
  83.6 0.7 collective-permute-start.8
  84.3 1.0 collective-permute-start.7
  86.0 3.3 %collective-permute-start.9 = (bf16[128,512]{1,0:T(8,128)(2,1)S(1)}, bf16[128,512]{1,0:T(8,128)(2,1)S(1)}, u32[]{:S(2)}, u32[]{:S(2)}) collective-permute-start(bf16[128,512]{1,0:T(8,128)(2,1)S(1)} %get-tuple-element.72), channel_id=1, source_target_pairs={{0,1},{1,2},{2,3},{3,0},{4,5},{5,6},{6,7},{7,4},{8,9},{9,10},{10,1... | collective-permute-start | bytes 393224 | tf_op jit(solution)/shard_map/ppermute | solution.py:43
  89.2 4.4 %collective-permute-start.10 = (bf16[128,512]{1,0:T(8,128)(2,1)S(1)}, bf16[128,512]{1,0:T(8,128)(2,1)S(1)}, u32[]{:S(2)}, u32[]{:S(2)}) collective-permute-start(bf16[128,512]{1,0:T(8,128)(2,1)S(1)} %get-tuple-element.72), channel_id=1, source_target_pairs={{0,2},{1,3},{2,0},{3,1},{4,6},{5,7},{6,4},{7,5},{8,10},{9,11},{10,... | collective-permute-start | bytes 393224 | tf_op jit(solution)/shard_map/ppermute | solution.py:43
  93.7 1.2 collective-permute-start.11
  95.8 1.6 %collective-permute-start.12 = (bf16[128,512]{1,0:T(8,128)(2,1)S(1)}, bf16[128,512]{1,0:T(8,128)(2,1)S(1)}, u32[]{:S(2)}, u32[]{:S(2)}) collective-permute-start(bf16[128,512]{1,0:T(8,128)(2,1)S(1)} %get-tuple-element.70), channel_id=1, source_target_pairs={{0,1},{1,2},{2,3},{3,0},{4,5},{5,6},{6,7},{7,4},{8,9},{9,10},{10,1... | collective-permute-start | bytes 393224 | tf_op jit(solution)/shard_map/ppermute | solution.py:43
  97.3 6.3 %collective-permute-start.13 = (bf16[128,512]{1,0:T(8,128)(2,1)S(1)}, bf16[128,512]{1,0:T(8,128)(2,1)S(1)}, u32[]{:S(2)}, u32[]{:S(2)}) collective-permute-start(bf16[128,512]{1,0:T(8,128)(2,1)S(1)} %get-tuple-element.70), channel_id=1, source_target_pairs={{0,2},{1,3},{2,0},{3,1},{4,6},{5,7},{6,4},{7,5},{8,10},{9,11},{10,... | collective-permute-start | bytes 393224 | tf_op jit(solution)/shard_map/ppermute | solution.py:43
  103.7 0.7 pad_maximum_fusion
  104.4 0.5 collective-permute-start.14
  105.0 4.5 %collective-permute-done.10 = bf16[128,512]{1,0:T(8,128)(2,1)S(1)} collective-permute-done((bf16[128,512]{1,0:T(8,128)(2,1)S(1)}, bf16[128,512]{1,0:T(8,128)(2,1)S(1)}, u32[]{:S(2)}, u32[]{:S(2)}) %collective-permute-start.10) | collective-permute-done | bytes 131104 | tf_op jit(solution)/shard_map/ppermute | solution.py:43
  109.7 1.0 collective-permute-done.11
  111.2 1.3 collective-permute-done.12
  112.5 2.3 %collective-permute-done.13 = bf16[128,512]{1,0:T(8,128)(2,1)S(1)} collective-permute-done((bf16[128,512]{1,0:T(8,128)(2,1)S(1)}, bf16[128,512]{1,0:T(8,128)(2,1)S(1)}, u32[]{:S(2)}, u32[]{:S(2)}) %collective-permute-start.13) | collective-permute-done | bytes 131104 | tf_op jit(solution)/shard_map/ppermute | solution.py:43
  114.9 1.0 collective-permute-done.14
  118.3 0.7 pad_maximum_fusion.1
  (131 shorter events, 11.9 us)
Async XLA Ops:
  7.2 103.6 %copy-start = (bf16[2048,320]{0,1:T(8,128)(2,1)S(1)}, bf16[2048,320]{0,1:T(8,128)(2,1)}, u32[]{:S(2)}) copy-start(bf16[2048,320]{0,1:T(8,128)(2,1)} %param.16) | copy-start | bytes 3932164
  7.2 9.1 %copy-start.16 = (s32[4]{0:T(128)S(1)}, s32[4]{0:T(128)}, u32[]{:S(2)}) copy-start(s32[4]{0:T(128)} %param.19) | copy-start | bytes 52
  7.2 12.5 %copy-start.28 = (s32[1,4]{1,0:T(1,128)S(1)}, s32[1,4]{1,0:T(1,128)}, u32[]{:S(2)}) copy-start(s32[1,4]{1,0:T(1,128)} %param.17) | copy-start | bytes 52
  7.2 12.6 %copy-start.9 = (bf16[256,1,256]{2,0,1:T(8,128)(2,1)S(1)}, bf16[256,1,256]{2,0,1:T(8,128)(2,1)}, u32[]{:S(2)}) copy-start(bf16[256,1,256]{2,0,1:T(8,128)(2,1)} %param.12) | copy-start | bytes 393220
  7.2 12.9 %copy-start.15 = (bf16[2048]{0:T(1024)(128)(2,1)S(1)}, bf16[2048]{0:T(1024)(128)(2,1)}, u32[]{:S(2)}) copy-start(bf16[2048]{0:T(1024)(128)(2,1)} %param.15) | copy-start | bytes 12292
  7.2 13.6 %copy-start.27 = (s32[1,4]{1,0:T(1,128)S(1)}, s32[1,4]{1,0:T(1,128)}, u32[]{:S(2)}) copy-start(s32[1,4]{1,0:T(1,128)} %param.18) | copy-start | bytes 52
  7.2 14.4 %copy-start.4 = (bf16[256,320]{0,1:T(8,128)(2,1)S(1)}, bf16[256,320]{0,1:T(8,128)(2,1)}, u32[]{:S(2)}) copy-start(bf16[256,320]{0,1:T(8,128)(2,1)} %param.11) | copy-start | bytes 491524
  7.2 40.7 %all-gather.3.cloned.1.call-start = ((), (), s32[]{:S(2)}) async-start(), calls=%async_computation | async-start | bytes 4718592 | tf_op jit(solution)/shard_map/all_gather | solution.py:33
  11.7 67.8 %collective-permute-start.1 = (bf16[320,512]{1,0:T(8,128)(2,1)}, bf16[320,512]{1,0:T(8,128)(2,1)S(1)}, u32[]{:S(2)}, u32[]{:S(2)}) collective-permute-start(bf16[320,512]{1,0:T(8,128)(2,1)} %get-tuple-element.17), channel_id=1, source_target_pairs={{0,1},{1,2},{2,3},{3,0},{4,5},{5,6},{6,7},{7,4},{8,9},{9,10},{10,1... | collective-permute-start | bytes 983048 | tf_op jit(solution)/shard_map/ppermute | solution.py:43
  13.3 70.4 %collective-permute-start.5 = (bf16[320,512]{1,0:T(8,128)(2,1)}, bf16[320,512]{1,0:T(8,128)(2,1)S(1)}, u32[]{:S(2)}, u32[]{:S(2)}) collective-permute-start(bf16[320,512]{1,0:T(8,128)(2,1)} %get-tuple-element.18), channel_id=1, source_target_pairs={{0,3},{1,0},{2,1},{3,2},{4,7},{5,4},{6,5},{7,6},{8,11},{9,8},{10,9... | collective-permute-start | bytes 983048 | tf_op jit(solution)/shard_map/ppermute | solution.py:43
  13.7 71.9 %collective-permute-start.3 = (bf16[320,512]{1,0:T(8,128)(2,1)S(1)}, bf16[320,512]{1,0:T(8,128)(2,1)S(1)}, u32[]{:S(2)}, u32[]{:S(2)}) collective-permute-start(bf16[320,512]{1,0:T(8,128)(2,1)S(1)} %get-tuple-element.16), channel_id=1, source_target_pairs={{0,2},{1,3},{2,0},{3,1},{4,6},{5,7},{6,4},{7,5},{8,10},{9,11},{10,... | collective-permute-start | bytes 983048 | tf_op jit(solution)/shard_map/ppermute | solution.py:43
  21.6 2.5 %copy-start.7 = (pred[128,256]{0,1:T(8,128)(4,1)}, pred[128,256]{0,1:T(8,128)(4,1)S(1)}, u32[]{:S(2)}) copy-start(pred[128,256]{0,1:T(8,128)(4,1)S(1)} %fusion.146) | copy-start | bytes 98308
  21.6 2.4 %copy-start.5 = (pred[128,256]{0,1:T(8,128)(4,1)}, pred[128,256]{0,1:T(8,128)(4,1)S(1)}, u32[]{:S(2)}) copy-start(pred[128,256]{0,1:T(8,128)(4,1)S(1)} %fusion.147) | copy-start | bytes 98308
  21.7 2.3 %copy-start.12 = (bf16[128,320]{0,1:T(8,128)(2,1)}, bf16[128,320]{0,1:T(8,128)(2,1)S(1)}, u32[]{:S(2)}) copy-start(bf16[128,320]{0,1:T(8,128)(2,1)S(1)} %get-tuple-element.27) | copy-start | bytes 245764
  21.7 2.3 %copy-start.10 = (bf16[128,320]{0,1:T(8,128)(2,1)}, bf16[128,320]{0,1:T(8,128)(2,1)S(1)}, u32[]{:S(2)}) copy-start(bf16[128,320]{0,1:T(8,128)(2,1)S(1)} %get-tuple-element.28) | copy-start | bytes 245764
  50.7 1.2 copy-start.13
  50.7 1.2 copy-start.25
  51.3 1.7 %copy-start.11 = (bf16[128,320]{0,1:T(8,128)(2,1)S(1)}, bf16[128,320]{0,1:T(8,128)(2,1)}, u32[]{:S(2)}) copy-start(bf16[128,320]{0,1:T(8,128)(2,1)} %copy-done.10) | copy-start | bytes 245764
  51.3 1.7 %copy-start.20 = (pred[128]{0:T(512)(128)(4,1)S(1)}, pred[128]{0:T(512)(128)(4,1)}, u32[]{:S(2)}) copy-start(pred[128]{0:T(512)(128)(4,1)} %get-tuple-element.40) | copy-start | bytes 388
  51.9 2.2 %copy-start.24 = (pred[128]{0:T(512)(128)(4,1)S(1)}, pred[128]{0:T(512)(128)(4,1)}, u32[]{:S(2)}) copy-start(pred[128]{0:T(512)(128)(4,1)} %get-tuple-element.36) | copy-start | bytes 388
  53.0 2.1 %copy-start.21 = (pred[128]{0:T(512)(128)(4,1)S(1)}, pred[128]{0:T(512)(128)(4,1)}, u32[]{:S(2)}) copy-start(pred[128]{0:T(512)(128)(4,1)} %get-tuple-element.39) | copy-start | bytes 388
  54.1 2.1 %copy-start.23 = (pred[128]{0:T(512)(128)(4,1)S(1)}, pred[128]{0:T(512)(128)(4,1)}, u32[]{:S(2)}) copy-start(pred[128]{0:T(512)(128)(4,1)} %get-tuple-element.35) | copy-start | bytes 388
  55.2 2.1 %copy-start.22 = (pred[128]{0:T(512)(128)(4,1)S(1)}, pred[128]{0:T(512)(128)(4,1)}, u32[]{:S(2)}) copy-start(pred[128]{0:T(512)(128)(4,1)} %get-tuple-element.42) | copy-start | bytes 388
  56.2 2.1 %copy-start.26 = (pred[128]{0:T(512)(128)(4,1)S(1)}, pred[128]{0:T(512)(128)(4,1)}, u32[]{:S(2)}) copy-start(pred[128]{0:T(512)(128)(4,1)} %get-tuple-element.38) | copy-start | bytes 388
  57.3 2.1 %copy-start.19 = (pred[128]{0:T(512)(128)(4,1)S(1)}, pred[128]{0:T(512)(128)(4,1)}, u32[]{:S(2)}) copy-start(pred[128]{0:T(512)(128)(4,1)} %get-tuple-element.41) | copy-start | bytes 388
  60.7 2.1 %copy-start.18 = (f32[5,128]{1,0:T(8,128)S(1)}, f32[5,128]{1,0:T(8,128)}, u32[]{:S(2)}) copy-start(f32[5,128]{1,0:T(8,128)} %get-tuple-element.65) | copy-start | bytes 7684
  60.7 2.2 %copy-start.2 = (f32[5,128,256]{1,2,0:T(8,128)S(1)}, f32[5,128,256]{1,2,0:T(8,128)}, u32[]{:S(2)}) copy-start(f32[5,128,256]{1,2,0:T(8,128)} %get-tuple-element.66) | copy-start | bytes 1966084
  60.7 2.2 %copy-start.8 = (pred[128,256]{0,1:T(8,128)(4,1)S(1)}, pred[128,256]{0,1:T(8,128)(4,1)}, u32[]{:S(2)}) copy-start(pred[128,256]{0,1:T(8,128)(4,1)} %copy-done.7) | copy-start | bytes 98308
  66.3 1.1 copy-start.17
  67.4 4.7 %copy-start.1 = (bf16[320,2048]{1,0:T(8,128)(2,1)S(1)}, bf16[320,2048]{1,0:T(8,128)(2,1)}, u32[]{:S(2)}) copy-start(bf16[320,2048]{1,0:T(8,128)(2,1)} %param.14) | copy-start | bytes 3932164
  72.4 9.6 %collective-permute-start = (bf16[128,320]{0,1:T(8,128)(2,1)S(1)}, bf16[128,320]{0,1:T(8,128)(2,1)S(1)}, u32[]{:S(2)}, u32[]{:S(2)}) collective-permute-start(bf16[128,320]{0,1:T(8,128)(2,1)S(1)} %bitcast.175), channel_id=1, source_target_pairs={{0,1},{1,2},{2,3},{3,0},{4,5},{5,6},{6,7},{7,4},{8,9},{9,10},{10,1... | collective-permute-start | bytes 245768 | tf_op jit(solution)/shard_map/ppermute | solution.py:43
  73.9 10.4 %collective-permute-start.4 = (bf16[128,320]{0,1:T(8,128)(2,1)S(1)}, bf16[128,320]{0,1:T(8,128)(2,1)S(1)}, u32[]{:S(2)}, u32[]{:S(2)}) collective-permute-start(bf16[128,320]{0,1:T(8,128)(2,1)S(1)} %bitcast.176), channel_id=1, source_target_pairs={{0,3},{1,0},{2,1},{3,2},{4,7},{5,4},{6,5},{7,6},{8,11},{9,8},{10,9... | collective-permute-start | bytes 245768 | tf_op jit(solution)/shard_map/ppermute | solution.py:43
  77.7 1.1 copy-start.6
  78.8 6.8 %copy-start.3 = (bf16[256,512]{1,0:T(8,128)(2,1)S(1)}, bf16[256,512]{1,0:T(8,128)(2,1)}, u32[]{:S(2)}) copy-start(bf16[256,512]{1,0:T(8,128)(2,1)} %param.10) | copy-start | bytes 786436
  79.5 6.1 %collective-permute-start.2 = (bf16[128,320]{0,1:T(8,128)(2,1)S(1)}, bf16[128,320]{0,1:T(8,128)(2,1)S(1)}, u32[]{:S(2)}, u32[]{:S(2)}) collective-permute-start(bf16[128,320]{0,1:T(8,128)(2,1)S(1)} %bitcast.177), channel_id=1, source_target_pairs={{0,2},{1,3},{2,0},{3,1},{4,6},{5,7},{6,4},{7,5},{8,10},{9,11},{10,... | collective-permute-start | bytes 245768 | tf_op jit(solution)/shard_map/ppermute | solution.py:43
  82.0 11.7 %collective-permute-start.6 = (bf16[128,320]{0,1:T(8,128)(2,1)S(1)}, bf16[128,320]{0,1:T(8,128)(2,1)S(1)}, u32[]{:S(2)}, u32[]{:S(2)}) collective-permute-start(bf16[128,320]{0,1:T(8,128)(2,1)S(1)} %bitcast.179), channel_id=1, source_target_pairs={{0,1},{1,2},{2,3},{3,0},{4,5},{5,6},{6,7},{7,4},{8,9},{9,10},{10,1... | collective-permute-start | bytes 245768 | tf_op jit(solution)/shard_map/ppermute | solution.py:43
  83.6 11.4 %collective-permute-start.8 = (bf16[128,320]{0,1:T(8,128)(2,1)S(1)}, bf16[128,320]{0,1:T(8,128)(2,1)S(1)}, u32[]{:S(2)}, u32[]{:S(2)}) collective-permute-start(bf16[128,320]{0,1:T(8,128)(2,1)S(1)} %bitcast.180), channel_id=1, source_target_pairs={{0,3},{1,0},{2,1},{3,2},{4,7},{5,4},{6,5},{7,6},{8,11},{9,8},{10,9... | collective-permute-start | bytes 245768 | tf_op jit(solution)/shard_map/ppermute | solution.py:43
  84.3 11.1 %collective-permute-start.7 = (bf16[128,320]{0,1:T(8,128)(2,1)S(1)}, bf16[128,320]{0,1:T(8,128)(2,1)S(1)}, u32[]{:S(2)}, u32[]{:S(2)}) collective-permute-start(bf16[128,320]{0,1:T(8,128)(2,1)S(1)} %bitcast.181), channel_id=1, source_target_pairs={{0,2},{1,3},{2,0},{3,1},{4,6},{5,7},{6,4},{7,5},{8,10},{9,11},{10,... | collective-permute-start | bytes 245768 | tf_op jit(solution)/shard_map/ppermute | solution.py:43
  85.5 25.3 %copy-start.14 = (f32[512]{0:T(512)S(1)}, f32[512]{0:T(512)}, u32[]{:S(2)}) copy-start(f32[512]{0:T(512)} %get-tuple-element.34) | copy-start | bytes 6148
  86.0 18.4 %collective-permute-start.9 = (bf16[128,512]{1,0:T(8,128)(2,1)S(1)}, bf16[128,512]{1,0:T(8,128)(2,1)S(1)}, u32[]{:S(2)}, u32[]{:S(2)}) collective-permute-start(bf16[128,512]{1,0:T(8,128)(2,1)S(1)} %get-tuple-element.72), channel_id=1, source_target_pairs={{0,1},{1,2},{2,3},{3,0},{4,5},{5,6},{6,7},{7,4},{8,9},{9,10},{10,1... | collective-permute-start | bytes 393224 | tf_op jit(solution)/shard_map/ppermute | solution.py:43
  89.2 20.3 %collective-permute-start.10 = (bf16[128,512]{1,0:T(8,128)(2,1)S(1)}, bf16[128,512]{1,0:T(8,128)(2,1)S(1)}, u32[]{:S(2)}, u32[]{:S(2)}) collective-permute-start(bf16[128,512]{1,0:T(8,128)(2,1)S(1)} %get-tuple-element.72), channel_id=1, source_target_pairs={{0,2},{1,3},{2,0},{3,1},{4,6},{5,7},{6,4},{7,5},{8,10},{9,11},{10,... | collective-permute-start | bytes 393224 | tf_op jit(solution)/shard_map/ppermute | solution.py:43
  93.7 17.0 %collective-permute-start.11 = (bf16[128,512]{1,0:T(8,128)(2,1)S(1)}, bf16[128,512]{1,0:T(8,128)(2,1)S(1)}, u32[]{:S(2)}, u32[]{:S(2)}) collective-permute-start(bf16[128,512]{1,0:T(8,128)(2,1)S(1)} %get-tuple-element.72), channel_id=1, source_target_pairs={{0,3},{1,0},{2,1},{3,2},{4,7},{5,4},{6,5},{7,6},{8,11},{9,8},{10,9... | collective-permute-start | bytes 393224 | tf_op jit(solution)/shard_map/ppermute | solution.py:43
  95.8 16.6 %collective-permute-start.12 = (bf16[128,512]{1,0:T(8,128)(2,1)S(1)}, bf16[128,512]{1,0:T(8,128)(2,1)S(1)}, u32[]{:S(2)}, u32[]{:S(2)}) collective-permute-start(bf16[128,512]{1,0:T(8,128)(2,1)S(1)} %get-tuple-element.70), channel_id=1, source_target_pairs={{0,1},{1,2},{2,3},{3,0},{4,5},{5,6},{6,7},{7,4},{8,9},{9,10},{10,1... | collective-permute-start | bytes 393224 | tf_op jit(solution)/shard_map/ppermute | solution.py:43
  97.3 17.4 %collective-permute-start.13 = (bf16[128,512]{1,0:T(8,128)(2,1)S(1)}, bf16[128,512]{1,0:T(8,128)(2,1)S(1)}, u32[]{:S(2)}, u32[]{:S(2)}) collective-permute-start(bf16[128,512]{1,0:T(8,128)(2,1)S(1)} %get-tuple-element.70), channel_id=1, source_target_pairs={{0,2},{1,3},{2,0},{3,1},{4,6},{5,7},{6,4},{7,5},{8,10},{9,11},{10,... | collective-permute-start | bytes 393224 | tf_op jit(solution)/shard_map/ppermute | solution.py:43
  104.4 11.5 %collective-permute-start.14 = (bf16[128,512]{1,0:T(8,128)(2,1)S(1)}, bf16[128,512]{1,0:T(8,128)(2,1)S(1)}, u32[]{:S(2)}, u32[]{:S(2)}) collective-permute-start(bf16[128,512]{1,0:T(8,128)(2,1)S(1)} %get-tuple-element.70), channel_id=1, source_target_pairs={{0,3},{1,0},{2,1},{3,2},{4,7},{5,4},{6,5},{7,6},{8,11},{9,8},{10,9... | collective-permute-start | bytes 393224 | tf_op jit(solution)/shard_map/ppermute | solution.py:43
Sparse Core Ops, SparseCore 0:
  10.0 37.8 all-gather.2

commit v6 on v4

--- a/solution.py
+++ b/solution.py
@@ -37,6 +37,11 @@
     return [from_root(own_slot, "req", owners[tenant_id]) for tenant_id in range(TENANTS)]
 
 
+def everyone(block, n_tp):
+    copies = jnp.broadcast_to(block[None], (n_tp,) + block.shape)
+    return lax.all_to_all(copies, "tp", 0, 0, tiled=False)
+
+
 def shifted(block, shift, n_tp):
     pairs = [(source, (source + shift) % n_tp) for source in range(n_tp)]
     return lax.ppermute(block, "tp", pairs)
@@ -61,11 +66,9 @@
     width = residual.shape[1]
     tp_index = lax.axis_index("tp")
 
-    weight_pieces = []
-    for shift in range(n_tp):
-        target = (tp_index + shift) % n_tp
-        piece = lax.dynamic_slice_in_dim(out_weight, target * width, width, 1)
-        weight_pieces.append(piece if shift == 0 else shifted(piece, shift, n_tp))
+    weight_pieces = lax.all_to_all(
+        out_weight.reshape(out_weight.shape[0], n_tp, width), "tp", 1, 0, tiled=False
+    )
 
     head_ids = tp_index * head_count + jnp.arange(head_count, dtype=jnp.int32)
     pair_ids = head_ids // (QH // KVH) - tp_index
@@ -140,26 +143,24 @@
         .reshape(row_count, -1)
     )
 
-    projected = jnp.dot(attended, weight_pieces[0], preferred_element_type=jnp.float32)
-    for shift in range(1, n_tp):
-        head_block = shifted(attended, shift, n_tp)
-        projected = projected + jnp.dot(
-            head_block, weight_pieces[shift], preferred_element_type=jnp.float32
-        )
+    head_blocks = everyone(attended, n_tp)
+    projected = None
+    for source in range(n_tp):
+        part = jnp.dot(head_blocks[source], weight_pieces[source], preferred_element_type=jnp.float32)
+        projected = part if projected is None else projected + part
     new_residual = (residual.astype(jnp.float32) + projected).astype(jnp.bfloat16)
 
-    blocks = [new_residual] + [shifted(new_residual, shift, n_tp) for shift in range(1, n_tp)]
-    widened = [block.astype(jnp.float32) for block in blocks]
+    blocks = everyone(new_residual, n_tp)
+    widened = [blocks[source].astype(jnp.float32) for source in range(n_tp)]
     square_sums = sum(jnp.sum(block * block, axis=1, keepdims=True) for block in widened)
     mean_square = square_sums / (width * n_tp)
     scale = lax.rsqrt(mean_square + 1e-05)
     gain = norm_gain.astype(jnp.float32)
     next_sums = None
-    for shift in range(n_tp):
-        source = (tp_index - shift) % n_tp
-        block_gain = lax.dynamic_slice_in_dim(gain, source * width, width, 0)
-        block_weight = lax.dynamic_slice_in_dim(next_query_weight, source * width, width, 0)
-        normed = (widened[shift] * scale * block_gain).astype(jnp.bfloat16)
+    for source in range(n_tp):
+        block_gain = gain[source * width:(source + 1) * width]
+        block_weight = next_query_weight[source * width:(source + 1) * width]
+        normed = (widened[source] * scale * block_gain).astype(jnp.bfloat16)
         part = jnp.dot(normed, block_weight, preferred_element_type=jnp.float32)
         next_sums = part if next_sums is None else next_sums + part
     return (new_residual, next_sums.astype(jnp.bfloat16))

time: 124 us -> 135 us (1.089)
  the two profiles are of different devices: /device:TPU:8 before, /device:TPU:0 now
where the time goes in v6:
time: 135 us; the launch traced here: 134 us
  waiting for transfers between devices  49.7 us (37%)
  blocking collectives  22.1 us (16%)
  matrix products  20 us (15%)
  between operations  17 us (13%)
  local copies, waits for them, and re-layouts  10.4 us (8%)
  starting transfers between devices  9.87 us (7%)
  other arithmetic  5.28 us (4%)
    all_to_all x1, waiting for transfers between devices, everyone(): return lax.all_to_all(copies, 'tp', 0, 0, tiled=False)  25.3 us
    all_gather x1, waiting for transfers between devices, tenant_prefixes(): every_slot = lax.all_gather(own_slot, 'req', axis=0, tiled=True)  24.4 us
    all_to_all x1, blocking collectives, everyone(): return lax.all_to_all(copies, 'tp', 0, 0, tiled=False)  22.1 us
    all_to_all x1, starting transfers between devices, local(): lax.all_to_all(out_weight.reshape(out_weight.shape[0], n_tp, width), 'tp'...  6.32 us
    dot_general x4, matrix products, local(): jnp.einsum('hrp,phd->rhd', prefix_weights.astype(jnp.bfloat16), picked[te...  5.75 us
    dot_general x4, matrix products, local(): jnp.einsum('rhd,phd->hrp', query_heads, picked[tenant_id][0], preferred_e...  5.41 us
    another operation x2, local copies, waits for them, and re-layouts, local(): lax.all_to_all(out_weight.reshape(out_weight.shape[0], n_tp, width), 'tp'...  4.53 us
    reduce_sum x1, other arithmetic, local(): denominator = denominator + jnp.sum(prefix_weights, axis=2)  4.3 us
  transfers between devices with their start and end apart: 3, of which 2 were waited for; matrix products, arithmetic and copies ran while one was open for 21% of the time, Pallas kernels for 0%

profile of v6, /device:TPU:0, one launch (start us, length us, event | category | flops | bytes accessed | tf_op | source)
XLA Modules:
  0.0 134.3 jit_solution(16930834622431837927)
XLA Ops:
  7.2 0.0 all-gather.3.cloned.1.call-start
  7.3 2.1 %copy.86 = bf16[1024,1,256]{0,2,1:T(8,128)(2,1)} copy(bf16[1024,1,256]{2,0,1:T(8,128)(2,1)} %param.13) | data formatting | bytes 1048576 | tf_op args[3]
  9.4 0.0 all-gather.3.cloned.1.call-update
  9.4 3.2 %broadcast_in_dim_reshape.4 = bf16[1,320,4,512]{3,2,1,0:T(4,128)(2,1)S(1)} reshape(bf16[320,2048]{1,0:T(8,128)(2,1)} %param.14) | data formatting | bytes 2621440 | tf_op jit(solution)/shard_map/broadcast_in_dim;reshape | solution.py:69
  12.7 1.3 copy.109
  14.0 6.3 %all-to-all-start.1 = ((bf16[1,320,4,512]{3,1,0,2:T(8,128)(2,1)}), bf16[1,320,4,512]{3,1,0,2:T(8,128)(2,1)S(1)}, u32[]{:S(2)}, u32[]{:S(2)}) async-start(bf16[1,320,4,512]{3,1,0,2:T(8,128)(2,1)} %copy.109), calls=%async_computation.1 | async-start | bytes 2621440 | tf_op jit(solution)/shard_map/all_to_all | solution.py:69
  20.3 0.6 fusion.121
  23.4 0.2 reduce-window.4
  23.6 0.1 copy.82
  23.7 0.1 convert_reduce_fusion
  23.8 0.1 select_reduce_fusion.6
  24.0 0.3 fusion.25
  24.3 0.3 fusion.24
  24.6 0.4 select_reduce_fusion.4
  25.0 24.4 %all-gather.3.cloned.1.call-done = bf16[8192,1,256]{0,2,1:T(8,128)(2,1)} async-done(((bf16[1024,1,256]{0,2,1:T(8,128)(2,1)}), bf16[8192,1,256]{0,2,1:T(8,128)(2,1)}) %all-gather.3.cloned.1.call-update) | async-done | bytes 4194320 | tf_op jit(solution)/shard_map/all_gather | solution.py:32
  49.4 1.7 %constant_dynamic-slice_fusion.2 = (bf16[1024,1,256]{0,2,1:T(8,128)(2,1)S(1)}, bf16[1024,1,256]{0,2,1:T(8,128)(2,1)S(1)}, bf16[1024,1,256]{0,2,1:T(8,128)(2,1)S(1)}, bf16[1024,1,256]{0,2,1:T(8,128)(2,1)S(1)}) fusion(bf16[8192,1,256]{0,2,1:T(8,128)(2,1)} %all-gather.3.cloned.1.call-done, s32[]{:T(128)S(6)} %select_n.80, s32[]{:T(128)S(6)} %select_n.84, ...), kind=kLoop, calls=%fused_computation.177 | loop fusion | bytes 4194320 | tf_op jit(solution)/shard_map/dynamic_slice | solution.py:34
  51.2 0.5 fusion.12
  51.7 0.5 fusion.11
  52.3 0.5 fusion.10
  52.9 0.5 fusion.9
  53.4 0.5 fusion.13
  53.9 0.5 fusion.14
  54.4 0.5 fusion.15
  55.0 1.4 %select_reduce_fusion = (f32[5,256]{1,0:T(8,128)S(1)}, f32[5,1024,256]{2,1,0:T(8,128)S(1)}) fusion(pred[256]{0:T(512)(128)(4,1)S(1)} %get-tuple-element.31, bf16[256,5,64]{0,2,1:T(8,128)(2,1)S(1)} %bitcast.175, bf16[1024,5,64]{0,1,2:T(8,128)(2,1)S(1)} %fusion.12), kind=kOutput, calls=%fused_computation.12 | convolution fusion | flops 171703040 | bytes 6067456 | tf_op jit(solution)/shard_map/rhd,phd->hrp/dot_general | solution.py:102
  56.4 1.3 select_reduce_fusion.1
  57.7 1.3 %select_reduce_fusion.2 = (f32[5,256]{1,0:T(8,128)S(1)}, f32[5,1024,256]{2,1,0:T(8,128)S(1)}) fusion(pred[256]{0:T(512)(128)(4,1)S(1)} %get-tuple-element.33, bf16[256,5,64]{0,2,1:T(8,128)(2,1)S(1)} %bitcast.173, bf16[1024,5,64]{0,1,2:T(8,128)(2,1)S(1)} %fusion.10), kind=kOutput, calls=%fused_computation.14 | convolution fusion | flops 171703040 | bytes 6067456 | tf_op jit(solution)/shard_map/rhd,phd->hrp/dot_general | solution.py:102
  59.1 1.3 select_reduce_fusion.3
  60.4 0.2 fusion.28
  60.7 1.4 %fusion = f32[5,64,256]{2,1,0:T(8,128)S(1)} fusion(f32[5,1024,256]{2,1,0:T(8,128)S(1)} %get-tuple-element.47, f32[5,256]{1,0:T(8,128)S(1)} %maximum_maximum_fusion, pred[256]{0:T(512)(128)(4,1)S(1)} %get-tuple-element.30, bf16[1024,5,64]{0,1,2:T(8,128)(2,1)S(1)} %fusion.13), kind=kOutput, calls=%fused_computation.16 | convolution fusion | flops 173015040 | bytes 6231296 | tf_op jit(solution)/shard_map/hrp,phd->rhd/dot_general | solution.py:134
  62.1 4.3 %bitcast_reduce_fusion.3 = (f32[5,256]{1,0:T(8,128)S(1)}, f32[5,256]{1,0:T(8,128)S(1)}, f32[5,256]{1,0:T(8,128)S(1)}, f32[5,256]{1,0:T(8,128)S(1)}) fusion(f32[5,1024,256]{2,1,0:T(8,128)S(1)} %get-tuple-element.47, f32[5,256]{1,0:T(8,128)S(1)} %maximum_maximum_fusion, pred[256]{0:T(512)(128)(4,1)S(1)} %get-tuple-element.30, ...), kind=kLoop, calls=%fused_computation.6 | loop fusion | flops 20966400 | bytes 20998144 | tf_op jit(solution)/shard_map/reduce_sum | solution.py:133
  66.4 0.5 fusion.16
  67.0 1.4 %fusion.1 = f32[5,64,256]{2,1,0:T(8,128)S(1)} fusion(f32[5,1024,256]{2,1,0:T(8,128)S(1)} %get-tuple-element.43, f32[5,256]{1,0:T(8,128)S(1)} %maximum_maximum_fusion, pred[256]{0:T(512)(128)(4,1)S(1)} %get-tuple-element.33, bf16[1024,5,64]{0,1,2:T(8,128)(2,1)S(1)} %fusion.14), kind=kOutput, calls=%fused_computation.17 | convolution fusion | flops 173015040 | bytes 6231296 | tf_op jit(solution)/shard_map/hrp,phd->rhd/dot_general | solution.py:134
  68.4 1.4 %fusion.2 = f32[5,64,256]{2,1,0:T(8,128)S(1)} fusion(f32[5,1024,256]{2,1,0:T(8,128)S(1)} %get-tuple-element.41, f32[5,256]{1,0:T(8,128)S(1)} %maximum_maximum_fusion, pred[256]{0:T(512)(128)(4,1)S(1)} %get-tuple-element.32, bf16[1024,5,64]{0,1,2:T(8,128)(2,1)S(1)} %fusion.15), kind=kOutput, calls=%fused_computation.18 | convolution fusion | flops 173015040 | bytes 6231296 | tf_op jit(solution)/shard_map/hrp,phd->rhd/dot_general | solution.py:134
  69.8 1.4 %fusion.3 = f32[5,64,256]{2,1,0:T(8,128)S(1)} fusion(f32[5,1024,256]{2,1,0:T(8,128)S(1)} %get-tuple-element.39, f32[5,256]{1,0:T(8,128)S(1)} %maximum_maximum_fusion, pred[256]{0:T(512)(128)(4,1)S(1)} %get-tuple-element.31, bf16[1024,5,64]{0,1,2:T(8,128)(2,1)S(1)} %fusion.16), kind=kOutput, calls=%fused_computation.19 | convolution fusion | flops 173015040 | bytes 6231296 | tf_op jit(solution)/shard_map/hrp,phd->rhd/dot_general | solution.py:134
  71.3 0.3 fusion.26
  71.7 22.1 %all_to_all.25 = bf16[4,256,320]{1,2,0:T(8,128)(2,1)S(1)} all-to-all(bf16[4,256,320]{1,2,0:T(8,128)(2,1)S(1)} %broadcast_in_dim.150), channel_id=1, replica_groups=mesh['req'=8,'tp'=4] {'tp'}, dimensions={0} | all-to-all | bytes 1310720 | tf_op jit(solution)/shard_map/all_to_all | solution.py:42
  93.8 0.3 fusion.58
  94.1 0.3 convolution_add_fusion.2
  94.5 0.3 convolution_add_fusion.1
  94.8 0.3 fusion.18
  95.2 1.1 broadcast_in_dim.151
  96.3 3.5 %all-to-all-start.2 = ((bf16[4,256,512]{2,1,0:T(8,128)(2,1)}), bf16[4,256,512]{2,1,0:T(8,128)(2,1)S(1)}, u32[]{:S(2)}, u32[]{:S(2)}) async-start(bf16[4,256,512]{2,1,0:T(8,128)(2,1)} %broadcast_in_dim.151), calls=%async_computation.2 | async-start | bytes 2097152 | tf_op jit(solution)/shard_map/all_to_all | solution.py:42
  99.8 25.3 %all-to-all-done.2 = bf16[4,256,512]{2,1,0:T(8,128)(2,1)S(1)} async-done(((bf16[4,256,512]{2,1,0:T(8,128)(2,1)}), bf16[4,256,512]{2,1,0:T(8,128)(2,1)S(1)}, u32[]{:S(2)}, u32[]{:S(2)}) %all-to-all-start.2) | async-done | bytes 1048608 | tf_op jit(solution)/shard_map/all_to_all | solution.py:42
  125.1 0.3 fusion.49
  125.4 0.4 fusion.62
  125.7 0.4 convolution_add_fusion.5
  126.1 0.4 convolution_add_fusion.4
  126.5 1.0 fusion.27
  (33 shorter events, 0.4 us)
Async XLA Ops:
  7.2 17.4 %copy-start = (bf16[256,320]{0,1:T(8,128)(2,1)S(1)}, bf16[256,320]{0,1:T(8,128)(2,1)}, u32[]{:S(2)}) copy-start(bf16[256,320]{0,1:T(8,128)(2,1)} %param.11) | copy-start | bytes 491524
  7.2 13.1 %copy-start.6 = (s32[4]{0:T(128)S(1)}, s32[4]{0:T(128)}, u32[]{:S(2)}) copy-start(s32[4]{0:T(128)} %param.19) | copy-start | bytes 52
  7.2 16.2 %copy-start.8 = (s32[1,4]{1,0:T(1,128)S(1)}, s32[1,4]{1,0:T(1,128)}, u32[]{:S(2)}) copy-start(s32[1,4]{1,0:T(1,128)} %param.17) | copy-start | bytes 52
  7.2 16.4 %copy-start.4 = (bf16[256,1,256]{2,0,1:T(8,128)(2,1)S(1)}, bf16[256,1,256]{2,0,1:T(8,128)(2,1)}, u32[]{:S(2)}) copy-start(bf16[256,1,256]{2,0,1:T(8,128)(2,1)} %param.12) | copy-start | bytes 393220
  7.2 16.6 %copy-start.7 = (s32[1,4]{1,0:T(1,128)S(1)}, s32[1,4]{1,0:T(1,128)}, u32[]{:S(2)}) copy-start(s32[1,4]{1,0:T(1,128)} %param.18) | copy-start | bytes 52
  7.2 42.2 %all-gather.3.cloned.1.call-start = ((), (), s32[]{:S(2)}) async-start(), calls=%async_computation.3 | async-start | bytes 4718592 | tf_op jit(solution)/shard_map/all_gather | solution.py:32
  14.0 57.7 %all-to-all-start.1 = ((bf16[1,320,4,512]{3,1,0,2:T(8,128)(2,1)}), bf16[1,320,4,512]{3,1,0,2:T(8,128)(2,1)S(1)}, u32[]{:S(2)}, u32[]{:S(2)}) async-start(bf16[1,320,4,512]{3,1,0,2:T(8,128)(2,1)} %copy.109), calls=%async_computation.1 | async-start | bytes 2621440 | tf_op jit(solution)/shard_map/all_to_all | solution.py:69
  71.3 23.5 %copy-start.3 = (bf16[256,512]{1,0:T(8,128)(2,1)S(1)}, bf16[256,512]{1,0:T(8,128)(2,1)}, u32[]{:S(2)}) copy-start(bf16[256,512]{1,0:T(8,128)(2,1)} %param.10) | copy-start | bytes 786436
  71.7 28.1 %copy-start.5 = (bf16[2048]{0:T(1024)(128)(2,1)S(1)}, bf16[2048]{0:T(1024)(128)(2,1)}, u32[]{:S(2)}) copy-start(bf16[2048]{0:T(1024)(128)(2,1)} %param.15) | copy-start | bytes 12292
  93.8 31.5 %copy-start.2 = (bf16[2048,320]{0,1:T(8,128)(2,1)S(1)}, bf16[2048,320]{0,1:T(8,128)(2,1)}, u32[]{:S(2)}) copy-start(bf16[2048,320]{0,1:T(8,128)(2,1)} %param.16) | copy-start | bytes 3932164
  95.2 32.3 %copy-start.1 = (bf16[256,512]{1,0:T(8,128)(2,1)}, bf16[256,512]{1,0:T(8,128)(2,1)S(1)}, u32[]{:S(2)}) copy-start(bf16[256,512]{1,0:T(8,128)(2,1)S(1)} %fusion.18) | copy-start | bytes 786436
  96.3 28.8 %all-to-all-start.2 = ((bf16[4,256,512]{2,1,0:T(8,128)(2,1)}), bf16[4,256,512]{2,1,0:T(8,128)(2,1)S(1)}, u32[]{:S(2)}, u32[]{:S(2)}) async-start(bf16[4,256,512]{2,1,0:T(8,128)(2,1)} %broadcast_in_dim.151), calls=%async_computation.2 | async-start | bytes 2097152 | tf_op jit(solution)/shard_map/all_to_all | solution.py:42
Sparse Core Ops, SparseCore 0:
  10.0 39.4 all-gather.2

commit v7 on v4

--- a/solution.py
+++ b/solution.py
@@ -7,6 +7,7 @@
 KVH = 5
 HD = 64
 TENANTS = 4
+MOSTLEN = 128
 GATHER_SLOTS_MAX = 16
 
 
@@ -26,15 +27,24 @@
     return (key_heads, value_heads)
 
 
-def tenant_prefixes(own_slot, owners, n_req):
+def tenant_slots(own_slot, owners, n_req):
     slot_rows = own_slot.shape[0]
     if n_req <= GATHER_SLOTS_MAX:
-        every_slot = lax.all_gather(own_slot, "req", axis=0, tiled=True)
-        return [
-            lax.dynamic_slice_in_dim(every_slot, owners[tenant_id] * slot_rows, slot_rows, 0)
-            for tenant_id in range(TENANTS)
-        ]
-    return [from_root(own_slot, "req", owners[tenant_id]) for tenant_id in range(TENANTS)]
+        gathered = lax.all_gather(own_slot, "req", axis=0, tiled=True)
+
+        def slot_of(tenant_id):
+            owner = owners[tenant_id]
+            return lax.dynamic_slice_in_dim(gathered, owner * slot_rows, slot_rows, 0)
+
+        return slot_of
+    blocks = jnp.stack(
+        [from_root(own_slot, "req", owners[tenant_id]) for tenant_id in range(TENANTS)]
+    )
+
+    def slot_of(tenant_id):
+        return lax.dynamic_index_in_dim(blocks, tenant_id, 0, keepdims=False)
+
+    return slot_of
 
 
 def shifted(block, shift, n_tp):
@@ -80,65 +90,58 @@
     row_start = jnp.sum(jnp.where(member, req_starts[None, :], 0), axis=1)
     row_tenant = jnp.sum(jnp.where(member, req_tenant[None, :], 0), axis=1)
     score_scale = HD ** (-0.5)
-    query_heads = queries.reshape(row_count, head_count, HD)
-    suffix_keys, suffix_values = pick_heads(suffix_kv.reshape(row_count, -1), select)
-    suffix_scores = (
-        jnp.einsum("rhd,khd->hrk", query_heads, suffix_keys, preferred_element_type=jnp.float32)
-        * score_scale
-    )
-    suffix_mask = (
-        (position[None, :] >= row_start[:, None]) & (position[None, :] <= position[:, None])
-    )[None]
-    own_slot = prefix_cache.reshape(prefix_cache.shape[0], -1)
-    prefix_blocks = tenant_prefixes(own_slot, owners, n_req)
-    picked = [pick_heads(block_rows, select) for block_rows in prefix_blocks]
-    row_top = jnp.max(jnp.where(suffix_mask, suffix_scores, -jnp.inf), axis=2)
-    for tenant_id in range(TENANTS):
-        tenant_mask = (row_tenant == tenant_id)[None, :, None]
+    pair_select = select[None, :, :, None]
+    own_slot = prefix_cache.reshape(prefix_cache.shape[0], 2, 2, HD)
+    every_slot = tenant_slots(own_slot, owners, n_req)
+    suffix_pairs = suffix_kv.reshape(row_count, 2, 2, HD)
+    window = min(MOSTLEN, row_count)
+    attended = jnp.zeros((row_count, head_count * HD), jnp.bfloat16)
+    for request in range(req_lengths.shape[0]):
+        first = jnp.minimum(req_starts[request], row_count - window)
+        window_queries = lax.dynamic_slice_in_dim(queries, first, window, 0)
+        spread = window_queries.reshape(window, head_count, 1, HD) * pair_select
+        window_pairs = lax.dynamic_slice_in_dim(suffix_pairs, first, window, 0)
+        prefix_pairs = every_slot(req_tenant[request])
+        key_position = first + jnp.arange(window, dtype=jnp.int32)
+        suffix_mask = (
+            (key_position[None, :] >= req_starts[request]) & (key_position[None, :] <= key_position[:, None])
+        )[None]
         prefix_scores = (
-            jnp.einsum(
-                "rhd,phd->hrp",
-                query_heads,
-                picked[tenant_id][0],
-                preferred_element_type=jnp.float32,
-            )
+            jnp.einsum("rhjd,pjd->hrp", spread, prefix_pairs[:, :, 0], preferred_element_type=jnp.float32)
+            * score_scale
+        )
+        suffix_scores = (
+            jnp.einsum("rhjd,kjd->hrk", spread, window_pairs[:, :, 0], preferred_element_type=jnp.float32)
             * score_scale
         )
         row_top = jnp.maximum(
-            row_top, jnp.max(jnp.where(tenant_mask, prefix_scores, -jnp.inf), axis=2)
+            jnp.max(prefix_scores, axis=2),
+            jnp.max(jnp.where(suffix_mask, suffix_scores, -jnp.inf), axis=2),
         )
-    suffix_weights = jnp.where(suffix_mask, jnp.exp(suffix_scores - row_top[:, :, None]), 0.0)
-    denominator = jnp.sum(suffix_weights, axis=2)
-    accumulated = jnp.einsum(
-        "hrk,khd->rhd",
-        suffix_weights.astype(jnp.bfloat16),
-        suffix_values,
-        preferred_element_type=jnp.float32,
-    )
-    for tenant_id in range(TENANTS):
-        tenant_mask = (row_tenant == tenant_id)[None, :, None]
-        prefix_scores = (
-            jnp.einsum(
-                "rhd,phd->hrp",
-                query_heads,
-                picked[tenant_id][0],
-                preferred_element_type=jnp.float32,
-            )
-            * score_scale
-        )
-        prefix_weights = jnp.where(tenant_mask, jnp.exp(prefix_scores - row_top[:, :, None]), 0.0)
-        denominator = denominator + jnp.sum(prefix_weights, axis=2)
-        accumulated = accumulated + jnp.einsum(
-            "hrp,phd->rhd",
+        prefix_weights = jnp.exp(prefix_scores - row_top[:, :, None])
+        suffix_weights = jnp.where(suffix_mask, jnp.exp(suffix_scores - row_top[:, :, None]), 0.0)
+        denominator = jnp.sum(prefix_weights, axis=2) + jnp.sum(suffix_weights, axis=2)
+        both_pairs = jnp.einsum(
+            "hrp,pjd->rhjd",
             prefix_weights.astype(jnp.bfloat16),
-            picked[tenant_id][1],
+            prefix_pairs[:, :, 1],
+            preferred_element_type=jnp.float32,
+        ) + jnp.einsum(
+            "hrk,kjd->rhjd",
+            suffix_weights.astype(jnp.bfloat16),
+            window_pairs[:, :, 1],
             preferred_element_type=jnp.float32,
         )
-    attended = (
-        (accumulated / jnp.transpose(denominator)[:, :, None])
-        .astype(jnp.bfloat16)
-        .reshape(row_count, -1)
-    )
+        accumulated = jnp.sum(jnp.where(pair_select > 0, both_pairs, 0.0), axis=2)
+        window_attended = (
+            (accumulated / jnp.transpose(denominator)[:, :, None])
+            .astype(jnp.bfloat16)
+            .reshape(window, -1)
+        )
+        placed = lax.dynamic_update_slice_in_dim(
+            jnp.zeros_like(attended), window_attended, first, 0
+        )
+        attended = jnp.where((request_ids == request)[:, None], placed, attended)
 
     projected = jnp.dot(attended, weight_pieces[0], preferred_element_type=jnp.float32)
     for shift in range(1, n_tp):

time: 124 us -> 121 us (0.976)
  between operations: 17 us -> 27.6 us
  waiting for transfers between devices: 52 us -> 42.3 us
  matrix products: 23.9 us -> 22.1 us
    all_gather x1, waiting for transfers between devices: 21.6 us -> 12.5 us  [tenant_slots(): gathered = lax.all_gather(own_slot, 'req', axis=0, tiled=True)]
    dot_general x20 -> x16, matrix products: 18.4 us -> 14.7 us  [the longest x4 6.26 us: local(): jnp.einsum('hrp,pjd->rhjd', prefix_weights.astype(jnp.bfloat16), prefix_p...]
    reduce_sum x3 -> x8, other arithmetic: 5.11 us -> 2.06 us  [the longest x4 1.76 us: local(): jnp.sum(prefix_weights, axis=2) + jnp.sum(suffix_weights, axis=2)]
    ge x0 -> x4, other arithmetic: none -> 2.64 us  [local(): key_position[None, :] >= req_starts[request]]
    dot_general x3, matrix products: 2.06 us -> 3.99 us  [local(): jnp.dot(head_block, weight_pieces[shift], preferred_element_type=jnp.floa...]
    unnamed x14 -> x22, local copies, waits for them, and re-layouts: 3.17 us -> 1.55 us
    dynamic_update_slice x0 -> x3, local copies, waits for them, and re-layouts: none -> 1.32 us  [local(): lax.dynamic_update_slice_in_dim(jnp.zeros_like(attended), window_attended...]
  transfers between devices with their start and end apart: 10 -> 10, of which waited for: 7 -> 7; matrix products, arithmetic and copies ran while one was open for 28% -> 25% of each run, Pallas kernels for 0% -> 0%
where the time goes in v7:
time: 121 us
  waiting for transfers between devices  42.3 us (35%)
  between operations  27.6 us (23%)
  matrix products  22.1 us (18%)
  starting transfers between devices  15 us (12%)
  local copies, waits for them, and re-layouts  7.62 us (6%)
  other arithmetic  5.99 us (5%)
    ppermute x9, waiting for transfers between devices, shifted(): return lax.ppermute(block, 'tp', pairs)  29.8 us
    ppermute x9, starting transfers between devices, shifted(): return lax.ppermute(block, 'tp', pairs)  14.9 us
    all_gather x1, waiting for transfers between devices, tenant_slots(): gathered = lax.all_gather(own_slot, 'req', axis=0, tiled=True)  12.5 us
    dot_general x4, matrix products, local(): jnp.einsum('hrp,pjd->rhjd', prefix_weights.astype(jnp.bfloat16), prefix_p...  6.26 us
    dot_general x4, matrix products, local(): jnp.einsum('rhjd,pjd->hrp', spread, prefix_pairs[:, :, 0], preferred_elem...  6.1 us
    dot_general x3, matrix products, local(): jnp.dot(head_block, weight_pieces[shift], preferred_element_type=jnp.floa...  3.99 us
    ge x4, other arithmetic, local(): key_position[None, :] >= req_starts[request]  2.64 us
  transfers between devices with their start and end apart: 10, of which 7 were waited for; matrix products, arithmetic and copies ran while one was open for 25% of the time, Pallas kernels for 0%

profile of v7, /device:TPU:8, one launch (start us, length us, event | category | flops | bytes accessed | tf_op | source)
XLA Modules:
  0.0 120.6 jit_solution(10508709122867498092)
XLA Ops:
  7.3 1.4 %copy.37 = bf16[1024,1,256]{0,2,1:T(8,128)(2,1)S(1)} copy(bf16[1024,1,256]{2,0,1:T(8,128)(2,1)} %param.13) | data formatting | bytes 1048576 | tf_op args[3]
  8.7 0.8 copy.38
  9.6 1.0 constant_dynamic-slice_fusion.1
  10.6 1.6 %collective-permute-start.1 = (bf16[320,512]{1,0:T(8,128)(2,1)}, bf16[320,512]{1,0:T(8,128)(2,1)}, u32[]{:S(2)}, u32[]{:S(2)}) collective-permute-start(bf16[320,512]{1,0:T(8,128)(2,1)} %get-tuple-element.3), channel_id=1, source_target_pairs={{0,1},{1,2},{2,3},{3,0},{4,5},{5,6},{6,7},{7,4},{8,9},{9,10},{10,1... | collective-permute-start | bytes 983048 | tf_op jit(solution)/shard_map/ppermute | solution.py:52
  12.2 0.5 collective-permute-start.5
  12.7 2.6 %collective-permute-start.3 = (bf16[320,512]{1,0:T(8,128)(2,1)}, bf16[320,512]{1,0:T(8,128)(2,1)}, u32[]{:S(2)}, u32[]{:S(2)}) collective-permute-start(bf16[320,512]{1,0:T(8,128)(2,1)} %get-tuple-element.2), channel_id=1, source_target_pairs={{0,2},{1,3},{2,0},{3,1},{4,6},{5,7},{6,4},{7,5},{8,10},{9,11},{10,... | collective-permute-start | bytes 983048 | tf_op jit(solution)/shard_map/ppermute | solution.py:52
  15.2 0.7 fusion.176
  21.2 0.7 fusion.174
  27.1 0.7 fusion.175
  30.8 0.7 broadcast_compare_fusion.4
  31.4 0.7 broadcast_compare_fusion.5
  32.1 0.7 broadcast_compare_fusion.6
  32.8 0.6 broadcast_compare_fusion.7
  34.1 0.3 select_reduce_fusion
  35.4 12.5 %all-gather.2.cloned.1.call-done = bf16[8192,2,2,64]{0,3,1,2:T(8,128)(2,1)} async-done(((bf16[1024,2,2,64]{0,3,1,2:T(8,128)(2,1)}), bf16[8192,2,2,64]{0,3,1,2:T(8,128)(2,1)}) %all-gather.2.cloned.1.call-update) | async-done | bytes 4194320 | tf_op jit(solution)/shard_map/all_gather | solution.py:33
  47.9 1.5 %bitcast_reduce_fusion = (f32[5,128]{1,0:T(8,128)S(1)}, f32[1024,128,5,1]{1,0,3,2:T(8,128)S(1)}) fusion(bf16[128,5,64]{0,2,1:T(8,128)(2,1)S(1)} %bitcast.359, bf16[5,2]{1,0:T(8,128)(2,1)S(1)} %copy.39, bf16[8192,2,2,64]{0,3,1,2:T(8,128)(2,1)} %all-gather.2.cloned.1.call-done, s32[]{:T(128)S(6)} %select_n.188), kind=kOutput, calls=%fused_computation.1 | convolution fusion | flops 169409920 | bytes 2968088 | tf_op jit(solution)/shard_map/rhjd,pjd->hrp/dot_general | solution.py:110
  49.4 0.4 fusion.10
  50.0 1.5 %bitcast_reduce_fusion.1 = (f32[5,128]{1,0:T(8,128)S(1)}, f32[1024,128,5,1]{1,0,3,2:T(8,128)S(1)}) fusion(bf16[128,5,64]{0,2,1:T(8,128)(2,1)S(1)} %bitcast.357, bf16[5,2]{1,0:T(8,128)(2,1)S(1)} %copy.39, bf16[8192,2,2,64]{0,3,1,2:T(8,128)(2,1)} %all-gather.2.cloned.1.call-done, s32[]{:T(128)S(6)} %select_n.181), kind=kOutput, calls=%fused_computation.5 | convolution fusion | flops 169409920 | bytes 2968088 | tf_op jit(solution)/shard_map/rhjd,pjd->hrp/dot_general | solution.py:110
  51.5 0.4 fusion.8
  52.0 1.6 %fusion.13 = f32[2,64,5,128]{3,1,2,0:T(8,128)S(1)} fusion(f32[1024,128,5,1]{1,0,3,2:T(8,128)S(1)} %get-tuple-element.44, f32[5,128]{1,0:T(8,128)S(1)} %max.31, bf16[8192,2,2,64]{0,3,1,2:T(8,128)(2,1)} %all-gather.2.cloned.1.call-done, s32[]{:T(128)S(6)} %select_n.188, s32[]{:T(128)S(6)} %add.363), kind=kOutput, calls=%fused_computation.25 | convolution fusion | flops 169738240 | bytes 3213832 | tf_op jit(solution)/shard_map/hrp,pjd->rhjd/dot_general | solution.py:124
  53.9 1.6 %fusion.16 = f32[2,64,5,128]{3,1,2,0:T(8,128)S(1)} fusion(f32[1024,128,5,1]{1,0,3,2:T(8,128)S(1)} %get-tuple-element.40, f32[5,128]{1,0:T(8,128)S(1)} %max.30, bf16[8192,2,2,64]{0,3,1,2:T(8,128)(2,1)} %all-gather.2.cloned.1.call-done, s32[]{:T(128)S(6)} %select_n.181, s32[]{:T(128)S(6)} %add.363), kind=kOutput, calls=%fused_computation.27 | convolution fusion | flops 169738240 | bytes 3213832 | tf_op jit(solution)/shard_map/hrp,pjd->rhjd/dot_general | solution.py:124
  55.7 1.5 %bitcast_reduce_fusion.2 = (f32[5,128]{1,0:T(8,128)S(1)}, f32[1024,128,5,1]{1,0,3,2:T(8,128)S(1)}) fusion(bf16[128,5,64]{0,2,1:T(8,128)(2,1)S(1)} %bitcast.355, bf16[5,2]{1,0:T(8,128)(2,1)S(1)} %copy.39, bf16[8192,2,2,64]{0,3,1,2:T(8,128)(2,1)} %all-gather.2.cloned.1.call-done, s32[]{:T(128)S(6)} %select_n.175), kind=kOutput, calls=%fused_computation.9 | convolution fusion | flops 169409920 | bytes 2968088 | tf_op jit(solution)/shard_map/rhjd,pjd->hrp/dot_general | solution.py:110
  57.2 0.4 fusion.6
  57.8 1.6 %fusion.19 = f32[2,64,5,128]{3,1,2,0:T(8,128)S(1)} fusion(f32[1024,128,5,1]{1,0,3,2:T(8,128)S(1)} %get-tuple-element.36, f32[5,128]{1,0:T(8,128)S(1)} %max.29, bf16[8192,2,2,64]{0,3,1,2:T(8,128)(2,1)} %all-gather.2.cloned.1.call-done, s32[]{:T(128)S(6)} %select_n.175, s32[]{:T(128)S(6)} %add.363), kind=kOutput, calls=%fused_computation.29 | convolution fusion | flops 169738240 | bytes 3213832 | tf_op jit(solution)/shard_map/hrp,pjd->rhjd/dot_general | solution.py:124
  59.6 1.5 %bitcast_reduce_fusion.3 = (f32[5,128]{1,0:T(8,128)S(1)}, f32[1024,128,5,1]{1,0,3,2:T(8,128)S(1)}) fusion(bf16[5,2]{1,0:T(8,128)(2,1)S(1)} %copy.39, bf16[128,5,64]{0,2,1:T(8,128)(2,1)S(1)} %bitcast.353, bf16[8192,2,2,64]{0,3,1,2:T(8,128)(2,1)} %all-gather.2.cloned.1.call-done, s32[]{:T(128)S(6)} %select_n.169), kind=kOutput, calls=%fused_computation.13 | convolution fusion | flops 169409920 | bytes 2968088 | tf_op jit(solution)/shard_map/rhjd,pjd->hrp/dot_general | solution.py:110
  61.2 0.4 fusion.4
  61.7 1.6 %fusion.22 = f32[2,64,5,128]{3,1,2,0:T(8,128)S(1)} fusion(f32[1024,128,5,1]{1,0,3,2:T(8,128)S(1)} %get-tuple-element.32, f32[5,128]{1,0:T(8,128)S(1)} %max.28, bf16[8192,2,2,64]{0,3,1,2:T(8,128)(2,1)} %all-gather.2.cloned.1.call-done, s32[]{:T(128)S(6)} %select_n.169, s32[]{:T(128)S(6)} %add.363), kind=kOutput, calls=%fused_computation.31 | convolution fusion | flops 169738240 | bytes 3213832 | tf_op jit(solution)/shard_map/hrp,pjd->rhjd/dot_general | solution.py:124
  63.6 0.4 select_n.194
  64.1 0.7 dynamic_update_slice.12
  65.6 1.5 %collective-permute-start = (bf16[256,320]{0,1:T(8,128)(2,1)S(1)}, bf16[256,320]{0,1:T(8,128)(2,1)S(1)}, u32[]{:S(2)}, u32[]{:S(2)}) collective-permute-start(bf16[256,320]{0,1:T(8,128)(2,1)S(1)} %select_select_fusion), channel_id=1, source_target_pairs={{0,1},{1,2},{2,3},{3,0},{4,5},{5,6},{6,7},{7,4},{8,9},{9,10},{10,1... | collective-permute-start | bytes 491528 | tf_op jit(solution)/shard_map/ppermute | solution.py:52
  67.1 0.6 collective-permute-start.4
  67.7 1.3 %fusion.73 = f32[256,512]{1,0:T(8,128)S(1)} fusion(bf16[256,320]{0,1:T(8,128)(2,1)S(1)} %select_select_fusion, bf16[320,2048]{1,0:T(8,128)(2,1)} %param.14, s32[]{:T(128)S(6)} %select_n.199), kind=kOutput, calls=%fused_computation.102 | convolution fusion | flops 83886080 | bytes 1015812 | tf_op jit(solution)/shard_map/dot_general | solution.py:146
  69.0 2.5 %collective-permute-start.2 = (bf16[256,320]{0,1:T(8,128)(2,1)S(1)}, bf16[256,320]{0,1:T(8,128)(2,1)S(1)}, u32[]{:S(2)}, u32[]{:S(2)}) collective-permute-start(bf16[256,320]{0,1:T(8,128)(2,1)S(1)} %select_select_fusion), channel_id=1, source_target_pairs={{0,2},{1,3},{2,0},{3,1},{4,6},{5,7},{6,4},{7,5},{8,10},{9,11},{10,... | collective-permute-start | bytes 491528 | tf_op jit(solution)/shard_map/ppermute | solution.py:52
  71.5 1.3 %collective-permute-done = bf16[256,320]{0,1:T(8,128)(2,1)S(1)} collective-permute-done((bf16[256,320]{0,1:T(8,128)(2,1)S(1)}, bf16[256,320]{0,1:T(8,128)(2,1)S(1)}, u32[]{:S(2)}, u32[]{:S(2)}) %collective-permute-start) | collective-permute-done | bytes 163872 | tf_op jit(solution)/shard_map/ppermute | solution.py:52
  72.7 1.3 %convolution_add_fusion.1 = f32[256,512]{1,0:T(8,128)S(1)} fusion(f32[256,512]{1,0:T(8,128)S(1)} %fusion.73, bf16[256,320]{0,1:T(8,128)(2,1)S(1)} %collective-permute-done, bf16[320,512]{1,0:T(8,128)(2,1)} %collective-permute-done.1), kind=kOutput, calls=%fused_computation.43 | convolution fusion | flops 84017152 | bytes 1540096 | tf_op jit(solution)/shard_map/dot_general | solution.py:149
  74.0 3.1 %collective-permute-done.4 = bf16[256,320]{0,1:T(8,128)(2,1)S(1)} collective-permute-done((bf16[256,320]{0,1:T(8,128)(2,1)S(1)}, bf16[256,320]{0,1:T(8,128)(2,1)S(1)}, u32[]{:S(2)}, u32[]{:S(2)}) %collective-permute-start.4) | collective-permute-done | bytes 163872 | tf_op jit(solution)/shard_map/ppermute | solution.py:52
  77.2 1.3 %fusion.177 = f32[256,512]{1,0:T(8,128)S(1)} fusion(bf16[256,320]{0,1:T(8,128)(2,1)S(1)} %collective-permute-done.4, bf16[320,512]{1,0:T(8,128)(2,1)} %collective-permute-done.5), kind=kOutput, calls=%fused_computation.265 | convolution fusion | flops 83886080 | bytes 1015808 | tf_op jit(solution)/shard_map/dot_general | solution.py:149
  78.5 3.5 %collective-permute-done.2 = bf16[256,320]{0,1:T(8,128)(2,1)S(1)} collective-permute-done((bf16[256,320]{0,1:T(8,128)(2,1)S(1)}, bf16[256,320]{0,1:T(8,128)(2,1)S(1)}, u32[]{:S(2)}, u32[]{:S(2)}) %collective-permute-start.2) | collective-permute-done | bytes 163872 | tf_op jit(solution)/shard_map/ppermute | solution.py:52
  81.9 1.4 %fusion.56 = (f32[256]{0:T(256)S(1)}, bf16[256,512]{1,0:T(8,128)(2,1)S(1)}) fusion(f32[256,512]{1,0:T(8,128)S(1)} %fusion.177, f32[256,512]{1,0:T(8,128)S(1)} %convolution_add_fusion.1, bf16[256,320]{0,1:T(8,128)(2,1)S(1)} %collective-permute-done.2, bf16[320,512]{1,0:T(8,128)(2,1)} %collective-permute-done.3, bf16[256,512]{1,0:T(8,128)(2,1)S(1)} %copy-done.4), kind=kOutput, calls=%fused_computation.85 | convolution fusion | flops 84934400 | bytes 2065408 | tf_op jit(solution)/shard_map/dot_general | solution.py:149
  83.4 1.5 %collective-permute-start.6 = (bf16[256,512]{1,0:T(8,128)(2,1)S(1)}, bf16[256,512]{1,0:T(8,128)(2,1)S(1)}, u32[]{:S(2)}, u32[]{:S(2)}) collective-permute-start(bf16[256,512]{1,0:T(8,128)(2,1)S(1)} %get-tuple-element.48), channel_id=1, source_target_pairs={{0,1},{1,2},{2,3},{3,0},{4,5},{5,6},{6,7},{7,4},{8,9},{9,10},{10,1... | collective-permute-start | bytes 786440 | tf_op jit(solution)/shard_map/ppermute | solution.py:52
  84.9 4.3 %collective-permute-start.7 = (bf16[256,512]{1,0:T(8,128)(2,1)S(1)}, bf16[256,512]{1,0:T(8,128)(2,1)S(1)}, u32[]{:S(2)}, u32[]{:S(2)}) collective-permute-start(bf16[256,512]{1,0:T(8,128)(2,1)S(1)} %get-tuple-element.48), channel_id=1, source_target_pairs={{0,2},{1,3},{2,0},{3,1},{4,6},{5,7},{6,4},{7,5},{8,10},{9,11},{10,... | collective-permute-start | bytes 786440 | tf_op jit(solution)/shard_map/ppermute | solution.py:52
  89.2 4.6 %collective-permute-done.6 = bf16[256,512]{1,0:T(8,128)(2,1)S(1)} collective-permute-done((bf16[256,512]{1,0:T(8,128)(2,1)S(1)}, bf16[256,512]{1,0:T(8,128)(2,1)S(1)}, u32[]{:S(2)}, u32[]{:S(2)}) %collective-permute-start.6) | collective-permute-done | bytes 262176 | tf_op jit(solution)/shard_map/ppermute | solution.py:52
  94.0 13.5 %collective-permute-done.7 = bf16[256,512]{1,0:T(8,128)(2,1)S(1)} collective-permute-done((bf16[256,512]{1,0:T(8,128)(2,1)S(1)}, bf16[256,512]{1,0:T(8,128)(2,1)S(1)}, u32[]{:S(2)}, u32[]{:S(2)}) %collective-permute-start.7) | collective-permute-done | bytes 262176 | tf_op jit(solution)/shard_map/ppermute | solution.py:52
  107.6 3.8 %collective-permute-done.8 = bf16[256,512]{1,0:T(8,128)(2,1)S(1)} collective-permute-done((bf16[256,512]{1,0:T(8,128)(2,1)S(1)}, bf16[256,512]{1,0:T(8,128)(2,1)S(1)}, u32[]{:S(2)}, u32[]{:S(2)}) %collective-permute-start.8) | collective-permute-done | bytes 262176 | tf_op jit(solution)/shard_map/ppermute | solution.py:52
  111.6 0.4 fusion.71
  111.9 0.4 convolution_add_fusion.4
  112.3 0.4 convolution_add_fusion.3
  112.7 1.0 fusion.55
  (80 shorter events, 5.0 us)
Async XLA Ops:
  7.2 104.4 %copy-start = (bf16[2048,320]{0,1:T(8,128)(2,1)S(1)}, bf16[2048,320]{0,1:T(8,128)(2,1)}, u32[]{:S(2)}) copy-start(bf16[2048,320]{0,1:T(8,128)(2,1)} %param.16) | copy-start | bytes 3932164
  7.2 2.4 %copy-start.1 = (bf16[320,2048]{1,0:T(8,128)(2,1)S(1)}, bf16[320,2048]{1,0:T(8,128)(2,1)}, u32[]{:S(2)}) copy-start(bf16[320,2048]{1,0:T(8,128)(2,1)} %param.14) | copy-start | bytes 3932164
  7.2 8.0 %copy-start.8 = (s32[1,4]{1,0:T(1,128)S(1)}, s32[1,4]{1,0:T(1,128)}, u32[]{:S(2)}) copy-start(s32[1,4]{1,0:T(1,128)} %param.18) | copy-start | bytes 52
  7.2 13.8 %copy-start.9 = (s32[1,4]{1,0:T(1,128)S(1)}, s32[1,4]{1,0:T(1,128)}, u32[]{:S(2)}) copy-start(s32[1,4]{1,0:T(1,128)} %param.17) | copy-start | bytes 52
  7.2 19.9 %copy-start.7 = (s32[4]{0:T(128)S(1)}, s32[4]{0:T(128)}, u32[]{:S(2)}) copy-start(s32[4]{0:T(128)} %param.19) | copy-start | bytes 52
  7.2 23.2 %copy-start.5 = (bf16[256,1,256]{2,0,1:T(8,128)(2,1)S(1)}, bf16[256,1,256]{2,0,1:T(8,128)(2,1)}, u32[]{:S(2)}) copy-start(bf16[256,1,256]{2,0,1:T(8,128)(2,1)} %param.12) | copy-start | bytes 393220
  7.2 26.2 %copy-start.3 = (bf16[256,320]{0,1:T(8,128)(2,1)S(1)}, bf16[256,320]{0,1:T(8,128)(2,1)}, u32[]{:S(2)}) copy-start(bf16[256,320]{0,1:T(8,128)(2,1)} %param.11) | copy-start | bytes 491524
  7.2 40.7 %all-gather.2.cloned.1.call-start = ((), (), s32[]{:S(2)}) async-start(), calls=%async_computation | async-start | bytes 4718592 | tf_op jit(solution)/shard_map/all_gather | solution.py:33
  10.6 58.4 %collective-permute-start.1 = (bf16[320,512]{1,0:T(8,128)(2,1)}, bf16[320,512]{1,0:T(8,128)(2,1)}, u32[]{:S(2)}, u32[]{:S(2)}) collective-permute-start(bf16[320,512]{1,0:T(8,128)(2,1)} %get-tuple-element.3), channel_id=1, source_target_pairs={{0,1},{1,2},{2,3},{3,0},{4,5},{5,6},{6,7},{7,4},{8,9},{9,10},{10,1... | collective-permute-start | bytes 983048 | tf_op jit(solution)/shard_map/ppermute | solution.py:52
  12.2 61.8 %collective-permute-start.5 = (bf16[320,512]{1,0:T(8,128)(2,1)}, bf16[320,512]{1,0:T(8,128)(2,1)}, u32[]{:S(2)}, u32[]{:S(2)}) collective-permute-start(bf16[320,512]{1,0:T(8,128)(2,1)} %get-tuple-element.4), channel_id=1, source_target_pairs={{0,3},{1,0},{2,1},{3,2},{4,7},{5,4},{6,5},{7,6},{8,11},{9,8},{10,9... | collective-permute-start | bytes 983048 | tf_op jit(solution)/shard_map/ppermute | solution.py:52
  12.7 65.8 %collective-permute-start.3 = (bf16[320,512]{1,0:T(8,128)(2,1)}, bf16[320,512]{1,0:T(8,128)(2,1)}, u32[]{:S(2)}, u32[]{:S(2)}) collective-permute-start(bf16[320,512]{1,0:T(8,128)(2,1)} %get-tuple-element.2), channel_id=1, source_target_pairs={{0,2},{1,3},{2,0},{3,1},{4,6},{5,7},{6,4},{7,5},{8,10},{9,11},{10,... | collective-permute-start | bytes 983048 | tf_op jit(solution)/shard_map/ppermute | solution.py:52
  64.8 17.1 %copy-start.4 = (bf16[256,512]{1,0:T(8,128)(2,1)S(1)}, bf16[256,512]{1,0:T(8,128)(2,1)}, u32[]{:S(2)}) copy-start(bf16[256,512]{1,0:T(8,128)(2,1)} %param.10) | copy-start | bytes 786436
  65.6 23.5 %copy-start.6 = (bf16[2048]{0:T(1024)(128)(2,1)S(1)}, bf16[2048]{0:T(1024)(128)(2,1)}, u32[]{:S(2)}) copy-start(bf16[2048]{0:T(1024)(128)(2,1)} %param.15) | copy-start | bytes 12292
  65.6 7.1 %collective-permute-start = (bf16[256,320]{0,1:T(8,128)(2,1)S(1)}, bf16[256,320]{0,1:T(8,128)(2,1)S(1)}, u32[]{:S(2)}, u32[]{:S(2)}) collective-permute-start(bf16[256,320]{0,1:T(8,128)(2,1)S(1)} %select_select_fusion), channel_id=1, source_target_pairs={{0,1},{1,2},{2,3},{3,0},{4,5},{5,6},{6,7},{7,4},{8,9},{9,10},{10,1... | collective-permute-start | bytes 491528 | tf_op jit(solution)/shard_map/ppermute | solution.py:52
  67.1 10.0 %collective-permute-start.4 = (bf16[256,320]{0,1:T(8,128)(2,1)S(1)}, bf16[256,320]{0,1:T(8,128)(2,1)S(1)}, u32[]{:S(2)}, u32[]{:S(2)}) collective-permute-start(bf16[256,320]{0,1:T(8,128)(2,1)S(1)} %select_select_fusion), channel_id=1, source_target_pairs={{0,3},{1,0},{2,1},{3,2},{4,7},{5,4},{6,5},{7,6},{8,11},{9,8},{10,9... | collective-permute-start | bytes 491528 | tf_op jit(solution)/shard_map/ppermute | solution.py:52
  69.0 13.0 %collective-permute-start.2 = (bf16[256,320]{0,1:T(8,128)(2,1)S(1)}, bf16[256,320]{0,1:T(8,128)(2,1)S(1)}, u32[]{:S(2)}, u32[]{:S(2)}) collective-permute-start(bf16[256,320]{0,1:T(8,128)(2,1)S(1)} %select_select_fusion), channel_id=1, source_target_pairs={{0,2},{1,3},{2,0},{3,1},{4,6},{5,7},{6,4},{7,5},{8,10},{9,11},{10,... | collective-permute-start | bytes 491528 | tf_op jit(solution)/shard_map/ppermute | solution.py:52
  83.4 30.3 %copy-start.2 = (bf16[256,512]{1,0:T(8,128)(2,1)}, bf16[256,512]{1,0:T(8,128)(2,1)S(1)}, u32[]{:S(2)}) copy-start(bf16[256,512]{1,0:T(8,128)(2,1)S(1)} %get-tuple-element.48) | copy-start | bytes 786436
  83.4 10.5 %collective-permute-start.6 = (bf16[256,512]{1,0:T(8,128)(2,1)S(1)}, bf16[256,512]{1,0:T(8,128)(2,1)S(1)}, u32[]{:S(2)}, u32[]{:S(2)}) collective-permute-start(bf16[256,512]{1,0:T(8,128)(2,1)S(1)} %get-tuple-element.48), channel_id=1, source_target_pairs={{0,1},{1,2},{2,3},{3,0},{4,5},{5,6},{6,7},{7,4},{8,9},{9,10},{10,1... | collective-permute-start | bytes 786440 | tf_op jit(solution)/shard_map/ppermute | solution.py:52
  84.9 22.6 %collective-permute-start.7 = (bf16[256,512]{1,0:T(8,128)(2,1)S(1)}, bf16[256,512]{1,0:T(8,128)(2,1)S(1)}, u32[]{:S(2)}, u32[]{:S(2)}) collective-permute-start(bf16[256,512]{1,0:T(8,128)(2,1)S(1)} %get-tuple-element.48), channel_id=1, source_target_pairs={{0,2},{1,3},{2,0},{3,1},{4,6},{5,7},{6,4},{7,5},{8,10},{9,11},{10,... | collective-permute-start | bytes 786440 | tf_op jit(solution)/shard_map/ppermute | solution.py:52
  89.1 22.3 %collective-permute-start.8 = (bf16[256,512]{1,0:T(8,128)(2,1)S(1)}, bf16[256,512]{1,0:T(8,128)(2,1)S(1)}, u32[]{:S(2)}, u32[]{:S(2)}) collective-permute-start(bf16[256,512]{1,0:T(8,128)(2,1)S(1)} %get-tuple-element.48), channel_id=1, source_target_pairs={{0,3},{1,0},{2,1},{3,2},{4,7},{5,4},{6,5},{7,6},{8,11},{9,8},{10,9... | collective-permute-start | bytes 786440 | tf_op jit(solution)/shard_map/ppermute | solution.py:52
Sparse Core Ops, SparseCore 0:
  10.0 37.8 all-gather.1

commit v8 on v7

--- a/solution.py
+++ b/solution.py
@@ -1,6 +1,8 @@
 import jax
 import jax.numpy as jnp
 from jax import lax
+from jax.experimental import pallas as pl
+from jax.experimental.pallas import tpu as pltpu
 from jax.sharding import PartitionSpec as P
 
 QH = 20
@@ -28,23 +30,65 @@
 
 
 def tenant_slots(own_slot, owners, n_req):
-    slot_rows = own_slot.shape[0]
     if n_req <= GATHER_SLOTS_MAX:
-        gathered = lax.all_gather(own_slot, "req", axis=0, tiled=True)
-
-        def slot_of(tenant_id):
-            owner = owners[tenant_id]
-            return lax.dynamic_slice_in_dim(gathered, owner * slot_rows, slot_rows, 0)
-
-        return slot_of
-    blocks = jnp.stack(
-        [from_root(own_slot, "req", owners[tenant_id]) for tenant_id in range(TENANTS)]
-    )
-
-    def slot_of(tenant_id):
-        return lax.dynamic_index_in_dim(blocks, tenant_id, 0, keepdims=False)
-
-    return slot_of
+        return lax.all_gather(own_slot, "req", axis=0, tiled=True), owners
+    blocks = [from_root(own_slot, "req", owners[tenant_id]) for tenant_id in range(TENANTS)]
+    return jnp.concatenate(blocks, axis=0), jnp.arange(TENANTS, dtype=jnp.int32)
+
+
+def attention_kernel(slot_ref, first_ref, start_ref, query_ref, prefix_ref, suffix_ref, row_ref, out_ref):
+    request = pl.program_id(0)
+    first = first_ref[request]
+    start = start_ref[request]
+    spread = query_ref[...]
+    prefix_rows = prefix_ref[...]
+    suffix_rows = suffix_ref[...]
+    contract = (((1,), (1,)), ((), ()))
+    score_scale = HD ** (-0.5)
+    prefix_scores = lax.dot_general(
+        spread, prefix_rows, contract, preferred_element_type=jnp.float32
+    ) * score_scale
+    suffix_scores = lax.dot_general(
+        spread, suffix_rows, contract, preferred_element_type=jnp.float32
+    ) * score_scale
+    key_position = first + lax.broadcasted_iota(jnp.int32, suffix_scores.shape, 1)
+    query_position = first + row_ref[...]
+    allowed = (key_position >= start) & (key_position <= query_position)
+    suffix_scores = jnp.where(allowed, suffix_scores, -jnp.inf)
+    row_top = jnp.maximum(
+        jnp.max(prefix_scores, axis=1, keepdims=True),
+        jnp.max(suffix_scores, axis=1, keepdims=True),
+    )
+    prefix_weights = jnp.exp(prefix_scores - row_top)
+    suffix_weights = jnp.where(allowed, jnp.exp(suffix_scores - row_top), 0.0)
+    denominator = jnp.sum(prefix_weights, axis=1, keepdims=True) + jnp.sum(
+        suffix_weights, axis=1, keepdims=True
+    )
+    accumulated = jnp.dot(
+        prefix_weights.astype(jnp.bfloat16), prefix_rows, preferred_element_type=jnp.float32
+    ) + jnp.dot(suffix_weights.astype(jnp.bfloat16), suffix_rows, preferred_element_type=jnp.float32)
+    out_ref[...] = accumulated / denominator
+
+
+def window_attention(slot_index, firsts, starts, spread, slots, suffix_windows, query_rows, slot_rows):
+    requests, flat_rows, lanes = spread.shape
+    window = suffix_windows.shape[1]
+    grid_spec = pltpu.PrefetchScalarGridSpec(
+        num_scalar_prefetch=3,
+        grid=(requests,),
+        in_specs=[
+            pl.BlockSpec((None, flat_rows, lanes), lambda k, slot, first, start: (k, 0, 0)),
+            pl.BlockSpec((slot_rows, lanes), lambda k, slot, first, start: (slot[k], 0)),
+            pl.BlockSpec((None, window, lanes), lambda k, slot, first, start: (k, 0, 0)),
+            pl.BlockSpec((flat_rows, 1), lambda k, slot, first, start: (0, 0)),
+        ],
+        out_specs=pl.BlockSpec((None, flat_rows, lanes), lambda k, slot, first, start: (k, 0, 0)),
+    )
+    return pl.pallas_call(
+        attention_kernel,
+        grid_spec=grid_spec,
+        out_shape=jax.ShapeDtypeStruct((requests, flat_rows, lanes), jnp.float32),
+    )(slot_index, firsts, starts, spread, slots, suffix_windows, query_rows)
 
 
 def shifted(block, shift, n_tp):
@@ -90,56 +134,48 @@
     row_start = jnp.sum(jnp.where(member, req_starts[None, :], 0), axis=1)
     row_tenant = jnp.sum(jnp.where(member, req_tenant[None, :], 0), axis=1)
     score_scale = HD ** (-0.5)
-    pair_select = select[None, :, :, None]
-    own_slot = prefix_cache.reshape(prefix_cache.shape[0], 2, 2, HD)
-    every_slot = tenant_slots(own_slot, owners, n_req)
-    suffix_pairs = suffix_kv.reshape(row_count, 2, 2, HD)
+    own_slot = prefix_cache.reshape(prefix_cache.shape[0], -1)
+    slots, slot_of_tenant = tenant_slots(own_slot, owners, n_req)
+    suffix_rows = suffix_kv.reshape(row_count, -1)
     window = min(MOSTLEN, row_count)
+    firsts = jnp.minimum(req_starts, row_count - window).astype(jnp.int32)
+    zeros = jnp.zeros((window, head_count, HD), queries.dtype)
+    spreads = []
+    suffix_windows = []
+    for request in range(req_lengths.shape[0]):
+        window_queries = lax.dynamic_slice_in_dim(queries, firsts[request], window, 0)
+        window_queries = window_queries.reshape(window, head_count, HD)
+        spread = jnp.concatenate(
+            [
+                window_queries * select[None, :, 0:1],
+                zeros,
+                window_queries * select[None, :, 1:2],
+                zeros,
+            ],
+            axis=2,
+        )
+        spreads.append(spread.reshape(window * head_count, 4 * HD))
+        suffix_windows.append(lax.dynamic_slice_in_dim(suffix_rows, firsts[request], window, 0))
+    query_rows = (jnp.arange(window * head_count, dtype=jnp.int32) // head_count)[:, None]
+    slot_index = slot_of_tenant[req_tenant].astype(jnp.int32)
+    results = window_attention(
+        slot_index,
+        firsts,
+        req_starts.astype(jnp.int32),
+        jnp.stack(spreads),
+        slots,
+        jnp.stack(suffix_windows),
+        query_rows,
+        own_slot.shape[0],
+    ).reshape(-1, window, head_count, 4 * HD)
+    value_of_pair = jnp.where(
+        select[None, None, :, 0:1] > 0, results[..., HD:2 * HD], results[..., 3 * HD:]
+    )
     attended = jnp.zeros((row_count, head_count * HD), jnp.bfloat16)
     for request in range(req_lengths.shape[0]):
-        first = jnp.minimum(req_starts[request], row_count - window)
-        window_queries = lax.dynamic_slice_in_dim(queries, first, window, 0)
-        spread = window_queries.reshape(window, head_count, 1, HD) * pair_select
-        window_pairs = lax.dynamic_slice_in_dim(suffix_pairs, first, window, 0)
-        prefix_pairs = every_slot(req_tenant[request])
-        key_position = first + jnp.arange(window, dtype=jnp.int32)
-        suffix_mask = (
-            (key_position[None, :] >= req_starts[request]) & (key_position[None, :] <= key_position[:, None])
-        )[None]
-        prefix_scores = (
-            jnp.einsum("rhjd,pjd->hrp", spread, prefix_pairs[:, :, 0], preferred_element_type=jnp.float32)
-            * score_scale
-        )
-        suffix_scores = (
-            jnp.einsum("rhjd,kjd->hrk", spread, window_pairs[:, :, 0], preferred_element_type=jnp.float32)
-            * score_scale
-        )
-        row_top = jnp.maximum(
-            jnp.max(prefix_scores, axis=2),
-            jnp.max(jnp.where(suffix_mask, suffix_scores, -jnp.inf), axis=2),
-        )
-        prefix_weights = jnp.exp(prefix_scores - row_top[:, :, None])
-        suffix_weights = jnp.where(suffix_mask, jnp.exp(suffix_scores - row_top[:, :, None]), 0.0)
-        denominator = jnp.sum(prefix_weights, axis=2) + jnp.sum(suffix_weights, axis=2)
-        both_pairs = jnp.einsum(
-            "hrp,pjd->rhjd",
-            prefix_weights.astype(jnp.bfloat16),
-            prefix_pairs[:, :, 1],
-            preferred_element_type=jnp.float32,
-        ) + jnp.einsum(
-            "hrk,kjd->rhjd",
-            suffix_weights.astype(jnp.bfloat16),
-            window_pairs[:, :, 1],
-            preferred_element_type=jnp.float32,
-        )
-        accumulated = jnp.sum(jnp.where(pair_select > 0, both_pairs, 0.0), axis=2)
-        window_attended = (
-            (accumulated / jnp.transpose(denominator)[:, :, None])
-            .astype(jnp.bfloat16)
-            .reshape(window, -1)
-        )
+        window_attended = value_of_pair[request].astype(jnp.bfloat16).reshape(window, -1)
         placed = lax.dynamic_update_slice_in_dim(
-            jnp.zeros_like(attended), window_attended, first, 0
+            jnp.zeros_like(attended), window_attended, firsts[request], 0
         )
         attended = jnp.where((request_ids == request)[:, None], placed, attended)
 

time: 121 us -> 121 us (level)
  matrix products: 22.1 us -> 5.45 us
  Pallas kernels: 0 us -> 11.8 us
  between operations: 27.6 us -> 22.3 us
  local copies, waits for them, and re-layouts: 7.62 us -> 12.9 us
  other arithmetic: 5.99 us -> 8.52 us
  waiting for transfers between devices: 42.3 us -> 44 us
    dot_general x16 -> x0, matrix products: 14.7 us -> none  [the longest x4 6.26 us: local(): jnp.einsum('hrp,pjd->rhjd', prefix_weights.astype(jnp.bfloat16), prefix_p...]
    pallas_call x0 -> x1, Pallas kernels: none -> 11.8 us  [window_attention(): pl.pallas_call(attention_kernel, grid_spec=grid_spec, out_shape=jax.Shape...]
    another operation x1 -> x4, other arithmetic: 0.18 us -> 5.77 us  [the longest x1 3.28 us: local(): jnp.stack(spreads)]
    pallas_call x0 -> x1, local copies, waits for them, and re-layouts: none -> 3.43 us  [window_attention(): pl.pallas_call(attention_kernel, grid_spec=grid_spec, out_shape=jax.Shape...]
    ge x4 -> x0, other arithmetic: 2.64 us -> none  [local(): key_position[None, :] >= req_starts[request]]
    reduce_sum x8 -> x0, other arithmetic: 2.06 us -> none  [the longest x4 1.76 us: local(): jnp.sum(prefix_weights, axis=2) + jnp.sum(suffix_weights, axis=2)]
    dot_general x3, matrix products: 3.99 us -> 2.06 us  [local(): jnp.dot(head_block, weight_pieces[shift], preferred_element_type=jnp.floa...]
    all_gather x1, waiting for transfers between devices: 12.5 us -> 14.1 us  [tenant_slots(): return (lax.all_gather(own_slot, 'req', axis=0, tiled=True), owners)]
  transfers between devices with their start and end apart: 10 -> 10, of which waited for: 7 -> 6; matrix products, arithmetic and copies ran while one was open for 25% -> 20% of each run, Pallas kernels for 0% -> 10%
where the time goes in v8:
time: 121 us; the launch traced here: 120 us
  waiting for transfers between devices  44 us (36%)
  between operations  22.3 us (18%)
  starting transfers between devices  14.7 us (12%)
  local copies, waits for them, and re-layouts  12.9 us (11%)
  Pallas kernels  11.8 us (10%)
  other arithmetic  8.52 us (7%)
  matrix products  5.45 us (5%)
    ppermute x9, waiting for transfers between devices, shifted(): return lax.ppermute(block, 'tp', pairs)  29.2 us
    ppermute x9, starting transfers between devices, shifted(): return lax.ppermute(block, 'tp', pairs)  14.6 us
    all_gather x1, waiting for transfers between devices, tenant_slots(): return (lax.all_gather(own_slot, 'req', axis=0, tiled=True), owners)  14.1 us
    pallas_call x1, Pallas kernels, window_attention(): pl.pallas_call(attention_kernel, grid_spec=grid_spec, out_shape=jax.Shape...  11.8 us
    pallas_call x1, local copies, waits for them, and re-layouts, window_attention(): pl.pallas_call(attention_kernel, grid_spec=grid_spec, out_shape=jax.Shape...  3.43 us
    another operation x1, other arithmetic, local(): jnp.stack(spreads)  3.28 us
  transfers between devices with their start and end apart: 10, of which 6 were waited for; matrix products, arithmetic and copies ran while one was open for 20% of the time, Pallas kernels for 10%

profile of v8, /device:TPU:8, one launch (start us, length us, event | category | flops | bytes accessed | tf_op | source)
XLA Modules:
  0.0 119.6 jit_solution(7761202986397738186)
XLA Ops:
  7.3 0.7 all-gather.3.cloned.1.call-update
  8.0 2.3 %constant_dynamic-slice_fusion.1 = (bf16[320,512]{1,0:T(8,128)(2,1)}, bf16[320,512]{1,0:T(8,128)(2,1)}, bf16[320,512]{1,0:T(8,128)(2,1)}) fusion(bf16[320,2048]{1,0:T(8,128)(2,1)} %param.14, s32[]{:T(128)S(6)} %select_n.150, s32[]{:T(128)S(6)} %select_n.148, s32[]{:T(128)S(6)} %select_n.152), kind=kLoop, calls=%fused_computation.77 | loop fusion | bytes 1966092 | tf_op jit(solution)/shard_map/dynamic_slice | solution.py:121
  10.3 1.6 %collective-permute-start.1 = (bf16[320,512]{1,0:T(8,128)(2,1)}, bf16[320,512]{1,0:T(8,128)(2,1)}, u32[]{:S(2)}, u32[]{:S(2)}) collective-permute-start(bf16[320,512]{1,0:T(8,128)(2,1)} %get-tuple-element.5), channel_id=1, source_target_pairs={{0,1},{1,2},{2,3},{3,0},{4,5},{5,6},{6,7},{7,4},{8,9},{9,10},{10,1... | collective-permute-start | bytes 983048 | tf_op jit(solution)/shard_map/ppermute | solution.py:96
  11.8 0.4 collective-permute-start.5
  12.3 2.6 %collective-permute-start.3 = (bf16[320,512]{1,0:T(8,128)(2,1)}, bf16[320,512]{1,0:T(8,128)(2,1)S(1)}, u32[]{:S(2)}, u32[]{:S(2)}) collective-permute-start(bf16[320,512]{1,0:T(8,128)(2,1)} %get-tuple-element.4), channel_id=1, source_target_pairs={{0,2},{1,3},{2,0},{3,1},{4,6},{5,7},{6,4},{7,5},{8,10},{9,11},{10,... | collective-permute-start | bytes 983048 | tf_op jit(solution)/shard_map/ppermute | solution.py:96
  14.9 0.8 reduce-window.8
  15.7 1.2 broadcast_minimum_fusion
  16.9 0.7 fusion.48
  25.4 0.2 constant_dynamic-slice_fusion.6
  25.8 0.2 reshape.477
  26.8 0.2 mul.219
  27.0 0.2 mul.224
  27.5 1.1 gather_fusion
  28.7 0.7 pad_maximum_fusion.suffix_ref
  29.4 0.8 add_select_fusion.row_ref
  30.2 0.2 broadcast_multiply_fusion.4
  30.5 3.3 %maximum_maximum_fusion.query_ref = bf16[4,640,256]{2,1,0:T(8,128)(2,1)} fusion(bf16[1,640,64]{2,1,0:T(8,128)(2,1)S(1)} %broadcast_in_dim.38, bf16[1,640,64]{2,1,0:T(8,128)(2,1)S(1)} %get-tuple-element.22, bf16[1,640,64]{2,1,0:T(8,128)(2,1)S(1)} %get-tuple-element.21, bf16[1,640,64]{2,1,0:T(8,128)(2,1)S(1)} %get-tuple-element.31, ...), kind=kLoop, calls=%fused_computation.3 | loop fusion | flops 20971520 | bytes 2048000 | tf_op jit(solution)/shard_map/stack | solution.py:165
  33.8 14.1 %all-gather.3.cloned.1.call-done = bf16[8192,1,256]{2,0,1:T(8,128)(2,1)} async-done(((bf16[1024,1,256]{2,0,1:T(8,128)(2,1)}), bf16[8192,1,256]{2,0,1:T(8,128)(2,1)}) %all-gather.3.cloned.1.call-update) | async-done | bytes 4194320 | tf_op jit(solution)/shard_map/all_gather | solution.py:34
  47.8 11.8 %shard_map.113 = f32[4,640,256]{2,1,0:T(8,128)} custom-call(s32[4]{0:T(128)} %gather_fusion, s32[4]{0:T(128)} %copy-done.6, s32[4]{0:T(128)} %get-tuple-element.3.start_ref, bf16[4,640,256]{2,1,0:T(8,128)(2,1)} %maximum_maximum_fusion.query_ref, bf16[8192,256]{1,0:T(8,128)(2,1)} %bitcast.44, bf16[4,128,256]{2,1,0:T(8,128)(2,1)} %pad_maximum_fusion.suffix_ref, ...), custom_call_target="tpu_custom_call" | custom-call | tf_op jit(solution)/shard_map/pallas_call | solution.py:87
  59.6 3.4 %copy.29 = bf16[4,640,256]{2,0,1:T(4,128)(2,1)S(1)} copy(f32[4,640,256]{2,1,0:T(8,128)} %shard_map.113) | data formatting | bytes 3932160 | tf_op jit(solution)/shard_map/pallas_call | solution.py:87
  63.1 0.9 fusion
  64.0 0.9 fusion.46
  64.9 0.2 copy.33
  65.1 0.2 copy.31
  65.3 0.2 copy.32
  65.4 0.2 copy.30
  65.7 0.4 select_n.141
  66.1 0.3 dynamic_update_slice.11
  66.4 0.7 dynamic_update_slice.12
  67.1 0.3 dynamic_update_slice.10
  67.5 1.5 %collective-permute-start = (bf16[256,320]{0,1:T(8,128)(2,1)S(1)}, bf16[256,320]{0,1:T(8,128)(2,1)S(1)}, u32[]{:S(2)}, u32[]{:S(2)}) collective-permute-start(bf16[256,320]{0,1:T(8,128)(2,1)S(1)} %select_select_fusion), channel_id=1, source_target_pairs={{0,1},{1,2},{2,3},{3,0},{4,5},{5,6},{6,7},{7,4},{8,9},{9,10},{10,1... | collective-permute-start | bytes 491528 | tf_op jit(solution)/shard_map/ppermute | solution.py:96
  69.1 0.5 collective-permute-start.4
  69.6 1.3 %fusion.24 = f32[256,512]{1,0:T(8,128)S(1)} fusion(bf16[256,320]{0,1:T(8,128)(2,1)S(1)} %select_select_fusion, bf16[320,2048]{1,0:T(8,128)(2,1)} %param.14, s32[]{:T(128)S(6)} %select_n.146), kind=kOutput, calls=%fused_computation.44 | convolution fusion | flops 83886080 | bytes 1015812 | tf_op jit(solution)/shard_map/dot_general | solution.py:182
  70.9 2.5 %collective-permute-start.2 = (bf16[256,320]{0,1:T(8,128)(2,1)S(1)}, bf16[256,320]{0,1:T(8,128)(2,1)S(1)}, u32[]{:S(2)}, u32[]{:S(2)}) collective-permute-start(bf16[256,320]{0,1:T(8,128)(2,1)S(1)} %select_select_fusion), channel_id=1, source_target_pairs={{0,2},{1,3},{2,0},{3,1},{4,6},{5,7},{6,4},{7,5},{8,10},{9,11},{10,... | collective-permute-start | bytes 491528 | tf_op jit(solution)/shard_map/ppermute | solution.py:96
  73.4 1.3 %collective-permute-done = bf16[256,320]{0,1:T(8,128)(2,1)S(1)} collective-permute-done((bf16[256,320]{0,1:T(8,128)(2,1)S(1)}, bf16[256,320]{0,1:T(8,128)(2,1)S(1)}, u32[]{:S(2)}, u32[]{:S(2)}) %collective-permute-start) | collective-permute-done | bytes 163872 | tf_op jit(solution)/shard_map/ppermute | solution.py:96
  74.6 1.3 %convolution_add_fusion.1 = f32[256,512]{1,0:T(8,128)S(1)} fusion(f32[256,512]{1,0:T(8,128)S(1)} %fusion.24, bf16[256,320]{0,1:T(8,128)(2,1)S(1)} %collective-permute-done, bf16[320,512]{1,0:T(8,128)(2,1)} %collective-permute-done.1), kind=kOutput, calls=%fused_computation.7 | convolution fusion | flops 84017152 | bytes 1540096 | tf_op jit(solution)/shard_map/dot_general | solution.py:185
  75.9 3.2 %collective-permute-done.4 = bf16[256,320]{0,1:T(8,128)(2,1)S(1)} collective-permute-done((bf16[256,320]{0,1:T(8,128)(2,1)S(1)}, bf16[256,320]{0,1:T(8,128)(2,1)S(1)}, u32[]{:S(2)}, u32[]{:S(2)}) %collective-permute-start.4) | collective-permute-done | bytes 163872 | tf_op jit(solution)/shard_map/ppermute | solution.py:96
  79.1 0.3 fusion.49
  79.5 3.8 %collective-permute-done.2 = bf16[256,320]{0,1:T(8,128)(2,1)S(1)} collective-permute-done((bf16[256,320]{0,1:T(8,128)(2,1)S(1)}, bf16[256,320]{0,1:T(8,128)(2,1)S(1)}, u32[]{:S(2)}, u32[]{:S(2)}) %collective-permute-start.2) | collective-permute-done | bytes 163872 | tf_op jit(solution)/shard_map/ppermute | solution.py:96
  83.3 0.5 fusion.5
  83.7 3.4 %collective-permute-start.7 = (bf16[256,512]{1,0:T(8,128)(2,1)S(1)}, bf16[256,512]{1,0:T(8,128)(2,1)S(1)}, u32[]{:S(2)}, u32[]{:S(2)}) collective-permute-start(bf16[256,512]{1,0:T(8,128)(2,1)S(1)} %get-tuple-element.48), channel_id=1, source_target_pairs={{0,2},{1,3},{2,0},{3,1},{4,6},{5,7},{6,4},{7,5},{8,10},{9,11},{10,... | collective-permute-start | bytes 786440 | tf_op jit(solution)/shard_map/ppermute | solution.py:96
  87.2 2.0 %collective-permute-start.6 = (bf16[256,512]{1,0:T(8,128)(2,1)S(1)}, bf16[256,512]{1,0:T(8,128)(2,1)S(1)}, u32[]{:S(2)}, u32[]{:S(2)}) collective-permute-start(bf16[256,512]{1,0:T(8,128)(2,1)S(1)} %get-tuple-element.48), channel_id=1, source_target_pairs={{0,1},{1,2},{2,3},{3,0},{4,5},{5,6},{6,7},{7,4},{8,9},{9,10},{10,1... | collective-permute-start | bytes 786440 | tf_op jit(solution)/shard_map/ppermute | solution.py:96
  89.3 14.7 %collective-permute-done.7 = bf16[256,512]{1,0:T(8,128)(2,1)S(1)} collective-permute-done((bf16[256,512]{1,0:T(8,128)(2,1)S(1)}, bf16[256,512]{1,0:T(8,128)(2,1)S(1)}, u32[]{:S(2)}, u32[]{:S(2)}) %collective-permute-start.7) | collective-permute-done | bytes 262176 | tf_op jit(solution)/shard_map/ppermute | solution.py:96
  104.1 6.3 %collective-permute-done.8 = bf16[256,512]{1,0:T(8,128)(2,1)S(1)} collective-permute-done((bf16[256,512]{1,0:T(8,128)(2,1)S(1)}, bf16[256,512]{1,0:T(8,128)(2,1)S(1)}, u32[]{:S(2)}, u32[]{:S(2)}) %collective-permute-start.8) | collective-permute-done | bytes 262176 | tf_op jit(solution)/shard_map/ppermute | solution.py:96
  110.7 0.4 fusion.22
  111.0 0.4 convolution_add_fusion.4
  111.4 0.4 convolution_add_fusion.3
  111.8 1.0 fusion.4
  (55 shorter events, 2.0 us)
Async XLA Ops:
  7.2 103.5 %copy-start = (bf16[2048,320]{0,1:T(8,128)(2,1)S(1)}, bf16[2048,320]{0,1:T(8,128)(2,1)}, u32[]{:S(2)}) copy-start(bf16[2048,320]{0,1:T(8,128)(2,1)} %param.16) | copy-start | bytes 3932164
  7.2 18.2 %copy-start.3 = (bf16[256,320]{0,1:T(8,128)(2,1)S(1)}, bf16[256,320]{0,1:T(8,128)(2,1)}, u32[]{:S(2)}) copy-start(bf16[256,320]{0,1:T(8,128)(2,1)} %param.11) | copy-start | bytes 491524
  7.2 20.2 %copy-start.8 = (s32[1,4]{1,0:T(1,128)S(1)}, s32[1,4]{1,0:T(1,128)}, u32[]{:S(2)}) copy-start(s32[1,4]{1,0:T(1,128)} %param.18) | copy-start | bytes 52
  7.2 20.3 %copy-start.1 = (s32[4]{0:T(128)S(1)}, s32[4]{0:T(128)}, u32[]{:S(2)}) copy-start(s32[4]{0:T(128)} %param.19) | copy-start | bytes 52
  7.2 40.6 %all-gather.3.cloned.1.call-start = ((), (), s32[]{:S(2)}) async-start(), calls=%async_computation | async-start | bytes 4718592 | tf_op jit(solution)/shard_map/all_gather | solution.py:34
  8.0 20.7 %copy-start.4 = (bf16[256,1,256]{2,0,1:T(8,128)(2,1)S(1)}, bf16[256,1,256]{2,0,1:T(8,128)(2,1)}, u32[]{:S(2)}) copy-start(bf16[256,1,256]{2,0,1:T(8,128)(2,1)} %param.12) | copy-start | bytes 393220
  10.3 60.6 %collective-permute-start.1 = (bf16[320,512]{1,0:T(8,128)(2,1)}, bf16[320,512]{1,0:T(8,128)(2,1)}, u32[]{:S(2)}, u32[]{:S(2)}) collective-permute-start(bf16[320,512]{1,0:T(8,128)(2,1)} %get-tuple-element.5), channel_id=1, source_target_pairs={{0,1},{1,2},{2,3},{3,0},{4,5},{5,6},{6,7},{7,4},{8,9},{9,10},{10,1... | collective-permute-start | bytes 983048 | tf_op jit(solution)/shard_map/ppermute | solution.py:96
  11.8 64.1 %collective-permute-start.5 = (bf16[320,512]{1,0:T(8,128)(2,1)}, bf16[320,512]{1,0:T(8,128)(2,1)S(1)}, u32[]{:S(2)}, u32[]{:S(2)}) collective-permute-start(bf16[320,512]{1,0:T(8,128)(2,1)} %get-tuple-element.6), channel_id=1, source_target_pairs={{0,3},{1,0},{2,1},{3,2},{4,7},{5,4},{6,5},{7,6},{8,11},{9,8},{10,9... | collective-permute-start | bytes 983048 | tf_op jit(solution)/shard_map/ppermute | solution.py:96
  12.3 67.2 %collective-permute-start.3 = (bf16[320,512]{1,0:T(8,128)(2,1)}, bf16[320,512]{1,0:T(8,128)(2,1)S(1)}, u32[]{:S(2)}, u32[]{:S(2)}) collective-permute-start(bf16[320,512]{1,0:T(8,128)(2,1)} %get-tuple-element.4), channel_id=1, source_target_pairs={{0,2},{1,3},{2,0},{3,1},{4,6},{5,7},{6,4},{7,5},{8,10},{9,11},{10,... | collective-permute-start | bytes 983048 | tf_op jit(solution)/shard_map/ppermute | solution.py:96
  16.9 13.6 %copy-start.6 = (s32[4]{0:T(128)}, s32[4]{0:T(128)S(1)}, u32[]{:S(2)}) copy-start(s32[4]{0:T(128)S(1)} %get-tuple-element.2.first_ref) | copy-start | bytes 52
  66.1 17.2 %copy-start.5 = (bf16[256,512]{1,0:T(8,128)(2,1)S(1)}, bf16[256,512]{1,0:T(8,128)(2,1)}, u32[]{:S(2)}) copy-start(bf16[256,512]{1,0:T(8,128)(2,1)} %param.10) | copy-start | bytes 786436
  67.5 21.7 %copy-start.7 = (bf16[2048]{0:T(1024)(128)(2,1)S(1)}, bf16[2048]{0:T(1024)(128)(2,1)}, u32[]{:S(2)}) copy-start(bf16[2048]{0:T(1024)(128)(2,1)} %param.15) | copy-start | bytes 12292
  67.5 7.1 %collective-permute-start = (bf16[256,320]{0,1:T(8,128)(2,1)S(1)}, bf16[256,320]{0,1:T(8,128)(2,1)S(1)}, u32[]{:S(2)}, u32[]{:S(2)}) collective-permute-start(bf16[256,320]{0,1:T(8,128)(2,1)S(1)} %select_select_fusion), channel_id=1, source_target_pairs={{0,1},{1,2},{2,3},{3,0},{4,5},{5,6},{6,7},{7,4},{8,9},{9,10},{10,1... | collective-permute-start | bytes 491528 | tf_op jit(solution)/shard_map/ppermute | solution.py:96
  69.1 10.1 %collective-permute-start.4 = (bf16[256,320]{0,1:T(8,128)(2,1)S(1)}, bf16[256,320]{0,1:T(8,128)(2,1)S(1)}, u32[]{:S(2)}, u32[]{:S(2)}) collective-permute-start(bf16[256,320]{0,1:T(8,128)(2,1)S(1)} %select_select_fusion), channel_id=1, source_target_pairs={{0,3},{1,0},{2,1},{3,2},{4,7},{5,4},{6,5},{7,6},{8,11},{9,8},{10,9... | collective-permute-start | bytes 491528 | tf_op jit(solution)/shard_map/ppermute | solution.py:96
  70.9 12.4 %collective-permute-start.2 = (bf16[256,320]{0,1:T(8,128)(2,1)S(1)}, bf16[256,320]{0,1:T(8,128)(2,1)S(1)}, u32[]{:S(2)}, u32[]{:S(2)}) collective-permute-start(bf16[256,320]{0,1:T(8,128)(2,1)S(1)} %select_select_fusion), channel_id=1, source_target_pairs={{0,2},{1,3},{2,0},{3,1},{4,6},{5,7},{6,4},{7,5},{8,10},{9,11},{10,... | collective-permute-start | bytes 491528 | tf_op jit(solution)/shard_map/ppermute | solution.py:96
  83.7 29.1 %copy-start.2 = (bf16[256,512]{1,0:T(8,128)(2,1)}, bf16[256,512]{1,0:T(8,128)(2,1)S(1)}, u32[]{:S(2)}) copy-start(bf16[256,512]{1,0:T(8,128)(2,1)S(1)} %get-tuple-element.48) | copy-start | bytes 786436
  83.7 20.2 %collective-permute-start.7 = (bf16[256,512]{1,0:T(8,128)(2,1)S(1)}, bf16[256,512]{1,0:T(8,128)(2,1)S(1)}, u32[]{:S(2)}, u32[]{:S(2)}) collective-permute-start(bf16[256,512]{1,0:T(8,128)(2,1)S(1)} %get-tuple-element.48), channel_id=1, source_target_pairs={{0,2},{1,3},{2,0},{3,1},{4,6},{5,7},{6,4},{7,5},{8,10},{9,11},{10,... | collective-permute-start | bytes 786440 | tf_op jit(solution)/shard_map/ppermute | solution.py:96
  87.2 23.2 %collective-permute-start.8 = (bf16[256,512]{1,0:T(8,128)(2,1)S(1)}, bf16[256,512]{1,0:T(8,128)(2,1)S(1)}, u32[]{:S(2)}, u32[]{:S(2)}) collective-permute-start(bf16[256,512]{1,0:T(8,128)(2,1)S(1)} %get-tuple-element.48), channel_id=1, source_target_pairs={{0,3},{1,0},{2,1},{3,2},{4,7},{5,4},{6,5},{7,6},{8,11},{9,8},{10,9... | collective-permute-start | bytes 786440 | tf_op jit(solution)/shard_map/ppermute | solution.py:96
  87.2 23.3 %collective-permute-start.6 = (bf16[256,512]{1,0:T(8,128)(2,1)S(1)}, bf16[256,512]{1,0:T(8,128)(2,1)S(1)}, u32[]{:S(2)}, u32[]{:S(2)}) collective-permute-start(bf16[256,512]{1,0:T(8,128)(2,1)S(1)} %get-tuple-element.48), channel_id=1, source_target_pairs={{0,1},{1,2},{2,3},{3,0},{4,5},{5,6},{6,7},{7,4},{8,9},{9,10},{10,1... | collective-permute-start | bytes 786440 | tf_op jit(solution)/shard_map/ppermute | solution.py:96
Sparse Core Ops, SparseCore 0:
  9.9 37.8 all-gather.2

commit v9 on v8

--- a/solution.py
+++ b/solution.py
@@ -36,7 +36,9 @@
     return jnp.concatenate(blocks, axis=0), jnp.arange(TENANTS, dtype=jnp.int32)
 
 
-def attention_kernel(slot_ref, first_ref, start_ref, query_ref, prefix_ref, suffix_ref, row_ref, out_ref):
+def attention_kernel(
+    slot_ref, first_ref, start_ref, query_ref, prefix_ref, suffix_ref, row_ref, pair_ref, out_ref
+):
     request = pl.program_id(0)
     first = first_ref[request]
     start = start_ref[request]
@@ -67,10 +69,15 @@
     accumulated = jnp.dot(
         prefix_weights.astype(jnp.bfloat16), prefix_rows, preferred_element_type=jnp.float32
     ) + jnp.dot(suffix_weights.astype(jnp.bfloat16), suffix_rows, preferred_element_type=jnp.float32)
-    out_ref[...] = accumulated / denominator
-
-
-def window_attention(slot_index, firsts, starts, spread, slots, suffix_windows, query_rows, slot_rows):
+    attended = accumulated / denominator
+    first_pair = attended[:, HD:2 * HD]
+    second_pair = attended[:, 3 * HD:]
+    out_ref[...] = jnp.where(pair_ref[...] > 0, second_pair, first_pair).astype(out_ref.dtype)
+
+
+def window_attention(
+    slot_index, firsts, starts, spread, slots, suffix_windows, query_rows, row_pairs, slot_rows
+):
     requests, flat_rows, lanes = spread.shape
     window = suffix_windows.shape[1]
     grid_spec = pltpu.PrefetchScalarGridSpec(
@@ -81,14 +88,15 @@
             pl.BlockSpec((slot_rows, lanes), lambda k, slot, first, start: (slot[k], 0)),
             pl.BlockSpec((None, window, lanes), lambda k, slot, first, start: (k, 0, 0)),
             pl.BlockSpec((flat_rows, 1), lambda k, slot, first, start: (0, 0)),
+            pl.BlockSpec((flat_rows, 1), lambda k, slot, first, start: (0, 0)),
         ],
-        out_specs=pl.BlockSpec((None, flat_rows, lanes), lambda k, slot, first, start: (k, 0, 0)),
+        out_specs=pl.BlockSpec((None, flat_rows, HD), lambda k, slot, first, start: (k, 0, 0)),
     )
     return pl.pallas_call(
         attention_kernel,
         grid_spec=grid_spec,
-        out_shape=jax.ShapeDtypeStruct((requests, flat_rows, lanes), jnp.float32),
-    )(slot_index, firsts, starts, spread, slots, suffix_windows, query_rows)
+        out_shape=jax.ShapeDtypeStruct((requests, flat_rows, HD), jnp.bfloat16),
+    )(slot_index, firsts, starts, spread, slots, suffix_windows, query_rows, row_pairs)
 
 
 def shifted(block, shift, n_tp):
@@ -139,24 +147,21 @@
     suffix_rows = suffix_kv.reshape(row_count, -1)
     window = min(MOSTLEN, row_count)
     firsts = jnp.minimum(req_starts, row_count - window).astype(jnp.int32)
-    zeros = jnp.zeros((window, head_count, HD), queries.dtype)
+    zeros = jnp.zeros((head_count, window, HD), queries.dtype)
+    head_select = jnp.transpose(select)[:, :, None, None]
     spreads = []
     suffix_windows = []
     for request in range(req_lengths.shape[0]):
         window_queries = lax.dynamic_slice_in_dim(queries, firsts[request], window, 0)
-        window_queries = window_queries.reshape(window, head_count, HD)
+        window_queries = jnp.transpose(window_queries.reshape(window, head_count, HD), (1, 0, 2))
         spread = jnp.concatenate(
-            [
-                window_queries * select[None, :, 0:1],
-                zeros,
-                window_queries * select[None, :, 1:2],
-                zeros,
-            ],
+            [window_queries * head_select[0], zeros, window_queries * head_select[1], zeros],
             axis=2,
         )
-        spreads.append(spread.reshape(window * head_count, 4 * HD))
+        spreads.append(spread.reshape(head_count * window, 4 * HD))
         suffix_windows.append(lax.dynamic_slice_in_dim(suffix_rows, firsts[request], window, 0))
-    query_rows = (jnp.arange(window * head_count, dtype=jnp.int32) // head_count)[:, None]
+    query_rows = (jnp.arange(head_count * window, dtype=jnp.int32) % window)[:, None]
+    row_pairs = jnp.repeat(pair_ids.astype(jnp.int32), window)[:, None]
     slot_index = slot_of_tenant[req_tenant].astype(jnp.int32)
     results = window_attention(
         slot_index,
@@ -166,14 +171,12 @@
         slots,
         jnp.stack(suffix_windows),
         query_rows,
+        row_pairs,
         own_slot.shape[0],
-    ).reshape(-1, window, head_count, 4 * HD)
-    value_of_pair = jnp.where(
-        select[None, None, :, 0:1] > 0, results[..., HD:2 * HD], results[..., 3 * HD:]
-    )
+    ).reshape(-1, head_count, window, HD)
     attended = jnp.zeros((row_count, head_count * HD), jnp.bfloat16)
     for request in range(req_lengths.shape[0]):
-        window_attended = value_of_pair[request].astype(jnp.bfloat16).reshape(window, -1)
+        window_attended = jnp.transpose(results[request], (1, 0, 2)).reshape(window, -1)
         placed = lax.dynamic_update_slice_in_dim(
             jnp.zeros_like(attended), window_attended, firsts[request], 0
         )

time: 121 us -> 117 us (0.967)
  other arithmetic: 8.52 us -> 4.42 us
  local copies, waits for them, and re-layouts: 12.9 us -> 10.1 us
  waiting for transfers between devices: 44 us -> 45.7 us
    pallas_call x1 -> x0, local copies, waits for them, and re-layouts: 3.43 us -> none  [window_attention(): pl.pallas_call(attention_kernel, grid_spec=grid_spec, out_shape=jax.Shape...]
    all_gather x1, waiting for transfers between devices: 14.1 us -> 17.3 us  [tenant_slots(): return (lax.all_gather(own_slot, 'req', axis=0, tiled=True), owners)]
    another operation x1, other arithmetic: 3.28 us -> 1.25 us  [local(): jnp.stack(spreads)]
    another operation x2 -> x1, other arithmetic: 1.75 us -> 0.18 us
    ppermute x9, waiting for transfers between devices: 29.2 us -> 27.7 us  [shifted(): return lax.ppermute(block, 'tp', pairs)]
  transfers between devices with their start and end apart: 10 -> 10, of which waited for: 6 -> 5; matrix products, arithmetic and copies ran while one was open for 20% -> 16% of each run, Pallas kernels for 10% -> 11%
where the time goes in v9:
time: 117 us; the launch traced here: 116 us
  waiting for transfers between devices  45.7 us (39%)
  between operations  22.1 us (19%)
  starting transfers between devices  14.7 us (13%)
  Pallas kernels  12.1 us (10%)
  local copies, waits for them, and re-layouts  10.1 us (9%)
  matrix products  6.41 us (5%)
  other arithmetic  4.42 us (4%)
    ppermute x9, waiting for transfers between devices, shifted(): return lax.ppermute(block, 'tp', pairs)  27.7 us
    all_gather x1, waiting for transfers between devices, tenant_slots(): return (lax.all_gather(own_slot, 'req', axis=0, tiled=True), owners)  17.3 us
    ppermute x9, starting transfers between devices, shifted(): return lax.ppermute(block, 'tp', pairs)  14.6 us
    pallas_call x1, Pallas kernels, window_attention(): pl.pallas_call(attention_kernel, grid_spec=grid_spec, out_shape=jax.Shape...  12.1 us
    dot_general x3, matrix products, local(): jnp.dot(head_block, weight_pieces[shift], preferred_element_type=jnp.floa...  3.03 us
  transfers between devices with their start and end apart: 10, of which 5 were waited for; matrix products, arithmetic and copies ran while one was open for 16% of the time, Pallas kernels for 11%

profile of v9, /device:TPU:8, one launch (start us, length us, event | category | flops | bytes accessed | tf_op | source)
XLA Modules:
  0.0 115.6 jit_solution(16734627567085933449)
XLA Ops:
  7.2 0.7 all-gather.3.cloned.1.call-update
  8.0 2.2 %constant_dynamic-slice_fusion.1 = (bf16[320,512]{1,0:T(8,128)(2,1)}, bf16[320,512]{1,0:T(8,128)(2,1)}, bf16[320,512]{1,0:T(8,128)(2,1)}) fusion(bf16[320,2048]{1,0:T(8,128)(2,1)} %param.14, s32[]{:T(128)S(6)} %select_n.146, s32[]{:T(128)S(6)} %select_n.144, s32[]{:T(128)S(6)} %select_n.148), kind=kLoop, calls=%fused_computation.85 | loop fusion | bytes 1966092 | tf_op jit(solution)/shard_map/dynamic_slice | solution.py:129
  10.2 1.6 %collective-permute-start.1 = (bf16[320,512]{1,0:T(8,128)(2,1)}, bf16[320,512]{1,0:T(8,128)(2,1)}, u32[]{:S(2)}, u32[]{:S(2)}) collective-permute-start(bf16[320,512]{1,0:T(8,128)(2,1)} %get-tuple-element.5), channel_id=1, source_target_pairs={{0,1},{1,2},{2,3},{3,0},{4,5},{5,6},{6,7},{7,4},{8,9},{9,10},{10,1... | collective-permute-start | bytes 983048 | tf_op jit(solution)/shard_map/ppermute | solution.py:104
  11.7 0.4 collective-permute-start.5
  12.2 2.6 %collective-permute-start.3 = (bf16[320,512]{1,0:T(8,128)(2,1)}, bf16[320,512]{1,0:T(8,128)(2,1)S(1)}, u32[]{:S(2)}, u32[]{:S(2)}) collective-permute-start(bf16[320,512]{1,0:T(8,128)(2,1)} %get-tuple-element.4), channel_id=1, source_target_pairs={{0,2},{1,3},{2,0},{3,1},{4,6},{5,7},{6,4},{7,5},{8,10},{9,11},{10,... | collective-permute-start | bytes 983048 | tf_op jit(solution)/shard_map/ppermute | solution.py:104
  14.8 0.2 reduce-window.8
  15.0 0.6 broadcast_minimum_fusion
  15.5 0.7 fusion.51
  23.9 0.2 constant_dynamic-slice_fusion.6
  24.3 0.2 pad_maximum_fusion.4
  24.5 0.2 copy.21
  24.7 0.2 copy.22
  24.9 0.2 copy.23
  25.1 0.2 copy.24
  25.4 0.9 copy.31
  26.5 1.1 gather_fusion
  27.7 0.7 pad_maximum_fusion.9.suffix_ref
  28.4 0.8 add_select_fusion.row_ref
  29.2 1.3 %pad_maximum_fusion.query_ref = bf16[4,640,256]{2,1,0:T(8,128)(2,1)} fusion(bf16[1,640,256]{2,1,0:T(8,128)(2,1)S(1)} %bitcast.87, bf16[1,640,256]{2,1,0:T(8,128)(2,1)S(1)} %bitcast.86, bf16[1,640,256]{2,1,0:T(8,128)(2,1)S(1)} %bitcast.85, bf16[1,640,256]{2,1,0:T(8,128)(2,1)S(1)} %bitcast.84), kind=kLoop, calls=%fused_computation.1 | loop fusion | flops 1966080 | bytes 2621440 | tf_op jit(solution)/shard_map/stack | solution.py:170
  30.5 17.3 %all-gather.3.cloned.1.call-done = bf16[8192,1,256]{2,0,1:T(8,128)(2,1)} async-done(((bf16[1024,1,256]{2,0,1:T(8,128)(2,1)}), bf16[8192,1,256]{2,0,1:T(8,128)(2,1)}) %all-gather.3.cloned.1.call-update) | async-done | bytes 4194320 | tf_op jit(solution)/shard_map/all_gather | solution.py:34
  47.8 12.1 %shard_map.113 = bf16[4,640,64]{2,1,0:T(8,128)(2,1)} custom-call(s32[4]{0:T(128)} %gather_fusion, s32[4]{0:T(128)} %copy-done.6, s32[4]{0:T(128)} %get-tuple-element.3.start_ref, bf16[4,640,256]{2,1,0:T(8,128)(2,1)} %pad_maximum_fusion.query_ref, bf16[8192,256]{1,0:T(8,128)(2,1)} %bitcast.83, bf16[4,128,256]{2,1,0:T(8,128)(2,1)} %pad_maximum_fusion.9.suffix_ref, ...), custom_call_target="tpu_custom_call" | custom-call | tf_op jit(solution)/shard_map/pallas_call | solution.py:95
  60.0 1.2 %fusion.49 = (bf16[1,640,64]{2,1,0:T(8,128)(2,1)S(1)}, bf16[1,640,64]{2,1,0:T(8,128)(2,1)S(1)}, bf16[1,640,64]{2,1,0:T(8,128)(2,1)S(1)}, bf16[1,640,64]{2,1,0:T(8,128)(2,1)S(1)}) fusion(bf16[4,640,64]{2,1,0:T(8,128)(2,1)} %shard_map.113), kind=kLoop, calls=%fused_computation.112 | loop fusion | bytes 655360 | tf_op jit(solution)/shard_map/slice | solution.py:179
  61.2 0.1 copy.29
  61.3 0.1 copy.27
  61.5 0.1 copy.28
  61.6 0.1 copy.26
  61.8 0.4 select_n.137
  62.2 0.7 dynamic_update_slice.11
  62.9 0.7 dynamic_update_slice.12
  63.6 0.3 dynamic_update_slice.10
  64.0 1.5 %collective-permute-start = (bf16[256,320]{0,1:T(8,128)(2,1)S(1)}, bf16[256,320]{0,1:T(8,128)(2,1)S(1)}, u32[]{:S(2)}, u32[]{:S(2)}) collective-permute-start(bf16[256,320]{0,1:T(8,128)(2,1)S(1)} %select_select_fusion), channel_id=1, source_target_pairs={{0,1},{1,2},{2,3},{3,0},{4,5},{5,6},{6,7},{7,4},{8,9},{9,10},{10,1... | collective-permute-start | bytes 491528 | tf_op jit(solution)/shard_map/ppermute | solution.py:104
  65.5 0.5 collective-permute-start.4
  66.1 1.3 %fusion.25 = f32[256,512]{1,0:T(8,128)S(1)} fusion(bf16[256,320]{0,1:T(8,128)(2,1)S(1)} %select_select_fusion, bf16[320,2048]{1,0:T(8,128)(2,1)} %param.14, s32[]{:T(128)S(6)} %select_n.142), kind=kOutput, calls=%fused_computation.49 | convolution fusion | flops 83886080 | bytes 1015812 | tf_op jit(solution)/shard_map/dot_general | solution.py:185
  67.4 2.5 %collective-permute-start.2 = (bf16[256,320]{0,1:T(8,128)(2,1)S(1)}, bf16[256,320]{0,1:T(8,128)(2,1)S(1)}, u32[]{:S(2)}, u32[]{:S(2)}) collective-permute-start(bf16[256,320]{0,1:T(8,128)(2,1)S(1)} %select_select_fusion), channel_id=1, source_target_pairs={{0,2},{1,3},{2,0},{3,1},{4,6},{5,7},{6,4},{7,5},{8,10},{9,11},{10,... | collective-permute-start | bytes 491528 | tf_op jit(solution)/shard_map/ppermute | solution.py:104
  69.9 6.4 %collective-permute-done = bf16[256,320]{0,1:T(8,128)(2,1)S(1)} collective-permute-done((bf16[256,320]{0,1:T(8,128)(2,1)S(1)}, bf16[256,320]{0,1:T(8,128)(2,1)S(1)}, u32[]{:S(2)}, u32[]{:S(2)}) %collective-permute-start) | collective-permute-done | bytes 163872 | tf_op jit(solution)/shard_map/ppermute | solution.py:104
  76.2 1.3 %convolution_add_fusion.1 = f32[256,512]{1,0:T(8,128)S(1)} fusion(f32[256,512]{1,0:T(8,128)S(1)} %fusion.25, bf16[256,320]{0,1:T(8,128)(2,1)S(1)} %collective-permute-done, bf16[320,512]{1,0:T(8,128)(2,1)} %collective-permute-done.1), kind=kOutput, calls=%fused_computation.5 | convolution fusion | flops 84017152 | bytes 1540096 | tf_op jit(solution)/shard_map/dot_general | solution.py:188
  77.5 1.3 %fusion.52 = f32[256,512]{1,0:T(8,128)S(1)} fusion(bf16[256,320]{0,1:T(8,128)(2,1)S(1)} %collective-permute-done.4, bf16[320,512]{1,0:T(8,128)(2,1)} %collective-permute-done.5), kind=kOutput, calls=%fused_computation.115 | convolution fusion | flops 83886080 | bytes 1015808 | tf_op jit(solution)/shard_map/dot_general | solution.py:188
  78.9 0.6 collective-permute-done.2
  79.4 0.5 fusion.4
  79.9 3.4 %collective-permute-start.7 = (bf16[256,512]{1,0:T(8,128)(2,1)S(1)}, bf16[256,512]{1,0:T(8,128)(2,1)S(1)}, u32[]{:S(2)}, u32[]{:S(2)}) collective-permute-start(bf16[256,512]{1,0:T(8,128)(2,1)S(1)} %get-tuple-element.52), channel_id=1, source_target_pairs={{0,2},{1,3},{2,0},{3,1},{4,6},{5,7},{6,4},{7,5},{8,10},{9,11},{10,... | collective-permute-start | bytes 786440 | tf_op jit(solution)/shard_map/ppermute | solution.py:104
  83.3 0.2 collective-permute-start.8
  83.5 1.9 %collective-permute-start.6 = (bf16[256,512]{1,0:T(8,128)(2,1)S(1)}, bf16[256,512]{1,0:T(8,128)(2,1)S(1)}, u32[]{:S(2)}, u32[]{:S(2)}) collective-permute-start(bf16[256,512]{1,0:T(8,128)(2,1)S(1)} %get-tuple-element.52), channel_id=1, source_target_pairs={{0,1},{1,2},{2,3},{3,0},{4,5},{5,6},{6,7},{7,4},{8,9},{9,10},{10,1... | collective-permute-start | bytes 786440 | tf_op jit(solution)/shard_map/ppermute | solution.py:104
  85.4 14.7 %collective-permute-done.7 = bf16[256,512]{1,0:T(8,128)(2,1)S(1)} collective-permute-done((bf16[256,512]{1,0:T(8,128)(2,1)S(1)}, bf16[256,512]{1,0:T(8,128)(2,1)S(1)}, u32[]{:S(2)}, u32[]{:S(2)}) %collective-permute-start.7) | collective-permute-done | bytes 262176 | tf_op jit(solution)/shard_map/ppermute | solution.py:104
  100.3 6.1 %collective-permute-done.8 = bf16[256,512]{1,0:T(8,128)(2,1)S(1)} collective-permute-done((bf16[256,512]{1,0:T(8,128)(2,1)S(1)}, bf16[256,512]{1,0:T(8,128)(2,1)S(1)}, u32[]{:S(2)}, u32[]{:S(2)}) %collective-permute-start.8) | collective-permute-done | bytes 262176 | tf_op jit(solution)/shard_map/ppermute | solution.py:104
  106.7 0.4 fusion.23
  107.0 0.4 convolution_add_fusion.4
  107.4 0.4 convolution_add_fusion.3
  107.8 1.0 fusion.3
  (50 shorter events, 1.2 us)
Async XLA Ops:
  7.2 99.5 %copy-start = (bf16[2048,320]{0,1:T(8,128)(2,1)S(1)}, bf16[2048,320]{0,1:T(8,128)(2,1)}, u32[]{:S(2)}) copy-start(bf16[2048,320]{0,1:T(8,128)(2,1)} %param.16) | copy-start | bytes 3932164
  7.2 7.6 %copy-start.8 = (s32[1,4]{1,0:T(1,128)S(1)}, s32[1,4]{1,0:T(1,128)}, u32[]{:S(2)}) copy-start(s32[1,4]{1,0:T(1,128)} %param.17) | copy-start | bytes 52
  7.2 16.7 %copy-start.3 = (bf16[256,320]{0,1:T(8,128)(2,1)S(1)}, bf16[256,320]{0,1:T(8,128)(2,1)}, u32[]{:S(2)}) copy-start(bf16[256,320]{0,1:T(8,128)(2,1)} %param.11) | copy-start | bytes 491524
  7.2 40.6 %all-gather.3.cloned.1.call-start = ((), (), s32[]{:S(2)}) async-start(), calls=%async_computation | async-start | bytes 4718592 | tf_op jit(solution)/shard_map/all_gather | solution.py:34
  10.2 57.2 %collective-permute-start.1 = (bf16[320,512]{1,0:T(8,128)(2,1)}, bf16[320,512]{1,0:T(8,128)(2,1)}, u32[]{:S(2)}, u32[]{:S(2)}) collective-permute-start(bf16[320,512]{1,0:T(8,128)(2,1)} %get-tuple-element.5), channel_id=1, source_target_pairs={{0,1},{1,2},{2,3},{3,0},{4,5},{5,6},{6,7},{7,4},{8,9},{9,10},{10,1... | collective-permute-start | bytes 983048 | tf_op jit(solution)/shard_map/ppermute | solution.py:104
  11.7 65.8 %collective-permute-start.5 = (bf16[320,512]{1,0:T(8,128)(2,1)}, bf16[320,512]{1,0:T(8,128)(2,1)}, u32[]{:S(2)}, u32[]{:S(2)}) collective-permute-start(bf16[320,512]{1,0:T(8,128)(2,1)} %get-tuple-element.6), channel_id=1, source_target_pairs={{0,3},{1,0},{2,1},{3,2},{4,7},{5,4},{6,5},{7,6},{8,11},{9,8},{10,9... | collective-permute-start | bytes 983048 | tf_op jit(solution)/shard_map/ppermute | solution.py:104
  12.2 66.7 %collective-permute-start.3 = (bf16[320,512]{1,0:T(8,128)(2,1)}, bf16[320,512]{1,0:T(8,128)(2,1)S(1)}, u32[]{:S(2)}, u32[]{:S(2)}) collective-permute-start(bf16[320,512]{1,0:T(8,128)(2,1)} %get-tuple-element.4), channel_id=1, source_target_pairs={{0,2},{1,3},{2,0},{3,1},{4,6},{5,7},{6,4},{7,5},{8,10},{9,11},{10,... | collective-permute-start | bytes 983048 | tf_op jit(solution)/shard_map/ppermute | solution.py:104
  15.5 8.9 %copy-start.6 = (s32[4]{0:T(128)}, s32[4]{0:T(128)S(1)}, u32[]{:S(2)}) copy-start(s32[4]{0:T(128)S(1)} %get-tuple-element.2.first_ref) | copy-start | bytes 52
  24.7 1.8 %copy-start.9 = (s32[1,4]{1,0:T(1,128)S(1)}, s32[1,4]{1,0:T(1,128)}, u32[]{:S(2)}) copy-start(s32[1,4]{1,0:T(1,128)} %param.18) | copy-start | bytes 52
  24.7 1.8 %copy-start.1 = (s32[4]{0:T(128)S(1)}, s32[4]{0:T(128)}, u32[]{:S(2)}) copy-start(s32[4]{0:T(128)} %param.19) | copy-start | bytes 52
  24.7 2.9 %copy-start.4 = (bf16[256,1,256]{2,0,1:T(8,128)(2,1)S(1)}, bf16[256,1,256]{2,0,1:T(8,128)(2,1)}, u32[]{:S(2)}) copy-start(bf16[256,1,256]{2,0,1:T(8,128)(2,1)} %param.12) | copy-start | bytes 393220
  64.0 12.2 %collective-permute-start = (bf16[256,320]{0,1:T(8,128)(2,1)S(1)}, bf16[256,320]{0,1:T(8,128)(2,1)S(1)}, u32[]{:S(2)}, u32[]{:S(2)}) collective-permute-start(bf16[256,320]{0,1:T(8,128)(2,1)S(1)} %select_select_fusion), channel_id=1, source_target_pairs={{0,1},{1,2},{2,3},{3,0},{4,5},{5,6},{6,7},{7,4},{8,9},{9,10},{10,1... | collective-permute-start | bytes 491528 | tf_op jit(solution)/shard_map/ppermute | solution.py:104
  65.5 12.0 %collective-permute-start.4 = (bf16[256,320]{0,1:T(8,128)(2,1)S(1)}, bf16[256,320]{0,1:T(8,128)(2,1)S(1)}, u32[]{:S(2)}, u32[]{:S(2)}) collective-permute-start(bf16[256,320]{0,1:T(8,128)(2,1)S(1)} %select_select_fusion), channel_id=1, source_target_pairs={{0,3},{1,0},{2,1},{3,2},{4,7},{5,4},{6,5},{7,6},{8,11},{9,8},{10,9... | collective-permute-start | bytes 491528 | tf_op jit(solution)/shard_map/ppermute | solution.py:104
  67.4 12.1 %copy-start.5 = (bf16[256,512]{1,0:T(8,128)(2,1)S(1)}, bf16[256,512]{1,0:T(8,128)(2,1)}, u32[]{:S(2)}) copy-start(bf16[256,512]{1,0:T(8,128)(2,1)} %param.10) | copy-start | bytes 786436
  67.4 12.0 %collective-permute-start.2 = (bf16[256,320]{0,1:T(8,128)(2,1)S(1)}, bf16[256,320]{0,1:T(8,128)(2,1)S(1)}, u32[]{:S(2)}, u32[]{:S(2)}) collective-permute-start(bf16[256,320]{0,1:T(8,128)(2,1)S(1)} %select_select_fusion), channel_id=1, source_target_pairs={{0,2},{1,3},{2,0},{3,1},{4,6},{5,7},{6,4},{7,5},{8,10},{9,11},{10,... | collective-permute-start | bytes 491528 | tf_op jit(solution)/shard_map/ppermute | solution.py:104
  78.8 6.5 %copy-start.7 = (bf16[2048]{0:T(1024)(128)(2,1)S(1)}, bf16[2048]{0:T(1024)(128)(2,1)}, u32[]{:S(2)}) copy-start(bf16[2048]{0:T(1024)(128)(2,1)} %param.15) | copy-start | bytes 12292
  79.9 27.5 %copy-start.2 = (bf16[256,512]{1,0:T(8,128)(2,1)}, bf16[256,512]{1,0:T(8,128)(2,1)S(1)}, u32[]{:S(2)}) copy-start(bf16[256,512]{1,0:T(8,128)(2,1)S(1)} %get-tuple-element.52) | copy-start | bytes 786436
  79.9 20.2 %collective-permute-start.7 = (bf16[256,512]{1,0:T(8,128)(2,1)S(1)}, bf16[256,512]{1,0:T(8,128)(2,1)S(1)}, u32[]{:S(2)}, u32[]{:S(2)}) collective-permute-start(bf16[256,512]{1,0:T(8,128)(2,1)S(1)} %get-tuple-element.52), channel_id=1, source_target_pairs={{0,2},{1,3},{2,0},{3,1},{4,6},{5,7},{6,4},{7,5},{8,10},{9,11},{10,... | collective-permute-start | bytes 786440 | tf_op jit(solution)/shard_map/ppermute | solution.py:104
  83.3 23.0 %collective-permute-start.8 = (bf16[256,512]{1,0:T(8,128)(2,1)S(1)}, bf16[256,512]{1,0:T(8,128)(2,1)S(1)}, u32[]{:S(2)}, u32[]{:S(2)}) collective-permute-start(bf16[256,512]{1,0:T(8,128)(2,1)S(1)} %get-tuple-element.52), channel_id=1, source_target_pairs={{0,3},{1,0},{2,1},{3,2},{4,7},{5,4},{6,5},{7,6},{8,11},{9,8},{10,9... | collective-permute-start | bytes 786440 | tf_op jit(solution)/shard_map/ppermute | solution.py:104
  83.5 23.0 %collective-permute-start.6 = (bf16[256,512]{1,0:T(8,128)(2,1)S(1)}, bf16[256,512]{1,0:T(8,128)(2,1)S(1)}, u32[]{:S(2)}, u32[]{:S(2)}) collective-permute-start(bf16[256,512]{1,0:T(8,128)(2,1)S(1)} %get-tuple-element.52), channel_id=1, source_target_pairs={{0,1},{1,2},{2,3},{3,0},{4,5},{5,6},{6,7},{7,4},{8,9},{9,10},{10,1... | collective-permute-start | bytes 786440 | tf_op jit(solution)/shard_map/ppermute | solution.py:104
Sparse Core Ops, SparseCore 0:
  9.9 37.8 all-gather.2

commit v10 on v9

--- a/solution.py
+++ b/solution.py
@@ -72,7 +72,10 @@
     attended = accumulated / denominator
     first_pair = attended[:, HD:2 * HD]
     second_pair = attended[:, 3 * HD:]
-    out_ref[...] = jnp.where(pair_ref[...] > 0, second_pair, first_pair).astype(out_ref.dtype)
+    picked = jnp.where(pair_ref[...] > 0, second_pair, first_pair).astype(out_ref.dtype)
+    window = out_ref.shape[0]
+    for head in range(out_ref.shape[1] // HD):
+        out_ref[:, head * HD:(head + 1) * HD] = picked[head * window:(head + 1) * window]
 
 
 def window_attention(
@@ -80,6 +83,7 @@
 ):
     requests, flat_rows, lanes = spread.shape
     window = suffix_windows.shape[1]
+    head_count = flat_rows // window
     grid_spec = pltpu.PrefetchScalarGridSpec(
         num_scalar_prefetch=3,
         grid=(requests,),
@@ -90,12 +94,12 @@
             pl.BlockSpec((flat_rows, 1), lambda k, slot, first, start: (0, 0)),
             pl.BlockSpec((flat_rows, 1), lambda k, slot, first, start: (0, 0)),
         ],
-        out_specs=pl.BlockSpec((None, flat_rows, HD), lambda k, slot, first, start: (k, 0, 0)),
+        out_specs=pl.BlockSpec((None, window, head_count * HD), lambda k, slot, first, start: (k, 0, 0)),
     )
     return pl.pallas_call(
         attention_kernel,
         grid_spec=grid_spec,
-        out_shape=jax.ShapeDtypeStruct((requests, flat_rows, HD), jnp.bfloat16),
+        out_shape=jax.ShapeDtypeStruct((requests, window, head_count * HD), jnp.bfloat16),
     )(slot_index, firsts, starts, spread, slots, suffix_windows, query_rows, row_pairs)
 
 
@@ -173,14 +177,9 @@
         query_rows,
         row_pairs,
         own_slot.shape[0],
-    ).reshape(-1, head_count, window, HD)
-    attended = jnp.zeros((row_count, head_count * HD), jnp.bfloat16)
-    for request in range(req_lengths.shape[0]):
-        window_attended = jnp.transpose(results[request], (1, 0, 2)).reshape(window, -1)
-        placed = lax.dynamic_update_slice_in_dim(
-            jnp.zeros_like(attended), window_attended, firsts[request], 0
-        )
-        attended = jnp.where((request_ids == request)[:, None], placed, attended)
+    ).reshape(-1, head_count * HD)
+    source_rows = request_ids * window + position - firsts[request_ids]
+    attended = jnp.take(results, source_rows, axis=0)
 
     projected = jnp.dot(attended, weight_pieces[0], preferred_element_type=jnp.float32)
     for shift in range(1, n_tp):

time: 117 us -> 119 us (1.017)
  other arithmetic: 4.42 us -> 6.95 us
  local copies, waits for them, and re-layouts: 10.1 us -> 8.29 us
  waiting for transfers between devices: 45.7 us -> 47.5 us
    ppermute x9, waiting for transfers between devices: 27.7 us -> 31.8 us  [shifted(): return lax.ppermute(block, 'tp', pairs)]
    gather x0 -> x2, local copies, waits for them, and re-layouts: none -> 2.85 us  [the longest x1 2.19 us: local(): attended = jnp.take(results, source_rows, axis=0)]
    select_n x2, other arithmetic: 0.06 us -> 2.67 us  [local(): attended = jnp.take(results, source_rows, axis=0)]
    all_gather x1, waiting for transfers between devices: 17.3 us -> 15 us  [tenant_slots(): return (lax.all_gather(own_slot, 'req', axis=0, tiled=True), owners)]
    slice x2 -> x0, local copies, waits for them, and re-layouts: 1.87 us -> none  [the longest x1 1.19 us: local(): results[request]]
    dynamic_update_slice x3 -> x0, local copies, waits for them, and re-layouts: 1.69 us -> none  [local(): lax.dynamic_update_slice_in_dim(jnp.zeros_like(attended), window_attended...]
  transfers between devices with their start and end apart: 10 -> 10, of which waited for: 5 -> 5; matrix products, arithmetic and copies ran while one was open for 16% -> 15% of each run, Pallas kernels for 11% -> 10%
where the time goes in v10:
time: 119 us; the launch traced here: 118 us
  waiting for transfers between devices  47.5 us (40%)
  between operations  22.1 us (19%)
  starting transfers between devices  14.7 us (12%)
  Pallas kernels  12 us (10%)
  local copies, waits for them, and re-layouts  8.29 us (7%)
  other arithmetic  6.95 us (6%)
  matrix products  6.31 us (5%)
    ppermute x9, waiting for transfers between devices, shifted(): return lax.ppermute(block, 'tp', pairs)  31.8 us
    all_gather x1, waiting for transfers between devices, tenant_slots(): return (lax.all_gather(own_slot, 'req', axis=0, tiled=True), owners)  15 us
    ppermute x9, starting transfers between devices, shifted(): return lax.ppermute(block, 'tp', pairs)  14.6 us
    pallas_call x1, Pallas kernels, window_attention(): pl.pallas_call(attention_kernel, grid_spec=grid_spec, out_shape=jax.Shape...  12 us
    dot_general x3, matrix products, local(): jnp.dot(head_block, weight_pieces[shift], preferred_element_type=jnp.floa...  2.94 us
    select_n x2, other arithmetic, local(): attended = jnp.take(results, source_rows, axis=0)  2.67 us
  transfers between devices with their start and end apart: 10, of which 5 were waited for; matrix products, arithmetic and copies ran while one was open for 15% of the time, Pallas kernels for 10%

profile of v10, /device:TPU:8, one launch (start us, length us, event | category | flops | bytes accessed | tf_op | source)
XLA Modules:
  0.0 117.8 jit_solution(18175600331833483561)
XLA Ops:
  7.2 0.7 all-gather.3.cloned.1.call-update
  8.0 2.2 %constant_dynamic-slice_fusion.1 = (bf16[320,512]{1,0:T(8,128)(2,1)}, bf16[320,512]{1,0:T(8,128)(2,1)}, bf16[320,512]{1,0:T(8,128)(2,1)}) fusion(bf16[320,2048]{1,0:T(8,128)(2,1)} %param.14, s32[]{:T(128)S(6)} %select_n.153, s32[]{:T(128)S(6)} %select_n.151, s32[]{:T(128)S(6)} %select_n.155), kind=kLoop, calls=%fused_computation.88 | loop fusion | bytes 1966092 | tf_op jit(solution)/shard_map/dynamic_slice | solution.py:133
  10.1 1.6 %collective-permute-start.1 = (bf16[320,512]{1,0:T(8,128)(2,1)}, bf16[320,512]{1,0:T(8,128)(2,1)}, u32[]{:S(2)}, u32[]{:S(2)}) collective-permute-start(bf16[320,512]{1,0:T(8,128)(2,1)} %get-tuple-element.7), channel_id=1, source_target_pairs={{0,1},{1,2},{2,3},{3,0},{4,5},{5,6},{6,7},{7,4},{8,9},{9,10},{10,1... | collective-permute-start | bytes 983048 | tf_op jit(solution)/shard_map/ppermute | solution.py:108
  11.7 0.4 collective-permute-start.5
  12.2 2.6 %collective-permute-start.3 = (bf16[320,512]{1,0:T(8,128)(2,1)}, bf16[320,512]{1,0:T(8,128)(2,1)}, u32[]{:S(2)}, u32[]{:S(2)}) collective-permute-start(bf16[320,512]{1,0:T(8,128)(2,1)} %get-tuple-element.6), channel_id=1, source_target_pairs={{0,2},{1,3},{2,0},{3,1},{4,6},{5,7},{6,4},{7,5},{8,10},{9,11},{10,... | collective-permute-start | bytes 983048 | tf_op jit(solution)/shard_map/ppermute | solution.py:108
  14.8 0.2 reduce-window.8
  14.9 0.5 broadcast_minimum_fusion
  15.4 0.7 fusion.50
  23.8 0.2 constant_dynamic-slice_fusion.6
  24.0 0.1 multiply_bitcast_fusion.1
  24.2 0.2 pad_maximum_fusion.4
  24.4 0.2 copy.17
  24.6 0.2 copy.18
  24.8 0.2 copy.19
  25.0 0.2 copy.20
  25.2 0.9 copy.23
  26.2 1.1 gather_fusion
  27.3 0.1 convert_reduce_fusion
  27.4 2.6 %compare_select_fusion = (s32[256,1]{0,1:T(1,128)S(1)}, s32[256,1]{0,1:T(1,128)S(1)}) fusion(s32[256,1]{0,1:T(1,128)S(1)} %bitcast.83, s32[]{:T(128)} %bitcast.7, s32[]{:T(128)} %bitcast.6, s32[]{:T(128)} %bitcast.5, s32[]{:T(128)} %bitcast.4), kind=kLoop, calls=%fused_computation.78 | loop fusion | flops 3840 | bytes 3088 | tf_op jit(solution)/shard_map/jit(_take)/jit(_where)/select_n | solution.py:182
  30.0 0.1 dynamic-slice_bitcast_fusion.3
  30.1 0.7 pad_maximum_fusion.9.suffix_ref
  30.8 0.8 add_select_fusion.row_ref
  31.6 1.3 %pad_maximum_fusion.query_ref = bf16[4,640,256]{2,1,0:T(8,128)(2,1)} fusion(bf16[1,640,256]{2,1,0:T(8,128)(2,1)S(1)} %bitcast.76, bf16[1,640,256]{2,1,0:T(8,128)(2,1)S(1)} %bitcast.75, bf16[1,640,256]{2,1,0:T(8,128)(2,1)S(1)} %bitcast.74, bf16[1,640,256]{2,1,0:T(8,128)(2,1)S(1)} %bitcast.73), kind=kLoop, calls=%fused_computation.2 | loop fusion | flops 1966080 | bytes 2621440 | tf_op jit(solution)/shard_map/stack | solution.py:174
  32.9 15.0 %all-gather.3.cloned.1.call-done = bf16[8192,1,256]{2,0,1:T(8,128)(2,1)} async-done(((bf16[1024,1,256]{2,0,1:T(8,128)(2,1)}), bf16[8192,1,256]{2,0,1:T(8,128)(2,1)}) %all-gather.3.cloned.1.call-update) | async-done | bytes 4194320 | tf_op jit(solution)/shard_map/all_gather | solution.py:34
  47.8 12.0 %shard_map.113 = bf16[4,128,320]{2,1,0:T(8,128)(2,1)} custom-call(s32[4]{0:T(128)} %gather_fusion, s32[4]{0:T(128)} %copy-done.6, s32[4]{0:T(128)} %get-tuple-element.5.start_ref, bf16[4,640,256]{2,1,0:T(8,128)(2,1)} %pad_maximum_fusion.query_ref, bf16[8192,256]{1,0:T(8,128)(2,1)} %bitcast.71, bf16[4,128,256]{2,1,0:T(8,128)(2,1)} %pad_maximum_fusion.9.suffix_ref, ...), custom_call_target="tpu_custom_call" | custom-call | tf_op jit(solution)/shard_map/pallas_call | solution.py:99
  59.8 2.2 %gather_fusion.1 = bf16[256,320]{1,0:T(8,128)(2,1)S(1)} fusion(bf16[512,320]{1,0:T(8,128)(2,1)} %bitcast.70, s32[1024]{0:T(1024)S(1)} %pad_clamp_fusion), kind=kCustom, calls=%fused_computation.1 | custom fusion | bytes 328704 | tf_op jit(solution)/shard_map/jit(_take)/gather | solution.py:182
  62.0 0.1 broadcast_select_fusion
  62.2 1.5 %collective-permute-start = (bf16[256,320]{1,0:T(8,128)(2,1)S(1)}, bf16[256,320]{1,0:T(8,128)(2,1)S(1)}, u32[]{:S(2)}, u32[]{:S(2)}) collective-permute-start(bf16[256,320]{1,0:T(8,128)(2,1)S(1)} %broadcast_select_fusion), channel_id=1, source_target_pairs={{0,1},{1,2},{2,3},{3,0},{4,5},{5,6},{6,7},{7,4},{8,9},{9,10},{10,1... | collective-permute-start | bytes 491528 | tf_op jit(solution)/shard_map/ppermute | solution.py:108
  63.7 0.5 collective-permute-start.4
  64.2 1.3 %fusion.25 = f32[256,512]{1,0:T(8,128)S(1)} fusion(bf16[256,320]{1,0:T(8,128)(2,1)S(1)} %broadcast_select_fusion, bf16[320,2048]{1,0:T(8,128)(2,1)} %param.14, s32[]{:T(128)S(6)} %select_n.149), kind=kOutput, calls=%fused_computation.50 | convolution fusion | flops 83886080 | bytes 1015812 | tf_op jit(solution)/shard_map/dot_general | solution.py:184
  65.5 2.5 %collective-permute-start.2 = (bf16[256,320]{1,0:T(8,128)(2,1)S(1)}, bf16[256,320]{1,0:T(8,128)(2,1)S(1)}, u32[]{:S(2)}, u32[]{:S(2)}) collective-permute-start(bf16[256,320]{1,0:T(8,128)(2,1)S(1)} %broadcast_select_fusion), channel_id=1, source_target_pairs={{0,2},{1,3},{2,0},{3,1},{4,6},{5,7},{6,4},{7,5},{8,10},{9,11},{10,... | collective-permute-start | bytes 491528 | tf_op jit(solution)/shard_map/ppermute | solution.py:108
  68.0 9.0 %collective-permute-done = bf16[256,320]{1,0:T(8,128)(2,1)S(1)} collective-permute-done((bf16[256,320]{1,0:T(8,128)(2,1)S(1)}, bf16[256,320]{1,0:T(8,128)(2,1)S(1)}, u32[]{:S(2)}, u32[]{:S(2)}) %collective-permute-start) | collective-permute-done | bytes 163872 | tf_op jit(solution)/shard_map/ppermute | solution.py:108
  77.0 1.3 %convolution_add_fusion.1 = f32[256,512]{1,0:T(8,128)S(1)} fusion(f32[256,512]{1,0:T(8,128)S(1)} %fusion.25, bf16[256,320]{1,0:T(8,128)(2,1)S(1)} %collective-permute-done, bf16[320,512]{1,0:T(8,128)(2,1)} %collective-permute-done.1), kind=kOutput, calls=%fused_computation.6 | convolution fusion | flops 84017152 | bytes 1540096 | tf_op jit(solution)/shard_map/dot_general | solution.py:187
  78.3 0.3 fusion.51
  78.6 2.1 %collective-permute-done.2 = bf16[256,320]{1,0:T(8,128)(2,1)S(1)} collective-permute-done((bf16[256,320]{1,0:T(8,128)(2,1)S(1)}, bf16[256,320]{1,0:T(8,128)(2,1)S(1)}, u32[]{:S(2)}, u32[]{:S(2)}) %collective-permute-start.2) | collective-permute-done | bytes 163872 | tf_op jit(solution)/shard_map/ppermute | solution.py:108
  80.8 1.4 %fusion.4 = (f32[256]{0:T(256)S(1)}, bf16[256,512]{1,0:T(8,128)(2,1)S(1)}) fusion(f32[256,512]{1,0:T(8,128)S(1)} %fusion.51, f32[256,512]{1,0:T(8,128)S(1)} %convolution_add_fusion.1, bf16[256,320]{1,0:T(8,128)(2,1)S(1)} %collective-permute-done.2, bf16[320,512]{1,0:T(8,128)(2,1)} %collective-permute-done.3, bf16[256,512]{1,0:T(8,128)(2,1)S(1)} %copy-done.5), kind=kOutput, calls=%fused_computation.28 | convolution fusion | flops 84934400 | bytes 2065408 | tf_op jit(solution)/shard_map/dot_general | solution.py:187
  82.2 3.4 %collective-permute-start.7 = (bf16[256,512]{1,0:T(8,128)(2,1)S(1)}, bf16[256,512]{1,0:T(8,128)(2,1)S(1)}, u32[]{:S(2)}, u32[]{:S(2)}) collective-permute-start(bf16[256,512]{1,0:T(8,128)(2,1)S(1)} %get-tuple-element.46), channel_id=1, source_target_pairs={{0,2},{1,3},{2,0},{3,1},{4,6},{5,7},{6,4},{7,5},{8,10},{9,11},{10,... | collective-permute-start | bytes 786440 | tf_op jit(solution)/shard_map/ppermute | solution.py:108
  85.6 2.0 %collective-permute-start.6 = (bf16[256,512]{1,0:T(8,128)(2,1)S(1)}, bf16[256,512]{1,0:T(8,128)(2,1)S(1)}, u32[]{:S(2)}, u32[]{:S(2)}) collective-permute-start(bf16[256,512]{1,0:T(8,128)(2,1)S(1)} %get-tuple-element.46), channel_id=1, source_target_pairs={{0,1},{1,2},{2,3},{3,0},{4,5},{5,6},{6,7},{7,4},{8,9},{9,10},{10,1... | collective-permute-start | bytes 786440 | tf_op jit(solution)/shard_map/ppermute | solution.py:108
  87.6 0.1 fusion.49
  87.7 14.7 %collective-permute-done.7 = bf16[256,512]{1,0:T(8,128)(2,1)S(1)} collective-permute-done((bf16[256,512]{1,0:T(8,128)(2,1)S(1)}, bf16[256,512]{1,0:T(8,128)(2,1)S(1)}, u32[]{:S(2)}, u32[]{:S(2)}) %collective-permute-start.7) | collective-permute-done | bytes 262176 | tf_op jit(solution)/shard_map/ppermute | solution.py:108
  102.4 0.1 fusion.10
  102.6 5.9 %collective-permute-done.8 = bf16[256,512]{1,0:T(8,128)(2,1)S(1)} collective-permute-done((bf16[256,512]{1,0:T(8,128)(2,1)S(1)}, bf16[256,512]{1,0:T(8,128)(2,1)S(1)}, u32[]{:S(2)}, u32[]{:S(2)}) %collective-permute-start.8) | collective-permute-done | bytes 262176 | tf_op jit(solution)/shard_map/ppermute | solution.py:108
  108.5 0.1 fusion.13
  108.6 0.1 fusion.7
  108.8 0.4 fusion.23
  109.1 0.4 convolution_add_fusion.4
  109.5 0.4 convolution_add_fusion.3
  109.9 1.0 fusion.3
  (38 shorter events, 0.3 us)
Async XLA Ops:
  7.2 101.6 %copy-start = (bf16[2048,320]{0,1:T(8,128)(2,1)S(1)}, bf16[2048,320]{0,1:T(8,128)(2,1)}, u32[]{:S(2)}) copy-start(bf16[2048,320]{0,1:T(8,128)(2,1)} %param.16) | copy-start | bytes 3932164
  7.2 7.6 %copy-start.8 = (s32[1,4]{1,0:T(1,128)S(1)}, s32[1,4]{1,0:T(1,128)}, u32[]{:S(2)}) copy-start(s32[1,4]{1,0:T(1,128)} %param.17) | copy-start | bytes 52
  7.2 16.6 %copy-start.3 = (bf16[256,320]{0,1:T(8,128)(2,1)S(1)}, bf16[256,320]{0,1:T(8,128)(2,1)}, u32[]{:S(2)}) copy-start(bf16[256,320]{0,1:T(8,128)(2,1)} %param.11) | copy-start | bytes 491524
  7.2 40.6 %all-gather.3.cloned.1.call-start = ((), (), s32[]{:S(2)}) async-start(), calls=%async_computation | async-start | bytes 4718592 | tf_op jit(solution)/shard_map/all_gather | solution.py:34
  10.1 55.4 %collective-permute-start.1 = (bf16[320,512]{1,0:T(8,128)(2,1)}, bf16[320,512]{1,0:T(8,128)(2,1)}, u32[]{:S(2)}, u32[]{:S(2)}) collective-permute-start(bf16[320,512]{1,0:T(8,128)(2,1)} %get-tuple-element.7), channel_id=1, source_target_pairs={{0,1},{1,2},{2,3},{3,0},{4,5},{5,6},{6,7},{7,4},{8,9},{9,10},{10,1... | collective-permute-start | bytes 983048 | tf_op jit(solution)/shard_map/ppermute | solution.py:108
  11.7 66.6 %collective-permute-start.5 = (bf16[320,512]{1,0:T(8,128)(2,1)}, bf16[320,512]{1,0:T(8,128)(2,1)S(1)}, u32[]{:S(2)}, u32[]{:S(2)}) collective-permute-start(bf16[320,512]{1,0:T(8,128)(2,1)} %get-tuple-element.8), channel_id=1, source_target_pairs={{0,3},{1,0},{2,1},{3,2},{4,7},{5,4},{6,5},{7,6},{8,11},{9,8},{10,9... | collective-permute-start | bytes 983048 | tf_op jit(solution)/shard_map/ppermute | solution.py:108
  12.2 66.4 %collective-permute-start.3 = (bf16[320,512]{1,0:T(8,128)(2,1)}, bf16[320,512]{1,0:T(8,128)(2,1)}, u32[]{:S(2)}, u32[]{:S(2)}) collective-permute-start(bf16[320,512]{1,0:T(8,128)(2,1)} %get-tuple-element.6), channel_id=1, source_target_pairs={{0,2},{1,3},{2,0},{3,1},{4,6},{5,7},{6,4},{7,5},{8,10},{9,11},{10,... | collective-permute-start | bytes 983048 | tf_op jit(solution)/shard_map/ppermute | solution.py:108
  15.4 8.9 %copy-start.6 = (s32[4]{0:T(128)}, s32[4]{0:T(128)S(1)}, u32[]{:S(2)}) copy-start(s32[4]{0:T(128)S(1)} %get-tuple-element.4.first_ref) | copy-start | bytes 52
  24.6 1.6 %copy-start.9 = (s32[1,4]{1,0:T(1,128)S(1)}, s32[1,4]{1,0:T(1,128)}, u32[]{:S(2)}) copy-start(s32[1,4]{1,0:T(1,128)} %param.18) | copy-start | bytes 52
  24.6 1.6 %copy-start.1 = (s32[4]{0:T(128)S(1)}, s32[4]{0:T(128)}, u32[]{:S(2)}) copy-start(s32[4]{0:T(128)} %param.19) | copy-start | bytes 52
  24.6 5.4 %copy-start.4 = (bf16[256,1,256]{2,0,1:T(8,128)(2,1)S(1)}, bf16[256,1,256]{2,0,1:T(8,128)(2,1)}, u32[]{:S(2)}) copy-start(bf16[256,1,256]{2,0,1:T(8,128)(2,1)} %param.12) | copy-start | bytes 393220
  62.2 14.9 %collective-permute-start = (bf16[256,320]{1,0:T(8,128)(2,1)S(1)}, bf16[256,320]{1,0:T(8,128)(2,1)S(1)}, u32[]{:S(2)}, u32[]{:S(2)}) collective-permute-start(bf16[256,320]{1,0:T(8,128)(2,1)S(1)} %broadcast_select_fusion), channel_id=1, source_target_pairs={{0,1},{1,2},{2,3},{3,0},{4,5},{5,6},{6,7},{7,4},{8,9},{9,10},{10,1... | collective-permute-start | bytes 491528 | tf_op jit(solution)/shard_map/ppermute | solution.py:108
  63.7 14.6 %collective-permute-start.4 = (bf16[256,320]{1,0:T(8,128)(2,1)S(1)}, bf16[256,320]{1,0:T(8,128)(2,1)S(1)}, u32[]{:S(2)}, u32[]{:S(2)}) collective-permute-start(bf16[256,320]{1,0:T(8,128)(2,1)S(1)} %broadcast_select_fusion), channel_id=1, source_target_pairs={{0,3},{1,0},{2,1},{3,2},{4,7},{5,4},{6,5},{7,6},{8,11},{9,8},{10,9... | collective-permute-start | bytes 491528 | tf_op jit(solution)/shard_map/ppermute | solution.py:108
  65.5 15.3 %copy-start.5 = (bf16[256,512]{1,0:T(8,128)(2,1)S(1)}, bf16[256,512]{1,0:T(8,128)(2,1)}, u32[]{:S(2)}) copy-start(bf16[256,512]{1,0:T(8,128)(2,1)} %param.10) | copy-start | bytes 786436
  65.5 15.2 %collective-permute-start.2 = (bf16[256,320]{1,0:T(8,128)(2,1)S(1)}, bf16[256,320]{1,0:T(8,128)(2,1)S(1)}, u32[]{:S(2)}, u32[]{:S(2)}) collective-permute-start(bf16[256,320]{1,0:T(8,128)(2,1)S(1)} %broadcast_select_fusion), channel_id=1, source_target_pairs={{0,2},{1,3},{2,0},{3,1},{4,6},{5,7},{6,4},{7,5},{8,10},{9,11},{10,... | collective-permute-start | bytes 491528 | tf_op jit(solution)/shard_map/ppermute | solution.py:108
  78.6 9.0 %copy-start.7 = (bf16[2048]{0:T(1024)(128)(2,1)S(1)}, bf16[2048]{0:T(1024)(128)(2,1)}, u32[]{:S(2)}) copy-start(bf16[2048]{0:T(1024)(128)(2,1)} %param.15) | copy-start | bytes 12292
  82.2 27.4 %copy-start.2 = (bf16[256,512]{1,0:T(8,128)(2,1)}, bf16[256,512]{1,0:T(8,128)(2,1)S(1)}, u32[]{:S(2)}) copy-start(bf16[256,512]{1,0:T(8,128)(2,1)S(1)} %get-tuple-element.46) | copy-start | bytes 786436
  82.2 20.3 %collective-permute-start.7 = (bf16[256,512]{1,0:T(8,128)(2,1)S(1)}, bf16[256,512]{1,0:T(8,128)(2,1)S(1)}, u32[]{:S(2)}, u32[]{:S(2)}) collective-permute-start(bf16[256,512]{1,0:T(8,128)(2,1)S(1)} %get-tuple-element.46), channel_id=1, source_target_pairs={{0,2},{1,3},{2,0},{3,1},{4,6},{5,7},{6,4},{7,5},{8,10},{9,11},{10,... | collective-permute-start | bytes 786440 | tf_op jit(solution)/shard_map/ppermute | solution.py:108
  85.6 22.9 %collective-permute-start.8 = (bf16[256,512]{1,0:T(8,128)(2,1)S(1)}, bf16[256,512]{1,0:T(8,128)(2,1)S(1)}, u32[]{:S(2)}, u32[]{:S(2)}) collective-permute-start(bf16[256,512]{1,0:T(8,128)(2,1)S(1)} %get-tuple-element.46), channel_id=1, source_target_pairs={{0,3},{1,0},{2,1},{3,2},{4,7},{5,4},{6,5},{7,6},{8,11},{9,8},{10,9... | collective-permute-start | bytes 786440 | tf_op jit(solution)/shard_map/ppermute | solution.py:108
  85.6 23.0 %collective-permute-start.6 = (bf16[256,512]{1,0:T(8,128)(2,1)S(1)}, bf16[256,512]{1,0:T(8,128)(2,1)S(1)}, u32[]{:S(2)}, u32[]{:S(2)}) collective-permute-start(bf16[256,512]{1,0:T(8,128)(2,1)S(1)} %get-tuple-element.46), channel_id=1, source_target_pairs={{0,1},{1,2},{2,3},{3,0},{4,5},{5,6},{6,7},{7,4},{8,9},{9,10},{10,1... | collective-permute-start | bytes 786440 | tf_op jit(solution)/shard_map/ppermute | solution.py:108
Sparse Core Ops, SparseCore 0:
  9.9 37.8 all-gather.2

commit v11 on v9

--- a/solution.py
+++ b/solution.py
@@ -43,15 +43,18 @@
     first = first_ref[request]
     start = start_ref[request]
     spread = query_ref[...]
-    prefix_rows = prefix_ref[...]
-    suffix_rows = suffix_ref[...]
+    pair_lanes = 2 * HD
+    prefix_keys = prefix_ref[:, :pair_lanes]
+    prefix_values = prefix_ref[:, pair_lanes:]
+    suffix_keys = suffix_ref[:, :pair_lanes]
+    suffix_values = suffix_ref[:, pair_lanes:]
     contract = (((1,), (1,)), ((), ()))
     score_scale = HD ** (-0.5)
     prefix_scores = lax.dot_general(
-        spread, prefix_rows, contract, preferred_element_type=jnp.float32
+        spread, prefix_keys, contract, preferred_element_type=jnp.float32
     ) * score_scale
     suffix_scores = lax.dot_general(
-        spread, suffix_rows, contract, preferred_element_type=jnp.float32
+        spread, suffix_keys, contract, preferred_element_type=jnp.float32
     ) * score_scale
     key_position = first + lax.broadcasted_iota(jnp.int32, suffix_scores.shape, 1)
     query_position = first + row_ref[...]
@@ -67,24 +70,27 @@
         suffix_weights, axis=1, keepdims=True
     )
     accumulated = jnp.dot(
-        prefix_weights.astype(jnp.bfloat16), prefix_rows, preferred_element_type=jnp.float32
-    ) + jnp.dot(suffix_weights.astype(jnp.bfloat16), suffix_rows, preferred_element_type=jnp.float32)
+        prefix_weights.astype(jnp.bfloat16), prefix_values, preferred_element_type=jnp.float32
+    ) + jnp.dot(
+        suffix_weights.astype(jnp.bfloat16), suffix_values, preferred_element_type=jnp.float32
+    )
     attended = accumulated / denominator
-    first_pair = attended[:, HD:2 * HD]
-    second_pair = attended[:, 3 * HD:]
+    first_pair = attended[:, :HD]
+    second_pair = attended[:, HD:]
     out_ref[...] = jnp.where(pair_ref[...] > 0, second_pair, first_pair).astype(out_ref.dtype)
 
 
 def window_attention(
     slot_index, firsts, starts, spread, slots, suffix_windows, query_rows, row_pairs, slot_rows
 ):
-    requests, flat_rows, lanes = spread.shape
+    requests, flat_rows, query_lanes = spread.shape
     window = suffix_windows.shape[1]
+    lanes = slots.shape[1]
     grid_spec = pltpu.PrefetchScalarGridSpec(
         num_scalar_prefetch=3,
         grid=(requests,),
         in_specs=[
-            pl.BlockSpec((None, flat_rows, lanes), lambda k, slot, first, start: (k, 0, 0)),
+            pl.BlockSpec((None, flat_rows, query_lanes), lambda k, slot, first, start: (k, 0, 0)),
             pl.BlockSpec((slot_rows, lanes), lambda k, slot, first, start: (slot[k], 0)),
             pl.BlockSpec((None, window, lanes), lambda k, slot, first, start: (k, 0, 0)),
             pl.BlockSpec((flat_rows, 1), lambda k, slot, first, start: (0, 0)),
@@ -142,12 +148,15 @@
     row_start = jnp.sum(jnp.where(member, req_starts[None, :], 0), axis=1)
     row_tenant = jnp.sum(jnp.where(member, req_tenant[None, :], 0), axis=1)
     score_scale = HD ** (-0.5)
-    own_slot = prefix_cache.reshape(prefix_cache.shape[0], -1)
+    own_slot = jnp.transpose(
+        prefix_cache.reshape(prefix_cache.shape[0], 2, 2, HD), (0, 2, 1, 3)
+    ).reshape(prefix_cache.shape[0], -1)
     slots, slot_of_tenant = tenant_slots(own_slot, owners, n_req)
-    suffix_rows = suffix_kv.reshape(row_count, -1)
+    suffix_rows = jnp.transpose(suffix_kv.reshape(row_count, 2, 2, HD), (0, 2, 1, 3)).reshape(
+        row_count, -1
+    )
     window = min(MOSTLEN, row_count)
     firsts = jnp.minimum(req_starts, row_count - window).astype(jnp.int32)
-    zeros = jnp.zeros((head_count, window, HD), queries.dtype)
     head_select = jnp.transpose(select)[:, :, None, None]
     spreads = []
     suffix_windows = []
@@ -155,10 +164,9 @@
         window_queries = lax.dynamic_slice_in_dim(queries, firsts[request], window, 0)
         window_queries = jnp.transpose(window_queries.reshape(window, head_count, HD), (1, 0, 2))
         spread = jnp.concatenate(
-            [window_queries * head_select[0], zeros, window_queries * head_select[1], zeros],
-            axis=2,
+            [window_queries * head_select[0], window_queries * head_select[1]], axis=2
         )
-        spreads.append(spread.reshape(head_count * window, 4 * HD))
+        spreads.append(spread.reshape(head_count * window, 2 * HD))
         suffix_windows.append(lax.dynamic_slice_in_dim(suffix_rows, firsts[request], window, 0))
     query_rows = (jnp.arange(head_count * window, dtype=jnp.int32) % window)[:, None]
     row_pairs = jnp.repeat(pair_ids.astype(jnp.int32), window)[:, None]

time: 117 us -> 116 us (level)
  waiting for transfers between devices: 45.7 us -> 39.2 us
  local copies, waits for them, and re-layouts: 10.1 us -> 14.8 us
  other arithmetic: 4.42 us -> 6.66 us
  Pallas kernels: 12.1 us -> 10.5 us
    all_gather x1, waiting for transfers between devices: 17.3 us -> 10.9 us  [tenant_slots(): return (lax.all_gather(own_slot, 'req', axis=0, tiled=True), owners)]
    unnamed x23 -> x27, local copies, waits for them, and re-layouts: 1.07 us -> 3.81 us
    dynamic_slice x0 -> x5, local copies, waits for them, and re-layouts: none -> 2.05 us  [local(): lax.dynamic_slice_in_dim(suffix_rows, firsts[request], window, 0)]
    pallas_call x1, Pallas kernels: 12.1 us -> 10.5 us  [window_attention(): pl.pallas_call(attention_kernel, grid_spec=grid_spec, out_shape=jax.Shape...]
    dynamic_slice x1, local copies, waits for them, and re-layouts: 2.19 us -> 0.99 us  [local(): piece = lax.dynamic_slice_in_dim(out_weight, target * width, width, 1)]
  transfers between devices with their start and end apart: 10 -> 10, of which waited for: 5 -> 4; matrix products, arithmetic and copies ran while one was open for 16% -> 19% of each run, Pallas kernels for 11% -> 9%
where the time goes in v11:
time: 116 us; the launch traced here: 114 us
  waiting for transfers between devices  39.2 us (34%)
  between operations  22 us (19%)
  local copies, waits for them, and re-layouts  14.8 us (13%)
  starting transfers between devices  14.6 us (13%)
  Pallas kernels  10.5 us (9%)
  other arithmetic  6.66 us (6%)
  matrix products  6.41 us (6%)
    ppermute x9, waiting for transfers between devices, shifted(): return lax.ppermute(block, 'tp', pairs)  28.3 us
    ppermute x9, starting transfers between devices, shifted(): return lax.ppermute(block, 'tp', pairs)  14.6 us
    all_gather x1, waiting for transfers between devices, tenant_slots(): return (lax.all_gather(own_slot, 'req', axis=0, tiled=True), owners)  10.9 us
    pallas_call x1, Pallas kernels, window_attention(): pl.pallas_call(attention_kernel, grid_spec=grid_spec, out_shape=jax.Shape...  10.5 us
    dot_general x3, matrix products, local(): jnp.dot(head_block, weight_pieces[shift], preferred_element_type=jnp.floa...  4 us
    unnamed x27, local copies, waits for them, and re-layouts  3.81 us
  transfers between devices with their start and end apart: 10, of which 4 were waited for; matrix products, arithmetic and copies ran while one was open for 19% of the time, Pallas kernels for 9%

profile of v11, /device:TPU:8, one launch (start us, length us, event | category | flops | bytes accessed | tf_op | source)
XLA Modules:
  0.0 114.2 jit_solution(1904275560365864157)
XLA Ops:
  7.2 1.3 %copy.36 = bf16[1024,1,256]{0,2,1:T(8,128)(2,1)S(1)} copy(bf16[1024,1,256]{2,0,1:T(8,128)(2,1)} %param.13) | data formatting | bytes 1048576 | tf_op args[3]
  8.6 1.0 copy.38
  9.7 0.4 copy-done.2
  10.1 1.0 constant_dynamic-slice_fusion.1
  11.1 1.6 %collective-permute-start.1 = (bf16[320,512]{1,0:T(8,128)(2,1)}, bf16[320,512]{1,0:T(8,128)(2,1)}, u32[]{:S(2)}, u32[]{:S(2)}) collective-permute-start(bf16[320,512]{1,0:T(8,128)(2,1)} %get-tuple-element.5), channel_id=1, source_target_pairs={{0,1},{1,2},{2,3},{3,0},{4,5},{5,6},{6,7},{7,4},{8,9},{9,10},{10,1... | collective-permute-start | bytes 983048 | tf_op jit(solution)/shard_map/ppermute | solution.py:110
  12.7 0.4 collective-permute-start.5
  13.1 2.6 %collective-permute-start.3 = (bf16[320,512]{1,0:T(8,128)(2,1)}, bf16[320,512]{1,0:T(8,128)(2,1)}, u32[]{:S(2)}, u32[]{:S(2)}) collective-permute-start(bf16[320,512]{1,0:T(8,128)(2,1)} %get-tuple-element.4), channel_id=1, source_target_pairs={{0,2},{1,3},{2,0},{3,1},{4,6},{5,7},{6,4},{7,5},{8,10},{9,11},{10,... | collective-permute-start | bytes 983048 | tf_op jit(solution)/shard_map/ppermute | solution.py:110
  15.9 0.5 broadcast_minimum_fusion
  16.4 0.6 fusion.47
  24.6 0.2 constant_dynamic-slice_fusion.10
  24.8 0.8 multiply_bitcast_fusion.1
  25.8 0.2 copy.33
  25.9 0.9 pad_maximum_fusion.4
  27.2 1.0 copy.39
  28.2 0.8 constant_dynamic-slice_fusion.6
  29.4 0.9 copy.44
  30.4 0.9 copy.51
  31.4 0.6 broadcast_compare_fusion.3
  32.0 0.6 dynamic-slice.7
  32.6 0.7 fusion.43
  33.3 1.1 %gather_fusion = s32[4]{0:T(128)} fusion(s32[4]{0:T(128)S(1)} %copy-done.1, s32[1024]{0:T(1024)S(1)} %pad_clamp_fusion), kind=kCustom, calls=%fused_computation | custom fusion | bytes 48 | tf_op jit(solution)/shard_map/gather | solution.py:173
  34.5 0.7 pad_maximum_fusion.1.suffix_ref
  35.2 0.8 add_select_fusion.row_ref
  36.0 0.9 pad_maximum_fusion.query_ref
  36.9 10.9 %all-gather.2.cloned.1.call-done.prefix_ref = bf16[8192,256]{1,0:T(8,128)(2,1)} async-done(((bf16[1024,256]{1,0:T(8,128)(2,1)}), bf16[8192,256]{1,0:T(8,128)(2,1)}) %all-gather.2.cloned.1.call-update) | async-done | bytes 4194320 | tf_op jit(solution)/shard_map/all_gather | solution.py:34
  47.8 10.5 %shard_map.113 = bf16[4,640,64]{2,1,0:T(8,128)(2,1)} custom-call(s32[4]{0:T(128)} %gather_fusion, s32[4]{0:T(128)} %copy-done.6, s32[4]{0:T(128)} %get-tuple-element.3.start_ref, bf16[4,640,128]{2,1,0:T(8,128)(2,1)} %pad_maximum_fusion.query_ref, bf16[8192,256]{1,0:T(8,128)(2,1)} %all-gather.2.cloned.1.call-done.prefix_ref, ...), custom_call_target="tpu_custom_call" | custom-call | tf_op jit(solution)/shard_map/pallas_call | solution.py:101
  58.4 1.2 %fusion.45 = (bf16[1,640,64]{2,1,0:T(8,128)(2,1)S(1)}, bf16[1,640,64]{2,1,0:T(8,128)(2,1)S(1)}, bf16[1,640,64]{2,1,0:T(8,128)(2,1)S(1)}, bf16[1,640,64]{2,1,0:T(8,128)(2,1)S(1)}) fusion(bf16[4,640,64]{2,1,0:T(8,128)(2,1)} %shard_map.113), kind=kLoop, calls=%fused_computation.104 | loop fusion | bytes 655360 | tf_op jit(solution)/shard_map/slice | solution.py:187
  60.2 0.4 select_n.137
  60.6 0.3 dynamic_update_slice.11
  60.9 0.7 dynamic_update_slice.12
  61.7 0.3 dynamic_update_slice.10
  62.0 1.5 %collective-permute-start = (bf16[256,320]{0,1:T(8,128)(2,1)S(1)}, bf16[256,320]{0,1:T(8,128)(2,1)S(1)}, u32[]{:S(2)}, u32[]{:S(2)}) collective-permute-start(bf16[256,320]{0,1:T(8,128)(2,1)S(1)} %select_select_fusion), channel_id=1, source_target_pairs={{0,1},{1,2},{2,3},{3,0},{4,5},{5,6},{6,7},{7,4},{8,9},{9,10},{10,1... | collective-permute-start | bytes 491528 | tf_op jit(solution)/shard_map/ppermute | solution.py:110
  63.6 0.5 collective-permute-start.4
  64.1 0.3 fusion.21
  64.5 2.5 %collective-permute-start.2 = (bf16[256,320]{0,1:T(8,128)(2,1)S(1)}, bf16[256,320]{0,1:T(8,128)(2,1)S(1)}, u32[]{:S(2)}, u32[]{:S(2)}) collective-permute-start(bf16[256,320]{0,1:T(8,128)(2,1)S(1)} %select_select_fusion), channel_id=1, source_target_pairs={{0,2},{1,3},{2,0},{3,1},{4,6},{5,7},{6,4},{7,5},{8,10},{9,11},{10,... | collective-permute-start | bytes 491528 | tf_op jit(solution)/shard_map/ppermute | solution.py:110
  66.9 7.9 %collective-permute-done = bf16[256,320]{0,1:T(8,128)(2,1)S(1)} collective-permute-done((bf16[256,320]{0,1:T(8,128)(2,1)S(1)}, bf16[256,320]{0,1:T(8,128)(2,1)S(1)}, u32[]{:S(2)}, u32[]{:S(2)}) %collective-permute-start) | collective-permute-done | bytes 163872 | tf_op jit(solution)/shard_map/ppermute | solution.py:110
  74.9 1.3 %convolution_add_fusion.1 = f32[256,512]{1,0:T(8,128)S(1)} fusion(f32[256,512]{1,0:T(8,128)S(1)} %fusion.21, bf16[256,320]{0,1:T(8,128)(2,1)S(1)} %collective-permute-done, bf16[320,512]{1,0:T(8,128)(2,1)} %collective-permute-done.1), kind=kOutput, calls=%fused_computation.4 | convolution fusion | flops 84017152 | bytes 1540096 | tf_op jit(solution)/shard_map/dot_general | solution.py:196
  76.2 1.3 %fusion.48 = f32[256,512]{1,0:T(8,128)S(1)} fusion(bf16[256,320]{0,1:T(8,128)(2,1)S(1)} %collective-permute-done.4, bf16[320,512]{1,0:T(8,128)(2,1)} %collective-permute-done.5), kind=kOutput, calls=%fused_computation.107 | convolution fusion | flops 83886080 | bytes 1015808 | tf_op jit(solution)/shard_map/dot_general | solution.py:196
  77.5 1.4 %fusion.4 = (f32[256]{0:T(256)S(1)}, bf16[256,512]{1,0:T(8,128)(2,1)S(1)}) fusion(f32[256,512]{1,0:T(8,128)S(1)} %fusion.48, f32[256,512]{1,0:T(8,128)S(1)} %convolution_add_fusion.1, bf16[256,320]{0,1:T(8,128)(2,1)S(1)} %collective-permute-done.2, bf16[320,512]{1,0:T(8,128)(2,1)} %collective-permute-done.3, bf16[256,512]{1,0:T(8,128)(2,1)S(1)} %copy-done.5), kind=kOutput, calls=%fused_computation.19 | convolution fusion | flops 84934400 | bytes 2065408 | tf_op jit(solution)/shard_map/dot_general | solution.py:196
  79.0 3.4 %collective-permute-start.7 = (bf16[256,512]{1,0:T(8,128)(2,1)S(1)}, bf16[256,512]{1,0:T(8,128)(2,1)S(1)}, u32[]{:S(2)}, u32[]{:S(2)}) collective-permute-start(bf16[256,512]{1,0:T(8,128)(2,1)S(1)} %get-tuple-element.48), channel_id=1, source_target_pairs={{0,2},{1,3},{2,0},{3,1},{4,6},{5,7},{6,4},{7,5},{8,10},{9,11},{10,... | collective-permute-start | bytes 786440 | tf_op jit(solution)/shard_map/ppermute | solution.py:110
  82.3 0.6 collective-permute-start.8
  83.0 1.4 %collective-permute-start.6 = (bf16[256,512]{1,0:T(8,128)(2,1)S(1)}, bf16[256,512]{1,0:T(8,128)(2,1)S(1)}, u32[]{:S(2)}, u32[]{:S(2)}) collective-permute-start(bf16[256,512]{1,0:T(8,128)(2,1)S(1)} %get-tuple-element.48), channel_id=1, source_target_pairs={{0,1},{1,2},{2,3},{3,0},{4,5},{5,6},{6,7},{7,4},{8,9},{9,10},{10,1... | collective-permute-start | bytes 786440 | tf_op jit(solution)/shard_map/ppermute | solution.py:110
  84.5 14.8 %collective-permute-done.7 = bf16[256,512]{1,0:T(8,128)(2,1)S(1)} collective-permute-done((bf16[256,512]{1,0:T(8,128)(2,1)S(1)}, bf16[256,512]{1,0:T(8,128)(2,1)S(1)}, u32[]{:S(2)}, u32[]{:S(2)}) %collective-permute-start.7) | collective-permute-done | bytes 262176 | tf_op jit(solution)/shard_map/ppermute | solution.py:110
  99.3 5.5 %collective-permute-done.8 = bf16[256,512]{1,0:T(8,128)(2,1)S(1)} collective-permute-done((bf16[256,512]{1,0:T(8,128)(2,1)S(1)}, bf16[256,512]{1,0:T(8,128)(2,1)S(1)}, u32[]{:S(2)}, u32[]{:S(2)}) %collective-permute-start.8) | collective-permute-done | bytes 262176 | tf_op jit(solution)/shard_map/ppermute | solution.py:110
  105.2 0.4 fusion.19
  105.5 0.4 convolution_add_fusion.4
  105.9 0.4 convolution_add_fusion.3
  106.3 1.0 fusion.3
  (61 shorter events, 2.6 us)
Async XLA Ops:
  7.2 98.0 %copy-start = (bf16[2048,320]{0,1:T(8,128)(2,1)S(1)}, bf16[2048,320]{0,1:T(8,128)(2,1)}, u32[]{:S(2)}) copy-start(bf16[2048,320]{0,1:T(8,128)(2,1)} %param.16) | copy-start | bytes 3932164
  7.2 40.6 %all-gather.2.cloned.1.call-start = ((), (), s32[]{:S(2)}) async-start(), calls=%async_computation | async-start | bytes 4718592 | tf_op jit(solution)/shard_map/all_gather | solution.py:34
  8.6 1.5 %copy-start.2 = (bf16[320,2048]{1,0:T(8,128)(2,1)S(1)}, bf16[320,2048]{1,0:T(8,128)(2,1)}, u32[]{:S(2)}) copy-start(bf16[320,2048]{1,0:T(8,128)(2,1)} %param.14) | copy-start | bytes 3932164
  9.6 6.1 %copy-start.10 = (s32[1,4]{1,0:T(1,128)S(1)}, s32[1,4]{1,0:T(1,128)}, u32[]{:S(2)}) copy-start(s32[1,4]{1,0:T(1,128)} %param.17) | copy-start | bytes 52
  9.6 14.9 %copy-start.4 = (bf16[256,320]{0,1:T(8,128)(2,1)S(1)}, bf16[256,320]{0,1:T(8,128)(2,1)}, u32[]{:S(2)}) copy-start(bf16[256,320]{0,1:T(8,128)(2,1)} %param.11) | copy-start | bytes 491524
  11.1 53.3 %collective-permute-start.1 = (bf16[320,512]{1,0:T(8,128)(2,1)}, bf16[320,512]{1,0:T(8,128)(2,1)}, u32[]{:S(2)}, u32[]{:S(2)}) collective-permute-start(bf16[320,512]{1,0:T(8,128)(2,1)} %get-tuple-element.5), channel_id=1, source_target_pairs={{0,1},{1,2},{2,3},{3,0},{4,5},{5,6},{6,7},{7,4},{8,9},{9,10},{10,1... | collective-permute-start | bytes 983048 | tf_op jit(solution)/shard_map/ppermute | solution.py:110
  12.7 63.5 %collective-permute-start.5 = (bf16[320,512]{1,0:T(8,128)(2,1)}, bf16[320,512]{1,0:T(8,128)(2,1)}, u32[]{:S(2)}, u32[]{:S(2)}) collective-permute-start(bf16[320,512]{1,0:T(8,128)(2,1)} %get-tuple-element.6), channel_id=1, source_target_pairs={{0,3},{1,0},{2,1},{3,2},{4,7},{5,4},{6,5},{7,6},{8,11},{9,8},{10,9... | collective-permute-start | bytes 983048 | tf_op jit(solution)/shard_map/ppermute | solution.py:110
  13.1 64.4 %collective-permute-start.3 = (bf16[320,512]{1,0:T(8,128)(2,1)}, bf16[320,512]{1,0:T(8,128)(2,1)}, u32[]{:S(2)}, u32[]{:S(2)}) collective-permute-start(bf16[320,512]{1,0:T(8,128)(2,1)} %get-tuple-element.4), channel_id=1, source_target_pairs={{0,2},{1,3},{2,0},{3,1},{4,6},{5,7},{6,4},{7,5},{8,10},{9,11},{10,... | collective-permute-start | bytes 983048 | tf_op jit(solution)/shard_map/ppermute | solution.py:110
  16.4 9.3 %copy-start.6 = (s32[4]{0:T(128)}, s32[4]{0:T(128)S(1)}, u32[]{:S(2)}) copy-start(s32[4]{0:T(128)S(1)} %get-tuple-element.2.first_ref) | copy-start | bytes 52
  26.9 6.5 %copy-start.1 = (s32[4]{0:T(128)S(1)}, s32[4]{0:T(128)}, u32[]{:S(2)}) copy-start(s32[4]{0:T(128)} %param.19) | copy-start | bytes 52
  58.4 1.8 %copy-start.9 = (pred[128]{0:T(512)(128)(4,1)S(1)}, pred[128]{0:T(512)(128)(4,1)}, u32[]{:S(2)}) copy-start(pred[128]{0:T(512)(128)(4,1)} %dynamic-slice.7) | copy-start | bytes 388
  59.6 2.4 %copy-start.8 = (pred[256]{0:T(512)(128)(4,1)S(1)}, pred[256]{0:T(512)(128)(4,1)}, u32[]{:S(2)}) copy-start(pred[256]{0:T(512)(128)(4,1)} %get-tuple-element.40) | copy-start | bytes 772
  62.0 12.8 %collective-permute-start = (bf16[256,320]{0,1:T(8,128)(2,1)S(1)}, bf16[256,320]{0,1:T(8,128)(2,1)S(1)}, u32[]{:S(2)}, u32[]{:S(2)}) collective-permute-start(bf16[256,320]{0,1:T(8,128)(2,1)S(1)} %select_select_fusion), channel_id=1, source_target_pairs={{0,1},{1,2},{2,3},{3,0},{4,5},{5,6},{6,7},{7,4},{8,9},{9,10},{10,1... | collective-permute-start | bytes 491528 | tf_op jit(solution)/shard_map/ppermute | solution.py:110
  63.6 12.6 %collective-permute-start.4 = (bf16[256,320]{0,1:T(8,128)(2,1)S(1)}, bf16[256,320]{0,1:T(8,128)(2,1)S(1)}, u32[]{:S(2)}, u32[]{:S(2)}) collective-permute-start(bf16[256,320]{0,1:T(8,128)(2,1)S(1)} %select_select_fusion), channel_id=1, source_target_pairs={{0,3},{1,0},{2,1},{3,2},{4,7},{5,4},{6,5},{7,6},{8,11},{9,8},{10,9... | collective-permute-start | bytes 491528 | tf_op jit(solution)/shard_map/ppermute | solution.py:110
  64.4 13.1 %copy-start.5 = (bf16[256,512]{1,0:T(8,128)(2,1)S(1)}, bf16[256,512]{1,0:T(8,128)(2,1)}, u32[]{:S(2)}) copy-start(bf16[256,512]{1,0:T(8,128)(2,1)} %param.10) | copy-start | bytes 786436
  64.5 13.1 %collective-permute-start.2 = (bf16[256,320]{0,1:T(8,128)(2,1)S(1)}, bf16[256,320]{0,1:T(8,128)(2,1)S(1)}, u32[]{:S(2)}, u32[]{:S(2)}) collective-permute-start(bf16[256,320]{0,1:T(8,128)(2,1)S(1)} %select_select_fusion), channel_id=1, source_target_pairs={{0,2},{1,3},{2,0},{3,1},{4,6},{5,7},{6,4},{7,5},{8,10},{9,11},{10,... | collective-permute-start | bytes 491528 | tf_op jit(solution)/shard_map/ppermute | solution.py:110
  77.5 6.9 %copy-start.7 = (bf16[2048]{0:T(1024)(128)(2,1)S(1)}, bf16[2048]{0:T(1024)(128)(2,1)}, u32[]{:S(2)}) copy-start(bf16[2048]{0:T(1024)(128)(2,1)} %param.15) | copy-start | bytes 12292
  79.0 27.0 %copy-start.3 = (bf16[256,512]{1,0:T(8,128)(2,1)}, bf16[256,512]{1,0:T(8,128)(2,1)S(1)}, u32[]{:S(2)}) copy-start(bf16[256,512]{1,0:T(8,128)(2,1)S(1)} %get-tuple-element.48) | copy-start | bytes 786436
  79.0 20.2 %collective-permute-start.7 = (bf16[256,512]{1,0:T(8,128)(2,1)S(1)}, bf16[256,512]{1,0:T(8,128)(2,1)S(1)}, u32[]{:S(2)}, u32[]{:S(2)}) collective-permute-start(bf16[256,512]{1,0:T(8,128)(2,1)S(1)} %get-tuple-element.48), channel_id=1, source_target_pairs={{0,2},{1,3},{2,0},{3,1},{4,6},{5,7},{6,4},{7,5},{8,10},{9,11},{10,... | collective-permute-start | bytes 786440 | tf_op jit(solution)/shard_map/ppermute | solution.py:110
  82.3 22.5 %collective-permute-start.8 = (bf16[256,512]{1,0:T(8,128)(2,1)S(1)}, bf16[256,512]{1,0:T(8,128)(2,1)S(1)}, u32[]{:S(2)}, u32[]{:S(2)}) collective-permute-start(bf16[256,512]{1,0:T(8,128)(2,1)S(1)} %get-tuple-element.48), channel_id=1, source_target_pairs={{0,3},{1,0},{2,1},{3,2},{4,7},{5,4},{6,5},{7,6},{8,11},{9,8},{10,9... | collective-permute-start | bytes 786440 | tf_op jit(solution)/shard_map/ppermute | solution.py:110
  83.0 22.0 %collective-permute-start.6 = (bf16[256,512]{1,0:T(8,128)(2,1)S(1)}, bf16[256,512]{1,0:T(8,128)(2,1)S(1)}, u32[]{:S(2)}, u32[]{:S(2)}) collective-permute-start(bf16[256,512]{1,0:T(8,128)(2,1)S(1)} %get-tuple-element.48), channel_id=1, source_target_pairs={{0,1},{1,2},{2,3},{3,0},{4,5},{5,6},{6,7},{7,4},{8,9},{9,10},{10,1... | collective-permute-start | bytes 786440 | tf_op jit(solution)/shard_map/ppermute | solution.py:110
Sparse Core Ops, SparseCore 0:
  9.9 37.8 all-gather.1

commit v12 on v11

--- a/solution.py
+++ b/solution.py
@@ -37,10 +37,10 @@
 
 
 def attention_kernel(
-    slot_ref, first_ref, start_ref, query_ref, prefix_ref, suffix_ref, row_ref, pair_ref, out_ref
+    slot_ref, first_ref, start_ref, end_ref, query_ref, prefix_ref, suffix_ref, row_ref, pair_ref, out_ref
 ):
     request = pl.program_id(0)
-    first = first_ref[request]
+    first = pl.multiple_of(first_ref[request], 8)
     start = start_ref[request]
     spread = query_ref[...]
     pair_lanes = 2 * HD
@@ -77,32 +77,45 @@
     attended = accumulated / denominator
     first_pair = attended[:, :HD]
     second_pair = attended[:, HD:]
-    out_ref[...] = jnp.where(pair_ref[...] > 0, second_pair, first_pair).astype(out_ref.dtype)
+    picked = jnp.where(pair_ref[...] > 0, second_pair, first_pair)
+    picked = picked.astype(jnp.bfloat16).astype(out_ref.dtype)
+    window = suffix_ref.shape[0]
+    row_position = first + lax.broadcasted_iota(jnp.int32, (window, HD), 0)
+    mine = (row_position >= start) & (row_position < end_ref[request])
+    for head in range(out_ref.shape[1] // HD):
+        lanes = slice(head * HD, (head + 1) * HD)
+        kept = out_ref[pl.ds(first, window), lanes]
+        out_ref[pl.ds(first, window), lanes] = jnp.where(
+            mine, picked[head * window:(head + 1) * window], kept
+        )
 
 
 def window_attention(
-    slot_index, firsts, starts, spread, slots, suffix_windows, query_rows, row_pairs, slot_rows
+    slot_index, firsts, starts, ends, spread, slots, suffix_windows, query_rows, row_pairs, slot_rows, row_count
 ):
     requests, flat_rows, query_lanes = spread.shape
     window = suffix_windows.shape[1]
     lanes = slots.shape[1]
+    head_count = flat_rows // window
     grid_spec = pltpu.PrefetchScalarGridSpec(
-        num_scalar_prefetch=3,
+        num_scalar_prefetch=4,
         grid=(requests,),
         in_specs=[
-            pl.BlockSpec((None, flat_rows, query_lanes), lambda k, slot, first, start: (k, 0, 0)),
-            pl.BlockSpec((slot_rows, lanes), lambda k, slot, first, start: (slot[k], 0)),
-            pl.BlockSpec((None, window, lanes), lambda k, slot, first, start: (k, 0, 0)),
-            pl.BlockSpec((flat_rows, 1), lambda k, slot, first, start: (0, 0)),
-            pl.BlockSpec((flat_rows, 1), lambda k, slot, first, start: (0, 0)),
+            pl.BlockSpec((None, flat_rows, query_lanes), lambda k, slot, first, start, end: (k, 0, 0)),
+            pl.BlockSpec((slot_rows, lanes), lambda k, slot, first, start, end: (slot[k], 0)),
+            pl.BlockSpec((None, window, lanes), lambda k, slot, first, start, end: (k, 0, 0)),
+            pl.BlockSpec((flat_rows, 1), lambda k, slot, first, start, end: (0, 0)),
+            pl.BlockSpec((flat_rows, 1), lambda k, slot, first, start, end: (0, 0)),
         ],
-        out_specs=pl.BlockSpec((None, flat_rows, HD), lambda k, slot, first, start: (k, 0, 0)),
+        out_specs=pl.BlockSpec(
+            (row_count, head_count * HD), lambda k, slot, first, start, end: (0, 0)
+        ),
     )
     return pl.pallas_call(
         attention_kernel,
         grid_spec=grid_spec,
-        out_shape=jax.ShapeDtypeStruct((requests, flat_rows, HD), jnp.bfloat16),
-    )(slot_index, firsts, starts, spread, slots, suffix_windows, query_rows, row_pairs)
+        out_shape=jax.ShapeDtypeStruct((row_count, head_count * HD), jnp.float32),
+    )(slot_index, firsts, starts, ends, spread, slots, suffix_windows, query_rows, row_pairs)
 
 
 def shifted(block, shift, n_tp):
@@ -155,8 +168,8 @@
     suffix_rows = jnp.transpose(suffix_kv.reshape(row_count, 2, 2, HD), (0, 2, 1, 3)).reshape(
         row_count, -1
     )
-    window = min(MOSTLEN, row_count)
-    firsts = jnp.minimum(req_starts, row_count - window).astype(jnp.int32)
+    window = min(MOSTLEN + 8, row_count)
+    firsts = jnp.minimum(req_starts // 8 * 8, row_count - window).astype(jnp.int32)
     head_select = jnp.transpose(select)[:, :, None, None]
     spreads = []
     suffix_windows = []
@@ -171,24 +184,19 @@
     query_rows = (jnp.arange(head_count * window, dtype=jnp.int32) % window)[:, None]
     row_pairs = jnp.repeat(pair_ids.astype(jnp.int32), window)[:, None]
     slot_index = slot_of_tenant[req_tenant].astype(jnp.int32)
-    results = window_attention(
+    attended = window_attention(
         slot_index,
         firsts,
         req_starts.astype(jnp.int32),
+        req_ends.astype(jnp.int32),
         jnp.stack(spreads),
         slots,
         jnp.stack(suffix_windows),
         query_rows,
         row_pairs,
         own_slot.shape[0],
-    ).reshape(-1, head_count, window, HD)
-    attended = jnp.zeros((row_count, head_count * HD), jnp.bfloat16)
-    for request in range(req_lengths.shape[0]):
-        window_attended = jnp.transpose(results[request], (1, 0, 2)).reshape(window, -1)
-        placed = lax.dynamic_update_slice_in_dim(
-            jnp.zeros_like(attended), window_attended, firsts[request], 0
-        )
-        attended = jnp.where((request_ids == request)[:, None], placed, attended)
+        row_count,
+    ).astype(jnp.bfloat16)
 
     projected = jnp.dot(attended, weight_pieces[0], preferred_element_type=jnp.float32)
     for shift in range(1, n_tp):

time: 116 us -> 119 us (1.026)
  waiting for transfers between devices: 39.2 us -> 36.3 us
  Pallas kernels: 10.5 us -> 13.4 us
  local copies, waits for them, and re-layouts: 14.8 us -> 16.6 us
  other arithmetic: 6.66 us -> 8.06 us
    all_gather x1, waiting for transfers between devices: 10.9 us -> 4.78 us  [tenant_slots(): return (lax.all_gather(own_slot, 'req', axis=0, tiled=True), owners)]
    dynamic_slice x5, local copies, waits for them, and re-layouts: 2.05 us -> 6.37 us  [local(): lax.dynamic_slice_in_dim(suffix_rows, firsts[request], window, 0)]
    ppermute x9, waiting for transfers between devices: 28.3 us -> 31.5 us  [shifted(): return lax.ppermute(block, 'tp', pairs)]
    pallas_call x1, Pallas kernels: 10.5 us -> 13.4 us  [window_attention(): pl.pallas_call(attention_kernel, grid_spec=grid_spec, out_shape=jax.Shape...]
    concatenate x4, local copies, waits for them, and re-layouts: 0.7 us -> 2.1 us  [local(): jnp.concatenate([window_queries * head_select[0], window_queries * head_s...]
    dynamic_update_slice x3 -> x0, local copies, waits for them, and re-layouts: 1.32 us -> none  [local(): lax.dynamic_update_slice_in_dim(jnp.zeros_like(attended), window_attended...]
    slice x1 -> x0, local copies, waits for them, and re-layouts: 1.2 us -> none  [local(): results[request]]
    unnamed x27 -> x28, local copies, waits for them, and re-layouts: 3.81 us -> 2.84 us
  transfers between devices with their start and end apart: 10 -> 10, of which waited for: 4 -> 5; matrix products, arithmetic and copies ran while one was open for 19% -> 21% of each run, Pallas kernels for 9% -> 11%
where the time goes in v12:
time: 119 us; the launch traced here: 118 us
  waiting for transfers between devices  36.3 us (31%)
  between operations  22.2 us (19%)
  local copies, waits for them, and re-layouts  16.6 us (14%)
  starting transfers between devices  14.7 us (12%)
  Pallas kernels  13.4 us (11%)
  other arithmetic  8.06 us (7%)
  matrix products  6.32 us (5%)
    ppermute x9, waiting for transfers between devices, shifted(): return lax.ppermute(block, 'tp', pairs)  31.5 us
    ppermute x9, starting transfers between devices, shifted(): return lax.ppermute(block, 'tp', pairs)  14.6 us
    pallas_call x1, Pallas kernels, window_attention(): pl.pallas_call(attention_kernel, grid_spec=grid_spec, out_shape=jax.Shape...  13.4 us
    dynamic_slice x5, local copies, waits for them, and re-layouts, local(): lax.dynamic_slice_in_dim(suffix_rows, firsts[request], window, 0)  6.37 us
    all_gather x1, waiting for transfers between devices, tenant_slots(): return (lax.all_gather(own_slot, 'req', axis=0, tiled=True), owners)  4.78 us
    dot_general x3, matrix products, local(): jnp.dot(head_block, weight_pieces[shift], preferred_element_type=jnp.floa...  3.92 us
    unnamed x28, local copies, waits for them, and re-layouts  2.84 us
  transfers between devices with their start and end apart: 10, of which 5 were waited for; matrix products, arithmetic and copies ran while one was open for 21% of the time, Pallas kernels for 11%

profile of v12, /device:TPU:8, one launch (start us, length us, event | category | flops | bytes accessed | tf_op | source)
XLA Modules:
  0.0 117.7 jit_solution(10025045128311669615)
XLA Ops:
  7.2 1.3 %copy.18 = bf16[1024,1,256]{0,2,1:T(8,128)(2,1)S(1)} copy(bf16[1024,1,256]{2,0,1:T(8,128)(2,1)} %param.13) | data formatting | bytes 1048576 | tf_op args[3]
  8.6 1.0 copy.20
  9.7 0.4 copy-done.3
  10.1 1.0 constant_dynamic-slice_fusion.1
  11.1 1.6 %collective-permute-start.1 = (bf16[320,512]{1,0:T(8,128)(2,1)}, bf16[320,512]{1,0:T(8,128)(2,1)}, u32[]{:S(2)}, u32[]{:S(2)}) collective-permute-start(bf16[320,512]{1,0:T(8,128)(2,1)} %get-tuple-element.5), channel_id=1, source_target_pairs={{0,1},{1,2},{2,3},{3,0},{4,5},{5,6},{6,7},{7,4},{8,9},{9,10},{10,1... | collective-permute-start | bytes 983048 | tf_op jit(solution)/shard_map/ppermute | solution.py:123
  12.7 0.4 collective-permute-start.5
  13.1 2.6 %collective-permute-start.3 = (bf16[320,512]{1,0:T(8,128)(2,1)}, bf16[320,512]{1,0:T(8,128)(2,1)}, u32[]{:S(2)}, u32[]{:S(2)}) collective-permute-start(bf16[320,512]{1,0:T(8,128)(2,1)} %get-tuple-element.4), channel_id=1, source_target_pairs={{0,2},{1,3},{2,0},{3,1},{4,6},{5,7},{6,4},{7,5},{8,10},{9,11},{10,... | collective-permute-start | bytes 983048 | tf_op jit(solution)/shard_map/ppermute | solution.py:123
  15.7 0.2 reduce-window.9
  15.9 0.6 multiply_minimum_fusion
  16.5 0.7 fusion.46
  25.0 0.3 constant_dynamic-slice_fusion.10
  25.3 1.0 multiply_bitcast_fusion.1
  26.4 0.2 copy.14
  26.6 0.8 copy.15
  27.5 1.3 %pad_maximum_fusion.3 = (bf16[5,136,128]{1,2,0:T(8,128)(2,1)S(1)}, bf16[5,136,128]{1,2,0:T(8,128)(2,1)S(1)}) fusion(bf16[5,136,64]{1,2,0:T(8,128)(2,1)} %get-tuple-element.31, bf16[5,136,64]{1,2,0:T(8,128)(2,1)} %get-tuple-element.32, bf16[5,136,64]{1,2,0:T(8,128)(2,1)} %get-tuple-element.18, bf16[5,136,64]{1,2,0:T(8,128)(2,1)} %get-tuple-element.17), kind=kLoop, calls=%fused_computation.38 | loop fusion | flops 696320 | bytes 696320 | tf_op jit(solution)/shard_map/concatenate | solution.py:179
  28.7 0.8 copy.16
  29.6 0.2 copy.17
  29.8 1.0 copy.21
  30.9 1.0 constant_dynamic-slice_fusion.6
  31.9 1.0 copy.23
  32.9 1.1 copy.24
  34.0 1.6 %copy.25 = bf16[136,256]{1,0:T(8,128)(2,1)} copy(bf16[136,256]{0,1:T(8,128)(2,1)} %get-tuple-element.21) | data formatting | bytes 139264 | tf_op jit(solution)/shard_map/dynamic_slice | solution.py:183
  35.6 1.6 %copy.26 = bf16[136,256]{1,0:T(8,128)(2,1)} copy(bf16[136,256]{0,1:T(8,128)(2,1)} %get-tuple-element.20) | data formatting | bytes 139264 | tf_op jit(solution)/shard_map/dynamic_slice | solution.py:183
  37.3 0.9 broadcast_in_dim_reshape.4.pair_ref
  38.3 1.2 %gather_fusion = s32[4]{0:T(128)} fusion(s32[4]{0:T(128)S(1)} %copy-done.1, s32[1024]{0:T(1024)S(1)} %pad_clamp_fusion), kind=kCustom, calls=%fused_computation | custom fusion | bytes 48 | tf_op jit(solution)/shard_map/gather | solution.py:186
  39.5 0.9 add_select_fusion.row_ref
  40.4 1.0 pad_maximum_fusion.query_ref
  41.3 1.7 %pad_maximum_fusion.5.suffix_ref = bf16[4,136,256]{2,1,0:T(8,128)(2,1)} fusion(bf16[1,136,256]{2,1,0:T(8,128)(2,1)} %bitcast.77, bf16[1,136,256]{2,1,0:T(8,128)(2,1)} %bitcast.76, bf16[1,136,256]{2,1,0:T(8,128)(2,1)S(1)} %bitcast.75, bf16[1,136,256]{2,1,0:T(8,128)(2,1)S(1)} %bitcast.74), kind=kLoop, calls=%fused_computation.47 | loop fusion | flops 417792 | bytes 557056 | tf_op jit(solution)/shard_map/stack | solution.py:194
  43.0 4.8 %all-gather.2.cloned.1.call-done.prefix_ref = bf16[8192,256]{1,0:T(8,128)(2,1)} async-done(((bf16[1024,256]{1,0:T(8,128)(2,1)}), bf16[8192,256]{1,0:T(8,128)(2,1)}) %all-gather.2.cloned.1.call-update) | async-done | bytes 4194320 | tf_op jit(solution)/shard_map/all_gather | solution.py:34
  47.8 13.4 %shard_map.113 = f32[256,320]{1,0:T(8,128)} custom-call(s32[4]{0:T(128)} %gather_fusion, s32[4]{0:T(128)} %copy-done.8, s32[4]{0:T(128)} %get-tuple-element.3.start_ref, s32[4]{0:T(128)} %bitcast.78, bf16[4,680,128]{2,1,0:T(8,128)(2,1)} %pad_maximum_fusion.query_ref, bf16[8192,256]{1,0:T(8,128)(2,1)} %all-gather.2.cloned.1.call-done.prefix_ref, ...), custom_call_target="tpu_custom_call" | custom-call | tf_op jit(solution)/shard_map/pallas_call | solution.py:114
  61.2 1.0 convert_element_type.45
  62.3 1.5 %collective-permute-start = (bf16[256,320]{1,0:T(8,128)(2,1)S(1)}, bf16[256,320]{1,0:T(8,128)(2,1)S(1)}, u32[]{:S(2)}, u32[]{:S(2)}) collective-permute-start(bf16[256,320]{1,0:T(8,128)(2,1)S(1)} %convert_element_type.45), channel_id=1, source_target_pairs={{0,1},{1,2},{2,3},{3,0},{4,5},{5,6},{6,7},{7,4},{8,9},{9,10},{10,1... | collective-permute-start | bytes 491528 | tf_op jit(solution)/shard_map/ppermute | solution.py:123
  63.8 0.5 collective-permute-start.4
  64.4 0.3 fusion.24
  64.7 2.5 %collective-permute-start.2 = (bf16[256,320]{1,0:T(8,128)(2,1)S(1)}, bf16[256,320]{1,0:T(8,128)(2,1)S(1)}, u32[]{:S(2)}, u32[]{:S(2)}) collective-permute-start(bf16[256,320]{1,0:T(8,128)(2,1)S(1)} %convert_element_type.45), channel_id=1, source_target_pairs={{0,2},{1,3},{2,0},{3,1},{4,6},{5,7},{6,4},{7,5},{8,10},{9,11},{10,... | collective-permute-start | bytes 491528 | tf_op jit(solution)/shard_map/ppermute | solution.py:123
  67.1 10.2 %collective-permute-done = bf16[256,320]{1,0:T(8,128)(2,1)S(1)} collective-permute-done((bf16[256,320]{1,0:T(8,128)(2,1)S(1)}, bf16[256,320]{1,0:T(8,128)(2,1)S(1)}, u32[]{:S(2)}, u32[]{:S(2)}) %collective-permute-start) | collective-permute-done | bytes 163872 | tf_op jit(solution)/shard_map/ppermute | solution.py:123
  77.4 1.3 %convolution_add_fusion.1 = f32[256,512]{1,0:T(8,128)S(1)} fusion(f32[256,512]{1,0:T(8,128)S(1)} %fusion.24, bf16[256,320]{1,0:T(8,128)(2,1)S(1)} %collective-permute-done, bf16[320,512]{1,0:T(8,128)(2,1)} %collective-permute-done.1), kind=kOutput, calls=%fused_computation.4 | convolution fusion | flops 84017152 | bytes 1540096 | tf_op jit(solution)/shard_map/dot_general | solution.py:204
  78.7 1.3 %fusion.47 = f32[256,512]{1,0:T(8,128)S(1)} fusion(bf16[256,320]{1,0:T(8,128)(2,1)S(1)} %collective-permute-done.4, bf16[320,512]{1,0:T(8,128)(2,1)} %collective-permute-done.5), kind=kOutput, calls=%fused_computation.100 | convolution fusion | flops 83886080 | bytes 1015808 | tf_op jit(solution)/shard_map/dot_general | solution.py:204
  80.0 0.9 collective-permute-done.2
  80.9 1.4 %fusion.4 = (f32[256]{0:T(256)S(1)}, bf16[256,512]{1,0:T(8,128)(2,1)S(1)}) fusion(f32[256,512]{1,0:T(8,128)S(1)} %fusion.47, f32[256,512]{1,0:T(8,128)S(1)} %convolution_add_fusion.1, bf16[256,320]{1,0:T(8,128)(2,1)S(1)} %collective-permute-done.2, bf16[320,512]{1,0:T(8,128)(2,1)} %collective-permute-done.3, bf16[256,512]{1,0:T(8,128)(2,1)S(1)} %copy-done.7), kind=kOutput, calls=%fused_computation.19 | convolution fusion | flops 84934400 | bytes 2065408 | tf_op jit(solution)/shard_map/dot_general | solution.py:204
  82.3 3.4 %collective-permute-start.7 = (bf16[256,512]{1,0:T(8,128)(2,1)S(1)}, bf16[256,512]{1,0:T(8,128)(2,1)S(1)}, u32[]{:S(2)}, u32[]{:S(2)}) collective-permute-start(bf16[256,512]{1,0:T(8,128)(2,1)S(1)} %get-tuple-element.40), channel_id=1, source_target_pairs={{0,2},{1,3},{2,0},{3,1},{4,6},{5,7},{6,4},{7,5},{8,10},{9,11},{10,... | collective-permute-start | bytes 786440 | tf_op jit(solution)/shard_map/ppermute | solution.py:123
  85.8 2.0 %collective-permute-start.6 = (bf16[256,512]{1,0:T(8,128)(2,1)S(1)}, bf16[256,512]{1,0:T(8,128)(2,1)S(1)}, u32[]{:S(2)}, u32[]{:S(2)}) collective-permute-start(bf16[256,512]{1,0:T(8,128)(2,1)S(1)} %get-tuple-element.40), channel_id=1, source_target_pairs={{0,1},{1,2},{2,3},{3,0},{4,5},{5,6},{6,7},{7,4},{8,9},{9,10},{10,1... | collective-permute-start | bytes 786440 | tf_op jit(solution)/shard_map/ppermute | solution.py:123
  87.9 14.7 %collective-permute-done.7 = bf16[256,512]{1,0:T(8,128)(2,1)S(1)} collective-permute-done((bf16[256,512]{1,0:T(8,128)(2,1)S(1)}, bf16[256,512]{1,0:T(8,128)(2,1)S(1)}, u32[]{:S(2)}, u32[]{:S(2)}) %collective-permute-start.7) | collective-permute-done | bytes 262176 | tf_op jit(solution)/shard_map/ppermute | solution.py:123
  102.7 5.6 %collective-permute-done.8 = bf16[256,512]{1,0:T(8,128)(2,1)S(1)} collective-permute-done((bf16[256,512]{1,0:T(8,128)(2,1)S(1)}, bf16[256,512]{1,0:T(8,128)(2,1)S(1)}, u32[]{:S(2)}, u32[]{:S(2)}) %collective-permute-start.8) | collective-permute-done | bytes 262176 | tf_op jit(solution)/shard_map/ppermute | solution.py:123
  108.7 0.4 fusion.22
  109.0 0.4 convolution_add_fusion.4
  109.4 0.4 convolution_add_fusion.3
  109.8 1.0 fusion.3
  (47 shorter events, 0.9 us)
Async XLA Ops:
  7.2 101.5 %copy-start = (bf16[2048,320]{0,1:T(8,128)(2,1)S(1)}, bf16[2048,320]{0,1:T(8,128)(2,1)}, u32[]{:S(2)}) copy-start(bf16[2048,320]{0,1:T(8,128)(2,1)} %param.16) | copy-start | bytes 3932164
  7.2 40.6 %all-gather.2.cloned.1.call-start = ((), (), s32[]{:S(2)}) async-start(), calls=%async_computation | async-start | bytes 4718592 | tf_op jit(solution)/shard_map/all_gather | solution.py:34
  8.6 1.5 %copy-start.3 = (bf16[320,2048]{1,0:T(8,128)(2,1)S(1)}, bf16[320,2048]{1,0:T(8,128)(2,1)}, u32[]{:S(2)}) copy-start(bf16[320,2048]{1,0:T(8,128)(2,1)} %param.14) | copy-start | bytes 3932164
  9.6 6.1 %copy-start.11 = (s32[1,4]{1,0:T(1,128)S(1)}, s32[1,4]{1,0:T(1,128)}, u32[]{:S(2)}) copy-start(s32[1,4]{1,0:T(1,128)} %param.17) | copy-start | bytes 52
  9.6 15.4 %copy-start.2 = (bf16[256,320]{0,1:T(8,128)(2,1)S(1)}, bf16[256,320]{0,1:T(8,128)(2,1)}, u32[]{:S(2)}) copy-start(bf16[256,320]{0,1:T(8,128)(2,1)} %param.11) | copy-start | bytes 491524
  11.1 53.6 %collective-permute-start.1 = (bf16[320,512]{1,0:T(8,128)(2,1)}, bf16[320,512]{1,0:T(8,128)(2,1)}, u32[]{:S(2)}, u32[]{:S(2)}) collective-permute-start(bf16[320,512]{1,0:T(8,128)(2,1)} %get-tuple-element.5), channel_id=1, source_target_pairs={{0,1},{1,2},{2,3},{3,0},{4,5},{5,6},{6,7},{7,4},{8,9},{9,10},{10,1... | collective-permute-start | bytes 983048 | tf_op jit(solution)/shard_map/ppermute | solution.py:123
  12.7 66.0 %collective-permute-start.5 = (bf16[320,512]{1,0:T(8,128)(2,1)}, bf16[320,512]{1,0:T(8,128)(2,1)}, u32[]{:S(2)}, u32[]{:S(2)}) collective-permute-start(bf16[320,512]{1,0:T(8,128)(2,1)} %get-tuple-element.6), channel_id=1, source_target_pairs={{0,3},{1,0},{2,1},{3,2},{4,7},{5,4},{6,5},{7,6},{8,11},{9,8},{10,9... | collective-permute-start | bytes 983048 | tf_op jit(solution)/shard_map/ppermute | solution.py:123
  13.1 66.8 %collective-permute-start.3 = (bf16[320,512]{1,0:T(8,128)(2,1)}, bf16[320,512]{1,0:T(8,128)(2,1)}, u32[]{:S(2)}, u32[]{:S(2)}) collective-permute-start(bf16[320,512]{1,0:T(8,128)(2,1)} %get-tuple-element.4), channel_id=1, source_target_pairs={{0,2},{1,3},{2,0},{3,1},{4,6},{5,7},{6,4},{7,5},{8,10},{9,11},{10,... | collective-permute-start | bytes 983048 | tf_op jit(solution)/shard_map/ppermute | solution.py:123
  15.9 10.4 %copy-start.10 = (s32[4,1]{0,1:T(1,128)}, s32[4,1]{0,1:T(1,128)S(1)}, u32[]{:S(2)}) copy-start(s32[4,1]{0,1:T(1,128)S(1)} %reduce-window.9) | copy-start | bytes 52
  16.5 9.8 %copy-start.8 = (s32[4]{0:T(128)}, s32[4]{0:T(128)S(1)}, u32[]{:S(2)}) copy-start(s32[4]{0:T(128)S(1)} %get-tuple-element.2.first_ref) | copy-start | bytes 52
  30.8 7.5 %copy-start.12 = (s32[1,4]{1,0:T(1,128)S(1)}, s32[1,4]{1,0:T(1,128)}, u32[]{:S(2)}) copy-start(s32[1,4]{1,0:T(1,128)} %param.18) | copy-start | bytes 52
  30.8 7.5 %copy-start.1 = (s32[4]{0:T(128)S(1)}, s32[4]{0:T(128)}, u32[]{:S(2)}) copy-start(s32[4]{0:T(128)} %param.19) | copy-start | bytes 52
  30.8 9.5 %copy-start.5 = (bf16[5,136,128]{2,1,0:T(8,128)(2,1)S(1)}, bf16[5,136,128]{2,1,0:T(8,128)(2,1)}, u32[]{:S(2)}) copy-start(bf16[5,136,128]{2,1,0:T(8,128)(2,1)} %copy.15) | copy-start | bytes 522244
  30.8 9.5 %copy-start.6 = (bf16[5,136,128]{2,1,0:T(8,128)(2,1)S(1)}, bf16[5,136,128]{2,1,0:T(8,128)(2,1)}, u32[]{:S(2)}) copy-start(bf16[5,136,128]{2,1,0:T(8,128)(2,1)} %copy.16) | copy-start | bytes 522244
  62.3 15.1 %collective-permute-start = (bf16[256,320]{1,0:T(8,128)(2,1)S(1)}, bf16[256,320]{1,0:T(8,128)(2,1)S(1)}, u32[]{:S(2)}, u32[]{:S(2)}) collective-permute-start(bf16[256,320]{1,0:T(8,128)(2,1)S(1)} %convert_element_type.45), channel_id=1, source_target_pairs={{0,1},{1,2},{2,3},{3,0},{4,5},{5,6},{6,7},{7,4},{8,9},{9,10},{10,1... | collective-permute-start | bytes 491528 | tf_op jit(solution)/shard_map/ppermute | solution.py:123
  63.8 14.8 %collective-permute-start.4 = (bf16[256,320]{1,0:T(8,128)(2,1)S(1)}, bf16[256,320]{1,0:T(8,128)(2,1)S(1)}, u32[]{:S(2)}, u32[]{:S(2)}) collective-permute-start(bf16[256,320]{1,0:T(8,128)(2,1)S(1)} %convert_element_type.45), channel_id=1, source_target_pairs={{0,3},{1,0},{2,1},{3,2},{4,7},{5,4},{6,5},{7,6},{8,11},{9,8},{10,9... | collective-permute-start | bytes 491528 | tf_op jit(solution)/shard_map/ppermute | solution.py:123
  64.7 16.2 %copy-start.7 = (bf16[256,512]{1,0:T(8,128)(2,1)S(1)}, bf16[256,512]{1,0:T(8,128)(2,1)}, u32[]{:S(2)}) copy-start(bf16[256,512]{1,0:T(8,128)(2,1)} %param.10) | copy-start | bytes 786436
  64.7 16.2 %collective-permute-start.2 = (bf16[256,320]{1,0:T(8,128)(2,1)S(1)}, bf16[256,320]{1,0:T(8,128)(2,1)S(1)}, u32[]{:S(2)}, u32[]{:S(2)}) collective-permute-start(bf16[256,320]{1,0:T(8,128)(2,1)S(1)} %convert_element_type.45), channel_id=1, source_target_pairs={{0,2},{1,3},{2,0},{3,1},{4,6},{5,7},{6,4},{7,5},{8,10},{9,11},{10,... | collective-permute-start | bytes 491528 | tf_op jit(solution)/shard_map/ppermute | solution.py:123
  79.9 7.8 %copy-start.9 = (bf16[2048]{0:T(1024)(128)(2,1)S(1)}, bf16[2048]{0:T(1024)(128)(2,1)}, u32[]{:S(2)}) copy-start(bf16[2048]{0:T(1024)(128)(2,1)} %param.15) | copy-start | bytes 12292
  82.3 27.1 %copy-start.4 = (bf16[256,512]{1,0:T(8,128)(2,1)}, bf16[256,512]{1,0:T(8,128)(2,1)S(1)}, u32[]{:S(2)}) copy-start(bf16[256,512]{1,0:T(8,128)(2,1)S(1)} %get-tuple-element.40) | copy-start | bytes 786436
  82.3 20.3 %collective-permute-start.7 = (bf16[256,512]{1,0:T(8,128)(2,1)S(1)}, bf16[256,512]{1,0:T(8,128)(2,1)S(1)}, u32[]{:S(2)}, u32[]{:S(2)}) collective-permute-start(bf16[256,512]{1,0:T(8,128)(2,1)S(1)} %get-tuple-element.40), channel_id=1, source_target_pairs={{0,2},{1,3},{2,0},{3,1},{4,6},{5,7},{6,4},{7,5},{8,10},{9,11},{10,... | collective-permute-start | bytes 786440 | tf_op jit(solution)/shard_map/ppermute | solution.py:123
  85.7 22.6 %collective-permute-start.8 = (bf16[256,512]{1,0:T(8,128)(2,1)S(1)}, bf16[256,512]{1,0:T(8,128)(2,1)S(1)}, u32[]{:S(2)}, u32[]{:S(2)}) collective-permute-start(bf16[256,512]{1,0:T(8,128)(2,1)S(1)} %get-tuple-element.40), channel_id=1, source_target_pairs={{0,3},{1,0},{2,1},{3,2},{4,7},{5,4},{6,5},{7,6},{8,11},{9,8},{10,9... | collective-permute-start | bytes 786440 | tf_op jit(solution)/shard_map/ppermute | solution.py:123
  85.8 22.7 %collective-permute-start.6 = (bf16[256,512]{1,0:T(8,128)(2,1)S(1)}, bf16[256,512]{1,0:T(8,128)(2,1)S(1)}, u32[]{:S(2)}, u32[]{:S(2)}) collective-permute-start(bf16[256,512]{1,0:T(8,128)(2,1)S(1)} %get-tuple-element.40), channel_id=1, source_target_pairs={{0,1},{1,2},{2,3},{3,0},{4,5},{5,6},{6,7},{7,4},{8,9},{9,10},{10,1... | collective-permute-start | bytes 786440 | tf_op jit(solution)/shard_map/ppermute | solution.py:123
Sparse Core Ops, SparseCore 0:
  9.9 37.8 all-gather.1

commit v13 on v11

--- a/solution.py
+++ b/solution.py
@@ -29,9 +29,24 @@
     return (key_heads, value_heads)
 
 
+def xor_permute(block, mask, n_req):
+    pairs = [(source, source ^ mask) for source in range(n_req)]
+    return lax.ppermute(block, "req", pairs)
+
+
 def tenant_slots(own_slot, owners, n_req):
-    if n_req <= GATHER_SLOTS_MAX:
-        return lax.all_gather(own_slot, "req", axis=0, tiled=True), owners
+    if n_req <= GATHER_SLOTS_MAX and n_req % 2 == 0 and (n_req & (n_req - 1)) == 0:
+        req_index = lax.axis_index("req")
+        mine = [own_slot] + [
+            xor_permute(own_slot, 2 * chip_mask, n_req) for chip_mask in range(1, n_req // 2)
+        ]
+        theirs = [xor_permute(block, 1, n_req) for block in mine]
+        slots = jnp.concatenate(
+            [block for pair in zip(mine, theirs) for block in pair], axis=0
+        )
+        chip_offset = (owners // 2) ^ (req_index // 2)
+        other_core = (owners % 2) != (req_index % 2)
+        return slots, 2 * chip_offset + other_core.astype(jnp.int32)
     blocks = [from_root(own_slot, "req", owners[tenant_id]) for tenant_id in range(TENANTS)]
     return jnp.concatenate(blocks, axis=0), jnp.arange(TENANTS, dtype=jnp.int32)
 

time: 116 us -> 109 us (0.940)
  the two profiles are of different devices: /device:TPU:8 before, /device:TPU:0 now
where the time goes in v13:
time: 109 us
  waiting for transfers between devices  32.3 us (30%)
  local copies, waits for them, and re-layouts  28 us (26%)
  starting transfers between devices  17.9 us (16%)
  Pallas kernels  10.4 us (10%)
  between operations  8.82 us (8%)
  matrix products  6.41 us (6%)
  other arithmetic  4.82 us (4%)
    ppermute x9, waiting for transfers between devices, shifted(): return lax.ppermute(block, 'tp', pairs)  32.3 us
    unnamed x30, local copies, waits for them, and re-layouts  13.4 us
    ppermute x9, starting transfers between devices, shifted(): return lax.ppermute(block, 'tp', pairs)  12.6 us
    pallas_call x1, Pallas kernels, window_attention(): pl.pallas_call(attention_kernel, grid_spec=grid_spec, out_shape=jax.Shape...  10.4 us
    ppermute x7, starting transfers between devices, xor_permute(): return lax.ppermute(block, 'req', pairs)  5.23 us
    dynamic_slice x5, local copies, waits for them, and re-layouts, local(): lax.dynamic_slice_in_dim(suffix_rows, firsts[request], window, 0)  5.01 us
    dot_general x3, matrix products, local(): jnp.dot(head_block, weight_pieces[shift], preferred_element_type=jnp.floa...  3.03 us
  transfers between devices with their start and end apart: 16, of which 4 were waited for; matrix products, arithmetic and copies ran while one was open for 32% of the time, Pallas kernels for 10%

profile of v13, /device:TPU:0, one launch (start us, length us, event | category | flops | bytes accessed | tf_op | source)
XLA Modules:
  0.0 108.6 jit_solution(8702723233113741551)
XLA Ops:
  0.7 1.4 %copy.40 = bf16[1024,1,256]{0,2,1:T(8,128)(2,1)S(1)} copy(bf16[1024,1,256]{2,0,1:T(8,128)(2,1)} %param.13) | data formatting | bytes 1048576 | tf_op args[3]
  2.3 0.5 collective-permute-start
  2.8 2.6 %collective-permute-start.1 = (bf16[1024,256]{1,0:T(8,128)(2,1)S(1)}, bf16[1024,256]{1,0:T(8,128)(2,1)}, u32[]{:S(2)}, u32[]{:S(2)}) collective-permute-start(bf16[1024,256]{1,0:T(8,128)(2,1)S(1)} %copy.46), channel_id=1, source_target_pairs={{0,8},{4,12},{8,0},{12,4},{16,24},{20,28},{24,16},{28,20},{1,9},{5... | collective-permute-start | bytes 1572872 | tf_op jit(solution)/shard_map/ppermute | solution.py:34
  5.4 1.5 %collective-permute-start.3 = (bf16[1024,256]{1,0:T(8,128)(2,1)S(1)}, bf16[1024,256]{1,0:T(8,128)(2,1)}, u32[]{:S(2)}, u32[]{:S(2)}) collective-permute-start(bf16[1024,256]{1,0:T(8,128)(2,1)S(1)} %copy.46), channel_id=1, source_target_pairs={{0,16},{4,20},{8,24},{12,28},{16,0},{20,4},{24,8},{28,12},{1,17},{... | collective-permute-start | bytes 1572872 | tf_op jit(solution)/shard_map/ppermute | solution.py:34
  6.9 2.1 %constant_dynamic-slice_fusion.1 = (bf16[320,512]{1,0:T(8,128)(2,1)S(1)}, bf16[320,512]{1,0:T(8,128)(2,1)}, bf16[320,512]{1,0:T(8,128)(2,1)}) fusion(bf16[320,2048]{1,0:T(8,128)(2,1)} %param.14, s32[]{:T(128)S(6)} %select_n.169, s32[]{:T(128)S(6)} %select_n.167, s32[]{:T(128)S(6)} %select_n.171), kind=kLoop, calls=%fused_computation.81 | loop fusion | bytes 1966092 | tf_op jit(solution)/shard_map/dynamic_slice | solution.py:150
  9.0 4.1 %collective-permute-start.12 = (bf16[320,512]{1,0:T(8,128)(2,1)}, bf16[320,512]{1,0:T(8,128)(2,1)}, u32[]{:S(2)}, u32[]{:S(2)}) collective-permute-start(bf16[320,512]{1,0:T(8,128)(2,1)} %get-tuple-element.6), channel_id=1, source_target_pairs={{0,3},{1,0},{2,1},{3,2},{4,7},{5,4},{6,5},{7,6},{8,11},{9,8},{10,9... | collective-permute-start | bytes 983048 | tf_op jit(solution)/shard_map/ppermute | solution.py:125
  13.2 0.5 broadcast_minimum_fusion
  13.8 0.7 fusion.48
  22.8 0.8 add_select_fusion.row_ref
  23.7 1.0 copy.47
  24.7 0.8 constant_dynamic-slice_fusion.6
  25.6 0.9 copy.51
  26.6 1.6 %copy.50 = bf16[128,256]{1,0:T(8,128)(2,1)} copy(bf16[128,256]{0,1:T(8,128)(2,1)} %get-tuple-element.18) | data formatting | bytes 131072 | tf_op jit(solution)/shard_map/dynamic_slice | solution.py:185
  28.2 1.6 %copy.49 = bf16[128,256]{1,0:T(8,128)(2,1)} copy(bf16[128,256]{0,1:T(8,128)(2,1)} %get-tuple-element.15) | data formatting | bytes 131072 | tf_op jit(solution)/shard_map/dynamic_slice | solution.py:185
  29.7 0.8 constant_dynamic-update-slice_fusion.7
  30.6 1.6 %pad_maximum_fusion.1.suffix_ref = bf16[4,128,256]{2,1,0:T(8,128)(2,1)} fusion(bf16[1,128,256]{2,1,0:T(8,128)(2,1)S(1)} %bitcast.106, bf16[1,128,256]{2,1,0:T(8,128)(2,1)S(1)} %bitcast.107, bf16[1,128,256]{2,1,0:T(8,128)(2,1)} %bitcast.108, bf16[1,128,256]{2,1,0:T(8,128)(2,1)} %bitcast.109), kind=kLoop, calls=%fused_computation.43 | loop fusion | flops 393216 | bytes 524288 | tf_op jit(solution)/shard_map/stack | solution.py:195
  32.9 0.9 pad_maximum_fusion.query_ref
  33.9 0.5 collective-permute-start.4
  34.4 1.0 copy.59
  35.4 1.1 %gather_fusion = s32[4]{0:T(128)} fusion(s32[4]{0:T(128)S(1)} %fusion.43, s32[1024]{0:T(1024)S(1)} %pad_clamp_fusion), kind=kCustom, calls=%fused_computation | custom fusion | bytes 48 | tf_op jit(solution)/shard_map/gather | solution.py:188
  36.7 1.9 %constant_dynamic-update-slice_fusion.6 = bf16[8192,256]{1,0:T(8,128)(2,1)} fusion(bf16[8192,256]{1,0:T(8,128)(2,1)} %constant_dynamic-update-slice_fusion.7, bf16[1024,256]{1,0:T(8,128)(2,1)} %collective-permute-done), kind=kLoop, calls=%fused_computation.72 | loop fusion | bytes 1048576
  38.5 1.9 %constant_dynamic-update-slice_fusion.5 = bf16[8192,256]{1,0:T(8,128)(2,1)} fusion(bf16[8192,256]{1,0:T(8,128)(2,1)} %constant_dynamic-update-slice_fusion.6, bf16[1024,256]{1,0:T(8,128)(2,1)} %collective-permute-done.1), kind=kLoop, calls=%fused_computation.71 | loop fusion | bytes 1048576
  40.4 0.9 collective-permute-start.10
  41.3 1.9 %constant_dynamic-update-slice_fusion.4 = bf16[8192,256]{1,0:T(8,128)(2,1)} fusion(bf16[8192,256]{1,0:T(8,128)(2,1)} %constant_dynamic-update-slice_fusion.5, bf16[1024,256]{1,0:T(8,128)(2,1)} %collective-permute-done.2), kind=kLoop, calls=%fused_computation.70 | loop fusion | bytes 1048576
  43.2 1.9 %constant_dynamic-update-slice_fusion.3 = bf16[8192,256]{1,0:T(8,128)(2,1)} fusion(bf16[8192,256]{1,0:T(8,128)(2,1)} %constant_dynamic-update-slice_fusion.4, bf16[1024,256]{1,0:T(8,128)(2,1)} %collective-permute-done.3), kind=kLoop, calls=%fused_computation.69 | loop fusion | bytes 1048576
  45.1 0.8 constant_dynamic-update-slice_fusion.2
  45.9 0.8 constant_dynamic-update-slice_fusion.1
  46.8 0.8 constant_dynamic-update-slice_fusion.prefix_ref
  47.6 10.4 %shard_map.113 = bf16[4,640,64]{2,1,0:T(8,128)(2,1)} custom-call(s32[4]{0:T(128)} %gather_fusion, s32[4]{0:T(128)} %copy-done.4, s32[4]{0:T(128)} %get-tuple-element.3.start_ref, bf16[4,640,128]{2,1,0:T(8,128)(2,1)} %pad_maximum_fusion.query_ref, bf16[8192,256]{1,0:T(8,128)(2,1)} %constant_dynamic-update-slice_fusion.prefix_ref, ...), custom_call_target="tpu_custom_call" | custom-call | tf_op jit(solution)/shard_map/pallas_call | solution.py:116
  58.0 1.2 %fusion.46 = (bf16[1,640,64]{2,1,0:T(8,128)(2,1)S(1)}, bf16[1,640,64]{2,1,0:T(8,128)(2,1)S(1)}, bf16[1,640,64]{2,1,0:T(8,128)(2,1)S(1)}, bf16[1,640,64]{2,1,0:T(8,128)(2,1)S(1)}) fusion(bf16[4,640,64]{2,1,0:T(8,128)(2,1)} %shard_map.113), kind=kLoop, calls=%fused_computation.119 | loop fusion | bytes 655360 | tf_op jit(solution)/shard_map/slice | solution.py:202
  60.5 0.7 dynamic_update_slice.12
  61.2 0.4 select_n.160
  61.7 2.9 %collective-permute-start.11 = (bf16[256,320]{0,1:T(8,128)(2,1)S(1)}, bf16[256,320]{0,1:T(8,128)(2,1)S(1)}, u32[]{:S(2)}, u32[]{:S(2)}) collective-permute-start(bf16[256,320]{0,1:T(8,128)(2,1)S(1)} %select_select_fusion), channel_id=1, source_target_pairs={{0,3},{1,0},{2,1},{3,2},{4,7},{5,4},{6,5},{7,6},{8,11},{9,8},{10,9... | collective-permute-start | bytes 491528 | tf_op jit(solution)/shard_map/ppermute | solution.py:125
  64.5 0.6 collective-permute-start.7
  65.2 1.3 %fusion.21 = f32[256,512]{1,0:T(8,128)S(1)} fusion(bf16[256,320]{0,1:T(8,128)(2,1)S(1)} %select_select_fusion, bf16[320,2048]{1,0:T(8,128)(2,1)} %param.14, s32[]{:T(128)S(6)} %select_n.165), kind=kOutput, calls=%fused_computation.37 | convolution fusion | flops 83886080 | bytes 1015812 | tf_op jit(solution)/shard_map/dot_general | solution.py:208
  66.5 1.5 %collective-permute-start.9 = (bf16[256,320]{0,1:T(8,128)(2,1)S(1)}, bf16[256,320]{0,1:T(8,128)(2,1)S(1)}, u32[]{:S(2)}, u32[]{:S(2)}) collective-permute-start(bf16[256,320]{0,1:T(8,128)(2,1)S(1)} %select_select_fusion), channel_id=1, source_target_pairs={{0,2},{1,3},{2,0},{3,1},{4,6},{5,7},{6,4},{7,5},{8,10},{9,11},{10,... | collective-permute-start | bytes 491528 | tf_op jit(solution)/shard_map/ppermute | solution.py:125
  67.9 5.9 %collective-permute-done.7 = bf16[256,320]{0,1:T(8,128)(2,1)S(1)} collective-permute-done((bf16[256,320]{0,1:T(8,128)(2,1)S(1)}, bf16[256,320]{0,1:T(8,128)(2,1)S(1)}, u32[]{:S(2)}, u32[]{:S(2)}) %collective-permute-start.7) | collective-permute-done | bytes 163872 | tf_op jit(solution)/shard_map/ppermute | solution.py:125
  73.9 1.3 %convolution_add_fusion.1 = f32[256,512]{1,0:T(8,128)S(1)} fusion(f32[256,512]{1,0:T(8,128)S(1)} %fusion.21, bf16[256,320]{0,1:T(8,128)(2,1)S(1)} %collective-permute-done.7, bf16[320,512]{1,0:T(8,128)(2,1)} %collective-permute-done.8), kind=kOutput, calls=%fused_computation.4 | convolution fusion | flops 84017152 | bytes 1540096 | tf_op jit(solution)/shard_map/dot_general | solution.py:211
  75.2 1.3 %fusion.49 = f32[256,512]{1,0:T(8,128)S(1)} fusion(bf16[256,320]{0,1:T(8,128)(2,1)S(1)} %collective-permute-done.11, bf16[320,512]{1,0:T(8,128)(2,1)} %collective-permute-done.12), kind=kOutput, calls=%fused_computation.122 | convolution fusion | flops 83886080 | bytes 1015808 | tf_op jit(solution)/shard_map/dot_general | solution.py:211
  76.5 5.4 %collective-permute-done.9 = bf16[256,320]{0,1:T(8,128)(2,1)S(1)} collective-permute-done((bf16[256,320]{0,1:T(8,128)(2,1)S(1)}, bf16[256,320]{0,1:T(8,128)(2,1)S(1)}, u32[]{:S(2)}, u32[]{:S(2)}) %collective-permute-start.9) | collective-permute-done | bytes 163872 | tf_op jit(solution)/shard_map/ppermute | solution.py:125
  81.9 0.5 fusion.4
  82.4 2.1 %collective-permute-start.15 = (bf16[256,512]{1,0:T(8,128)(2,1)S(1)}, bf16[256,512]{1,0:T(8,128)(2,1)S(1)}, u32[]{:S(2)}, u32[]{:S(2)}) collective-permute-start(bf16[256,512]{1,0:T(8,128)(2,1)S(1)} %get-tuple-element.48), channel_id=1, source_target_pairs={{0,3},{1,0},{2,1},{3,2},{4,7},{5,4},{6,5},{7,6},{8,11},{9,8},{10,9... | collective-permute-start | bytes 786440 | tf_op jit(solution)/shard_map/ppermute | solution.py:125
  84.5 0.6 collective-permute-start.13
  85.2 7.1 %collective-permute-done.15 = bf16[256,512]{1,0:T(8,128)(2,1)S(1)} collective-permute-done((bf16[256,512]{1,0:T(8,128)(2,1)S(1)}, bf16[256,512]{1,0:T(8,128)(2,1)S(1)}, u32[]{:S(2)}, u32[]{:S(2)}) %collective-permute-start.15) | collective-permute-done | bytes 262176 | tf_op jit(solution)/shard_map/ppermute | solution.py:125
  92.4 13.8 %collective-permute-done.14 = bf16[256,512]{1,0:T(8,128)(2,1)S(1)} collective-permute-done((bf16[256,512]{1,0:T(8,128)(2,1)S(1)}, bf16[256,512]{1,0:T(8,128)(2,1)S(1)}, u32[]{:S(2)}, u32[]{:S(2)}) %collective-permute-start.14) | collective-permute-done | bytes 262176 | tf_op jit(solution)/shard_map/ppermute | solution.py:125
  106.5 0.4 fusion.19
  107.2 0.4 convolution_add_fusion.3
  107.6 1.0 fusion.3
  (77 shorter events, 4.2 us)
Async XLA Ops:
  0.6 105.9 %copy-start = (bf16[2048,320]{0,1:T(8,128)(2,1)S(1)}, bf16[2048,320]{0,1:T(8,128)(2,1)}, u32[]{:S(2)}) copy-start(bf16[2048,320]{0,1:T(8,128)(2,1)} %param.16) | copy-start | bytes 3932164
  0.6 12.4 %copy-start.6 = (s32[1,4]{1,0:T(1,128)S(1)}, s32[1,4]{1,0:T(1,128)}, u32[]{:S(2)}) copy-start(s32[1,4]{1,0:T(1,128)} %param.17) | copy-start | bytes 52
  0.7 19.1 %copy-start.8 = (s32[1,4]{1,0:T(1,128)S(1)}, s32[1,4]{1,0:T(1,128)}, u32[]{:S(2)}) copy-start(s32[1,4]{1,0:T(1,128)} %param.18) | copy-start | bytes 52
  0.7 21.8 %copy-start.7 = (s32[4]{0:T(128)S(1)}, s32[4]{0:T(128)}, u32[]{:S(2)}) copy-start(s32[4]{0:T(128)} %param.19) | copy-start | bytes 52
  0.7 21.8 %copy-start.2 = (bf16[256,320]{0,1:T(8,128)(2,1)S(1)}, bf16[256,320]{0,1:T(8,128)(2,1)}, u32[]{:S(2)}) copy-start(bf16[256,320]{0,1:T(8,128)(2,1)} %param.11) | copy-start | bytes 491524
  2.3 34.3 %collective-permute-start = (bf16[1024,256]{1,0:T(8,128)(2,1)S(1)}, bf16[1024,256]{1,0:T(8,128)(2,1)}, u32[]{:S(2)}, u32[]{:S(2)}) collective-permute-start(bf16[1024,256]{1,0:T(8,128)(2,1)S(1)} %copy.46), channel_id=1, source_target_pairs={{0,4},{4,0},{8,12},{12,8},{16,20},{20,16},{24,28},{28,24},{1,5},{5... | collective-permute-start | bytes 1572872 | tf_op jit(solution)/shard_map/ppermute | solution.py:34
  2.8 27.7 %collective-permute-start.1 = (bf16[1024,256]{1,0:T(8,128)(2,1)S(1)}, bf16[1024,256]{1,0:T(8,128)(2,1)}, u32[]{:S(2)}, u32[]{:S(2)}) collective-permute-start(bf16[1024,256]{1,0:T(8,128)(2,1)S(1)} %copy.46), channel_id=1, source_target_pairs={{0,8},{4,12},{8,0},{12,4},{16,24},{20,28},{24,16},{28,20},{1,9},{5... | collective-permute-start | bytes 1572872 | tf_op jit(solution)/shard_map/ppermute | solution.py:34
  5.4 28.5 %collective-permute-start.3 = (bf16[1024,256]{1,0:T(8,128)(2,1)S(1)}, bf16[1024,256]{1,0:T(8,128)(2,1)}, u32[]{:S(2)}, u32[]{:S(2)}) collective-permute-start(bf16[1024,256]{1,0:T(8,128)(2,1)S(1)} %copy.46), channel_id=1, source_target_pairs={{0,16},{4,20},{8,24},{12,28},{16,0},{20,4},{24,8},{28,12},{1,17},{... | collective-permute-start | bytes 1572872 | tf_op jit(solution)/shard_map/ppermute | solution.py:34
  6.9 29.7 %collective-permute-start.5 = (bf16[1024,256]{1,0:T(8,128)(2,1)S(1)}, bf16[1024,256]{1,0:T(8,128)(2,1)S(1)}, u32[]{:S(2)}, u32[]{:S(2)}) collective-permute-start(bf16[1024,256]{1,0:T(8,128)(2,1)S(1)} %copy.46), channel_id=1, source_target_pairs={{0,24},{4,28},{8,16},{12,20},{16,8},{20,12},{24,0},{28,4},{1,25},{... | collective-permute-start | bytes 1572872 | tf_op jit(solution)/shard_map/ppermute | solution.py:34
  9.0 66.1 %collective-permute-start.12 = (bf16[320,512]{1,0:T(8,128)(2,1)}, bf16[320,512]{1,0:T(8,128)(2,1)}, u32[]{:S(2)}, u32[]{:S(2)}) collective-permute-start(bf16[320,512]{1,0:T(8,128)(2,1)} %get-tuple-element.6), channel_id=1, source_target_pairs={{0,3},{1,0},{2,1},{3,2},{4,7},{5,4},{6,5},{7,6},{8,11},{9,8},{10,9... | collective-permute-start | bytes 983048 | tf_op jit(solution)/shard_map/ppermute | solution.py:125
  13.8 20.1 %copy-start.4 = (s32[4]{0:T(128)}, s32[4]{0:T(128)S(1)}, u32[]{:S(2)}) copy-start(s32[4]{0:T(128)S(1)} %get-tuple-element.2.first_ref) | copy-start | bytes 52
  30.6 9.9 %collective-permute-start.2 = (bf16[1024,256]{1,0:T(8,128)(2,1)}, bf16[1024,256]{1,0:T(8,128)(2,1)}, u32[]{:S(2)}, u32[]{:S(2)}) collective-permute-start(bf16[1024,256]{1,0:T(8,128)(2,1)} %collective-permute-done.1), channel_id=1, source_target_pairs={{0,4},{4,0},{8,12},{12,8},{16,20},{20,16},{24,28},{28,24},{1,5},{5... | collective-permute-start | bytes 1572872 | tf_op jit(solution)/shard_map/ppermute | solution.py:34
  33.9 11.3 %collective-permute-start.4 = (bf16[1024,256]{1,0:T(8,128)(2,1)}, bf16[1024,256]{1,0:T(8,128)(2,1)S(1)}, u32[]{:S(2)}, u32[]{:S(2)}) collective-permute-start(bf16[1024,256]{1,0:T(8,128)(2,1)} %collective-permute-done.3), channel_id=1, source_target_pairs={{0,4},{4,0},{8,12},{12,8},{16,20},{20,16},{24,28},{28,24},{1,5},{5... | collective-permute-start | bytes 1572872 | tf_op jit(solution)/shard_map/ppermute | solution.py:34
  36.6 29.9 %collective-permute-start.8 = (bf16[320,512]{1,0:T(8,128)(2,1)}, bf16[320,512]{1,0:T(8,128)(2,1)}, u32[]{:S(2)}, u32[]{:S(2)}) collective-permute-start(bf16[320,512]{1,0:T(8,128)(2,1)} %get-tuple-element.5), channel_id=1, source_target_pairs={{0,1},{1,2},{2,3},{3,0},{4,5},{5,6},{6,7},{7,4},{8,9},{9,10},{10,1... | collective-permute-start | bytes 983048 | tf_op jit(solution)/shard_map/ppermute | solution.py:125
  36.6 10.2 %collective-permute-start.6 = (bf16[1024,256]{1,0:T(8,128)(2,1)S(1)}, bf16[1024,256]{1,0:T(8,128)(2,1)S(1)}, u32[]{:S(2)}, u32[]{:S(2)}) collective-permute-start(bf16[1024,256]{1,0:T(8,128)(2,1)S(1)} %collective-permute-done.5), channel_id=1, source_target_pairs={{0,4},{4,0},{8,12},{12,8},{16,20},{20,16},{24,28},{28,24},{1,5},{5... | collective-permute-start | bytes 1572872 | tf_op jit(solution)/shard_map/ppermute | solution.py:34
  40.4 36.0 %collective-permute-start.10 = (bf16[320,512]{1,0:T(8,128)(2,1)S(1)}, bf16[320,512]{1,0:T(8,128)(2,1)S(1)}, u32[]{:S(2)}, u32[]{:S(2)}) collective-permute-start(bf16[320,512]{1,0:T(8,128)(2,1)S(1)} %get-tuple-element.4), channel_id=1, source_target_pairs={{0,2},{1,3},{2,0},{3,1},{4,6},{5,7},{6,4},{7,5},{8,10},{9,11},{10,... | collective-permute-start | bytes 983048 | tf_op jit(solution)/shard_map/ppermute | solution.py:125
  58.0 24.0 %copy-start.3 = (bf16[256,512]{1,0:T(8,128)(2,1)S(1)}, bf16[256,512]{1,0:T(8,128)(2,1)}, u32[]{:S(2)}) copy-start(bf16[256,512]{1,0:T(8,128)(2,1)} %param.10) | copy-start | bytes 786436
  59.6 25.5 %copy-start.5 = (bf16[2048]{0:T(1024)(128)(2,1)S(1)}, bf16[2048]{0:T(1024)(128)(2,1)}, u32[]{:S(2)}) copy-start(bf16[2048]{0:T(1024)(128)(2,1)} %param.15) | copy-start | bytes 12292
  61.7 13.5 %collective-permute-start.11 = (bf16[256,320]{0,1:T(8,128)(2,1)S(1)}, bf16[256,320]{0,1:T(8,128)(2,1)S(1)}, u32[]{:S(2)}, u32[]{:S(2)}) collective-permute-start(bf16[256,320]{0,1:T(8,128)(2,1)S(1)} %select_select_fusion), channel_id=1, source_target_pairs={{0,3},{1,0},{2,1},{3,2},{4,7},{5,4},{6,5},{7,6},{8,11},{9,8},{10,9... | collective-permute-start | bytes 491528 | tf_op jit(solution)/shard_map/ppermute | solution.py:125
  64.5 9.3 %collective-permute-start.7 = (bf16[256,320]{0,1:T(8,128)(2,1)S(1)}, bf16[256,320]{0,1:T(8,128)(2,1)S(1)}, u32[]{:S(2)}, u32[]{:S(2)}) collective-permute-start(bf16[256,320]{0,1:T(8,128)(2,1)S(1)} %select_select_fusion), channel_id=1, source_target_pairs={{0,1},{1,2},{2,3},{3,0},{4,5},{5,6},{6,7},{7,4},{8,9},{9,10},{10,1... | collective-permute-start | bytes 491528 | tf_op jit(solution)/shard_map/ppermute | solution.py:125
  66.5 15.5 %collective-permute-start.9 = (bf16[256,320]{0,1:T(8,128)(2,1)S(1)}, bf16[256,320]{0,1:T(8,128)(2,1)S(1)}, u32[]{:S(2)}, u32[]{:S(2)}) collective-permute-start(bf16[256,320]{0,1:T(8,128)(2,1)S(1)} %select_select_fusion), channel_id=1, source_target_pairs={{0,2},{1,3},{2,0},{3,1},{4,6},{5,7},{6,4},{7,5},{8,10},{9,11},{10,... | collective-permute-start | bytes 491528 | tf_op jit(solution)/shard_map/ppermute | solution.py:125
  82.4 26.2 %copy-start.1 = (bf16[256,512]{1,0:T(8,128)(2,1)}, bf16[256,512]{1,0:T(8,128)(2,1)S(1)}, u32[]{:S(2)}) copy-start(bf16[256,512]{1,0:T(8,128)(2,1)S(1)} %get-tuple-element.48) | copy-start | bytes 786436
  82.4 9.9 %collective-permute-start.15 = (bf16[256,512]{1,0:T(8,128)(2,1)S(1)}, bf16[256,512]{1,0:T(8,128)(2,1)S(1)}, u32[]{:S(2)}, u32[]{:S(2)}) collective-permute-start(bf16[256,512]{1,0:T(8,128)(2,1)S(1)} %get-tuple-element.48), channel_id=1, source_target_pairs={{0,3},{1,0},{2,1},{3,2},{4,7},{5,4},{6,5},{7,6},{8,11},{9,8},{10,9... | collective-permute-start | bytes 786440 | tf_op jit(solution)/shard_map/ppermute | solution.py:125
  84.5 21.7 %collective-permute-start.14 = (bf16[256,512]{1,0:T(8,128)(2,1)S(1)}, bf16[256,512]{1,0:T(8,128)(2,1)S(1)}, u32[]{:S(2)}, u32[]{:S(2)}) collective-permute-start(bf16[256,512]{1,0:T(8,128)(2,1)S(1)} %get-tuple-element.48), channel_id=1, source_target_pairs={{0,2},{1,3},{2,0},{3,1},{4,6},{5,7},{6,4},{7,5},{8,10},{9,11},{10,... | collective-permute-start | bytes 786440 | tf_op jit(solution)/shard_map/ppermute | solution.py:125
  84.5 21.9 %collective-permute-start.13 = (bf16[256,512]{1,0:T(8,128)(2,1)S(1)}, bf16[256,512]{1,0:T(8,128)(2,1)S(1)}, u32[]{:S(2)}, u32[]{:S(2)}) collective-permute-start(bf16[256,512]{1,0:T(8,128)(2,1)S(1)} %get-tuple-element.48), channel_id=1, source_target_pairs={{0,1},{1,2},{2,3},{3,0},{4,5},{5,6},{6,7},{7,4},{8,9},{9,10},{10,1... | collective-permute-start | bytes 786440 | tf_op jit(solution)/shard_map/ppermute | solution.py:125
